TPU v7x, 32 devices: a whole 2x2x4 slice. The times are simulated.
32 devices in a mesh: clips: 2 (over y), space: 8 (over z, x), tm: 2 (over core).
Axes of the slice: x: 2, y: 2, z: 4, core: 2. Of those that a mesh axis runs over, the one named last changes fastest.
Arguments:
- frames: bfloat16 [2, 2, 16, 112, 192], P('clips', 'tm', 'space'), parts along dimension 0, may hold values from -100 to 100
- norm1_gain: float32 [192], replicated, may hold values from 0.1 to 1.9
- conv1_weight: bfloat16 [3, 3, 3, 192, 192], replicated, may hold values from -0.078125 to 0.078125
- conv1_bias: float32 [192], replicated, may hold values from -3 to 3
- norm2_gain: float32 [192], replicated, may hold values from 0.1 to 1.9
- conv2_weight: bfloat16 [3, 3, 3, 192, 192], replicated, may hold values from -0.078125 to 0.078125
- conv2_bias: float32 [192], replicated, may hold values from -3 to 3
- attn_gain: float32 [192], replicated, may hold values from 0.5 to 3
- w_query: bfloat16 [192, 192], replicated, may hold values from -3 to 3
- b_query: float32 [192], replicated, may hold values from -4 to 4
- w_key: bfloat16 [192, 192], replicated, may hold values from -1 to 2
- w_value: bfloat16 [192, 192], replicated, may hold values from -0.4375 to 0.4375
- b_value: float32 [192], replicated, may hold values from -3 to 3
- w_out: bfloat16 [192, 192], replicated, may hold values from -0.4375 to 0.4375
- b_out: float32 [192], replicated, may hold values from -3 to 3
Outputs:
- decoded: float32 [2, 2, 16, 112, 192], P('clips', 'tm', 'space'), parts along dimension 0
There are 2 independent parts, one for each index of `clips`. A program takes and returns all parts, laid end to end along the dimension named above; an argument that names none is the same for every part. Nothing has to cross between parts.
All inputs are finite; a program needn't handle non-finite values.
Results may differ from a plain program's by a relative error of at most 0.02.
Values may be sent and summed in bfloat16 or wider, within the bound.
No kernel may reach another device: no remote copies, remote signals or barrier semaphores. Data moves between devices by JAX's collectives and lax.ppermute only.
A program may use at most 128 MiB of HBM per device.

v0:
```python
import math

import jax
import jax.numpy as jnp
from jax import lax
from jax.sharding import PartitionSpec as P

epsilon = 1e-06


def shifted(block, axis, distance):
    devices = range(lax.axis_size(axis))
    route = [((i - distance) % len(devices), i) for i in devices]
    return lax.ppermute(block, axis, route)


def extended(value, sides, width):
    for axis, dim in sides:
        size, length = (lax.axis_size(axis), value.shape[dim])
        up = [(i, (i + 1) % size) for i in range(size - 1)]
        down = [(j, i) for i, j in up]
        last = lax.slice_in_dim(value, length - width, length, axis=dim)
        first = lax.slice_in_dim(value, 0, width, axis=dim)
        before = lax.ppermute(last, axis, up)
        after = lax.ppermute(first, axis, down)
        value = jnp.concatenate([before, value, after], axis=dim)
    return value


def rms_scale(values, gain):
    return values * lax.rsqrt(jnp.mean(values * values, axis=-1, keepdims=True) + epsilon) * gain


def causal_conv(inputs, weight, bias):
    frame_count, row_count, col_count, channels = inputs.shape
    is_first = lax.axis_index("tm") == 0
    remote = shifted(inputs, "tm", 1)
    earlier = jnp.concatenate([jnp.zeros_like(remote), remote[:-1]], axis=0)
    previous = jnp.where(is_first, earlier, remote)
    paired = extended(jnp.stack([inputs, previous]), (("space", 2),), 1)
    current = paired[0]
    previous = paired[1]
    oldest = jnp.concatenate([jnp.zeros_like(current), current[:-1]], axis=0)
    tap_list = []
    for source in (oldest, previous, current):
        widened = jnp.pad(source, ((0, 0), (0, 0), (1, 1), (0, 0)))
        for row_off in range(3):
            for col_off in range(3):
                tap_list.append(
                    widened[:, row_off : row_off + row_count, col_off : col_off + col_count, :]
                )
    patches = jnp.concatenate(tap_list, axis=-1).reshape(
        frame_count * row_count * col_count, 27 * channels
    )
    summed = jnp.dot(
        patches, weight.reshape(27 * channels, channels), preferred_element_type=jnp.float32
    )
    return summed.reshape(frame_count, row_count, col_count, channels) + bias


def absorb(running, queries, key_rows):
    top_old, total_old, accum = running
    scores = jnp.einsum("fqc,fkc->fqk", queries, key_rows, preferred_element_type=jnp.float32)
    top_new = jnp.maximum(top_old, jnp.max(scores, axis=-1))
    weights = jnp.exp(scores - top_new[..., None])
    total_new = jnp.sum(weights, axis=-1)
    accum = jnp.einsum(
        "fqk,fkc->fqc", weights.astype(jnp.bfloat16), key_rows, preferred_element_type=jnp.float32
    )
    return (top_new, total_new, accum)


def local(
    frames,
    norm1_gain,
    conv1_weight,
    conv1_bias,
    norm2_gain,
    conv2_weight,
    conv2_bias,
    attn_gain,
    w_query,
    b_query,
    w_key,
    w_value,
    b_value,
    w_out,
    b_out,
):
    local_frames = frames[:, 0]
    frame_count, row_count, col_count, channels = local_frames.shape
    frame_values = local_frames.astype(jnp.float32)
    first_act = jax.nn.silu(rms_scale(frame_values, norm1_gain)).astype(jnp.bfloat16)
    first_out = causal_conv(first_act, conv1_weight, conv1_bias)
    second_act = jax.nn.silu(rms_scale(first_out, norm2_gain)).astype(jnp.bfloat16)
    second_out = causal_conv(second_act, conv2_weight, conv2_bias)
    residual = frame_values + second_out
    normed = rms_scale(residual, attn_gain).astype(jnp.bfloat16)
    token_count = row_count * col_count
    flat = normed.reshape(frame_count * token_count, channels)
    query = (jnp.dot(flat, w_query, preferred_element_type=jnp.float32) + b_query).astype(
        jnp.bfloat16
    )
    folded = (
        jnp.dot(query, w_key.T, preferred_element_type=jnp.float32) * (1.0 / math.sqrt(channels))
    ).astype(jnp.bfloat16)
    folded = folded.reshape(frame_count, token_count, channels)
    initial = (
        jnp.full((frame_count, token_count), -1e30, jnp.float32),
        jnp.zeros((frame_count, token_count), jnp.float32),
        jnp.zeros((frame_count, token_count, channels), jnp.float32),
    )
    slot_queries = folded

    def absorb_one(running, received, offset, slot_queries=slot_queries):
        return absorb(running, slot_queries, received.reshape(1, -1, channels))

    start_state = tuple((item for item in initial))
    results = [
        absorb_one(
            start_state, lax.all_gather(normed[0], "space", axis=0, tiled=True), jnp.int32(0)
        )
    ]
    total = jnp.concatenate([item[1] for item in results], axis=0)
    accum = jnp.concatenate([item[2] for item in results], axis=0)
    mixed = (accum / total[..., None]).astype(jnp.bfloat16).reshape(-1, channels)
    value = (jnp.dot(mixed, w_value, preferred_element_type=jnp.float32) + b_value).astype(
        jnp.bfloat16
    )
    decoded = (
        residual.reshape(-1, channels)
        + jnp.dot(value, w_out, preferred_element_type=jnp.float32)
        + b_out
    )
    return decoded.reshape(frame_count, 1, row_count, col_count, channels)


def solution(mesh):
    placed = (
        P("clips", "tm", "space", None, None),
        P(),
        P(),
        P(),
        P(),
        P(),
        P(),
        P(),
        P(),
        P(),
        P(),
        P(),
        P(),
        P(),
        P(),
    )
    return jax.shard_map(
        local,
        mesh=mesh,
        in_specs=placed,
        out_specs=P("clips", "tm", "space", None, None),
        check_vma=False,
    )
```

profile of v0, /device:TPU:0, one launch (start us, length us, event | category | flops | bytes accessed | tf_op | source)
XLA Modules:
  0.0 90.7 jit_solution(12605600663512206442)
XLA Ops:
  0.0 1.1 %copy.31 = bf16[1,1,2,112,192]{4,3,2,1,0:T(8,128)(2,1)S(1)} copy(bf16[1,1,2,112,192]{3,4,2,1,0:T(8,128)(2,1)} %param.15) | data formatting | bytes 172032 | tf_op args[0]
  1.3 0.8 fusion.31
  2.1 0.5 collective-permute-start
  2.6 0.8 fusion.38
  3.7 4.8 %collective-permute-start.1 = (bf16[2,1,1,112,192]{4,3,2,1,0:T(8,128)(2,1)S(1)}, bf16[2,1,1,112,192]{4,3,2,1,0:T(8,128)(2,1)S(1)}, u32[]{:S(2)}, u32[]{:S(2)}) collective-permute-start(bf16[2,1,1,112,192]{4,3,2,1,0:T(8,128)(2,1)S(1)} %get-tuple-element.47), channel_id=1, source_target_pairs={{0,2},{2,4},{4,6},{6,8},{8,10},{10,12},{12,14},{1,3},{3,5},{5,7},{... | collective-permute-start | bytes 258056 | tf_op jit(solution)/shard_map/ppermute | solution.py:24
  8.4 1.3 %collective-permute-start.2 = (bf16[2,1,1,112,192]{4,3,2,1,0:T(8,128)(2,1)S(1)}, bf16[2,1,1,112,192]{4,3,2,1,0:T(8,128)(2,1)S(1)}, u32[]{:S(2)}, u32[]{:S(2)}) collective-permute-start(bf16[2,1,1,112,192]{4,3,2,1,0:T(8,128)(2,1)S(1)} %get-tuple-element.48), channel_id=1, source_target_pairs={{2,0},{4,2},{6,4},{8,6},{10,8},{12,10},{14,12},{3,1},{5,3},{7,5},{... | collective-permute-start | bytes 258056 | tf_op jit(solution)/shard_map/ppermute | solution.py:25
  9.8 1.3 %collective-permute-done.1 = bf16[2,1,1,112,192]{4,3,2,1,0:T(8,128)(2,1)S(1)} collective-permute-done((bf16[2,1,1,112,192]{4,3,2,1,0:T(8,128)(2,1)S(1)}, bf16[2,1,1,112,192]{4,3,2,1,0:T(8,128)(2,1)S(1)}, u32[]{:S(2)}, u32[]{:S(2)}) %collective-permute-start.1) | collective-permute-done | bytes 86048 | tf_op jit(solution)/shard_map/ppermute | solution.py:24
  11.1 4.1 %collective-permute-done.2 = bf16[2,1,1,112,192]{4,3,2,1,0:T(8,128)(2,1)S(1)} collective-permute-done((bf16[2,1,1,112,192]{4,3,2,1,0:T(8,128)(2,1)S(1)}, bf16[2,1,1,112,192]{4,3,2,1,0:T(8,128)(2,1)S(1)}, u32[]{:S(2)}, u32[]{:S(2)}) %collective-permute-start.2) | collective-permute-done | bytes 86048 | tf_op jit(solution)/shard_map/ppermute | solution.py:25
  15.4 1.2 %pad_slice_fusion.16 = (bf16[1,2,112,192]{3,2,1,0:T(8,128)(2,1)S(1)}, bf16[1,2,112,192]{3,2,1,0:T(8,128)(2,1)S(1)}, bf16[1,2,112,192]{3,2,1,0:T(8,128)(2,1)S(1)}...) fusion(bf16[1,4,112,192]{3,2,1,0:T(8,128)(2,1)S(1)} %get-tuple-, ...), kind=kLoop, calls=%fused_computation.67 | loop fusion | bytes 2695168 | tf_op jit(solution)/shard_map/slice | solution.py:50
  16.8 5.4 %concatenate.13 = bf16[1,2,112,5184]{3,2,1,0:T(8,128)(2,1)} concatenate(bf16[1,2,112,192]{3,2,1,0:T(8,128)(2,1)S(1)} %pad.24, bf16[1,2,112,192]{3,2,1,0:T(8,128)(2,1)S(1)} %pad.25, bf16[1,2,112,192]{3,2,1,0:T(8,128)(2,1)S(1)} %pad.26, bf16[1,2,112,192]{3,2,1,0:T(8,128)(2,1)S(1)} %pad.24, bf16[1,2,112,192]{3,2,1,0:T(8,128)(2,1)S(1)} %pad.25, bf16[1,2,112,192]{3,2,1,0:T(8,128)(2,1)S(1)} %pad.26, ...), dimensions={3} | concatenate | bytes 4644864 | tf_op jit(solution)/shard_map/concatenate | solution.py:52
  22.3 2.5 %multiply_reduce_fusion.1 = (f32[2,112]{1,0:T(2,128)S(1)}, f32[2,112,192]{2,1,0:T(8,128)S(1)}) fusion(f32[192]{0:T(256)S(1)} %copy-done.7, bf16[5184,192,1]{1,0,2:T(8,128)(2,1)S(1)} %bitcast.83, bf16[1,2,112,5184]{3,2,1,0:T(8,128)(2,1)} %concatenate.13), kind=kOutput, calls=%fused_computation.54 | convolution fusion | flops 446035744 | bytes 4486784 | tf_op jit(solution)/shard_map/dot_general | solution.py:55
  24.8 0.1 fusion.55
  25.2 1.2 %collective-permute-done.3 = bf16[1,2,112,192]{3,2,1,0:T(8,128)(2,1)S(1)} collective-permute-done((bf16[1,2,112,192]{3,2,1,0:T(8,128)(2,1)S(1)}, bf16[1,2,112,192]{3,2,1,0:T(8,128)(2,1)S(1)}, u32[]{:S(2)}, u32[]{:S(2)}) %collective-permute-start.3) | collective-permute-done | bytes 86048 | tf_op jit(solution)/shard_map/ppermute | solution.py:14
  26.4 4.4 %collective-permute-start.4 = (bf16[2,1,1,112,192]{4,3,2,1,0:T(8,128)(2,1)S(1)}, bf16[2,1,1,112,192]{4,3,2,1,0:T(8,128)(2,1)S(1)}, u32[]{:S(2)}, u32[]{:S(2)}) collective-permute-start(bf16[2,1,1,112,192]{4,3,2,1,0:T(8,128)(2,1)S(1)} %get-tuple-element.27), channel_id=1, source_target_pairs={{0,2},{2,4},{4,6},{6,8},{8,10},{10,12},{12,14},{1,3},{3,5},{5,7},{... | collective-permute-start | bytes 258056 | tf_op jit(solution)/shard_map/ppermute | solution.py:24
  30.8 1.3 %collective-permute-start.5 = (bf16[2,1,1,112,192]{4,3,2,1,0:T(8,128)(2,1)S(1)}, bf16[2,1,1,112,192]{4,3,2,1,0:T(8,128)(2,1)S(1)}, u32[]{:S(2)}, u32[]{:S(2)}) collective-permute-start(bf16[2,1,1,112,192]{4,3,2,1,0:T(8,128)(2,1)S(1)} %get-tuple-element.28), channel_id=1, source_target_pairs={{2,0},{4,2},{6,4},{8,6},{10,8},{12,10},{14,12},{3,1},{5,3},{7,5},{... | collective-permute-start | bytes 258056 | tf_op jit(solution)/shard_map/ppermute | solution.py:25
  32.1 1.4 %collective-permute-done.4 = bf16[2,1,1,112,192]{4,3,2,1,0:T(8,128)(2,1)S(1)} collective-permute-done((bf16[2,1,1,112,192]{4,3,2,1,0:T(8,128)(2,1)S(1)}, bf16[2,1,1,112,192]{4,3,2,1,0:T(8,128)(2,1)S(1)}, u32[]{:S(2)}, u32[]{:S(2)}) %collective-permute-start.4) | collective-permute-done | bytes 86048 | tf_op jit(solution)/shard_map/ppermute | solution.py:24
  33.5 4.1 %collective-permute-done.5 = bf16[2,1,1,112,192]{4,3,2,1,0:T(8,128)(2,1)S(1)} collective-permute-done((bf16[2,1,1,112,192]{4,3,2,1,0:T(8,128)(2,1)S(1)}, bf16[2,1,1,112,192]{4,3,2,1,0:T(8,128)(2,1)S(1)}, u32[]{:S(2)}, u32[]{:S(2)}) %collective-permute-start.5) | collective-permute-done | bytes 86048 | tf_op jit(solution)/shard_map/ppermute | solution.py:25
  37.8 0.9 %pad_slice_fusion.4 = (bf16[1,2,112,192]{3,2,1,0:T(8,128)(2,1)S(1)}, bf16[1,2,112,192]{3,2,1,0:T(8,128)(2,1)S(1)}, bf16[1,2,112,192]{3,2,1,0:T(8,128)(2,1)S(1)},...) fusion(bf16[1,4,112,192]{3,2,1,0:T(8,128)(2,1)S(1)} %get-tuple-, ...), kind=kLoop, calls=%fused_computation.55 | loop fusion | bytes 1347584 | tf_op jit(solution)/shard_map/slice | solution.py:50
  38.7 1.0 %pad_slice_fusion.10 = (bf16[1,2,112,192]{3,2,1,0:T(8,128)(2,1)}, bf16[1,2,112,192]{3,2,1,0:T(8,128)(2,1)}, bf16[1,2,112,192]{3,2,1,0:T(8,128)(2,1)}, bf16[1,2,1...) fusion(bf16[1,4,112,192]{3,2,1,0:T(8,128)(2,1)S(1)} %get-tuple-, ...), kind=kLoop, calls=%fused_computation.61 | loop fusion | bytes 1347584 | tf_op jit(solution)/shard_map/slice | solution.py:50
  39.7 5.4 %concatenate.15 = bf16[1,2,112,5184]{3,2,1,0:T(8,128)(2,1)} concatenate(bf16[1,2,112,192]{3,2,1,0:T(8,128)(2,1)S(1)} %pad.24, bf16[1,2,112,192]{3,2,1,0:T(8,128)(2,1)S(1)} %pad.25, bf16[1,2,112,192]{3,2,1,0:T(8,128)(2,1)S(1)} %pad.26, bf16[1,2,112,192]{3,2,1,0:T(8,128)(2,1)S(1)} %pad.24, bf16[1,2,112,192]{3,2,1,0:T(8,128)(2,1)S(1)} %pad.25, bf16[1,2,112,192]{3,2,1,0:T(8,128)(2,1)S(1)} %pad.26, ...), dimensions={3} | concatenate | bytes 4644864 | tf_op jit(solution)/shard_map/concatenate | solution.py:52
  45.1 3.3 %multiply_reduce_fusion = (f32[2,112]{1,0:T(2,128)S(1)}, f32[2,112,192]{2,1,0:T(8,128)S(1)}) fusion(f32[192]{0:T(256)S(1)} %copy-done.8, bf16[5184,192,1]{1,0,2:T(8,128)(2,1)} %bitcast.86, bf16[1,2,112,5184]{3,2,1,0:T(8,128)(2,1)} %concatenate.15, bf16[1,1,2,112,192]{4,3,2,1,0:T(8,128)(2,1)S(1)} %copy.31), kind=kOutput, calls=%fused_computation.52 | convolution fusion | flops 446121760 | bytes 4572800 | tf_op jit(solution)/shard_map/dot_general | solution.py:55
  48.7 0.8 copy.38
  49.5 32.1 %all_gather.3 = bf16[16,112,192]{1,2,0:T(8,128)(2,1)S(1)} all-gather(bf16[2,112,192]{1,2,0:T(8,128)(2,1)S(1)} %copy.36), channel_id=1, replica_groups=mesh['clips'=2,'space'=8,'tm'=2] {'space'}, dimensions={0}, use_global_device_ids=true | all-gather | bytes 774144 | tf_op jit(solution)/shard_map/all_gather | solution.py:121
  81.5 0.5 copy.37
  82.0 1.8 %reshape.197 = bf16[1792,192]{0,1:T(8,128)(2,1)} reshape(bf16[16,112,192]{1,0,2:T(8,128)(2,1)S(1)} %copy.37) | data formatting | bytes 1376256 | tf_op jit(solution)/shard_map/reshape.9
  83.9 1.4 %fusion.19 = bf16[224,192]{0,1:T(8,128)(2,1)S(1)} fusion(bf16[192,192]{1,0:T(8,128)(2,1)} %param.25, bf16[224,192]{1,0:T(8,128)(2,1)S(1)} %bitcast.84, bf16[192,192]{1,0:T(8,128)(2,1)} %param.23, f32[192]{0:T(256)} %param.24), kind=kOutput, calls=%fused_computation.19 | convolution fusion | flops 33202176 | bytes 320256 | tf_op jit(solution)/shard_map/dot_general | solution.py:105
  85.3 1.6 %fusion.43 = (f32[224]{0:T(256)S(1)}, f32[224,1792]{1,0:T(8,128)S(1)}) fusion(bf16[224,192]{0,1:T(8,128)(2,1)S(1)} %fusion.19, bf16[1792,192]{0,1:T(8,128)(2,1)} %reshape.197), kind=kOutput, calls=%fused_computation.93 | convolution fusion | flops 154541856 | bytes 2380672 | tf_op jit(solution)/shard_map/fqc,fkc->fqk/dot_general | solution.py:63
  86.9 0.4 fusion.4
  87.3 1.1 %fusion.17 = bf16[224,192]{0,1:T(8,128)(2,1)} fusion(bf16[1792,192]{0,1:T(8,128)(2,1)S(1)} %copy-done.1, f32[224,1792]{1,0:T(8,128)S(1)} %get-tuple-element.56, f32[224]{0:T(256)S(1)} %broadcast_maximum_fusion, f32[224]{0:T(256)S(1)} %fusion.4), kind=kOutput, calls=%fused_computation.17 | convolution fusion | flops 155029504 | bytes 2381568 | tf_op jit(solution)/shard_map/fqk,fkc->fqc/dot_general | solution.py:67
  88.4 1.4 %fusion.15 = f32[224,192]{0,1:T(8,128)S(1)} fusion(f32[224,192]{0,1:T(8,128)S(1)} %copy-done.2, bf16[192,192]{1,0:T(8,128)(2,1)} %param.28, bf16[224,192]{0,1:T(8,128)(2,1)} %fusion.17, bf16[192,192]{1,0:T(8,128)(2,1)} %param.26, f32[192]{0:T(256)S(1)} %copy-done.5, f32[192]{0:T(256)S(1)} %copy-done.6), kind=kOutput, calls=%fused_computation.12 | convolution fusion | flops 33202176 | bytes 579072 | tf_op jit(solution)/shard_map/dot_general | solution.py:132
  89.8 0.2 reshape.198
  90.0 0.7 copy.39
  (41 shorter events, 1.4 us)
Async XLA Ops:
  0.0 22.2 %copy-start = (bf16[3,3,3,192,192]{4,3,2,1,0:T(8,128)(2,1)S(1)}, bf16[3,3,3,192,192]{4,3,2,1,0:T(8,128)(2,1)}, u32[]{:S(2)}) copy-start(bf16[3,3,3,192,192]{4,3,2,1,0:T(8,128)(2,1)} %param.17) | copy-start | bytes 5971972
  2.1 1.5 %collective-permute-start = (bf16[1,2,112,192]{3,2,1,0:T(8,128)(2,1)S(1)}, bf16[1,2,112,192]{3,2,1,0:T(8,128)(2,1)S(1)}, u32[]{:S(2)}, u32[]{:S(2)}) collective-permute-start(bf16[1,2,112,192]{3,2,1,0:T(8,128)(2,1)S(1)} %fusion.31), channel_id=1, source_target_pairs={{1,0},{0,1},{3,2},{2,3},{5,4},{4,5},{7,6},{6,7},{9,8},{8,9},{11,10... | collective-permute-start | bytes 258056 | tf_op jit(solution)/shard_map/ppermute | solution.py:14
  3.7 7.5 %collective-permute-start.1 = (bf16[2,1,1,112,192]{4,3,2,1,0:T(8,128)(2,1)S(1)}, bf16[2,1,1,112,192]{4,3,2,1,0:T(8,128)(2,1)S(1)}, u32[]{:S(2)}, u32[]{:S(2)}) collective-permute-start(bf16[2,1,1,112,192]{4,3,2,1,0:T(8,128)(2,1)S(1)} %get-tuple-element.47), channel_id=1, source_target_pairs={{0,2},{2,4},{4,6},{6,8},{8,10},{10,12},{12,14},{1,3},{3,5},{5,7},{... | collective-permute-start | bytes 258056 | tf_op jit(solution)/shard_map/ppermute | solution.py:24
  8.4 6.8 %collective-permute-start.2 = (bf16[2,1,1,112,192]{4,3,2,1,0:T(8,128)(2,1)S(1)}, bf16[2,1,1,112,192]{4,3,2,1,0:T(8,128)(2,1)S(1)}, u32[]{:S(2)}, u32[]{:S(2)}) collective-permute-start(bf16[2,1,1,112,192]{4,3,2,1,0:T(8,128)(2,1)S(1)} %get-tuple-element.48), channel_id=1, source_target_pairs={{2,0},{4,2},{6,4},{8,6},{10,8},{12,10},{14,12},{3,1},{5,3},{7,5},{... | collective-permute-start | bytes 258056 | tf_op jit(solution)/shard_map/ppermute | solution.py:25
  16.8 5.4 %copy-start.7 = (f32[192]{0:T(256)S(1)}, f32[192]{0:T(256)}, u32[]{:S(2)}) copy-start(f32[192]{0:T(256)} %param.18) | copy-start | bytes 2308
  22.3 2.6 %copy-start.3 = (f32[192]{0:T(256)S(1)}, f32[192]{0:T(256)}, u32[]{:S(2)}) copy-start(f32[192]{0:T(256)} %param.19) | copy-start | bytes 2308
  25.0 1.4 %collective-permute-start.3 = (bf16[1,2,112,192]{3,2,1,0:T(8,128)(2,1)S(1)}, bf16[1,2,112,192]{3,2,1,0:T(8,128)(2,1)S(1)}, u32[]{:S(2)}, u32[]{:S(2)}) collective-permute-start(bf16[1,2,112,192]{3,2,1,0:T(8,128)(2,1)S(1)} %fusion.55), channel_id=1, source_target_pairs={{1,0},{0,1},{3,2},{2,3},{5,4},{4,5},{7,6},{6,7},{9,8},{8,9},{11,10... | collective-permute-start | bytes 258056 | tf_op jit(solution)/shard_map/ppermute | solution.py:14
  26.4 7.1 %collective-permute-start.4 = (bf16[2,1,1,112,192]{4,3,2,1,0:T(8,128)(2,1)S(1)}, bf16[2,1,1,112,192]{4,3,2,1,0:T(8,128)(2,1)S(1)}, u32[]{:S(2)}, u32[]{:S(2)}) collective-permute-start(bf16[2,1,1,112,192]{4,3,2,1,0:T(8,128)(2,1)S(1)} %get-tuple-element.27), channel_id=1, source_target_pairs={{0,2},{2,4},{4,6},{6,8},{8,10},{10,12},{12,14},{1,3},{3,5},{5,7},{... | collective-permute-start | bytes 258056 | tf_op jit(solution)/shard_map/ppermute | solution.py:24
  30.8 6.8 %collective-permute-start.5 = (bf16[2,1,1,112,192]{4,3,2,1,0:T(8,128)(2,1)S(1)}, bf16[2,1,1,112,192]{4,3,2,1,0:T(8,128)(2,1)S(1)}, u32[]{:S(2)}, u32[]{:S(2)}) collective-permute-start(bf16[2,1,1,112,192]{4,3,2,1,0:T(8,128)(2,1)S(1)} %get-tuple-element.28), channel_id=1, source_target_pairs={{2,0},{4,2},{6,4},{8,6},{10,8},{12,10},{14,12},{3,1},{5,3},{7,5},{... | collective-permute-start | bytes 258056 | tf_op jit(solution)/shard_map/ppermute | solution.py:25
  39.7 5.4 %copy-start.8 = (f32[192]{0:T(256)S(1)}, f32[192]{0:T(256)}, u32[]{:S(2)}) copy-start(f32[192]{0:T(256)} %param.21) | copy-start | bytes 2308
  45.1 3.4 %copy-start.4 = (f32[192]{0:T(256)S(1)}, f32[192]{0:T(256)}, u32[]{:S(2)}) copy-start(f32[192]{0:T(256)} %param.22) | copy-start | bytes 2308
  83.8 3.4 %copy-start.1 = (bf16[1792,192]{0,1:T(8,128)(2,1)S(1)}, bf16[1792,192]{0,1:T(8,128)(2,1)}, u32[]{:S(2)}) copy-start(bf16[1792,192]{0,1:T(8,128)(2,1)} %reshape.197) | copy-start | bytes 2064388
  86.9 1.6 %copy-start.2 = (f32[224,192]{0,1:T(8,128)S(1)}, f32[224,192]{0,1:T(8,128)}, u32[]{:S(2)}) copy-start(f32[224,192]{0,1:T(8,128)} %copy.38) | copy-start | bytes 516100
  86.9 1.6 %copy-start.5 = (f32[192]{0:T(256)S(1)}, f32[192]{0:T(256)}, u32[]{:S(2)}) copy-start(f32[192]{0:T(256)} %param.29) | copy-start | bytes 2308
  86.9 1.5 %copy-start.6 = (f32[192]{0:T(256)S(1)}, f32[192]{0:T(256)}, u32[]{:S(2)}) copy-start(f32[192]{0:T(256)} %param.27) | copy-start | bytes 2308
where the time goes:
time: 91.8 us; the launch traced here: 90.7 us
  blocking collectives  32.1 us (35%)
  local copies, waits for them, and re-layouts  19.6 us (21%)
  starting transfers between devices  12.3 us (13%)
  waiting for transfers between devices  12.2 us (13%)
  matrix products  11.4 us (12%)
  other arithmetic  2.82 us (3%)
    all_gather x1, blocking collectives, local(): lax.all_gather(normed[0], 'space', axis=0, tiled=True)  32.1 us
    concatenate x2, local copies, waits for them, and re-layouts, causal_conv(): jnp.concatenate(tap_list, axis=-1)  10.8 us
    ppermute x2, starting transfers between devices, extended(): before = lax.ppermute(last, axis, up)  9.11 us
    ppermute x2, waiting for transfers between devices, extended(): after = lax.ppermute(first, axis, down)  8.24 us
    dot_general x2, matrix products, causal_conv(): jnp.dot(patches, weight.reshape(27 * channels, channels), preferred_eleme...  5.88 us
    slice x5, local copies, waits for them, and re-layouts, causal_conv(): widened[:, row_off:row_off + row_count, col_off:col_off + col_count, :]  3.21 us
    ppermute x2, waiting for transfers between devices, extended(): before = lax.ppermute(last, axis, up)  2.7 us
    ppermute x2, starting transfers between devices, extended(): after = lax.ppermute(first, axis, down)  2.58 us
  transfers between devices with their start and end apart: 6, of which 6 were waited for; matrix products, arithmetic and copies ran while one was open for 1% of the time, Pallas kernels for 0%

commit v1 on v0

v1 whole, which is shorter than its diff:
```python
import math

import jax
import jax.numpy as jnp
from jax import lax
from jax.sharding import PartitionSpec as P

epsilon = 1e-06
HALO = 2


def rms_scale(values, gain):
    return values * lax.rsqrt(jnp.mean(values * values, axis=-1, keepdims=True) + epsilon) * gain


def conv_rows(source, taps):
    return lax.conv_general_dilated(
        source,
        taps,
        window_strides=(1, 1),
        padding=((0, 0), (1, 1)),
        dimension_numbers=("NHWC", "HWIO", "NHWC"),
        preferred_element_type=jnp.float32,
    )


def causal_time_conv(seq, weight):
    frame_total = seq.shape[0]
    out = None
    for p in range(3):
        lag = 2 - p
        if lag >= frame_total:
            continue
        part = conv_rows(seq[: frame_total - lag], weight[p])
        if lag:
            part = jnp.pad(part, ((lag, 0), (0, 0), (0, 0), (0, 0)))
        out = part if out is None else out + part
    return out


def local(
    frames,
    norm1_gain,
    conv1_weight,
    conv1_bias,
    norm2_gain,
    conv2_weight,
    conv2_bias,
    attn_gain,
    w_query,
    b_query,
    w_key,
    w_value,
    b_value,
    w_out,
    b_out,
):
    own = frames[:, 0]
    frame_count, row_count, col_count, channels = own.shape
    bands = lax.axis_size("space")
    band = lax.axis_index("space")
    is_first = lax.axis_index("tm") == 0
    height = bands * row_count

    partner = lax.ppermute(own, "tm", [(0, 1), (1, 0)])
    even = jnp.where(is_first, own, partner)
    odd = jnp.where(is_first, partner, own)
    seq = jnp.stack([even, odd], axis=1).reshape(2 * frame_count, row_count, col_count, channels)

    up = [(i, i + 1) for i in range(bands - 1)]
    down = [(i + 1, i) for i in range(bands - 1)]
    above = lax.ppermute(seq[:, row_count - HALO :], "space", up)
    below = lax.ppermute(seq[:, :HALO], "space", down)
    ext = jnp.concatenate([above, seq, below], axis=1)

    first_act = jax.nn.silu(rms_scale(ext.astype(jnp.float32), norm1_gain)).astype(jnp.bfloat16)
    first_out = causal_time_conv(first_act, conv1_weight) + conv1_bias
    rows = band * row_count - 1 + lax.broadcasted_iota(jnp.int32, (1, row_count + 2, 1, 1), 1)
    inside = (rows >= 0) & (rows < height)
    second_act = jnp.where(
        inside, jax.nn.silu(rms_scale(first_out, norm2_gain)), 0.0
    ).astype(jnp.bfloat16)

    pairs = second_act.reshape(frame_count, 2, row_count + 2, col_count, channels)
    sa_even = pairs[:, 0]
    sa_odd = pairs[:, 1]
    zero = jnp.zeros_like(sa_even[:1])
    odd_before = jnp.concatenate([zero, sa_odd[:-1]], axis=0)
    even_before = jnp.concatenate([zero, sa_even[:-1]], axis=0)
    current = jnp.where(is_first, sa_even, sa_odd)
    previous = jnp.where(is_first, odd_before, sa_even)
    second_out = conv_rows(current, conv2_weight[2]) + conv_rows(previous, conv2_weight[1])
    if frame_count > 1:
        oldest = jnp.where(is_first, even_before, odd_before)
        second_out = second_out + conv_rows(oldest, conv2_weight[0])
    second_out = second_out + conv2_bias

    frame_values = own.astype(jnp.float32)
    residual = frame_values + second_out
    normed = rms_scale(residual, attn_gain).astype(jnp.bfloat16)
    token_count = row_count * col_count
    flat = normed.reshape(frame_count * token_count, channels)
    query = (jnp.dot(flat, w_query, preferred_element_type=jnp.float32) + b_query).astype(
        jnp.bfloat16
    )
    folded = (
        jnp.dot(query, w_key.T, preferred_element_type=jnp.float32) * (1.0 / math.sqrt(channels))
    ).astype(jnp.bfloat16)
    folded = folded.reshape(frame_count, token_count, channels)

    keys = lax.all_gather(normed, "space", axis=1, tiled=True)
    keys = keys.reshape(frame_count, height * col_count, channels)
    scores = jnp.einsum("fqc,fkc->fqk", folded, keys, preferred_element_type=jnp.float32)
    top = jnp.max(scores, axis=-1, keepdims=True)
    weights = jnp.exp(scores - top)
    total = jnp.sum(weights, axis=-1, keepdims=True)
    accum = jnp.einsum(
        "fqk,fkc->fqc", weights.astype(jnp.bfloat16), keys, preferred_element_type=jnp.float32
    )
    mixed = (accum / total).astype(jnp.bfloat16).reshape(-1, channels)
    value = (jnp.dot(mixed, w_value, preferred_element_type=jnp.float32) + b_value).astype(
        jnp.bfloat16
    )
    decoded = (
        residual.reshape(-1, channels)
        + jnp.dot(value, w_out, preferred_element_type=jnp.float32)
        + b_out
    )
    return decoded.reshape(frame_count, 1, row_count, col_count, channels)


def solution(mesh):
    placed = (P("clips", "tm", "space", None, None),) + (P(),) * 14
    return jax.shard_map(
        local,
        mesh=mesh,
        in_specs=placed,
        out_specs=P("clips", "tm", "space", None, None),
        check_vma=False,
    )
```

time: 91.8 us -> 69.8 us (0.76)
  local copies, waits for them, and re-layouts: 19.6 us -> 8.25 us
  starting transfers between devices: 12.3 us -> 7.13 us
  matrix products: 11.4 us -> 6.79 us
  waiting for transfers between devices: 12.2 us -> 8.78 us
  other arithmetic: 2.82 us -> 5.01 us
    concatenate x2 -> x0, local copies, waits for them, and re-layouts: 10.8 us -> none  [causal_conv(): jnp.concatenate(tap_list, axis=-1)]
    dot_general x4 -> x2, matrix products: 8.61 us -> 1 us  [the longest x1 0.51 us: local(): jnp.einsum('fqk,fkc->fqc', weights.astype(jnp.bfloat16), keys, preferred_...]
    ppermute x6 -> x3, starting transfers between devices: 12.3 us -> 7.13 us  [the longest x1 5.39 us: local(): above = lax.ppermute(seq[:, row_count - HALO:], 'space', up)]
    conv_general_dilated x0 -> x4, matrix products: none -> 4.99 us  [conv_rows(): lax.conv_general_dilated(source, taps, window_strides=(1, 1), padding=((0...]
    ppermute x6 -> x3, waiting for transfers between devices: 12.2 us -> 8.78 us  [the longest x1 4.38 us: local(): above = lax.ppermute(seq[:, row_count - HALO:], 'space', up)]
    slice x5 -> x2, local copies, waits for them, and re-layouts: 3.21 us -> 0.12 us  [causal_time_conv(): part = conv_rows(seq[:frame_total - lag], weight[p])]
    unnamed x19 -> x33, local copies, waits for them, and re-layouts: 1.19 us -> 3.01 us
    conv_general_dilated x0 -> x11, local copies, waits for them, and re-layouts: none -> 1.27 us  [conv_rows(): lax.conv_general_dilated(source, taps, window_strides=(1, 1), padding=((0...]
  transfers between devices with their start and end apart: 6 -> 3, of which waited for: 6 -> 3; matrix products, arithmetic and copies ran while one was open for 1% -> 0% of each run, Pallas kernels for 0% -> 0%
where the time goes in v1:
time: 69.8 us; the launch traced here: 69.4 us
  blocking collectives  32.9 us (47%)
  waiting for transfers between devices  8.78 us (13%)
  local copies, waits for them, and re-layouts  8.25 us (12%)
  starting transfers between devices  7.13 us (10%)
  matrix products  6.79 us (10%)
  other arithmetic  5.01 us (7%)
    all_gather x1, blocking collectives, local(): keys = lax.all_gather(normed, 'space', axis=1, tiled=True)  32.9 us
    ppermute x1, starting transfers between devices, local(): above = lax.ppermute(seq[:, row_count - HALO:], 'space', up)  5.39 us
    conv_general_dilated x4, matrix products, conv_rows(): lax.conv_general_dilated(source, taps, window_strides=(1, 1), padding=((0...  4.99 us
    ppermute x1, waiting for transfers between devices, local(): above = lax.ppermute(seq[:, row_count - HALO:], 'space', up)  4.38 us
    ppermute x1, waiting for transfers between devices, local(): below = lax.ppermute(seq[:, :HALO], 'space', down)  3.25 us
    unnamed x33, local copies, waits for them, and re-layouts  3.01 us
  transfers between devices with their start and end apart: 3, of which 3 were waited for; matrix products, arithmetic and copies ran while one was open for 0% of the time, Pallas kernels for 0%

profile of v1, /device:TPU:0, one launch (start us, length us, event | category | flops | bytes accessed | tf_op | source)
XLA Modules:
  0.0 69.4 jit_solution(3165660581323077289)
XLA Ops:
  0.0 0.5 collective-permute-start
  0.5 1.2 %collective-permute-done = bf16[1,2,112,192]{2,3,1,0:T(8,128)(2,1)S(1)} collective-permute-done((bf16[1,2,112,192]{2,3,1,0:T(8,128)(2,1)}, bf16[1,2,112,192]{2,3,1,0:T(8,128)(2,1)S(1)}, u32[]{:S(2)}, u32[]{:S(2)}) %collective-permute-start) | collective-permute-done | bytes 86048 | tf_op jit(solution)/shard_map/ppermute | solution.py:65
  1.6 0.9 %select_bitcast_fusion.2 = (bf16[1,1,2,112,192]{3,4,2,1,0:T(8,128)(2,1)S(1)}, bf16[1,1,2,112,192]{3,4,2,1,0:T(8,128)(2,1)S(1)}) fusion(bf16[1,2,112,192]{2,3,1,0:T(8,128)(2,1)S(1)} %collective-permute-done, pred[]{:T(512)S(6)} %eq.3, bf16[1,1,2,112,192]{3,4,2,1,0:T(8,128)(2,1)} %param.15), kind=kLoop, calls=%fused_computation.86 | loop fusion | flops 86016 | bytes 344065 | tf_op jit(solution)/shard_map/stack | solution.py:68
  2.6 1.3 %collective-permute-start.2 = (bf16[2,2,112,192]{2,3,1,0:T(8,128)(2,1)S(1)}, bf16[2,2,112,192]{2,3,1,0:T(8,128)(2,1)S(1)}, u32[]{:S(2)}, u32[]{:S(2)}) collective-permute-start(bf16[2,2,112,192]{2,3,1,0:T(8,128)(2,1)S(1)} %maximum_bitcast_fusion), channel_id=1, source_target_pairs={{2,0},{4,2},{6,4},{8,6},{10,8},{12,10},{14,12},{3,1},{5,3},{7,5},{... | collective-permute-start | bytes 516104 | tf_op jit(solution)/shard_map/ppermute | solution.py:73
  3.9 5.4 %collective-permute-start.1 = (bf16[2,2,112,192]{2,3,1,0:T(8,128)(2,1)S(1)}, bf16[2,2,112,192]{2,3,1,0:T(8,128)(2,1)S(1)}, u32[]{:S(2)}, u32[]{:S(2)}) collective-permute-start(bf16[2,2,112,192]{2,3,1,0:T(8,128)(2,1)S(1)} %maximum_bitcast_fusion), channel_id=1, source_target_pairs={{0,2},{2,4},{4,6},{6,8},{8,10},{10,12},{12,14},{1,3},{3,5},{5,7},{... | collective-permute-start | bytes 516104 | tf_op jit(solution)/shard_map/ppermute | solution.py:72
  9.3 3.2 %collective-permute-done.2 = bf16[2,2,112,192]{2,3,1,0:T(8,128)(2,1)S(1)} collective-permute-done((bf16[2,2,112,192]{2,3,1,0:T(8,128)(2,1)S(1)}, bf16[2,2,112,192]{2,3,1,0:T(8,128)(2,1)S(1)}, u32[]{:S(2)}, u32[]{:S(2)}) %collective-permute-start.2) | collective-permute-done | bytes 172064 | tf_op jit(solution)/shard_map/ppermute | solution.py:73
  12.5 4.4 %collective-permute-done.1 = bf16[2,2,112,192]{2,3,1,0:T(8,128)(2,1)S(1)} collective-permute-done((bf16[2,2,112,192]{2,3,1,0:T(8,128)(2,1)S(1)}, bf16[2,2,112,192]{2,3,1,0:T(8,128)(2,1)S(1)}, u32[]{:S(2)}, u32[]{:S(2)}) %collective-permute-start.1) | collective-permute-done | bytes 172064 | tf_op jit(solution)/shard_map/ppermute | solution.py:72
  16.9 0.2 fusion.2
  17.1 1.1 %fusion.9 = bf16[2,6,112,192]{2,3,1,0:T(8,128)(2,1)S(1)} fusion(f32[192]{0:T(256)} %param.16, f32[2,6,112]{2,1,0:T(8,128)S(1)} %add_rsqrt_fusion.1, bf16[2,2,112,192]{2,3,1,0:T(8,128)(2,1)S(1)} %collective-permute-done.2, bf16[2,2,112,192]{2,3,1,0:T(8,128)(2,1)S(1)} %maximum_bitcast_fusion, bf16[2,2,112,192]{2,3,1,0:T(8,128)(2,1)S(1)} %collective-permute-done.1), kind=kLoop, calls=%fused_computation.15 | loop fusion | flops 2580480 | bytes 1038336 | tf_op jit(solution)/shard_map/convert_element_type | solution.py:76
  19.0 1.8 %convolution_select_fusion.1 = f32[4,8,15,192]{3,1,2,0:T(8,128)S(1)} fusion(bf16[3,3,3,192,192]{4,3,2,1,0:T(8,128)(2,1)} %param.17, bf16[6,1,7,2,192]{4,2,3,0,1:T(8,128)(2,1)S(1)} %slice.36, bf16[6,1,8,15,192]{4,2,3,0,1:T(8,128)(2,1)S(1)} %copy.94, pred[8,15]{0,1:T(8,128)(4,1)S(1)} %copy-done.13), kind=kOutput, calls=%fused_computation.7 | convolution fusion | flops 319537152 | bytes 1562232 | tf_op jit(solution)/shard_map/conv_general_dilated | solution.py:17
  20.8 0.2 copy.95
  21.1 0.6 copy.114
  21.7 0.6 pad.7.clone
  22.4 0.8 %fusion.27 = bf16[6,2,8,17,192]{4,1,3,2,0:T(2,128)(2,1)S(1)} fusion(bf16[6,2,7,2,192]{4,1,3,2,0:T(2,128)(2,1)S(1)} %slice.38, bf16[6,2,8,15,192]{4,1,3,2,0:T(2,128)(2,1)S(1)} %bitcast.94), kind=kLoop, calls=%fused_computation.44 | loop fusion | flops 1880064 | bytes 1244160 | tf_op jit(solution)/shard_map/conv_general_dilated | solution.py:17
  23.2 2.3 %convolution_select_fusion = f32[4,16,15,192]{3,1,2,0:T(8,128)S(1)} fusion(bf16[3,3,3,192,192]{4,3,2,1,0:T(8,128)(2,1)} %param.17, bf16[6,2,8,17,192]{4,1,3,2,0:T(2,128)(2,1)S(1)} %fusion.27, pred[16,15]{0,1:T(8,128)(4,1)S(1)} %copy-done.14), kind=kOutput, calls=%fused_computation.6 | convolution fusion | flops 637194240 | bytes 2248944 | tf_op jit(solution)/shard_map/conv_general_dilated | solution.py:17
  25.5 0.6 copy.98
  26.2 0.4 multiply_reduce_fusion
  26.6 0.7 %fusion.35 = bf16[1,2,4,112,192]{4,2,3,1,0:T(4,128)(2,1)S(1)} fusion(f32[192]{0:T(256)S(1)} %copy-done.6, f32[2,4,112]{1,2,0:T(8,128)S(1)} %add_rsqrt_fusion, pred[4]{0:T(512)(128)(4,1)S(1)} %compare_and_fusion, f32[192]{0:T(256)S(1)} %copy-done.4, f32[4,2,120,192]{3,0,2,1:T(4,128)S(1)} %bitcast.91, f32[1,4,112,192]{3,1,2,0:T(4,128)S(1)} %slice_bitcast_fusion.1), kind=kLoop, calls=%fused_computation.55 | loop fusion | flops 1720320 | bytes 1381380 | tf_op jit(solution)/shard_map/reshape | solution.py:84
  27.9 1.2 %copy-done.9 = bf16[3,3,3,192,192]{4,3,2,1,0:T(8,128)(2,1)S(1)} copy-done((bf16[3,3,3,192,192]{4,3,2,1,0:T(8,128)(2,1)S(1)}, bf16[3,3,3,192,192]{4,3,2,1,0:T(8,128)(2,1)}, u32[]{:S(2)}) %copy-start.9) | copy-done | bytes 1990680
  29.1 0.4 convolution_select_fusion.3
  29.6 0.4 fusion.11
  30.5 0.2 copy-done.5
  31.4 32.9 %all_gather.3 = bf16[1,16,112,192]{2,3,0,1:T(8,128)(2,1)S(1)} all-gather(bf16[1,2,112,192]{2,3,0,1:T(8,128)(2,1)S(1)} %fusion.79), channel_id=1, replica_groups=mesh['clips'=2,'space'=8,'tm'=2] {'space'}, dimensions={1}, use_global_device_ids=true | all-gather | bytes 774144 | tf_op jit(solution)/shard_map/all_gather | solution.py:111
  64.4 0.5 copy.110
  64.9 0.9 %reshape.151 = bf16[1792,192]{0,1:T(8,128)(2,1)S(1)} reshape(bf16[1,16,112,192]{2,1,3,0:T(8,128)(2,1)S(1)} %copy.110) | data formatting | bytes 1376256 | tf_op jit(solution)/shard_map/reshape.4
  65.9 0.4 fusion.16
  66.3 0.5 fusion.69
  66.8 0.4 fusion
  67.2 0.5 fusion.14
  67.7 0.3 copy-done.2
  68.1 0.4 fusion.12
  68.7 0.7 copy.111
  (58 shorter events, 2.8 us)
Async XLA Ops:
  0.0 65.8 %copy-start = (bf16[192,192]{1,0:T(8,128)(2,1)S(1)}, bf16[192,192]{1,0:T(8,128)(2,1)}, u32[]{:S(2)}) copy-start(bf16[192,192]{1,0:T(8,128)(2,1)} %param.25) | copy-start | bytes 221188
  0.0 1.6 %collective-permute-start = (bf16[1,2,112,192]{2,3,1,0:T(8,128)(2,1)}, bf16[1,2,112,192]{2,3,1,0:T(8,128)(2,1)S(1)}, u32[]{:S(2)}, u32[]{:S(2)}) collective-permute-start(bf16[1,2,112,192]{2,3,1,0:T(8,128)(2,1)} %bitcast.99), channel_id=1, source_target_pairs={{0,1},{1,0},{2,3},{3,2},{4,5},{5,4},{6,7},{7,6},{8,9},{9,8},{10,11... | collective-permute-start | bytes 258056 | tf_op jit(solution)/shard_map/ppermute | solution.py:65
  2.6 10.0 %collective-permute-start.2 = (bf16[2,2,112,192]{2,3,1,0:T(8,128)(2,1)S(1)}, bf16[2,2,112,192]{2,3,1,0:T(8,128)(2,1)S(1)}, u32[]{:S(2)}, u32[]{:S(2)}) collective-permute-start(bf16[2,2,112,192]{2,3,1,0:T(8,128)(2,1)S(1)} %maximum_bitcast_fusion), channel_id=1, source_target_pairs={{2,0},{4,2},{6,4},{8,6},{10,8},{12,10},{14,12},{3,1},{5,3},{7,5},{... | collective-permute-start | bytes 516104 | tf_op jit(solution)/shard_map/ppermute | solution.py:73
  3.9 13.0 %collective-permute-start.1 = (bf16[2,2,112,192]{2,3,1,0:T(8,128)(2,1)S(1)}, bf16[2,2,112,192]{2,3,1,0:T(8,128)(2,1)S(1)}, u32[]{:S(2)}, u32[]{:S(2)}) collective-permute-start(bf16[2,2,112,192]{2,3,1,0:T(8,128)(2,1)S(1)} %maximum_bitcast_fusion), channel_id=1, source_target_pairs={{0,2},{2,4},{4,6},{6,8},{8,10},{10,12},{12,14},{1,3},{3,5},{5,7},{... | collective-permute-start | bytes 516104 | tf_op jit(solution)/shard_map/ppermute | solution.py:72
  18.3 0.7 copy-start.13
  21.7 1.5 %copy-start.14 = (pred[16,15]{0,1:T(8,128)(4,1)S(1)}, pred[16,15]{0,1:T(8,128)(4,1)}, u32[]{:S(2)}) copy-start(pred[16,15]{0,1:T(8,128)(4,1)} %constant.64) | copy-start | bytes 724
  25.5 0.7 copy-start.4
  25.5 1.1 %copy-start.6 = (f32[192]{0:T(256)S(1)}, f32[192]{0:T(256)}, u32[]{:S(2)}) copy-start(f32[192]{0:T(256)} %param.19) | copy-start | bytes 2308
  27.3 1.8 %copy-start.9 = (bf16[3,3,3,192,192]{4,3,2,1,0:T(8,128)(2,1)S(1)}, bf16[3,3,3,192,192]{4,3,2,1,0:T(8,128)(2,1)}, u32[]{:S(2)}) copy-start(bf16[3,3,3,192,192]{4,3,2,1,0:T(8,128)(2,1)} %param.20) | copy-start | bytes 5971972
  27.8 1.7 %copy-start.11 = (f32[192]{0:T(256)S(1)}, f32[192]{0:T(256)}, u32[]{:S(2)}) copy-start(f32[192]{0:T(256)} %param.21) | copy-start | bytes 2308
  29.5 0.9 %copy-start.1 = (bf16[1,1,2,112,192]{3,4,2,1,0:T(8,128)(2,1)S(1)}, bf16[1,1,2,112,192]{3,4,2,1,0:T(8,128)(2,1)}, u32[]{:S(2)}) copy-start(bf16[1,1,2,112,192]{3,4,2,1,0:T(8,128)(2,1)} %param.15) | copy-start | bytes 258052
  30.0 0.7 %copy-start.5 = (f32[192]{0:T(256)S(1)}, f32[192]{0:T(256)}, u32[]{:S(2)}) copy-start(f32[192]{0:T(256)} %param.22) | copy-start | bytes 2308
  64.4 1.5 %copy-start.10 = (bf16[192,192]{1,0:T(8,128)(2,1)S(1)}, bf16[192,192]{1,0:T(8,128)(2,1)}, u32[]{:S(2)}) copy-start(bf16[192,192]{1,0:T(8,128)(2,1)} %param.23) | copy-start | bytes 221188
  64.4 1.5 %copy-start.12 = (f32[192]{0:T(256)S(1)}, f32[192]{0:T(256)}, u32[]{:S(2)}) copy-start(f32[192]{0:T(256)} %param.24) | copy-start | bytes 2308
  67.1 0.9 %copy-start.2 = (bf16[192,192]{1,0:T(8,128)(2,1)S(1)}, bf16[192,192]{1,0:T(8,128)(2,1)}, u32[]{:S(2)}) copy-start(bf16[192,192]{1,0:T(8,128)(2,1)} %param.28) | copy-start | bytes 221188
  67.1 0.9 %copy-start.3 = (bf16[192,192]{1,0:T(8,128)(2,1)S(1)}, bf16[192,192]{1,0:T(8,128)(2,1)}, u32[]{:S(2)}) copy-start(bf16[192,192]{1,0:T(8,128)(2,1)} %param.26) | copy-start | bytes 221188
  67.2 0.9 %copy-start.7 = (f32[192]{0:T(256)S(1)}, f32[192]{0:T(256)}, u32[]{:S(2)}) copy-start(f32[192]{0:T(256)} %param.29) | copy-start | bytes 2308
  67.2 0.9 %copy-start.8 = (f32[192]{0:T(256)S(1)}, f32[192]{0:T(256)}, u32[]{:S(2)}) copy-start(f32[192]{0:T(256)} %param.27) | copy-start | bytes 2308

commit v2 on v1

--- a/solution.py
+++ b/solution.py
@@ -57,8 +57,9 @@
 ):
     own = frames[:, 0]
     frame_count, row_count, col_count, channels = own.shape
-    bands = lax.axis_size("space")
-    band = lax.axis_index("space")
+    inner = lax.axis_size("inner")
+    bands = lax.axis_size("outer") * inner
+    band = lax.axis_index("outer") * inner + lax.axis_index("inner")
     is_first = lax.axis_index("tm") == 0
     height = bands * row_count
 
@@ -67,10 +68,13 @@
     odd = jnp.where(is_first, partner, own)
     seq = jnp.stack([even, odd], axis=1).reshape(2 * frame_count, row_count, col_count, channels)
 
-    up = [(i, i + 1) for i in range(bands - 1)]
-    down = [(i + 1, i) for i in range(bands - 1)]
-    above = lax.ppermute(seq[:, row_count - HALO :], "space", up)
-    below = lax.ppermute(seq[:, :HALO], "space", down)
+    up = [(2 * i, 2 * i + 2) for i in range(bands - 1)]
+    down = [(2 * i + 3, 2 * i + 1) for i in range(bands - 1)]
+    edge = jnp.where(is_first, seq[:, row_count - HALO :], seq[:, :HALO])
+    arrived = lax.ppermute(edge, ("outer", "inner", "tm"), up + down)
+    swapped = lax.ppermute(arrived, "tm", [(0, 1), (1, 0)])
+    above = jnp.where(is_first, arrived, swapped)
+    below = jnp.where(is_first, swapped, arrived)
     ext = jnp.concatenate([above, seq, below], axis=1)
 
     first_act = jax.nn.silu(rms_scale(ext.astype(jnp.float32), norm1_gain)).astype(jnp.bfloat16)
@@ -108,7 +112,9 @@
     ).astype(jnp.bfloat16)
     folded = folded.reshape(frame_count, token_count, channels)
 
-    keys = lax.all_gather(normed, "space", axis=1, tiled=True)
+    keys = lax.all_gather(normed, "outer", axis=1, tiled=True)
+    keys = keys.reshape(frame_count, -1, 1, row_count, col_count, channels)
+    keys = lax.all_gather(keys, "inner", axis=2, tiled=True)
     keys = keys.reshape(frame_count, height * col_count, channels)
     scores = jnp.einsum("fqc,fkc->fqk", folded, keys, preferred_element_type=jnp.float32)
     top = jnp.max(scores, axis=-1, keepdims=True)
@@ -130,11 +136,16 @@
 
 
 def solution(mesh):
-    placed = (P("clips", "tm", "space", None, None),) + (P(),) * 14
+    clips, bands, cores = mesh.devices.shape
+    split = jax.sharding.Mesh(
+        mesh.devices.reshape(clips, bands // 2, 2, cores), ("clips", "outer", "inner", "tm")
+    )
+    banded = P("clips", "tm", ("outer", "inner"), None, None)
+    placed = (banded,) + (P(),) * 14
     return jax.shard_map(
         local,
-        mesh=mesh,
+        mesh=split,
         in_specs=placed,
-        out_specs=P("clips", "tm", "space", None, None),
+        out_specs=banded,
         check_vma=False,
     )

time: 69.8 us -> 58.8 us (0.84)
  blocking collectives: 32.9 us -> 25.1 us
  starting transfers between devices: 7.13 us -> 5.21 us
  waiting for transfers between devices: 8.78 us -> 7.85 us
    all_gather x1 -> x2, blocking collectives: 32.9 us -> 25.1 us  [the longest x1 14.8 us: local(): keys = lax.all_gather(normed, 'outer', axis=1, tiled=True)]
    ppermute x2, starting transfers between devices: 6.68 us -> 4.76 us  [the longest x1 4.76 us: local(): arrived = lax.ppermute(edge, ('outer', 'inner', 'tm'), up + down)]
    ppermute x2, waiting for transfers between devices: 7.63 us -> 6.7 us  [the longest x1 5.27 us: local(): arrived = lax.ppermute(edge, ('outer', 'inner', 'tm'), up + down)]
    unnamed x33 -> x35, local copies, waits for them, and re-layouts: 3.01 us -> 3.02 us
where the time goes in v2:
time: 58.8 us; the launch traced here: 58.4 us
  blocking collectives  25.1 us (43%)
  local copies, waits for them, and re-layouts  8.55 us (15%)
  waiting for transfers between devices  7.85 us (13%)
  matrix products  6.78 us (12%)
  starting transfers between devices  5.21 us (9%)
  other arithmetic  4.38 us (7%)
    all_gather x1, blocking collectives, local(): keys = lax.all_gather(normed, 'outer', axis=1, tiled=True)  14.8 us
    all_gather x1, blocking collectives, local(): keys = lax.all_gather(keys, 'inner', axis=2, tiled=True)  10.4 us
    ppermute x1, waiting for transfers between devices, local(): arrived = lax.ppermute(edge, ('outer', 'inner', 'tm'), up + down)  5.27 us
    conv_general_dilated x4, matrix products, conv_rows(): lax.conv_general_dilated(source, taps, window_strides=(1, 1), padding=((0...  4.98 us
    ppermute x1, starting transfers between devices, local(): arrived = lax.ppermute(edge, ('outer', 'inner', 'tm'), up + down)  4.76 us
    unnamed x35, local copies, waits for them, and re-layouts  3.02 us
    ppermute x1, waiting for transfers between devices, local(): swapped = lax.ppermute(arrived, 'tm', [(0, 1), (1, 0)])  1.43 us
    conv_general_dilated x11, local copies, waits for them, and re-layouts, conv_rows(): lax.conv_general_dilated(source, taps, window_strides=(1, 1), padding=((0...  1.27 us
  transfers between devices with their start and end apart: 3, of which 3 were waited for; matrix products, arithmetic and copies ran while one was open for 0% of the time, Pallas kernels for 0%

profile of v2, /device:TPU:0, one launch (start us, length us, event | category | flops | bytes accessed | tf_op | source)
XLA Modules:
  0.0 58.4 jit_solution(1767126460293616746)
XLA Ops:
  0.0 0.5 collective-permute-start
  0.5 1.2 %collective-permute-done = bf16[1,2,112,192]{2,3,1,0:T(8,128)(2,1)S(1)} collective-permute-done((bf16[1,2,112,192]{2,3,1,0:T(8,128)(2,1)}, bf16[1,2,112,192]{2,3,1,0:T(8,128)(2,1)S(1)}, u32[]{:S(2)}, u32[]{:S(2)}) %collective-permute-start) | collective-permute-done | bytes 86048 | tf_op jit(solution)/shard_map/ppermute | solution.py:66
  1.6 0.9 %select_bitcast_fusion.2 = (bf16[1,1,2,112,192]{3,4,2,1,0:T(8,128)(2,1)S(1)}, bf16[1,1,2,112,192]{3,4,2,1,0:T(8,128)(2,1)S(1)}) fusion(bf16[1,2,112,192]{2,3,1,0:T(8,128)(2,1)S(1)} %collective-permute-done, pred[]{:T(512)S(6)} %eq.3, bf16[1,1,2,112,192]{3,4,2,1,0:T(8,128)(2,1)} %param.15), kind=kLoop, calls=%fused_computation.88 | loop fusion | flops 86016 | bytes 344065 | tf_op jit(solution)/shard_map/stack | solution.py:69
  2.6 4.8 %collective-permute-start.1 = (bf16[2,2,112,192]{2,3,1,0:T(8,128)(2,1)S(1)}, bf16[2,2,112,192]{2,3,1,0:T(8,128)(2,1)S(1)}, u32[]{:S(2)}, u32[]{:S(2)}) collective-permute-start(bf16[2,2,112,192]{2,3,1,0:T(8,128)(2,1)S(1)} %maximum_bitcast_fusion), channel_id=1, source_target_pairs={{0,2},{2,4},{4,6},{6,8},{8,10},{10,12},{12,14},{3,1},{5,3},{7,5},{... | collective-permute-start | bytes 516104 | tf_op jit(solution)/shard_map/ppermute | solution.py:74
  7.3 5.3 %collective-permute-done.1 = bf16[2,2,112,192]{2,3,1,0:T(8,128)(2,1)S(1)} collective-permute-done((bf16[2,2,112,192]{2,3,1,0:T(8,128)(2,1)S(1)}, bf16[2,2,112,192]{2,3,1,0:T(8,128)(2,1)S(1)}, u32[]{:S(2)}, u32[]{:S(2)}) %collective-permute-start.1) | collective-permute-done | bytes 172064 | tf_op jit(solution)/shard_map/ppermute | solution.py:74
  12.6 1.4 %collective-permute-done.2 = bf16[2,2,112,192]{2,3,1,0:T(8,128)(2,1)S(1)} collective-permute-done((bf16[2,2,112,192]{2,3,1,0:T(8,128)(2,1)S(1)}, bf16[2,2,112,192]{2,3,1,0:T(8,128)(2,1)S(1)}, u32[]{:S(2)}, u32[]{:S(2)}) %collective-permute-start.2) | collective-permute-done | bytes 172064 | tf_op jit(solution)/shard_map/ppermute | solution.py:75
  14.1 0.2 fusion.2
  14.3 0.5 fusion.9
  15.5 1.8 %convolution_select_fusion.1 = f32[4,8,15,192]{3,1,2,0:T(8,128)S(1)} fusion(bf16[3,3,3,192,192]{4,3,2,1,0:T(8,128)(2,1)} %param.17, bf16[6,1,7,2,192]{4,2,3,0,1:T(8,128)(2,1)S(1)} %slice.36, bf16[6,1,8,15,192]{4,2,3,0,1:T(8,128)(2,1)S(1)} %copy.112, pred[8,15]{0,1:T(8,128)(4,1)S(1)} %copy-done.14), kind=kOutput, calls=%fused_computation.7 | convolution fusion | flops 319537152 | bytes 1562232 | tf_op jit(solution)/shard_map/conv_general_dilated | solution.py:17
  17.3 0.2 copy.113
  17.6 0.6 %copy.132 = bf16[6,2,112,192]{3,1,2,0:T(2,128)(2,1)S(1)} copy(bf16[6,2,112,192]{2,3,0,1:T(8,128)(2,1)S(1)} %bitcast.91) | data formatting | bytes 1032192
  18.2 0.6 %pad.7.clone = bf16[6,2,120,192]{3,1,2,0:T(2,128)(2,1)S(1)} pad(bf16[6,2,112,192]{3,1,2,0:T(2,128)(2,1)S(1)} %copy.132, bf16[]{:T(256)} %constant.43.clone.1), padding=0_0x0_0x1_7x0_0 | pad | bytes 1069058 | tf_op jit(solution)/shard_map/convert_element_type | solution.py:80
  18.9 0.8 %fusion.27 = bf16[6,2,8,17,192]{4,1,3,2,0:T(2,128)(2,1)S(1)} fusion(bf16[6,2,7,2,192]{4,1,3,2,0:T(2,128)(2,1)S(1)} %slice.38, bf16[6,2,8,15,192]{4,1,3,2,0:T(2,128)(2,1)S(1)} %bitcast.93), kind=kLoop, calls=%fused_computation.44 | loop fusion | flops 1880064 | bytes 1244160 | tf_op jit(solution)/shard_map/conv_general_dilated | solution.py:17
  19.7 2.3 %convolution_select_fusion = f32[4,16,15,192]{3,1,2,0:T(8,128)S(1)} fusion(bf16[3,3,3,192,192]{4,3,2,1,0:T(8,128)(2,1)} %param.17, bf16[6,2,8,17,192]{4,1,3,2,0:T(2,128)(2,1)S(1)} %fusion.27, pred[16,15]{0,1:T(8,128)(4,1)S(1)} %copy-done.15), kind=kOutput, calls=%fused_computation.6 | convolution fusion | flops 637194240 | bytes 2248944 | tf_op jit(solution)/shard_map/conv_general_dilated | solution.py:17
  22.0 0.6 %copy.116 = f32[4,16,15,192]{3,0,2,1:T(4,128)S(1)} copy(f32[4,16,15,192]{3,1,2,0:T(8,128)S(1)} %convolution_select_fusion) | data formatting | bytes 1474560 | tf_op jit(solution)/shard_map/conv_general_dilated | solution.py:17
  22.7 0.4 multiply_reduce_fusion
  23.1 0.7 %fusion.35 = bf16[1,2,4,112,192]{4,2,3,1,0:T(4,128)(2,1)S(1)} fusion(f32[192]{0:T(256)S(1)} %copy-done.6, f32[2,4,112]{1,2,0:T(8,128)S(1)} %add_rsqrt_fusion, pred[4]{0:T(512)(128)(4,1)S(1)} %compare_and_fusion, f32[192]{0:T(256)S(1)} %copy-done.4, f32[4,2,120,192]{3,0,2,1:T(4,128)S(1)} %bitcast.90, f32[1,4,112,192]{3,1,2,0:T(4,128)S(1)} %slice_bitcast_fusion.1), kind=kLoop, calls=%fused_computation.55 | loop fusion | flops 1720320 | bytes 1381380 | tf_op jit(solution)/shard_map/reshape | solution.py:88
  24.4 1.2 %copy-done.10 = bf16[3,3,3,192,192]{4,3,2,1,0:T(8,128)(2,1)S(1)} copy-done((bf16[3,3,3,192,192]{4,3,2,1,0:T(8,128)(2,1)S(1)}, bf16[3,3,3,192,192]{4,3,2,1,0:T(8,128)(2,1)}, u32[]{:S(2)}) %copy-start.10) | copy-done | bytes 1990680
  25.6 0.4 convolution_select_fusion.3
  26.1 0.4 fusion.11
  27.0 0.2 copy-done.5
  28.0 14.8 %all_gather.6 = bf16[1,8,112,192]{2,3,0,1:T(8,128)(2,1)S(1)} all-gather(bf16[1,2,112,192]{2,3,0,1:T(8,128)(2,1)S(1)} %fusion.79), channel_id=1, replica_groups=mesh['clips'=2,'outer'=4,'inner'=2,'tm'=2] {'outer'}, dimensions={1}, use_global_device_ids=true | all-gather | bytes 430080 | tf_op jit(solution)/shard_map/all_gather | solution.py:115
  42.7 10.4 %all_gather.7 = bf16[1,4,2,2,112,192]{4,5,3,2,1,0:T(8,128)(2,1)S(1)} all-gather(bf16[1,4,1,2,112,192]{4,5,3,2,1,0:T(8,128)(2,1)S(1)} %bitcast.95), channel_id=1, replica_groups=mesh['clips'=2,'outer'=4,'inner'=2,'tm'=2] {'inner'}, dimensions={2}, use_global_device_ids=true | all-gather | bytes 1032192 | tf_op jit(solution)/shard_map/all_gather | solution.py:117
  53.1 0.8 %copy.128 = bf16[1,4,2,2,112,192]{4,3,2,1,5,0:T(2,128)(2,1)S(1)} copy(bf16[1,4,2,2,112,192]{4,5,3,2,1,0:T(8,128)(2,1)S(1)} %all_gather.7) | data formatting | bytes 1376256 | tf_op jit(solution)/shard_map/all_gather | solution.py:117
  53.9 0.9 %reshape.155 = bf16[1792,192]{0,1:T(8,128)(2,1)S(1)} reshape(bf16[1,4,2,2,112,192]{4,3,2,1,5,0:T(2,128)(2,1)S(1)} %copy.128) | data formatting | bytes 1376256 | tf_op jit(solution)/shard_map/reshape.4
  54.9 0.4 fusion.16
  55.3 0.5 fusion.69
  55.8 0.4 fusion
  56.2 0.5 fusion.14
  56.7 0.3 copy-done.2
  57.1 0.4 fusion.12
  57.7 0.7 %copy.129 = f32[1,1,2,112,192]{3,4,2,1,0:T(8,128)} copy(f32[1,1,2,112,192]{3,2,4,1,0:T(2,128)S(1)} %reshape.156) | data formatting | bytes 344064 | tf_op jit(solution)/shard_map/reshape | solution.py:135
  (62 shorter events, 2.8 us)
Async XLA Ops:
  0.0 54.8 %copy-start = (bf16[192,192]{1,0:T(8,128)(2,1)S(1)}, bf16[192,192]{1,0:T(8,128)(2,1)}, u32[]{:S(2)}) copy-start(bf16[192,192]{1,0:T(8,128)(2,1)} %param.25) | copy-start | bytes 221188
  0.0 14.3 %copy-start.9 = (f32[192]{0:T(256)S(1)}, f32[192]{0:T(256)}, u32[]{:S(2)}) copy-start(f32[192]{0:T(256)} %param.16) | copy-start | bytes 2308
  0.0 1.6 %collective-permute-start = (bf16[1,2,112,192]{2,3,1,0:T(8,128)(2,1)}, bf16[1,2,112,192]{2,3,1,0:T(8,128)(2,1)S(1)}, u32[]{:S(2)}, u32[]{:S(2)}) collective-permute-start(bf16[1,2,112,192]{2,3,1,0:T(8,128)(2,1)} %bitcast.99), channel_id=1, source_target_pairs={{0,1},{1,0},{2,3},{3,2},{4,5},{5,4},{6,7},{7,6},{8,9},{9,8},{10,11... | collective-permute-start | bytes 258056 | tf_op jit(solution)/shard_map/ppermute | solution.py:66
  2.6 10.0 %collective-permute-start.1 = (bf16[2,2,112,192]{2,3,1,0:T(8,128)(2,1)S(1)}, bf16[2,2,112,192]{2,3,1,0:T(8,128)(2,1)S(1)}, u32[]{:S(2)}, u32[]{:S(2)}) collective-permute-start(bf16[2,2,112,192]{2,3,1,0:T(8,128)(2,1)S(1)} %maximum_bitcast_fusion), channel_id=1, source_target_pairs={{0,2},{2,4},{4,6},{6,8},{8,10},{10,12},{12,14},{3,1},{5,3},{7,5},{... | collective-permute-start | bytes 516104 | tf_op jit(solution)/shard_map/ppermute | solution.py:74
  12.6 1.4 %collective-permute-start.2 = (bf16[2,2,112,192]{2,3,1,0:T(8,128)(2,1)S(1)}, bf16[2,2,112,192]{2,3,1,0:T(8,128)(2,1)S(1)}, u32[]{:S(2)}, u32[]{:S(2)}) collective-permute-start(bf16[2,2,112,192]{2,3,1,0:T(8,128)(2,1)S(1)} %collective-permute-done.1), channel_id=1, source_target_pairs={{0,1},{1,0},{2,3},{3,2},{4,5},{5,4},{6,7},{7,6},{8,9},{9,8},{10,11... | collective-permute-start | bytes 516104 | tf_op jit(solution)/shard_map/ppermute | solution.py:75
  14.8 0.7 %copy-start.14 = (pred[8,15]{0,1:T(8,128)(4,1)S(1)}, pred[8,15]{0,1:T(8,128)(4,1)}, u32[]{:S(2)}) copy-start(pred[8,15]{0,1:T(8,128)(4,1)} %constant.65) | copy-start | bytes 364
  18.2 1.5 %copy-start.15 = (pred[16,15]{0,1:T(8,128)(4,1)S(1)}, pred[16,15]{0,1:T(8,128)(4,1)}, u32[]{:S(2)}) copy-start(pred[16,15]{0,1:T(8,128)(4,1)} %constant.67) | copy-start | bytes 724
  22.0 0.7 %copy-start.4 = (f32[192]{0:T(256)S(1)}, f32[192]{0:T(256)}, u32[]{:S(2)}) copy-start(f32[192]{0:T(256)} %param.18) | copy-start | bytes 2308
  22.0 1.1 %copy-start.6 = (f32[192]{0:T(256)S(1)}, f32[192]{0:T(256)}, u32[]{:S(2)}) copy-start(f32[192]{0:T(256)} %param.19) | copy-start | bytes 2308
  23.9 1.8 %copy-start.10 = (bf16[3,3,3,192,192]{4,3,2,1,0:T(8,128)(2,1)S(1)}, bf16[3,3,3,192,192]{4,3,2,1,0:T(8,128)(2,1)}, u32[]{:S(2)}) copy-start(bf16[3,3,3,192,192]{4,3,2,1,0:T(8,128)(2,1)} %param.20) | copy-start | bytes 5971972
  24.3 1.7 %copy-start.12 = (f32[192]{0:T(256)S(1)}, f32[192]{0:T(256)}, u32[]{:S(2)}) copy-start(f32[192]{0:T(256)} %param.21) | copy-start | bytes 2308
  26.1 0.9 %copy-start.1 = (bf16[1,1,2,112,192]{3,4,2,1,0:T(8,128)(2,1)S(1)}, bf16[1,1,2,112,192]{3,4,2,1,0:T(8,128)(2,1)}, u32[]{:S(2)}) copy-start(bf16[1,1,2,112,192]{3,4,2,1,0:T(8,128)(2,1)} %param.15) | copy-start | bytes 258052
  26.5 0.7 %copy-start.5 = (f32[192]{0:T(256)S(1)}, f32[192]{0:T(256)}, u32[]{:S(2)}) copy-start(f32[192]{0:T(256)} %param.22) | copy-start | bytes 2308
  53.1 1.8 %copy-start.11 = (bf16[192,192]{1,0:T(8,128)(2,1)S(1)}, bf16[192,192]{1,0:T(8,128)(2,1)}, u32[]{:S(2)}) copy-start(bf16[192,192]{1,0:T(8,128)(2,1)} %param.23) | copy-start | bytes 221188
  53.1 1.8 %copy-start.13 = (f32[192]{0:T(256)S(1)}, f32[192]{0:T(256)}, u32[]{:S(2)}) copy-start(f32[192]{0:T(256)} %param.24) | copy-start | bytes 2308
  56.1 0.9 %copy-start.2 = (bf16[192,192]{1,0:T(8,128)(2,1)S(1)}, bf16[192,192]{1,0:T(8,128)(2,1)}, u32[]{:S(2)}) copy-start(bf16[192,192]{1,0:T(8,128)(2,1)} %param.28) | copy-start | bytes 221188
  56.1 0.9 %copy-start.3 = (bf16[192,192]{1,0:T(8,128)(2,1)S(1)}, bf16[192,192]{1,0:T(8,128)(2,1)}, u32[]{:S(2)}) copy-start(bf16[192,192]{1,0:T(8,128)(2,1)} %param.26) | copy-start | bytes 221188
  56.2 0.9 %copy-start.7 = (f32[192]{0:T(256)S(1)}, f32[192]{0:T(256)}, u32[]{:S(2)}) copy-start(f32[192]{0:T(256)} %param.29) | copy-start | bytes 2308
  56.2 0.9 %copy-start.8 = (f32[192]{0:T(256)S(1)}, f32[192]{0:T(256)}, u32[]{:S(2)}) copy-start(f32[192]{0:T(256)} %param.27) | copy-start | bytes 2308

commit v3 on v2

--- a/solution.py
+++ b/solution.py
@@ -1,8 +1,11 @@
+import functools
 import math
 
 import jax
 import jax.numpy as jnp
 from jax import lax
+from jax.experimental import pallas as pl
+from jax.experimental.pallas import tpu as pltpu
 from jax.sharding import PartitionSpec as P
 
 epsilon = 1e-06
@@ -36,6 +39,85 @@
             part = jnp.pad(part, ((lag, 0), (0, 0), (0, 0), (0, 0)))
         out = part if out is None else out + part
     return out
+
+
+def _rms(v, g):
+    return v * lax.rsqrt(jnp.mean(v * v, axis=-1, keepdims=True) + epsilon) * g
+
+def _silu(v):
+    return v * (1.0 / (1.0 + jnp.exp(-v)))
+
+def block_kernel(cols, frame_count, params, ext_ref, own_ref, g1_ref, w1_ref, b1_ref, g2_ref,
+                 w2_ref, b2_ref, ga_ref, res_ref, normed_ref):
+    total = 2 * frame_count
+    p_in = ext_ref.shape[1]
+    p_mid = p_in - 2 * cols
+    p_out = p_mid - 2 * cols
+
+    def shifted(a):
+        n = a.shape[0]
+        col = lax.broadcasted_iota(jnp.int32, (n, 1), 0) % cols
+        left = jnp.where(col == 0, 0.0, pltpu.roll(a, 1, 0))
+        right = jnp.where(col == cols - 1, 0.0, pltpu.roll(a, n - 1, 0))
+        return [left.astype(jnp.bfloat16), a.astype(jnp.bfloat16), right.astype(jnp.bfloat16)]
+
+    def conv_frame(sources, w_ref, out_rows):
+        acc = None
+        for p, trip in enumerate(sources):
+            if trip is None:
+                continue
+            for q in range(3):
+                for s in range(3):
+                    window = trip[s][q * cols: q * cols + out_rows]
+                    part = jnp.dot(window, w_ref[(p * 3 + q) * 3 + s], preferred_element_type=jnp.float32)
+                    acc = part if acc is None else acc + part
+        return acc
+
+    g1 = g1_ref[...]
+    act1 = [shifted(_silu(_rms(ext_ref[t].astype(jnp.float32), g1)).astype(jnp.bfloat16).astype(jnp.float32)) for t in range(total)]
+    lo = params[0]
+    hi = params[1]
+    first = params[2] == 1
+    row = lax.broadcasted_iota(jnp.int32, (p_mid, 1), 0) // cols
+    inside = (row >= lo) & (row < hi)
+    g2 = g2_ref[...]
+    b1 = b1_ref[...]
+    act2 = []
+    for j in range(total):
+        srcs = [act1[j + p - 2] if j + p - 2 >= 0 else None for p in range(3)]
+        out1 = conv_frame(srcs, w1_ref, p_mid) + b1
+        act2.append(jnp.where(inside, _silu(_rms(out1, g2)), 0.0).astype(jnp.bfloat16).astype(jnp.float32))
+    b2 = b2_ref[...]
+    ga = ga_ref[...]
+    zero = None
+    for k in range(frame_count):
+        def pick(t_even):
+            a = act2[t_even] if 0 <= t_even < total else None
+            b = act2[t_even + 1] if 0 <= t_even + 1 < total else None
+            if a is None and b is None:
+                return None
+            a = jnp.zeros_like(act2[0]) if a is None else a
+            b = jnp.zeros_like(act2[0]) if b is None else b
+            return shifted(jnp.where(first, a, b))
+        srcs = [pick(2 * k - 2), pick(2 * k - 1), pick(2 * k)]
+        out2 = conv_frame(srcs, w2_ref, p_out) + b2
+        res = own_ref[k].astype(jnp.float32) + out2
+        res_ref[k] = res
+        normed_ref[k] = _rms(res, ga).astype(jnp.bfloat16)
+
+def resnet_block(ext, own, params, g1, w1, b1, g2, w2, b2, ga, cols):
+    total, p_in, c = ext.shape
+    frame_count, p_out, _ = own.shape
+    vm = pl.BlockSpec(memory_space=pltpu.VMEM)
+    sm = pl.BlockSpec(memory_space=pltpu.SMEM)
+    return pl.pallas_call(
+        functools.partial(block_kernel, cols, frame_count),
+        out_shape=(jax.ShapeDtypeStruct((frame_count, p_out, c), jnp.float32),
+                   jax.ShapeDtypeStruct((frame_count, p_out, c), jnp.bfloat16)),
+        in_specs=[sm] + [vm] * 9,
+        out_specs=(vm, vm),
+    )(params, ext, own, g1.reshape(1, c), w1.reshape(27, c, c), b1.reshape(1, c), g2.reshape(1, c),
+      w2.reshape(27, c, c), b2.reshape(1, c), ga.reshape(1, c))
 
 
 def local(
@@ -77,32 +159,24 @@
     below = jnp.where(is_first, swapped, arrived)
     ext = jnp.concatenate([above, seq, below], axis=1)
 
-    first_act = jax.nn.silu(rms_scale(ext.astype(jnp.float32), norm1_gain)).astype(jnp.bfloat16)
-    first_out = causal_time_conv(first_act, conv1_weight) + conv1_bias
-    rows = band * row_count - 1 + lax.broadcasted_iota(jnp.int32, (1, row_count + 2, 1, 1), 1)
-    inside = (rows >= 0) & (rows < height)
-    second_act = jnp.where(
-        inside, jax.nn.silu(rms_scale(first_out, norm2_gain)), 0.0
-    ).astype(jnp.bfloat16)
-
-    pairs = second_act.reshape(frame_count, 2, row_count + 2, col_count, channels)
-    sa_even = pairs[:, 0]
-    sa_odd = pairs[:, 1]
-    zero = jnp.zeros_like(sa_even[:1])
-    odd_before = jnp.concatenate([zero, sa_odd[:-1]], axis=0)
-    even_before = jnp.concatenate([zero, sa_even[:-1]], axis=0)
-    current = jnp.where(is_first, sa_even, sa_odd)
-    previous = jnp.where(is_first, odd_before, sa_even)
-    second_out = conv_rows(current, conv2_weight[2]) + conv_rows(previous, conv2_weight[1])
-    if frame_count > 1:
-        oldest = jnp.where(is_first, even_before, odd_before)
-        second_out = second_out + conv_rows(oldest, conv2_weight[0])
-    second_out = second_out + conv2_bias
-
-    frame_values = own.astype(jnp.float32)
-    residual = frame_values + second_out
-    normed = rms_scale(residual, attn_gain).astype(jnp.bfloat16)
     token_count = row_count * col_count
+    params = jnp.stack(
+        [1 - band * row_count, height - band * row_count + 1, is_first.astype(jnp.int32)]
+    ).astype(jnp.int32)
+    residual, normed = resnet_block(
+        ext.reshape(2 * frame_count, -1, channels),
+        own.reshape(frame_count, token_count, channels),
+        params,
+        norm1_gain,
+        conv1_weight,
+        conv1_bias,
+        norm2_gain,
+        conv2_weight,
+        conv2_bias,
+        attn_gain,
+        col_count,
+    )
+    normed = normed.reshape(frame_count, row_count, col_count, channels)
     flat = normed.reshape(frame_count * token_count, channels)
     query = (jnp.dot(flat, w_query, preferred_element_type=jnp.float32) + b_query).astype(
         jnp.bfloat16

time: 58.8 us -> 55.4 us (0.942)
  Pallas kernels: 0 us -> 7.31 us
  matrix products: 6.78 us -> 1.86 us
  other arithmetic: 4.38 us -> 2.11 us
  local copies, waits for them, and re-layouts: 8.55 us -> 6.46 us
  waiting for transfers between devices: 7.85 us -> 6.42 us
  blocking collectives: 25.1 us -> 25.7 us
    pallas_call x0 -> x1, Pallas kernels: none -> 7.31 us  [resnet_block(): pl.pallas_call(functools.partial(block_kernel, cols, frame_count), out_sh...]
    conv_general_dilated x4 -> x0, matrix products: 4.98 us -> none  [conv_rows(): lax.conv_general_dilated(source, taps, window_strides=(1, 1), padding=((0...]
    ppermute x1, waiting for transfers between devices: 1.43 us -> 0.01 us  [local(): swapped = lax.ppermute(arrived, 'tm', [(0, 1), (1, 0)])]
    conv_general_dilated x11 -> x0, local copies, waits for them, and re-layouts: 1.27 us -> none  [conv_rows(): lax.conv_general_dilated(source, taps, window_strides=(1, 1), padding=((0...]
    reshape x2, local copies, waits for them, and re-layouts: 0.27 us -> 1.42 us  [the longest x1 1.01 us: local(): normed = normed.reshape(frame_count, row_count, col_count, channels)]
    concatenate x0 -> x1, local copies, waits for them, and re-layouts: none -> 1.13 us  [local(): ext = jnp.concatenate([above, seq, below], axis=1)]
    unnamed x35 -> x19, local copies, waits for them, and re-layouts: 3.02 us -> 2.17 us
    all_gather x1 -> x0, local copies, waits for them, and re-layouts: 0.81 us -> none  [local(): keys = lax.all_gather(keys, 'inner', axis=2, tiled=True)]
  transfers between devices with their start and end apart: 3 -> 3, of which waited for: 3 -> 2; matrix products, arithmetic and copies ran while one was open for 0% -> 4% of each run, Pallas kernels for 0% -> 0%
where the time goes in v3:
time: 55.4 us; the launch traced here: 55.2 us
  blocking collectives  25.7 us (46%)
  Pallas kernels  7.31 us (13%)
  local copies, waits for them, and re-layouts  6.46 us (12%)
  waiting for transfers between devices  6.42 us (12%)
  starting transfers between devices  5.21 us (9%)
  other arithmetic  2.11 us (4%)
  matrix products  1.86 us (3%)
    all_gather x1, blocking collectives, local(): keys = lax.all_gather(normed, 'outer', axis=1, tiled=True)  15.1 us
    all_gather x1, blocking collectives, local(): keys = lax.all_gather(keys, 'inner', axis=2, tiled=True)  10.6 us
    pallas_call x1, Pallas kernels, resnet_block(): pl.pallas_call(functools.partial(block_kernel, cols, frame_count), out_sh...  7.31 us
    ppermute x1, waiting for transfers between devices, local(): arrived = lax.ppermute(edge, ('outer', 'inner', 'tm'), up + down)  5.27 us
    ppermute x1, starting transfers between devices, local(): arrived = lax.ppermute(edge, ('outer', 'inner', 'tm'), up + down)  4.76 us
    unnamed x19, local copies, waits for them, and re-layouts  2.17 us
    ppermute x1, waiting for transfers between devices, local(): partner = lax.ppermute(own, 'tm', [(0, 1), (1, 0)])  1.15 us
    concatenate x1, local copies, waits for them, and re-layouts, local(): ext = jnp.concatenate([above, seq, below], axis=1)  1.13 us
  transfers between devices with their start and end apart: 3, of which 2 were waited for; matrix products, arithmetic and copies ran while one was open for 4% of the time, Pallas kernels for 0%

profile of v3, /device:TPU:0, one launch (start us, length us, event | category | flops | bytes accessed | tf_op | source)
XLA Modules:
  0.0 55.2 jit_solution(6590006350141508224)
XLA Ops:
  0.0 0.0 copy-start
  0.0 0.5 collective-permute-start
  0.5 1.2 %collective-permute-done = bf16[1,2,112,192]{2,3,1,0:T(8,128)(2,1)S(1)} collective-permute-done((bf16[1,2,112,192]{2,3,1,0:T(8,128)(2,1)}, bf16[1,2,112,192]{2,3,1,0:T(8,128)(2,1)S(1)}, u32[]{:S(2)}, u32[]{:S(2)}) %collective-permute-start) | collective-permute-done | bytes 86048 | tf_op jit(solution)/shard_map/ppermute | solution.py:148
  1.6 0.9 %select_bitcast_fusion.1 = (bf16[1,1,2,112,192]{3,4,2,1,0:T(8,128)(2,1)S(1)}, bf16[1,1,2,112,192]{3,4,2,1,0:T(8,128)(2,1)S(1)}) fusion(bf16[1,2,112,192]{2,3,1,0:T(8,128)(2,1)S(1)} %collective-permute-done, pred[]{:T(512)S(6)} %eq.3, bf16[1,1,2,112,192]{3,4,2,1,0:T(8,128)(2,1)} %param.15), kind=kLoop, calls=%fused_computation.22 | loop fusion | flops 86016 | bytes 344065 | tf_op jit(solution)/shard_map/stack | solution.py:151
  2.6 4.8 %collective-permute-start.1 = (bf16[2,2,112,192]{2,3,1,0:T(8,128)(2,1)S(1)}, bf16[2,2,112,192]{2,3,1,0:T(8,128)(2,1)S(1)}, u32[]{:S(2)}, u32[]{:S(2)}) collective-permute-start(bf16[2,2,112,192]{2,3,1,0:T(8,128)(2,1)S(1)} %maximum_bitcast_fusion), channel_id=1, source_target_pairs={{0,2},{2,4},{4,6},{6,8},{8,10},{10,12},{12,14},{3,1},{5,3},{7,5},{... | collective-permute-start | bytes 516104 | tf_op jit(solution)/shard_map/ppermute | solution.py:156
  7.3 5.3 %collective-permute-done.1 = bf16[2,2,112,192]{2,3,1,0:T(8,128)(2,1)S(1)} collective-permute-done((bf16[2,2,112,192]{2,3,1,0:T(8,128)(2,1)S(1)}, bf16[2,2,112,192]{2,3,1,0:T(8,128)(2,1)S(1)}, u32[]{:S(2)}, u32[]{:S(2)}) %collective-permute-start.1) | collective-permute-done | bytes 172064 | tf_op jit(solution)/shard_map/ppermute | solution.py:156
  12.6 0.0 collective-permute-start.2
  12.6 1.6 %copy.26 = bf16[1,1,2,112,192]{4,3,2,1,0:T(8,128)(2,1)} copy(bf16[1,1,2,112,192]{3,4,2,1,0:T(8,128)(2,1)} %param.15) | data formatting | bytes 172032 | tf_op args[0]
  14.3 0.6 %pad_add_fusion.params = s32[3]{0:T(128)} fusion(s32[1]{0:T(128)} %bitcast.2, s32[1]{0:T(128)} %bitcast.1, s32[1]{0:T(128)} %bitcast), kind=kLoop, calls=%fused_computation.23 | loop fusion | flops 6 | bytes 24 | tf_op jit(solution)/shard_map/stack | solution.py:163
  14.9 0.0 collective-permute-done.2
  14.9 0.1 pad_maximum_fusion
  15.0 1.1 %copy.25 = bf16[2,6,112,192]{3,2,1,0:T(8,128)(2,1)} copy(bf16[2,6,112,192]{2,3,1,0:T(8,128)(2,1)S(1)} %pad_maximum_fusion) | data formatting | bytes 1032192 | tf_op jit(solution)/shard_map/concatenate | solution.py:160
  16.2 7.3 %shard_map.145 = (f32[1,224,192]{2,1,0:T(8,128)}, bf16[1,224,192]{2,1,0:T(8,128)(2,1)}) custom-call(s32[3]{0:T(128)} %pad_add_fusion.params, bf16[2,672,192]{2,1,0:T(8,128)(2,1)} %bitcast.40, bf16[1,224,192]{2,1,0:T(8,128)(2,1)} %bitcast.46, f32[1,192]{1,0:T(1,128)} %bitcast.48, bf16[27,192,192]{2,1,0:T(8,128)(2,1)} %bitcast.41, f32[1,192]{1,0:T(1,128)} %bitcast.49, ...), custom_call_target="tpu_custom_call" | custom-call | tf_op jit(solution)/shard_map/pallas_call | solution.py:113
  23.5 1.0 %copy.27 = bf16[1,2,112,192]{2,3,0,1:T(8,128)(2,1)S(1)} copy(bf16[1,2,112,192]{3,2,1,0:T(8,128)(2,1)} %bitcast.45) | data formatting | bytes 172032 | tf_op jit(solution)/shard_map/reshape | solution.py:179
  24.5 15.1 %all_gather.6 = bf16[1,8,112,192]{2,3,0,1:T(8,128)(2,1)S(1)} all-gather(bf16[1,2,112,192]{2,3,0,1:T(8,128)(2,1)S(1)} %copy.27), channel_id=1, replica_groups=mesh['clips'=2,'outer'=4,'inner'=2,'tm'=2] {'outer'}, dimensions={1}, use_global_device_ids=true | all-gather | bytes 430080 | tf_op jit(solution)/shard_map/all_gather | solution.py:189
  39.6 0.4 copy.28
  40.0 10.6 %all_gather.7 = bf16[1,4,2,2,112,192]{4,3,2,1,5,0:T(2,128)(2,1)S(1)} all-gather(bf16[1,4,1,2,112,192]{4,3,2,1,5,0:T(2,128)(2,1)S(1)} %copy.28), channel_id=1, replica_groups=mesh['clips'=2,'outer'=4,'inner'=2,'tm'=2] {'inner'}, dimensions={2}, use_global_device_ids=true | all-gather | bytes 1032192 | tf_op jit(solution)/shard_map/all_gather | solution.py:191
  50.6 0.9 %reshape.85 = bf16[1792,192]{0,1:T(8,128)(2,1)S(1)} reshape(bf16[1,4,2,2,112,192]{4,3,2,1,5,0:T(2,128)(2,1)S(1)} %all_gather.7) | data formatting | bytes 1376256 | tf_op jit(solution)/shard_map/reshape.1
  51.5 0.4 fusion.6
  52.0 0.5 fusion.13
  52.5 0.4 fusion
  52.8 0.0 copy-start.4
  52.8 0.0 copy-start.5
  52.9 0.0 copy-start.7
  52.9 0.0 copy-start.8
  52.9 0.5 fusion.4
  53.4 0.4 copy-done.2
  53.8 0.1 copy-done.4
  53.8 0.0 copy-done.5
  53.9 0.0 copy-done.7
  53.9 0.5 fusion.2
  54.4 0.8 %copy.30 = f32[1,1,2,112,192]{3,4,2,1,0:T(8,128)} copy(f32[1,1,2,112,192]{4,3,2,1,0:T(8,128)S(1)} %bitcast.44) | data formatting | bytes 344064 | tf_op jit(solution)/shard_map/reshape | solution.py:209
  (11 shorter events, 0.1 us)
Async XLA Ops:
  0.0 51.5 %copy-start = (bf16[192,192]{1,0:T(8,128)(2,1)S(1)}, bf16[192,192]{1,0:T(8,128)(2,1)}, u32[]{:S(2)}) copy-start(bf16[192,192]{1,0:T(8,128)(2,1)} %param.25) | copy-start | bytes 221188
  0.0 1.6 %collective-permute-start = (bf16[1,2,112,192]{2,3,1,0:T(8,128)(2,1)}, bf16[1,2,112,192]{2,3,1,0:T(8,128)(2,1)S(1)}, u32[]{:S(2)}, u32[]{:S(2)}) collective-permute-start(bf16[1,2,112,192]{2,3,1,0:T(8,128)(2,1)} %bitcast.47), channel_id=1, source_target_pairs={{0,1},{1,0},{2,3},{3,2},{4,5},{5,4},{6,7},{7,6},{8,9},{9,8},{10,11... | collective-permute-start | bytes 258056 | tf_op jit(solution)/shard_map/ppermute | solution.py:148
  2.6 10.0 %collective-permute-start.1 = (bf16[2,2,112,192]{2,3,1,0:T(8,128)(2,1)S(1)}, bf16[2,2,112,192]{2,3,1,0:T(8,128)(2,1)S(1)}, u32[]{:S(2)}, u32[]{:S(2)}) collective-permute-start(bf16[2,2,112,192]{2,3,1,0:T(8,128)(2,1)S(1)} %maximum_bitcast_fusion), channel_id=1, source_target_pairs={{0,2},{2,4},{4,6},{6,8},{8,10},{10,12},{12,14},{3,1},{5,3},{7,5},{... | collective-permute-start | bytes 516104 | tf_op jit(solution)/shard_map/ppermute | solution.py:156
  12.6 2.3 %collective-permute-start.2 = (bf16[2,2,112,192]{2,3,1,0:T(8,128)(2,1)S(1)}, bf16[2,2,112,192]{2,3,1,0:T(8,128)(2,1)S(1)}, u32[]{:S(2)}, u32[]{:S(2)}) collective-permute-start(bf16[2,2,112,192]{2,3,1,0:T(8,128)(2,1)S(1)} %collective-permute-done.1), channel_id=1, source_target_pairs={{0,1},{1,0},{2,3},{3,2},{4,5},{5,4},{6,7},{7,6},{8,9},{9,8},{10,11... | collective-permute-start | bytes 516104 | tf_op jit(solution)/shard_map/ppermute | solution.py:157
  39.5 12.0 %copy-start.1 = (bf16[1,224,192]{2,1,0:T(8,128)(2,1)S(1)}, bf16[1,224,192]{2,1,0:T(8,128)(2,1)}, u32[]{:S(2)}) copy-start(bf16[1,224,192]{2,1,0:T(8,128)(2,1)} %get-tuple-element.8) | copy-start | bytes 258052
  39.5 12.0 %copy-start.3 = (bf16[192,192]{1,0:T(8,128)(2,1)S(1)}, bf16[192,192]{1,0:T(8,128)(2,1)}, u32[]{:S(2)}) copy-start(bf16[192,192]{1,0:T(8,128)(2,1)} %param.23) | copy-start | bytes 221188
  39.6 12.0 %copy-start.6 = (f32[192]{0:T(256)S(1)}, f32[192]{0:T(256)}, u32[]{:S(2)}) copy-start(f32[192]{0:T(256)} %param.24) | copy-start | bytes 2308
  52.8 0.9 %copy-start.2 = (f32[1,224,192]{2,1,0:T(8,128)S(1)}, f32[1,224,192]{2,1,0:T(8,128)}, u32[]{:S(2)}) copy-start(f32[1,224,192]{2,1,0:T(8,128)} %get-tuple-element.7) | copy-start | bytes 516100
  52.8 1.0 %copy-start.4 = (bf16[192,192]{1,0:T(8,128)(2,1)S(1)}, bf16[192,192]{1,0:T(8,128)(2,1)}, u32[]{:S(2)}) copy-start(bf16[192,192]{1,0:T(8,128)(2,1)} %param.28) | copy-start | bytes 221188
  52.8 1.0 %copy-start.5 = (bf16[192,192]{1,0:T(8,128)(2,1)S(1)}, bf16[192,192]{1,0:T(8,128)(2,1)}, u32[]{:S(2)}) copy-start(bf16[192,192]{1,0:T(8,128)(2,1)} %param.26) | copy-start | bytes 221188
  52.9 1.0 %copy-start.7 = (f32[192]{0:T(256)S(1)}, f32[192]{0:T(256)}, u32[]{:S(2)}) copy-start(f32[192]{0:T(256)} %param.29) | copy-start | bytes 2308
  52.9 1.0 %copy-start.8 = (f32[192]{0:T(256)S(1)}, f32[192]{0:T(256)}, u32[]{:S(2)}) copy-start(f32[192]{0:T(256)} %param.27) | copy-start | bytes 2308

commit v4 on v3

--- a/solution.py
+++ b/solution.py
@@ -186,17 +186,28 @@
     ).astype(jnp.bfloat16)
     folded = folded.reshape(frame_count, token_count, channels)
 
+    swap = [(0, 1), (1, 0)]
+    partner_queries = lax.ppermute(folded, "inner", swap)
     keys = lax.all_gather(normed, "outer", axis=1, tiled=True)
-    keys = keys.reshape(frame_count, -1, 1, row_count, col_count, channels)
-    keys = lax.all_gather(keys, "inner", axis=2, tiled=True)
-    keys = keys.reshape(frame_count, height * col_count, channels)
-    scores = jnp.einsum("fqc,fkc->fqk", folded, keys, preferred_element_type=jnp.float32)
+    keys = keys.reshape(frame_count, -1, channels)
+    queries = jnp.concatenate([folded, partner_queries], axis=1)
+    scores = jnp.einsum("fqc,fkc->fqk", queries, keys, preferred_element_type=jnp.float32)
     top = jnp.max(scores, axis=-1, keepdims=True)
     weights = jnp.exp(scores - top)
     total = jnp.sum(weights, axis=-1, keepdims=True)
     accum = jnp.einsum(
         "fqk,fkc->fqc", weights.astype(jnp.bfloat16), keys, preferred_element_type=jnp.float32
     )
+    packed = jnp.concatenate([accum, top, total], axis=-1)
+    returned = lax.ppermute(packed[:, token_count:], "inner", swap)
+    mine = packed[:, :token_count]
+    top_mine = mine[..., channels : channels + 1]
+    top_back = returned[..., channels : channels + 1]
+    highest = jnp.maximum(top_mine, top_back)
+    scale_mine = jnp.exp(top_mine - highest)
+    scale_back = jnp.exp(top_back - highest)
+    total = mine[..., channels + 1 :] * scale_mine + returned[..., channels + 1 :] * scale_back
+    accum = mine[..., :channels] * scale_mine + returned[..., :channels] * scale_back
     mixed = (accum / total).astype(jnp.bfloat16).reshape(-1, channels)
     value = (jnp.dot(mixed, w_value, preferred_element_type=jnp.float32) + b_value).astype(
         jnp.bfloat16

time: 55.4 us -> 53.5 us (0.966)
  blocking collectives: 25.7 us -> 15.3 us
  waiting for transfers between devices: 6.42 us -> 12.2 us
  starting transfers between devices: 5.21 us -> 7.83 us
  local copies, waits for them, and re-layouts: 6.46 us -> 5.21 us
  matrix products: 1.86 us -> 2.94 us
    all_gather x1 -> x0, blocking collectives: 10.6 us -> none  [local(): keys = lax.all_gather(keys, 'inner', axis=2, tiled=True)]
    ppermute x0 -> x2, waiting for transfers between devices: none -> 5.75 us  [the longest x1 5.74 us: local(): returned = lax.ppermute(packed[:, token_count:], 'inner', swap)]
    ppermute x0 -> x2, starting transfers between devices: none -> 2.61 us  [the longest x1 2.54 us: local(): partner_queries = lax.ppermute(folded, 'inner', swap)]
    dot_general x1, matrix products: 0.4 us -> 1.3 us  [local(): jnp.dot(query, w_key.T, preferred_element_type=jnp.float32)]
    another operation x1, local copies, waits for them, and re-layouts: 0.94 us -> 0.31 us
    unnamed x19 -> x17, local copies, waits for them, and re-layouts: 2.17 us -> 1.68 us
  transfers between devices with their start and end apart: 3 -> 5, of which waited for: 2 -> 3; matrix products, arithmetic and copies ran while one was open for 4% -> 5% of each run, Pallas kernels for 0% -> 0%
where the time goes in v4:
time: 53.5 us; the launch traced here: 53.3 us
  blocking collectives  15.3 us (29%)
  waiting for transfers between devices  12.2 us (23%)
  starting transfers between devices  7.83 us (15%)
  Pallas kernels  7.32 us (14%)
  local copies, waits for them, and re-layouts  5.21 us (10%)
  matrix products  2.94 us (5%)
  other arithmetic  2.25 us (4%)
    all_gather x1, blocking collectives, local(): keys = lax.all_gather(normed, 'outer', axis=1, tiled=True)  15.3 us
    pallas_call x1, Pallas kernels, resnet_block(): pl.pallas_call(functools.partial(block_kernel, cols, frame_count), out_sh...  7.32 us
    ppermute x1, waiting for transfers between devices, local(): returned = lax.ppermute(packed[:, token_count:], 'inner', swap)  5.74 us
    ppermute x1, waiting for transfers between devices, local(): arrived = lax.ppermute(edge, ('outer', 'inner', 'tm'), up + down)  5.27 us
    ppermute x1, starting transfers between devices, local(): arrived = lax.ppermute(edge, ('outer', 'inner', 'tm'), up + down)  4.76 us
    ppermute x1, starting transfers between devices, local(): partner_queries = lax.ppermute(folded, 'inner', swap)  2.54 us
    unnamed x17, local copies, waits for them, and re-layouts  1.68 us
    dot_general x1, matrix products, local(): jnp.dot(query, w_key.T, preferred_element_type=jnp.float32)  1.3 us
  transfers between devices with their start and end apart: 5, of which 3 were waited for; matrix products, arithmetic and copies ran while one was open for 5% of the time, Pallas kernels for 0%

profile of v4, /device:TPU:0, one launch (start us, length us, event | category | flops | bytes accessed | tf_op | source)
XLA Modules:
  0.0 53.3 jit_solution(10673728412736198362)
XLA Ops:
  0.0 0.0 copy-start
  0.0 0.5 collective-permute-start
  0.5 1.2 %collective-permute-done = bf16[1,2,112,192]{2,3,1,0:T(8,128)(2,1)S(1)} collective-permute-done((bf16[1,2,112,192]{2,3,1,0:T(8,128)(2,1)}, bf16[1,2,112,192]{2,3,1,0:T(8,128)(2,1)S(1)}, u32[]{:S(2)}, u32[]{:S(2)}) %collective-permute-start) | collective-permute-done | bytes 86048 | tf_op jit(solution)/shard_map/ppermute | solution.py:148
  1.6 0.9 %select_bitcast_fusion.1 = (bf16[1,1,2,112,192]{3,4,2,1,0:T(8,128)(2,1)S(1)}, bf16[1,1,2,112,192]{3,4,2,1,0:T(8,128)(2,1)S(1)}) fusion(bf16[1,2,112,192]{2,3,1,0:T(8,128)(2,1)S(1)} %collective-permute-done, pred[]{:T(512)S(6)} %eq.3, bf16[1,1,2,112,192]{3,4,2,1,0:T(8,128)(2,1)} %param.15), kind=kLoop, calls=%fused_computation.36 | loop fusion | flops 86016 | bytes 344065 | tf_op jit(solution)/shard_map/stack | solution.py:151
  2.6 4.8 %collective-permute-start.1 = (bf16[2,2,112,192]{2,3,1,0:T(8,128)(2,1)S(1)}, bf16[2,2,112,192]{2,3,1,0:T(8,128)(2,1)S(1)}, u32[]{:S(2)}, u32[]{:S(2)}) collective-permute-start(bf16[2,2,112,192]{2,3,1,0:T(8,128)(2,1)S(1)} %maximum_bitcast_fusion), channel_id=1, source_target_pairs={{0,2},{2,4},{4,6},{6,8},{8,10},{10,12},{12,14},{3,1},{5,3},{7,5},{... | collective-permute-start | bytes 516104 | tf_op jit(solution)/shard_map/ppermute | solution.py:156
  7.3 5.3 %collective-permute-done.1 = bf16[2,2,112,192]{2,3,1,0:T(8,128)(2,1)S(1)} collective-permute-done((bf16[2,2,112,192]{2,3,1,0:T(8,128)(2,1)S(1)}, bf16[2,2,112,192]{2,3,1,0:T(8,128)(2,1)S(1)}, u32[]{:S(2)}, u32[]{:S(2)}) %collective-permute-start.1) | collective-permute-done | bytes 172064 | tf_op jit(solution)/shard_map/ppermute | solution.py:156
  12.6 0.0 collective-permute-start.2
  12.6 1.6 %copy.26 = bf16[1,1,2,112,192]{4,3,2,1,0:T(8,128)(2,1)} copy(bf16[1,1,2,112,192]{3,4,2,1,0:T(8,128)(2,1)} %param.15) | data formatting | bytes 172032 | tf_op args[0]
  14.3 0.6 %pad_add_fusion.params = s32[3]{0:T(128)} fusion(s32[1]{0:T(128)} %bitcast.2, s32[1]{0:T(128)} %bitcast.1, s32[1]{0:T(128)} %bitcast), kind=kLoop, calls=%fused_computation.44 | loop fusion | flops 6 | bytes 24 | tf_op jit(solution)/shard_map/stack | solution.py:163
  14.8 0.0 collective-permute-done.2
  14.9 0.1 pad_maximum_fusion
  15.0 1.1 %copy.25 = bf16[2,6,112,192]{3,2,1,0:T(8,128)(2,1)} copy(bf16[2,6,112,192]{2,3,1,0:T(8,128)(2,1)S(1)} %pad_maximum_fusion) | data formatting | bytes 1032192 | tf_op jit(solution)/shard_map/concatenate | solution.py:160
  16.1 7.3 %shard_map.145 = (f32[1,224,192]{2,1,0:T(8,128)}, bf16[1,224,192]{2,1,0:T(8,128)(2,1)}) custom-call(s32[3]{0:T(128)} %pad_add_fusion.params, bf16[2,672,192]{2,1,0:T(8,128)(2,1)} %bitcast.57, bf16[1,224,192]{2,1,0:T(8,128)(2,1)} %bitcast.61, f32[1,192]{1,0:T(1,128)} %bitcast.68, bf16[27,192,192]{2,1,0:T(8,128)(2,1)} %bitcast.58, f32[1,192]{1,0:T(1,128)} %bitcast.69, ...), custom_call_target="tpu_custom_call" | custom-call | tf_op jit(solution)/shard_map/pallas_call | solution.py:113
  23.5 1.0 %copy.27 = bf16[1,2,112,192]{2,3,0,1:T(8,128)(2,1)S(1)} copy(bf16[1,2,112,192]{3,2,1,0:T(8,128)(2,1)} %bitcast.60) | data formatting | bytes 172032 | tf_op jit(solution)/shard_map/reshape | solution.py:179
  24.5 1.3 %fusion.6 = bf16[1,224,192]{1,2,0:T(8,128)(2,1)S(1)} fusion(bf16[192,192]{1,0:T(8,128)(2,1)S(1)} %copy-done, bf16[192,192]{1,0:T(8,128)(2,1)S(1)} %copy-done.1, bf16[1,224,192]{2,1,0:T(8,128)(2,1)} %get-tuple-element.8, f32[192]{0:T(256)S(1)} %copy-done.2), kind=kOutput, calls=%fused_computation.12 | convolution fusion | flops 33202176 | bytes 320256 | tf_op jit(solution)/shard_map/dot_general | solution.py:185
  25.8 2.5 %collective-permute-start.3 = (bf16[1,224,192]{1,2,0:T(8,128)(2,1)S(1)}, bf16[1,224,192]{1,2,0:T(8,128)(2,1)S(1)}, u32[]{:S(2)}, u32[]{:S(2)}) collective-permute-start(bf16[1,224,192]{1,2,0:T(8,128)(2,1)S(1)} %fusion.6), channel_id=1, source_target_pairs={{0,2},{2,0},{1,3},{3,1},{4,6},{6,4},{5,7},{7,5},{8,10},{10,8},{9,1... | collective-permute-start | bytes 258056 | tf_op jit(solution)/shard_map/ppermute | solution.py:190
  28.4 15.3 %all_gather.3 = bf16[1,8,112,192]{2,3,0,1:T(8,128)(2,1)S(1)} all-gather(bf16[1,2,112,192]{2,3,0,1:T(8,128)(2,1)S(1)} %copy.27), channel_id=1, replica_groups=mesh['clips'=2,'outer'=4,'inner'=2,'tm'=2] {'outer'}, dimensions={1}, use_global_device_ids=true | all-gather | bytes 430080 | tf_op jit(solution)/shard_map/all_gather | solution.py:191
  43.7 0.3 copy.28
  44.0 0.3 reshape.88
  44.3 0.0 collective-permute-done.3
  44.3 0.6 %fusion.33 = (f32[448]{0:T(512)S(1)}, f32[448,896]{1,0:T(8,128)S(1)}) fusion(bf16[896,192]{0,1:T(8,128)(2,1)S(1)} %reshape.88, bf16[1,224,192]{1,2,0:T(8,128)(2,1)S(1)} %collective-permute-done.3, bf16[1,224,192]{1,2,0:T(8,128)(2,1)S(1)} %fusion.6), kind=kOutput, calls=%fused_computation.46 | convolution fusion | flops 154885696 | bytes 2123520 | tf_op jit(solution)/shard_map/fqc,fkc->fqk/dot_general | solution.py:194
  44.9 0.5 %convolution_bitcast_fusion = f32[1,448,192]{1,2,0:T(8,128)S(1)} fusion(bf16[896,192]{0,1:T(8,128)(2,1)S(1)} %reshape.88, f32[448,896]{1,0:T(8,128)S(1)} %get-tuple-element.17, f32[448]{0:T(512)S(1)} %get-tuple-element.16), kind=kOutput, calls=%fused_computation.3 | convolution fusion | flops 154943488 | bytes 2295552 | tf_op jit(solution)/shard_map/fqk,fkc->fqc/dot_general | solution.py:198
  45.5 0.0 copy-start.4
  45.5 0.0 copy-start.5
  45.5 0.0 copy-start.6
  45.5 0.0 copy-start.7
  45.5 0.4 fusion
  46.0 0.1 pad_maximum_fusion.1
  46.1 0.1 collective-permute-start.4
  46.2 5.7 %collective-permute-done.4 = f32[1,224,194]{1,2,0:T(8,128)S(1)} collective-permute-done((f32[1,224,194]{1,2,0:T(8,128)S(1)}, f32[1,224,194]{1,2,0:T(8,128)S(1)}, u32[]{:S(2)}, u32[]{:S(2)}) %collective-permute-start.4) | collective-permute-done | bytes 173856 | tf_op jit(solution)/shard_map/ppermute | solution.py:202
  52.0 0.5 fusion.2
  52.5 0.8 %copy.30 = f32[1,1,2,112,192]{3,4,2,1,0:T(8,128)} copy(f32[1,1,2,112,192]{4,3,2,1,0:T(8,128)S(1)} %bitcast.63) | data formatting | bytes 344064 | tf_op jit(solution)/shard_map/reshape | solution.py:220
  (14 shorter events, 0.1 us)
Async XLA Ops:
  0.0 24.5 %copy-start = (bf16[192,192]{1,0:T(8,128)(2,1)S(1)}, bf16[192,192]{1,0:T(8,128)(2,1)}, u32[]{:S(2)}) copy-start(bf16[192,192]{1,0:T(8,128)(2,1)} %param.25) | copy-start | bytes 221188
  0.0 1.6 %collective-permute-start = (bf16[1,2,112,192]{2,3,1,0:T(8,128)(2,1)}, bf16[1,2,112,192]{2,3,1,0:T(8,128)(2,1)S(1)}, u32[]{:S(2)}, u32[]{:S(2)}) collective-permute-start(bf16[1,2,112,192]{2,3,1,0:T(8,128)(2,1)} %bitcast.62), channel_id=1, source_target_pairs={{0,1},{1,0},{2,3},{3,2},{4,5},{5,4},{6,7},{7,6},{8,9},{9,8},{10,11... | collective-permute-start | bytes 258056 | tf_op jit(solution)/shard_map/ppermute | solution.py:148
  2.6 10.0 %collective-permute-start.1 = (bf16[2,2,112,192]{2,3,1,0:T(8,128)(2,1)S(1)}, bf16[2,2,112,192]{2,3,1,0:T(8,128)(2,1)S(1)}, u32[]{:S(2)}, u32[]{:S(2)}) collective-permute-start(bf16[2,2,112,192]{2,3,1,0:T(8,128)(2,1)S(1)} %maximum_bitcast_fusion), channel_id=1, source_target_pairs={{0,2},{2,4},{4,6},{6,8},{8,10},{10,12},{12,14},{3,1},{5,3},{7,5},{... | collective-permute-start | bytes 516104 | tf_op jit(solution)/shard_map/ppermute | solution.py:156
  12.6 2.2 %collective-permute-start.2 = (bf16[2,2,112,192]{2,3,1,0:T(8,128)(2,1)S(1)}, bf16[2,2,112,192]{2,3,1,0:T(8,128)(2,1)S(1)}, u32[]{:S(2)}, u32[]{:S(2)}) collective-permute-start(bf16[2,2,112,192]{2,3,1,0:T(8,128)(2,1)S(1)} %collective-permute-done.1), channel_id=1, source_target_pairs={{0,1},{1,0},{2,3},{3,2},{4,5},{5,4},{6,7},{7,6},{8,9},{9,8},{10,11... | collective-permute-start | bytes 516104 | tf_op jit(solution)/shard_map/ppermute | solution.py:157
  16.1 8.4 %copy-start.1 = (bf16[192,192]{1,0:T(8,128)(2,1)S(1)}, bf16[192,192]{1,0:T(8,128)(2,1)}, u32[]{:S(2)}) copy-start(bf16[192,192]{1,0:T(8,128)(2,1)} %param.23) | copy-start | bytes 221188
  16.1 8.4 %copy-start.2 = (f32[192]{0:T(256)S(1)}, f32[192]{0:T(256)}, u32[]{:S(2)}) copy-start(f32[192]{0:T(256)} %param.24) | copy-start | bytes 2308
  25.8 18.5 %collective-permute-start.3 = (bf16[1,224,192]{1,2,0:T(8,128)(2,1)S(1)}, bf16[1,224,192]{1,2,0:T(8,128)(2,1)S(1)}, u32[]{:S(2)}, u32[]{:S(2)}) collective-permute-start(bf16[1,224,192]{1,2,0:T(8,128)(2,1)S(1)} %fusion.6), channel_id=1, source_target_pairs={{0,2},{2,0},{1,3},{3,1},{4,6},{6,4},{5,7},{7,5},{8,10},{10,8},{9,1... | collective-permute-start | bytes 258056 | tf_op jit(solution)/shard_map/ppermute | solution.py:190
  45.5 6.4 %copy-start.3 = (f32[1,224,192]{2,1,0:T(8,128)S(1)}, f32[1,224,192]{2,1,0:T(8,128)}, u32[]{:S(2)}) copy-start(f32[1,224,192]{2,1,0:T(8,128)} %get-tuple-element.7) | copy-start | bytes 516100
  45.5 6.4 %copy-start.4 = (bf16[192,192]{1,0:T(8,128)(2,1)S(1)}, bf16[192,192]{1,0:T(8,128)(2,1)}, u32[]{:S(2)}) copy-start(bf16[192,192]{1,0:T(8,128)(2,1)} %param.28) | copy-start | bytes 221188
  45.5 6.4 %copy-start.5 = (bf16[192,192]{1,0:T(8,128)(2,1)S(1)}, bf16[192,192]{1,0:T(8,128)(2,1)}, u32[]{:S(2)}) copy-start(bf16[192,192]{1,0:T(8,128)(2,1)} %param.26) | copy-start | bytes 221188
  45.5 6.4 %copy-start.6 = (f32[192]{0:T(256)S(1)}, f32[192]{0:T(256)}, u32[]{:S(2)}) copy-start(f32[192]{0:T(256)} %param.29) | copy-start | bytes 2308
  45.5 6.4 %copy-start.7 = (f32[192]{0:T(256)S(1)}, f32[192]{0:T(256)}, u32[]{:S(2)}) copy-start(f32[192]{0:T(256)} %param.27) | copy-start | bytes 2308
  46.1 5.8 %collective-permute-start.4 = (f32[1,224,194]{1,2,0:T(8,128)S(1)}, f32[1,224,194]{1,2,0:T(8,128)S(1)}, u32[]{:S(2)}, u32[]{:S(2)}) collective-permute-start(f32[1,224,194]{1,2,0:T(8,128)S(1)} %pad_maximum_fusion.1), channel_id=1, source_target_pairs={{0,2},{2,0},{1,3},{3,1},{4,6},{6,4},{5,7},{7,5},{8,10},{10,8},{9,1... | collective-permute-start | bytes 521480 | tf_op jit(solution)/shard_map/ppermute | solution.py:202

commit v5 on v4

--- a/solution.py
+++ b/solution.py
@@ -47,7 +47,7 @@
 def _silu(v):
     return v * (1.0 / (1.0 + jnp.exp(-v)))
 
-def block_kernel(cols, frame_count, params, ext_ref, own_ref, g1_ref, w1_ref, b1_ref, g2_ref,
+def block_kernel(cols, frame_count, ext_ref, g1_ref, w1_ref, b1_ref, g2_ref,
                  w2_ref, b2_ref, ga_ref, res_ref, normed_ref):
     total = 2 * frame_count
     p_in = ext_ref.shape[1]
@@ -75,9 +75,13 @@
 
     g1 = g1_ref[...]
     act1 = [shifted(_silu(_rms(ext_ref[t].astype(jnp.float32), g1)).astype(jnp.bfloat16).astype(jnp.float32)) for t in range(total)]
-    lo = params[0]
-    hi = params[1]
-    first = params[2] == 1
+    inner = lax.axis_size("inner")
+    band = lax.axis_index("outer") * inner + lax.axis_index("inner")
+    band_rows = p_out // cols
+    height = lax.axis_size("outer") * inner * band_rows
+    lo = 1 - band * band_rows
+    hi = height - band * band_rows + 1
+    first = lax.axis_index("tm") == 0
     row = lax.broadcasted_iota(jnp.int32, (p_mid, 1), 0) // cols
     inside = (row >= lo) & (row < hi)
     g2 = g2_ref[...]
@@ -101,22 +105,24 @@
             return shifted(jnp.where(first, a, b))
         srcs = [pick(2 * k - 2), pick(2 * k - 1), pick(2 * k)]
         out2 = conv_frame(srcs, w2_ref, p_out) + b2
-        res = own_ref[k].astype(jnp.float32) + out2
+        body = slice(HALO * cols, HALO * cols + p_out)
+        own = jnp.where(first, ext_ref[2 * k, body], ext_ref[2 * k + 1, body])
+        res = own.astype(jnp.float32) + out2
         res_ref[k] = res
         normed_ref[k] = _rms(res, ga).astype(jnp.bfloat16)
 
-def resnet_block(ext, own, params, g1, w1, b1, g2, w2, b2, ga, cols):
+def resnet_block(ext, g1, w1, b1, g2, w2, b2, ga, cols):
     total, p_in, c = ext.shape
-    frame_count, p_out, _ = own.shape
+    frame_count = total // 2
+    p_out = p_in - 4 * cols
     vm = pl.BlockSpec(memory_space=pltpu.VMEM)
-    sm = pl.BlockSpec(memory_space=pltpu.SMEM)
     return pl.pallas_call(
         functools.partial(block_kernel, cols, frame_count),
         out_shape=(jax.ShapeDtypeStruct((frame_count, p_out, c), jnp.float32),
                    jax.ShapeDtypeStruct((frame_count, p_out, c), jnp.bfloat16)),
-        in_specs=[sm] + [vm] * 9,
+        in_specs=[vm] * 8,
         out_specs=(vm, vm),
-    )(params, ext, own, g1.reshape(1, c), w1.reshape(27, c, c), b1.reshape(1, c), g2.reshape(1, c),
+    )(ext, g1.reshape(1, c), w1.reshape(27, c, c), b1.reshape(1, c), g2.reshape(1, c),
       w2.reshape(27, c, c), b2.reshape(1, c), ga.reshape(1, c))
 
 
@@ -160,13 +166,8 @@
     ext = jnp.concatenate([above, seq, below], axis=1)
 
     token_count = row_count * col_count
-    params = jnp.stack(
-        [1 - band * row_count, height - band * row_count + 1, is_first.astype(jnp.int32)]
-    ).astype(jnp.int32)
     residual, normed = resnet_block(
         ext.reshape(2 * frame_count, -1, channels),
-        own.reshape(frame_count, token_count, channels),
-        params,
         norm1_gain,
         conv1_weight,
         conv1_bias,
@@ -190,17 +191,18 @@
     partner_queries = lax.ppermute(folded, "inner", swap)
     keys = lax.all_gather(normed, "outer", axis=1, tiled=True)
     keys = keys.reshape(frame_count, -1, channels)
-    queries = jnp.concatenate([folded, partner_queries], axis=1)
-    scores = jnp.einsum("fqc,fkc->fqk", queries, keys, preferred_element_type=jnp.float32)
-    top = jnp.max(scores, axis=-1, keepdims=True)
-    weights = jnp.exp(scores - top)
-    total = jnp.sum(weights, axis=-1, keepdims=True)
-    accum = jnp.einsum(
-        "fqk,fkc->fqc", weights.astype(jnp.bfloat16), keys, preferred_element_type=jnp.float32
-    )
-    packed = jnp.concatenate([accum, top, total], axis=-1)
-    returned = lax.ppermute(packed[:, token_count:], "inner", swap)
-    mine = packed[:, :token_count]
+    def partial(queries):
+        scores = jnp.einsum("fqc,fkc->fqk", queries, keys, preferred_element_type=jnp.float32)
+        top = jnp.max(scores, axis=-1, keepdims=True)
+        weights = jnp.exp(scores - top)
+        total = jnp.sum(weights, axis=-1, keepdims=True)
+        accum = jnp.einsum(
+            "fqk,fkc->fqc", weights.astype(jnp.bfloat16), keys, preferred_element_type=jnp.float32
+        )
+        return jnp.concatenate([accum, top, total], axis=-1)
+
+    returned = lax.ppermute(partial(partner_queries), "inner", swap)
+    mine = partial(folded)
     top_mine = mine[..., channels : channels + 1]
     top_back = returned[..., channels : channels + 1]
     highest = jnp.maximum(top_mine, top_back)

time: 53.5 us -> 52.2 us (0.976)
  local copies, waits for them, and re-layouts: 5.21 us -> 3.55 us
  waiting for transfers between devices: 12.2 us -> 12.9 us
    unnamed x17 -> x16, local copies, waits for them, and re-layouts: 1.68 us -> 0.04 us
    ppermute x1, waiting for transfers between devices: 0.01 us -> 1.44 us  [local(): swapped = lax.ppermute(arrived, 'tm', [(0, 1), (1, 0)])]
    ppermute x1, waiting for transfers between devices: 5.74 us -> 5.06 us  [local(): returned = lax.ppermute(partial(partner_queries), 'inner', swap)]
    another operation x1 -> x0, other arithmetic: 0.58 us -> none  [local(): jnp.stack([1 - band * row_count, height - band * row_count + 1, is_first....]
    dot_general x2 -> x4, matrix products: 1.18 us -> 1.63 us  [the longest x2 0.85 us: partial(): jnp.einsum('fqk,fkc->fqc', weights.astype(jnp.bfloat16), keys, preferred_...]
  transfers between devices with their start and end apart: 5 -> 5, of which waited for: 3 -> 4; matrix products, arithmetic and copies ran while one was open for 5% -> 2% of each run, Pallas kernels for 0% -> 0%
where the time goes in v5:
time: 52.2 us; the launch traced here: 52 us
  blocking collectives  15.1 us (29%)
  waiting for transfers between devices  12.9 us (25%)
  starting transfers between devices  7.83 us (15%)
  Pallas kernels  7.24 us (14%)
  local copies, waits for them, and re-layouts  3.55 us (7%)
  matrix products  3.39 us (6%)
  other arithmetic  1.73 us (3%)
    all_gather x1, blocking collectives, local(): keys = lax.all_gather(normed, 'outer', axis=1, tiled=True)  15.1 us
    pallas_call x1, Pallas kernels, resnet_block(): pl.pallas_call(functools.partial(block_kernel, cols, frame_count), out_sh...  7.24 us
    ppermute x1, waiting for transfers between devices, local(): arrived = lax.ppermute(edge, ('outer', 'inner', 'tm'), up + down)  5.27 us
    ppermute x1, waiting for transfers between devices, local(): returned = lax.ppermute(partial(partner_queries), 'inner', swap)  5.06 us
    ppermute x1, starting transfers between devices, local(): arrived = lax.ppermute(edge, ('outer', 'inner', 'tm'), up + down)  4.76 us
    ppermute x1, starting transfers between devices, local(): partner_queries = lax.ppermute(folded, 'inner', swap)  2.54 us
    ppermute x1, waiting for transfers between devices, local(): swapped = lax.ppermute(arrived, 'tm', [(0, 1), (1, 0)])  1.44 us
    dot_general x1, matrix products, local(): jnp.dot(query, w_key.T, preferred_element_type=jnp.float32)  1.3 us
  transfers between devices with their start and end apart: 5, of which 4 were waited for; matrix products, arithmetic and copies ran while one was open for 2% of the time, Pallas kernels for 0%

profile of v5, /device:TPU:0, one launch (start us, length us, event | category | flops | bytes accessed | tf_op | source)
XLA Modules:
  0.0 52.0 jit_solution(10878354960770372812)
XLA Ops:
  0.0 0.0 copy-start
  0.0 0.5 collective-permute-start
  0.5 1.2 %collective-permute-done = bf16[1,2,112,192]{2,3,1,0:T(8,128)(2,1)S(1)} collective-permute-done((bf16[1,2,112,192]{2,3,1,0:T(8,128)(2,1)}, bf16[1,2,112,192]{2,3,1,0:T(8,128)(2,1)S(1)}, u32[]{:S(2)}, u32[]{:S(2)}) %collective-permute-start) | collective-permute-done | bytes 86048 | tf_op jit(solution)/shard_map/ppermute | solution.py:154
  1.6 0.9 %select_bitcast_fusion.1 = (bf16[1,1,2,112,192]{3,4,2,1,0:T(8,128)(2,1)S(1)}, bf16[1,1,2,112,192]{3,4,2,1,0:T(8,128)(2,1)S(1)}) fusion(bf16[1,2,112,192]{2,3,1,0:T(8,128)(2,1)S(1)} %collective-permute-done, pred[]{:T(512)S(6)} %eq.3, bf16[1,1,2,112,192]{3,4,2,1,0:T(8,128)(2,1)} %param.15), kind=kLoop, calls=%fused_computation.36 | loop fusion | flops 86016 | bytes 344065 | tf_op jit(solution)/shard_map/stack | solution.py:157
  2.6 4.8 %collective-permute-start.1 = (bf16[2,2,112,192]{2,3,1,0:T(8,128)(2,1)S(1)}, bf16[2,2,112,192]{2,3,1,0:T(8,128)(2,1)S(1)}, u32[]{:S(2)}, u32[]{:S(2)}) collective-permute-start(bf16[2,2,112,192]{2,3,1,0:T(8,128)(2,1)S(1)} %maximum_bitcast_fusion), channel_id=1, source_target_pairs={{0,2},{2,4},{4,6},{6,8},{8,10},{10,12},{12,14},{3,1},{5,3},{7,5},{... | collective-permute-start | bytes 516104 | tf_op jit(solution)/shard_map/ppermute | solution.py:162
  7.3 5.3 %collective-permute-done.1 = bf16[2,2,112,192]{2,3,1,0:T(8,128)(2,1)S(1)} collective-permute-done((bf16[2,2,112,192]{2,3,1,0:T(8,128)(2,1)S(1)}, bf16[2,2,112,192]{2,3,1,0:T(8,128)(2,1)S(1)}, u32[]{:S(2)}, u32[]{:S(2)}) %collective-permute-start.1) | collective-permute-done | bytes 172064 | tf_op jit(solution)/shard_map/ppermute | solution.py:162
  12.6 0.0 collective-permute-start.2
  12.6 1.4 %collective-permute-done.2 = bf16[2,2,112,192]{2,3,1,0:T(8,128)(2,1)S(1)} collective-permute-done((bf16[2,2,112,192]{2,3,1,0:T(8,128)(2,1)S(1)}, bf16[2,2,112,192]{2,3,1,0:T(8,128)(2,1)S(1)}, u32[]{:S(2)}, u32[]{:S(2)}) %collective-permute-start.2) | collective-permute-done | bytes 172064 | tf_op jit(solution)/shard_map/ppermute | solution.py:163
  14.1 0.1 pad_maximum_fusion
  14.2 1.1 %copy.23 = bf16[2,6,112,192]{3,2,1,0:T(8,128)(2,1)} copy(bf16[2,6,112,192]{2,3,1,0:T(8,128)(2,1)S(1)} %pad_maximum_fusion) | data formatting | bytes 1032192 | tf_op jit(solution)/shard_map/concatenate | solution.py:166
  15.4 7.2 %shard_map.145 = (f32[1,224,192]{2,1,0:T(8,128)}, bf16[1,224,192]{2,1,0:T(8,128)(2,1)}) custom-call(bf16[2,672,192]{2,1,0:T(8,128)(2,1)} %bitcast.59, f32[1,192]{1,0:T(1,128)} %bitcast.73, bf16[27,192,192]{2,1,0:T(8,128)(2,1)} %bitcast.60, f32[1,192]{1,0:T(1,128)} %bitcast.74, f32[1,192]{1,0:T(1,128)} %bitcast.75, bf16[27,192,192]{2,1,0:T(8,128)(2,1)} %bitcast.61, ...), custom_call_target="tpu_custom_call" | custom-call | tf_op jit(solution)/shard_map/pallas_call | solution.py:119
  22.6 1.0 %copy.24 = bf16[1,2,112,192]{2,3,0,1:T(8,128)(2,1)S(1)} copy(bf16[1,2,112,192]{3,2,1,0:T(8,128)(2,1)} %bitcast.62) | data formatting | bytes 172032 | tf_op jit(solution)/shard_map/reshape | solution.py:180
  23.6 1.3 %fusion.4 = bf16[224,192]{0,1:T(8,128)(2,1)S(1)} fusion(bf16[192,192]{1,0:T(8,128)(2,1)S(1)} %copy-done, bf16[192,192]{1,0:T(8,128)(2,1)S(1)} %copy-done.1, bf16[1,224,192]{2,1,0:T(8,128)(2,1)} %get-tuple-element.8, f32[192]{0:T(256)S(1)} %copy-done.2), kind=kOutput, calls=%fused_computation.10 | convolution fusion | flops 33202176 | bytes 320256 | tf_op jit(solution)/shard_map/dot_general | solution.py:186
  24.9 2.5 %collective-permute-start.3 = (bf16[1,224,192]{1,2,0:T(8,128)(2,1)S(1)}, bf16[1,224,192]{1,2,0:T(8,128)(2,1)S(1)}, u32[]{:S(2)}, u32[]{:S(2)}) collective-permute-start(bf16[1,224,192]{1,2,0:T(8,128)(2,1)S(1)} %bitcast.63), channel_id=1, source_target_pairs={{0,2},{2,0},{1,3},{3,1},{4,6},{6,4},{5,7},{7,5},{8,10},{10,8},{9,1... | collective-permute-start | bytes 258056 | tf_op jit(solution)/shard_map/ppermute | solution.py:191
  27.5 15.1 %all_gather.3 = bf16[1,8,112,192]{2,3,0,1:T(8,128)(2,1)S(1)} all-gather(bf16[1,2,112,192]{2,3,0,1:T(8,128)(2,1)S(1)} %copy.24), channel_id=1, replica_groups=mesh['clips'=2,'outer'=4,'inner'=2,'tm'=2] {'outer'}, dimensions={1}, use_global_device_ids=true | all-gather | bytes 430080 | tf_op jit(solution)/shard_map/all_gather | solution.py:192
  42.6 0.3 copy.25
  42.8 0.3 reshape.107
  43.2 0.0 collective-permute-done.3
  43.2 0.4 fusion.34
  43.5 0.3 fusion.7
  43.9 0.0 copy-start.4
  43.9 0.0 copy-start.5
  43.9 0.0 copy-start.6
  43.9 0.0 copy-start.7
  43.9 0.4 convolution_bitcast_fusion
  44.4 0.1 collective-permute-start.4
  44.4 0.4 fusion.33
  44.8 0.3 fusion.5
  45.1 5.1 %collective-permute-done.4 = f32[1,224,194]{1,2,0:T(8,128)S(1)} collective-permute-done((f32[1,224,194]{1,2,0:T(8,128)S(1)}, f32[1,224,194]{1,2,0:T(8,128)S(1)}, u32[]{:S(2)}, u32[]{:S(2)}) %collective-permute-start.4) | collective-permute-done | bytes 173856 | tf_op jit(solution)/shard_map/ppermute | solution.py:204
  50.2 0.4 fusion.1
  50.7 0.5 fusion
  51.2 0.8 %copy.27 = f32[1,1,2,112,192]{3,4,2,1,0:T(8,128)} copy(f32[1,1,2,112,192]{4,3,2,1,0:T(8,128)S(1)} %bitcast.64) | data formatting | bytes 344064 | tf_op jit(solution)/shard_map/reshape | solution.py:222
  (15 shorter events, 0.1 us)
Async XLA Ops:
  0.0 23.6 %copy-start = (bf16[192,192]{1,0:T(8,128)(2,1)S(1)}, bf16[192,192]{1,0:T(8,128)(2,1)}, u32[]{:S(2)}) copy-start(bf16[192,192]{1,0:T(8,128)(2,1)} %param.25) | copy-start | bytes 221188
  0.0 1.6 %collective-permute-start = (bf16[1,2,112,192]{2,3,1,0:T(8,128)(2,1)}, bf16[1,2,112,192]{2,3,1,0:T(8,128)(2,1)S(1)}, u32[]{:S(2)}, u32[]{:S(2)}) collective-permute-start(bf16[1,2,112,192]{2,3,1,0:T(8,128)(2,1)} %bitcast.65), channel_id=1, source_target_pairs={{0,1},{1,0},{2,3},{3,2},{4,5},{5,4},{6,7},{7,6},{8,9},{9,8},{10,11... | collective-permute-start | bytes 258056 | tf_op jit(solution)/shard_map/ppermute | solution.py:154
  2.6 10.0 %collective-permute-start.1 = (bf16[2,2,112,192]{2,3,1,0:T(8,128)(2,1)S(1)}, bf16[2,2,112,192]{2,3,1,0:T(8,128)(2,1)S(1)}, u32[]{:S(2)}, u32[]{:S(2)}) collective-permute-start(bf16[2,2,112,192]{2,3,1,0:T(8,128)(2,1)S(1)} %maximum_bitcast_fusion), channel_id=1, source_target_pairs={{0,2},{2,4},{4,6},{6,8},{8,10},{10,12},{12,14},{3,1},{5,3},{7,5},{... | collective-permute-start | bytes 516104 | tf_op jit(solution)/shard_map/ppermute | solution.py:162
  12.6 1.4 %collective-permute-start.2 = (bf16[2,2,112,192]{2,3,1,0:T(8,128)(2,1)S(1)}, bf16[2,2,112,192]{2,3,1,0:T(8,128)(2,1)S(1)}, u32[]{:S(2)}, u32[]{:S(2)}) collective-permute-start(bf16[2,2,112,192]{2,3,1,0:T(8,128)(2,1)S(1)} %collective-permute-done.1), channel_id=1, source_target_pairs={{0,1},{1,0},{2,3},{3,2},{4,5},{5,4},{6,7},{7,6},{8,9},{9,8},{10,11... | collective-permute-start | bytes 516104 | tf_op jit(solution)/shard_map/ppermute | solution.py:163
  15.3 8.3 %copy-start.1 = (bf16[192,192]{1,0:T(8,128)(2,1)S(1)}, bf16[192,192]{1,0:T(8,128)(2,1)}, u32[]{:S(2)}) copy-start(bf16[192,192]{1,0:T(8,128)(2,1)} %param.23) | copy-start | bytes 221188
  15.3 8.3 %copy-start.2 = (f32[192]{0:T(256)S(1)}, f32[192]{0:T(256)}, u32[]{:S(2)}) copy-start(f32[192]{0:T(256)} %param.24) | copy-start | bytes 2308
  24.9 18.2 %collective-permute-start.3 = (bf16[1,224,192]{1,2,0:T(8,128)(2,1)S(1)}, bf16[1,224,192]{1,2,0:T(8,128)(2,1)S(1)}, u32[]{:S(2)}, u32[]{:S(2)}) collective-permute-start(bf16[1,224,192]{1,2,0:T(8,128)(2,1)S(1)} %bitcast.63), channel_id=1, source_target_pairs={{0,2},{2,0},{1,3},{3,1},{4,6},{6,4},{5,7},{7,5},{8,10},{10,8},{9,1... | collective-permute-start | bytes 258056 | tf_op jit(solution)/shard_map/ppermute | solution.py:191
  43.8 6.8 %copy-start.3 = (f32[1,224,192]{2,1,0:T(8,128)S(1)}, f32[1,224,192]{2,1,0:T(8,128)}, u32[]{:S(2)}) copy-start(f32[1,224,192]{2,1,0:T(8,128)} %get-tuple-element.7) | copy-start | bytes 516100
  43.9 6.8 %copy-start.4 = (bf16[192,192]{1,0:T(8,128)(2,1)S(1)}, bf16[192,192]{1,0:T(8,128)(2,1)}, u32[]{:S(2)}) copy-start(bf16[192,192]{1,0:T(8,128)(2,1)} %param.28) | copy-start | bytes 221188
  43.9 6.8 %copy-start.5 = (bf16[192,192]{1,0:T(8,128)(2,1)S(1)}, bf16[192,192]{1,0:T(8,128)(2,1)}, u32[]{:S(2)}) copy-start(bf16[192,192]{1,0:T(8,128)(2,1)} %param.26) | copy-start | bytes 221188
  43.9 6.8 %copy-start.6 = (f32[192]{0:T(256)S(1)}, f32[192]{0:T(256)}, u32[]{:S(2)}) copy-start(f32[192]{0:T(256)} %param.29) | copy-start | bytes 2308
  43.9 6.8 %copy-start.7 = (f32[192]{0:T(256)S(1)}, f32[192]{0:T(256)}, u32[]{:S(2)}) copy-start(f32[192]{0:T(256)} %param.27) | copy-start | bytes 2308
  44.4 5.8 %collective-permute-start.4 = (f32[1,224,194]{1,2,0:T(8,128)S(1)}, f32[1,224,194]{1,2,0:T(8,128)S(1)}, u32[]{:S(2)}, u32[]{:S(2)}) collective-permute-start(f32[1,224,194]{1,2,0:T(8,128)S(1)} %pad_maximum_fusion.1), channel_id=1, source_target_pairs={{0,2},{2,0},{1,3},{3,1},{4,6},{6,4},{5,7},{7,5},{8,10},{10,8},{9,1... | collective-permute-start | bytes 521480 | tf_op jit(solution)/shard_map/ppermute | solution.py:204

commit v6 on v5

--- a/solution.py
+++ b/solution.py
@@ -47,9 +47,28 @@
 def _silu(v):
     return v * (1.0 / (1.0 + jnp.exp(-v)))
 
-def block_kernel(cols, frame_count, ext_ref, g1_ref, w1_ref, b1_ref, g2_ref,
-                 w2_ref, b2_ref, ga_ref, res_ref, normed_ref):
+def taps_used(total, frame_count):
+    first_conv = [p for p in range(3) if total - 1 + p - 2 >= 0]
+    second_conv = [p for p in range(3) if 2 * frame_count - 1 + p - 2 >= 0]
+    return first_conv, second_conv
+
+
+def block_kernel(cols, frame_count, ext_ref, g1_ref, w1_hbm, b1_ref, g2_ref,
+                 w2_hbm, b2_ref, ga_ref, res_ref, normed_ref, w1_ref, w2_ref, sems):
     total = 2 * frame_count
+    used1, used2 = taps_used(total, frame_count)
+    pending = {}
+    for slot, (hbm, buf, used) in enumerate(((w1_hbm, w1_ref, used1), (w2_hbm, w2_ref, used2))):
+        for p in used:
+            chunk = pl.ds(p * 9, 9)
+            copy = pltpu.make_async_copy(hbm.at[chunk], buf.at[chunk], sems.at[slot * 3 + p])
+            copy.start()
+            pending[(slot, p)] = copy
+
+    def ready(slot, p):
+        copy = pending.pop((slot, p), None)
+        if copy is not None:
+            copy.wait()
     p_in = ext_ref.shape[1]
     p_mid = p_in - 2 * cols
     p_out = p_mid - 2 * cols
@@ -66,6 +85,7 @@
         for p, trip in enumerate(sources):
             if trip is None:
                 continue
+            ready(0 if w_ref is w1_ref else 1, p)
             for q in range(3):
                 for s in range(3):
                     window = trip[s][q * cols: q * cols + out_rows]
@@ -116,12 +136,18 @@
     frame_count = total // 2
     p_out = p_in - 4 * cols
     vm = pl.BlockSpec(memory_space=pltpu.VMEM)
+    hbm = pl.BlockSpec(memory_space=pl.ANY)
     return pl.pallas_call(
         functools.partial(block_kernel, cols, frame_count),
         out_shape=(jax.ShapeDtypeStruct((frame_count, p_out, c), jnp.float32),
                    jax.ShapeDtypeStruct((frame_count, p_out, c), jnp.bfloat16)),
-        in_specs=[vm] * 8,
+        in_specs=[vm, vm, hbm, vm, vm, hbm, vm, vm],
         out_specs=(vm, vm),
+        scratch_shapes=[
+            pltpu.VMEM((27, c, c), jnp.bfloat16),
+            pltpu.VMEM((27, c, c), jnp.bfloat16),
+            pltpu.SemaphoreType.DMA((6,)),
+        ],
     )(ext, g1.reshape(1, c), w1.reshape(27, c, c), b1.reshape(1, c), g2.reshape(1, c),
       w2.reshape(27, c, c), b2.reshape(1, c), ga.reshape(1, c))
 

time: 52.2 us -> 53.8 us (1.031)
  Pallas kernels: 7.24 us -> 8.8 us
    pallas_call x1, Pallas kernels: 7.24 us -> 8.8 us  [resnet_block(): pl.pallas_call(functools.partial(block_kernel, cols, frame_count), out_sh...]
where the time goes in v6:
time: 53.8 us; the launch traced here: 53.5 us
  blocking collectives  15.1 us (28%)
  waiting for transfers between devices  12.9 us (24%)
  Pallas kernels  8.8 us (16%)
  starting transfers between devices  7.83 us (15%)
  local copies, waits for them, and re-layouts  3.55 us (7%)
  matrix products  3.38 us (6%)
  other arithmetic  1.73 us (3%)
    all_gather x1, blocking collectives, local(): keys = lax.all_gather(normed, 'outer', axis=1, tiled=True)  15.1 us
    pallas_call x1, Pallas kernels, resnet_block(): pl.pallas_call(functools.partial(block_kernel, cols, frame_count), out_sh...  8.8 us
    ppermute x1, waiting for transfers between devices, local(): arrived = lax.ppermute(edge, ('outer', 'inner', 'tm'), up + down)  5.27 us
    ppermute x1, waiting for transfers between devices, local(): returned = lax.ppermute(partial(partner_queries), 'inner', swap)  5.06 us
    ppermute x1, starting transfers between devices, local(): arrived = lax.ppermute(edge, ('outer', 'inner', 'tm'), up + down)  4.76 us
    ppermute x1, starting transfers between devices, local(): partner_queries = lax.ppermute(folded, 'inner', swap)  2.54 us
    ppermute x1, waiting for transfers between devices, local(): swapped = lax.ppermute(arrived, 'tm', [(0, 1), (1, 0)])  1.44 us
    dot_general x1, matrix products, local(): jnp.dot(query, w_key.T, preferred_element_type=jnp.float32)  1.3 us
  transfers between devices with their start and end apart: 5, of which 4 were waited for; matrix products, arithmetic and copies ran while one was open for 2% of the time, Pallas kernels for 0%

profile of v6, /device:TPU:0, one launch (start us, length us, event | category | flops | bytes accessed | tf_op | source)
XLA Modules:
  0.0 53.5 jit_solution(16924888528490891886)
XLA Ops:
  0.0 0.5 collective-permute-start
  0.5 1.2 %collective-permute-done = bf16[1,2,112,192]{2,3,1,0:T(8,128)(2,1)S(1)} collective-permute-done((bf16[1,2,112,192]{2,3,1,0:T(8,128)(2,1)}, bf16[1,2,112,192]{2,3,1,0:T(8,128)(2,1)S(1)}, u32[]{:S(2)}, u32[]{:S(2)}) %collective-permute-start) | collective-permute-done | bytes 86048 | tf_op jit(solution)/shard_map/ppermute | solution.py:180
  1.6 0.9 %select_bitcast_fusion.1 = (bf16[1,1,2,112,192]{3,4,2,1,0:T(8,128)(2,1)S(1)}, bf16[1,1,2,112,192]{3,4,2,1,0:T(8,128)(2,1)S(1)}) fusion(bf16[1,2,112,192]{2,3,1,0:T(8,128)(2,1)S(1)} %collective-permute-done, pred[]{:T(512)S(6)} %eq.3, bf16[1,1,2,112,192]{3,4,2,1,0:T(8,128)(2,1)} %param.15), kind=kLoop, calls=%fused_computation.36 | loop fusion | flops 86016 | bytes 344065 | tf_op jit(solution)/shard_map/stack | solution.py:183
  2.6 4.8 %collective-permute-start.1 = (bf16[2,2,112,192]{2,3,1,0:T(8,128)(2,1)S(1)}, bf16[2,2,112,192]{2,3,1,0:T(8,128)(2,1)S(1)}, u32[]{:S(2)}, u32[]{:S(2)}) collective-permute-start(bf16[2,2,112,192]{2,3,1,0:T(8,128)(2,1)S(1)} %maximum_bitcast_fusion), channel_id=1, source_target_pairs={{0,2},{2,4},{4,6},{6,8},{8,10},{10,12},{12,14},{3,1},{5,3},{7,5},{... | collective-permute-start | bytes 516104 | tf_op jit(solution)/shard_map/ppermute | solution.py:188
  7.3 5.3 %collective-permute-done.1 = bf16[2,2,112,192]{2,3,1,0:T(8,128)(2,1)S(1)} collective-permute-done((bf16[2,2,112,192]{2,3,1,0:T(8,128)(2,1)S(1)}, bf16[2,2,112,192]{2,3,1,0:T(8,128)(2,1)S(1)}, u32[]{:S(2)}, u32[]{:S(2)}) %collective-permute-start.1) | collective-permute-done | bytes 172064 | tf_op jit(solution)/shard_map/ppermute | solution.py:188
  12.6 0.0 collective-permute-start.2
  12.6 1.4 %collective-permute-done.2 = bf16[2,2,112,192]{2,3,1,0:T(8,128)(2,1)S(1)} collective-permute-done((bf16[2,2,112,192]{2,3,1,0:T(8,128)(2,1)S(1)}, bf16[2,2,112,192]{2,3,1,0:T(8,128)(2,1)S(1)}, u32[]{:S(2)}, u32[]{:S(2)}) %collective-permute-start.2) | collective-permute-done | bytes 172064 | tf_op jit(solution)/shard_map/ppermute | solution.py:189
  14.1 0.1 pad_maximum_fusion
  14.2 1.1 %copy.23 = bf16[2,6,112,192]{3,2,1,0:T(8,128)(2,1)} copy(bf16[2,6,112,192]{2,3,1,0:T(8,128)(2,1)S(1)} %pad_maximum_fusion) | data formatting | bytes 1032192 | tf_op jit(solution)/shard_map/concatenate | solution.py:192
  15.4 8.8 %shard_map.145 = (f32[1,224,192]{2,1,0:T(8,128)}, bf16[1,224,192]{2,1,0:T(8,128)(2,1)}) custom-call(bf16[2,672,192]{2,1,0:T(8,128)(2,1)} %bitcast.59, f32[1,192]{1,0:T(1,128)} %bitcast.73, bf16[27,192,192]{2,1,0:T(8,128)(2,1)} %bitcast.60, f32[1,192]{1,0:T(1,128)} %bitcast.74, f32[1,192]{1,0:T(1,128)} %bitcast.75, bf16[27,192,192]{2,1,0:T(8,128)(2,1)} %bitcast.61, ...), custom_call_target="tpu_custom_call" | custom-call | tf_op jit(solution)/shard_map/pallas_call | solution.py:140
  24.2 1.0 %copy.24 = bf16[1,2,112,192]{2,3,0,1:T(8,128)(2,1)S(1)} copy(bf16[1,2,112,192]{3,2,1,0:T(8,128)(2,1)} %bitcast.62) | data formatting | bytes 172032 | tf_op jit(solution)/shard_map/reshape | solution.py:206
  25.2 0.0 copy-done
  25.2 1.3 %fusion.4 = bf16[224,192]{0,1:T(8,128)(2,1)S(1)} fusion(bf16[192,192]{1,0:T(8,128)(2,1)S(1)} %copy-done, bf16[192,192]{1,0:T(8,128)(2,1)S(1)} %copy-done.1, bf16[1,224,192]{2,1,0:T(8,128)(2,1)} %get-tuple-element.8, f32[192]{0:T(256)S(1)} %copy-done.2), kind=kOutput, calls=%fused_computation.10 | convolution fusion | flops 33202176 | bytes 320256 | tf_op jit(solution)/shard_map/dot_general | solution.py:212
  26.5 2.5 %collective-permute-start.3 = (bf16[1,224,192]{1,2,0:T(8,128)(2,1)S(1)}, bf16[1,224,192]{1,2,0:T(8,128)(2,1)S(1)}, u32[]{:S(2)}, u32[]{:S(2)}) collective-permute-start(bf16[1,224,192]{1,2,0:T(8,128)(2,1)S(1)} %bitcast.63), channel_id=1, source_target_pairs={{0,2},{2,0},{1,3},{3,1},{4,6},{6,4},{5,7},{7,5},{8,10},{10,8},{9,1... | collective-permute-start | bytes 258056 | tf_op jit(solution)/shard_map/ppermute | solution.py:217
  29.1 15.1 %all_gather.3 = bf16[1,8,112,192]{2,3,0,1:T(8,128)(2,1)S(1)} all-gather(bf16[1,2,112,192]{2,3,0,1:T(8,128)(2,1)S(1)} %copy.24), channel_id=1, replica_groups=mesh['clips'=2,'outer'=4,'inner'=2,'tm'=2] {'outer'}, dimensions={1}, use_global_device_ids=true | all-gather | bytes 430080 | tf_op jit(solution)/shard_map/all_gather | solution.py:218
  44.1 0.3 copy.25
  44.4 0.3 reshape.107
  44.7 0.0 collective-permute-done.3
  44.7 0.4 fusion.34
  45.1 0.3 fusion.7
  45.4 0.0 copy-start.4
  45.4 0.0 copy-start.5
  45.4 0.0 copy-start.6
  45.4 0.0 copy-start.7
  45.5 0.4 convolution_bitcast_fusion
  45.9 0.1 collective-permute-start.4
  46.0 0.4 fusion.33
  46.4 0.3 fusion.5
  46.7 5.1 %collective-permute-done.4 = f32[1,224,194]{1,2,0:T(8,128)S(1)} collective-permute-done((f32[1,224,194]{1,2,0:T(8,128)S(1)}, f32[1,224,194]{1,2,0:T(8,128)S(1)}, u32[]{:S(2)}, u32[]{:S(2)}) %collective-permute-start.4) | collective-permute-done | bytes 173856 | tf_op jit(solution)/shard_map/ppermute | solution.py:230
  51.7 0.4 fusion.1
  52.2 0.5 fusion
  52.7 0.8 %copy.27 = f32[1,1,2,112,192]{3,4,2,1,0:T(8,128)} copy(f32[1,1,2,112,192]{4,3,2,1,0:T(8,128)S(1)} %bitcast.64) | data formatting | bytes 344064 | tf_op jit(solution)/shard_map/reshape | solution.py:248
  (15 shorter events, 0.1 us)
Async XLA Ops:
  0.0 25.2 %copy-start = (bf16[192,192]{1,0:T(8,128)(2,1)S(1)}, bf16[192,192]{1,0:T(8,128)(2,1)}, u32[]{:S(2)}) copy-start(bf16[192,192]{1,0:T(8,128)(2,1)} %param.25) | copy-start | bytes 221188
  0.0 1.6 %collective-permute-start = (bf16[1,2,112,192]{2,3,1,0:T(8,128)(2,1)}, bf16[1,2,112,192]{2,3,1,0:T(8,128)(2,1)S(1)}, u32[]{:S(2)}, u32[]{:S(2)}) collective-permute-start(bf16[1,2,112,192]{2,3,1,0:T(8,128)(2,1)} %bitcast.65), channel_id=1, source_target_pairs={{0,1},{1,0},{2,3},{3,2},{4,5},{5,4},{6,7},{7,6},{8,9},{9,8},{10,11... | collective-permute-start | bytes 258056 | tf_op jit(solution)/shard_map/ppermute | solution.py:180
  2.6 10.0 %collective-permute-start.1 = (bf16[2,2,112,192]{2,3,1,0:T(8,128)(2,1)S(1)}, bf16[2,2,112,192]{2,3,1,0:T(8,128)(2,1)S(1)}, u32[]{:S(2)}, u32[]{:S(2)}) collective-permute-start(bf16[2,2,112,192]{2,3,1,0:T(8,128)(2,1)S(1)} %maximum_bitcast_fusion), channel_id=1, source_target_pairs={{0,2},{2,4},{4,6},{6,8},{8,10},{10,12},{12,14},{3,1},{5,3},{7,5},{... | collective-permute-start | bytes 516104 | tf_op jit(solution)/shard_map/ppermute | solution.py:188
  12.6 1.4 %collective-permute-start.2 = (bf16[2,2,112,192]{2,3,1,0:T(8,128)(2,1)S(1)}, bf16[2,2,112,192]{2,3,1,0:T(8,128)(2,1)S(1)}, u32[]{:S(2)}, u32[]{:S(2)}) collective-permute-start(bf16[2,2,112,192]{2,3,1,0:T(8,128)(2,1)S(1)} %collective-permute-done.1), channel_id=1, source_target_pairs={{0,1},{1,0},{2,3},{3,2},{4,5},{5,4},{6,7},{7,6},{8,9},{9,8},{10,11... | collective-permute-start | bytes 516104 | tf_op jit(solution)/shard_map/ppermute | solution.py:189
  15.3 9.8 %copy-start.1 = (bf16[192,192]{1,0:T(8,128)(2,1)S(1)}, bf16[192,192]{1,0:T(8,128)(2,1)}, u32[]{:S(2)}) copy-start(bf16[192,192]{1,0:T(8,128)(2,1)} %param.23) | copy-start | bytes 221188
  15.3 9.8 %copy-start.2 = (f32[192]{0:T(256)S(1)}, f32[192]{0:T(256)}, u32[]{:S(2)}) copy-start(f32[192]{0:T(256)} %param.24) | copy-start | bytes 2308
  26.5 18.2 %collective-permute-start.3 = (bf16[1,224,192]{1,2,0:T(8,128)(2,1)S(1)}, bf16[1,224,192]{1,2,0:T(8,128)(2,1)S(1)}, u32[]{:S(2)}, u32[]{:S(2)}) collective-permute-start(bf16[1,224,192]{1,2,0:T(8,128)(2,1)S(1)} %bitcast.63), channel_id=1, source_target_pairs={{0,2},{2,0},{1,3},{3,1},{4,6},{6,4},{5,7},{7,5},{8,10},{10,8},{9,1... | collective-permute-start | bytes 258056 | tf_op jit(solution)/shard_map/ppermute | solution.py:217
  45.4 6.8 %copy-start.3 = (f32[1,224,192]{2,1,0:T(8,128)S(1)}, f32[1,224,192]{2,1,0:T(8,128)}, u32[]{:S(2)}) copy-start(f32[1,224,192]{2,1,0:T(8,128)} %get-tuple-element.7) | copy-start | bytes 516100
  45.4 6.8 %copy-start.4 = (bf16[192,192]{1,0:T(8,128)(2,1)S(1)}, bf16[192,192]{1,0:T(8,128)(2,1)}, u32[]{:S(2)}) copy-start(bf16[192,192]{1,0:T(8,128)(2,1)} %param.28) | copy-start | bytes 221188
  45.4 6.8 %copy-start.5 = (bf16[192,192]{1,0:T(8,128)(2,1)S(1)}, bf16[192,192]{1,0:T(8,128)(2,1)}, u32[]{:S(2)}) copy-start(bf16[192,192]{1,0:T(8,128)(2,1)} %param.26) | copy-start | bytes 221188
  45.4 6.8 %copy-start.6 = (f32[192]{0:T(256)S(1)}, f32[192]{0:T(256)}, u32[]{:S(2)}) copy-start(f32[192]{0:T(256)} %param.29) | copy-start | bytes 2308
  45.4 6.8 %copy-start.7 = (f32[192]{0:T(256)S(1)}, f32[192]{0:T(256)}, u32[]{:S(2)}) copy-start(f32[192]{0:T(256)} %param.27) | copy-start | bytes 2308
  45.9 5.8 %collective-permute-start.4 = (f32[1,224,194]{1,2,0:T(8,128)S(1)}, f32[1,224,194]{1,2,0:T(8,128)S(1)}, u32[]{:S(2)}, u32[]{:S(2)}) collective-permute-start(f32[1,224,194]{1,2,0:T(8,128)S(1)} %pad_maximum_fusion.1), channel_id=1, source_target_pairs={{0,2},{2,0},{1,3},{3,1},{4,6},{6,4},{5,7},{7,5},{8,10},{10,8},{9,1... | collective-permute-start | bytes 521480 | tf_op jit(solution)/shard_map/ppermute | solution.py:230

commit v7 on v5

--- a/solution.py
+++ b/solution.py
@@ -47,12 +47,17 @@
 def _silu(v):
     return v * (1.0 / (1.0 + jnp.exp(-v)))
 
-def block_kernel(cols, frame_count, ext_ref, g1_ref, w1_ref, b1_ref, g2_ref,
+def block_kernel(cols, frame_count, seq_ref, arrived_ref, swapped_ref, g1_ref, w1_ref, b1_ref, g2_ref,
                  w2_ref, b2_ref, ga_ref, res_ref, normed_ref):
     total = 2 * frame_count
-    p_in = ext_ref.shape[1]
-    p_mid = p_in - 2 * cols
-    p_out = p_mid - 2 * cols
+    p_out = seq_ref.shape[1]
+    p_mid = p_out + 2 * cols
+    first = lax.axis_index("tm") == 0
+
+    def extended(t):
+        above = jnp.where(first, arrived_ref[t], swapped_ref[t])
+        below = jnp.where(first, swapped_ref[t], arrived_ref[t])
+        return jnp.concatenate([above, seq_ref[t], below], axis=0)
 
     def shifted(a):
         n = a.shape[0]
@@ -74,14 +79,13 @@
         return acc
 
     g1 = g1_ref[...]
-    act1 = [shifted(_silu(_rms(ext_ref[t].astype(jnp.float32), g1)).astype(jnp.bfloat16).astype(jnp.float32)) for t in range(total)]
+    act1 = [shifted(_silu(_rms(extended(t).astype(jnp.float32), g1)).astype(jnp.bfloat16).astype(jnp.float32)) for t in range(total)]
     inner = lax.axis_size("inner")
     band = lax.axis_index("outer") * inner + lax.axis_index("inner")
     band_rows = p_out // cols
     height = lax.axis_size("outer") * inner * band_rows
     lo = 1 - band * band_rows
     hi = height - band * band_rows + 1
-    first = lax.axis_index("tm") == 0
     row = lax.broadcasted_iota(jnp.int32, (p_mid, 1), 0) // cols
     inside = (row >= lo) & (row < hi)
     g2 = g2_ref[...]
@@ -105,24 +109,22 @@
             return shifted(jnp.where(first, a, b))
         srcs = [pick(2 * k - 2), pick(2 * k - 1), pick(2 * k)]
         out2 = conv_frame(srcs, w2_ref, p_out) + b2
-        body = slice(HALO * cols, HALO * cols + p_out)
-        own = jnp.where(first, ext_ref[2 * k, body], ext_ref[2 * k + 1, body])
+        own = jnp.where(first, seq_ref[2 * k], seq_ref[2 * k + 1])
         res = own.astype(jnp.float32) + out2
         res_ref[k] = res
         normed_ref[k] = _rms(res, ga).astype(jnp.bfloat16)
 
-def resnet_block(ext, g1, w1, b1, g2, w2, b2, ga, cols):
-    total, p_in, c = ext.shape
+def resnet_block(seq, arrived, swapped, g1, w1, b1, g2, w2, b2, ga, cols):
+    total, p_out, c = seq.shape
     frame_count = total // 2
-    p_out = p_in - 4 * cols
     vm = pl.BlockSpec(memory_space=pltpu.VMEM)
     return pl.pallas_call(
         functools.partial(block_kernel, cols, frame_count),
         out_shape=(jax.ShapeDtypeStruct((frame_count, p_out, c), jnp.float32),
                    jax.ShapeDtypeStruct((frame_count, p_out, c), jnp.bfloat16)),
-        in_specs=[vm] * 8,
+        in_specs=[vm] * 10,
         out_specs=(vm, vm),
-    )(ext, g1.reshape(1, c), w1.reshape(27, c, c), b1.reshape(1, c), g2.reshape(1, c),
+    )(seq, arrived, swapped, g1.reshape(1, c), w1.reshape(27, c, c), b1.reshape(1, c), g2.reshape(1, c),
       w2.reshape(27, c, c), b2.reshape(1, c), ga.reshape(1, c))
 
 
@@ -161,13 +163,12 @@
     edge = jnp.where(is_first, seq[:, row_count - HALO :], seq[:, :HALO])
     arrived = lax.ppermute(edge, ("outer", "inner", "tm"), up + down)
     swapped = lax.ppermute(arrived, "tm", [(0, 1), (1, 0)])
-    above = jnp.where(is_first, arrived, swapped)
-    below = jnp.where(is_first, swapped, arrived)
-    ext = jnp.concatenate([above, seq, below], axis=1)
 
     token_count = row_count * col_count
     residual, normed = resnet_block(
-        ext.reshape(2 * frame_count, -1, channels),
+        seq.reshape(2 * frame_count, -1, channels),
+        arrived.reshape(2 * frame_count, -1, channels),
+        swapped.reshape(2 * frame_count, -1, channels),
         norm1_gain,
         conv1_weight,
         conv1_bias,

time: 52.2 us -> 52.4 us (level)
  waiting for transfers between devices: 12.9 us -> 11.5 us
  local copies, waits for them, and re-layouts: 3.55 us -> 4.29 us
  other arithmetic: 1.73 us -> 2.32 us
    ppermute x0 -> x2, local copies, waits for them, and re-layouts: none -> 1.65 us  [the longest x1 0.83 us: local(): swapped = lax.ppermute(arrived, 'tm', [(0, 1), (1, 0)])]
    ppermute x1, waiting for transfers between devices: 1.44 us -> 0.01 us  [local(): swapped = lax.ppermute(arrived, 'tm', [(0, 1), (1, 0)])]
    concatenate x1 -> x0, local copies, waits for them, and re-layouts: 1.12 us -> none  [local(): ext = jnp.concatenate([above, seq, below], axis=1)]
    select_n x1, other arithmetic: 0.03 us -> 0.91 us  [local(): even = jnp.where(is_first, own, partner)]
  transfers between devices with their start and end apart: 5 -> 5, of which waited for: 4 -> 3; matrix products, arithmetic and copies ran while one was open for 2% -> 6% of each run, Pallas kernels for 0% -> 0%
where the time goes in v7:
time: 52.4 us; the launch traced here: 52.2 us
  blocking collectives  15.3 us (29%)
  waiting for transfers between devices  11.5 us (22%)
  starting transfers between devices  7.83 us (15%)
  Pallas kernels  7.34 us (14%)
  local copies, waits for them, and re-layouts  4.29 us (8%)
  matrix products  3.39 us (6%)
  other arithmetic  2.32 us (4%)
    all_gather x1, blocking collectives, local(): keys = lax.all_gather(normed, 'outer', axis=1, tiled=True)  15.3 us
    pallas_call x1, Pallas kernels, resnet_block(): pl.pallas_call(functools.partial(block_kernel, cols, frame_count), out_sh...  7.34 us
    ppermute x1, waiting for transfers between devices, local(): arrived = lax.ppermute(edge, ('outer', 'inner', 'tm'), up + down)  5.27 us
    ppermute x1, waiting for transfers between devices, local(): returned = lax.ppermute(partial(partner_queries), 'inner', swap)  5.06 us
    ppermute x1, starting transfers between devices, local(): arrived = lax.ppermute(edge, ('outer', 'inner', 'tm'), up + down)  4.76 us
    ppermute x1, starting transfers between devices, local(): partner_queries = lax.ppermute(folded, 'inner', swap)  2.55 us
    dot_general x1, matrix products, local(): jnp.dot(query, w_key.T, preferred_element_type=jnp.float32)  1.3 us
    ppermute x1, waiting for transfers between devices, local(): partner = lax.ppermute(own, 'tm', [(0, 1), (1, 0)])  1.15 us
  transfers between devices with their start and end apart: 5, of which 3 were waited for; matrix products, arithmetic and copies ran while one was open for 6% of the time, Pallas kernels for 0%

profile of v7, /device:TPU:0, one launch (start us, length us, event | category | flops | bytes accessed | tf_op | source)
XLA Modules:
  0.0 52.2 jit_solution(10710255911897874164)
XLA Ops:
  0.0 0.5 collective-permute-start
  0.5 1.2 %collective-permute-done = bf16[1,2,112,192]{2,3,1,0:T(8,128)(2,1)S(1)} collective-permute-done((bf16[1,2,112,192]{2,3,1,0:T(8,128)(2,1)}, bf16[1,2,112,192]{2,3,1,0:T(8,128)(2,1)S(1)}, u32[]{:S(2)}, u32[]{:S(2)}) %collective-permute-start) | collective-permute-done | bytes 86048 | tf_op jit(solution)/shard_map/ppermute | solution.py:156
  1.6 0.9 %broadcast_select_fusion.1 = (bf16[1,2,112,192]{2,3,1,0:T(8,128)(2,1)S(1)}, bf16[1,2,112,192]{2,3,1,0:T(8,128)(2,1)S(1)}) fusion(bf16[1,2,112,192]{2,3,1,0:T(8,128)(2,1)S(1)} %collective-permute-done, pred[]{:T(512)S(6)} %eq.3, bf16[1,1,2,112,192]{3,4,2,1,0:T(8,128)(2,1)} %param.15), kind=kLoop, calls=%fused_computation.35 | loop fusion | flops 86016 | bytes 344065 | tf_op jit(solution)/shard_map/jit(_where)/select_n | solution.py:157
  2.6 4.8 %collective-permute-start.1 = (bf16[2,2,112,192]{2,3,1,0:T(8,128)(2,1)S(1)}, bf16[2,2,112,192]{2,3,1,0:T(8,128)(2,1)S(1)}, u32[]{:S(2)}, u32[]{:S(2)}) collective-permute-start(bf16[2,2,112,192]{2,3,1,0:T(8,128)(2,1)S(1)} %maximum_bitcast_fusion), channel_id=1, source_target_pairs={{0,2},{2,4},{4,6},{6,8},{8,10},{10,12},{12,14},{3,1},{5,3},{7,5},{... | collective-permute-start | bytes 516104 | tf_op jit(solution)/shard_map/ppermute | solution.py:164
  7.3 5.3 %collective-permute-done.1 = bf16[2,2,112,192]{2,3,1,0:T(8,128)(2,1)S(1)} collective-permute-done((bf16[2,2,112,192]{2,3,1,0:T(8,128)(2,1)S(1)}, bf16[2,2,112,192]{2,3,1,0:T(8,128)(2,1)S(1)}, u32[]{:S(2)}, u32[]{:S(2)}) %collective-permute-start.1) | collective-permute-done | bytes 172064 | tf_op jit(solution)/shard_map/ppermute | solution.py:164
  12.6 0.0 collective-permute-start.2
  12.6 0.1 copy.29
  12.7 0.1 copy.30
  12.8 0.7 %pad_maximum_fusion.seq_ref = bf16[2,224,192]{2,1,0:T(8,128)(2,1)} fusion(bf16[1,224,192]{2,1,0:T(8,128)(2,1)S(1)} %bitcast.70, bf16[1,224,192]{2,1,0:T(8,128)(2,1)S(1)} %bitcast.69), kind=kLoop, calls=%fused_computation.18 | loop fusion | flops 86016 | bytes 344064 | tf_op jit(solution)/shard_map/stack | solution.py:159
  13.6 0.8 %copy.31 = bf16[2,2,112,192]{3,2,1,0:T(8,128)(2,1)} copy(bf16[2,2,112,192]{2,3,1,0:T(8,128)(2,1)S(1)} %collective-permute-done.1) | data formatting | bytes 344064 | tf_op jit(solution)/shard_map/ppermute | solution.py:164
  14.4 0.8 %copy.32 = bf16[2,2,112,192]{3,2,1,0:T(8,128)(2,1)} copy(bf16[2,2,112,192]{2,3,1,0:T(8,128)(2,1)S(1)} %collective-permute-done.2) | data formatting | bytes 344064 | tf_op jit(solution)/shard_map/ppermute | solution.py:165
  15.2 7.3 %shard_map.145 = (f32[1,224,192]{2,1,0:T(8,128)}, bf16[1,224,192]{2,1,0:T(8,128)(2,1)}) custom-call(bf16[2,224,192]{2,1,0:T(8,128)(2,1)} %pad_maximum_fusion.seq_ref, bf16[2,224,192]{2,1,0:T(8,128)(2,1)} %bitcast.64, bf16[2,224,192]{2,1,0:T(8,128)(2,1)} %bitcast.65, f32[1,192]{1,0:T(1,128)} %bitcast.81, bf16[27,192,192]{2,1,0:T(8,128)(2,1)} %bitcast.62, ...), custom_call_target="tpu_custom_call" | custom-call | tf_op jit(solution)/shard_map/pallas_call | solution.py:121
  22.6 1.0 %copy.33 = bf16[1,2,112,192]{2,3,0,1:T(8,128)(2,1)S(1)} copy(bf16[1,2,112,192]{3,2,1,0:T(8,128)(2,1)} %bitcast.71) | data formatting | bytes 172032 | tf_op jit(solution)/shard_map/reshape | solution.py:181
  23.6 1.3 %fusion.3 = bf16[224,192]{0,1:T(8,128)(2,1)S(1)} fusion(bf16[192,192]{1,0:T(8,128)(2,1)S(1)} %copy-done, bf16[192,192]{1,0:T(8,128)(2,1)S(1)} %copy-done.2, bf16[1,224,192]{2,1,0:T(8,128)(2,1)} %get-tuple-element.8, f32[192]{0:T(256)S(1)} %copy-done.3), kind=kOutput, calls=%fused_computation.8 | convolution fusion | flops 33202176 | bytes 320256 | tf_op jit(solution)/shard_map/dot_general | solution.py:187
  24.9 2.5 %collective-permute-start.3 = (bf16[1,224,192]{1,2,0:T(8,128)(2,1)S(1)}, bf16[1,224,192]{1,2,0:T(8,128)(2,1)S(1)}, u32[]{:S(2)}, u32[]{:S(2)}) collective-permute-start(bf16[1,224,192]{1,2,0:T(8,128)(2,1)S(1)} %bitcast.72), channel_id=1, source_target_pairs={{0,2},{2,0},{1,3},{3,1},{4,6},{6,4},{5,7},{7,5},{8,10},{10,8},{9,1... | collective-permute-start | bytes 258056 | tf_op jit(solution)/shard_map/ppermute | solution.py:192
  27.5 15.3 %all_gather.3 = bf16[1,8,112,192]{2,3,0,1:T(8,128)(2,1)S(1)} all-gather(bf16[1,2,112,192]{2,3,0,1:T(8,128)(2,1)S(1)} %copy.33), channel_id=1, replica_groups=mesh['clips'=2,'outer'=4,'inner'=2,'tm'=2] {'outer'}, dimensions={1}, use_global_device_ids=true | all-gather | bytes 430080 | tf_op jit(solution)/shard_map/all_gather | solution.py:193
  42.8 0.3 copy.34
  43.0 0.3 reshape.115
  43.4 0.4 fusion.35
  43.8 0.3 fusion.7
  44.1 0.0 copy-start.5
  44.1 0.0 copy-start.6
  44.1 0.0 copy-start.7
  44.1 0.4 convolution_bitcast_fusion
  44.5 0.0 copy-start.4
  44.6 0.1 collective-permute-start.4
  44.6 0.4 fusion.34
  45.0 0.3 fusion.5
  45.3 5.1 %collective-permute-done.4 = f32[1,224,194]{1,2,0:T(8,128)S(1)} collective-permute-done((f32[1,224,194]{1,2,0:T(8,128)S(1)}, f32[1,224,194]{1,2,0:T(8,128)S(1)}, u32[]{:S(2)}, u32[]{:S(2)}) %collective-permute-start.4) | collective-permute-done | bytes 173856 | tf_op jit(solution)/shard_map/ppermute | solution.py:205
  50.4 0.4 fusion
  50.9 0.5 fusion.4
  51.4 0.8 %copy.36 = f32[1,1,2,112,192]{3,4,2,1,0:T(8,128)} copy(f32[1,1,2,112,192]{4,3,2,1,0:T(8,128)S(1)} %bitcast.66) | data formatting | bytes 344064 | tf_op jit(solution)/shard_map/reshape | solution.py:223
  (18 shorter events, 0.1 us)
Async XLA Ops:
  0.0 23.6 %copy-start = (bf16[192,192]{1,0:T(8,128)(2,1)S(1)}, bf16[192,192]{1,0:T(8,128)(2,1)}, u32[]{:S(2)}) copy-start(bf16[192,192]{1,0:T(8,128)(2,1)} %param.25) | copy-start | bytes 221188
  0.0 1.6 %collective-permute-start = (bf16[1,2,112,192]{2,3,1,0:T(8,128)(2,1)}, bf16[1,2,112,192]{2,3,1,0:T(8,128)(2,1)S(1)}, u32[]{:S(2)}, u32[]{:S(2)}) collective-permute-start(bf16[1,2,112,192]{2,3,1,0:T(8,128)(2,1)} %bitcast.73), channel_id=1, source_target_pairs={{0,1},{1,0},{2,3},{3,2},{4,5},{5,4},{6,7},{7,6},{8,9},{9,8},{10,11... | collective-permute-start | bytes 258056 | tf_op jit(solution)/shard_map/ppermute | solution.py:156
  2.6 10.0 %collective-permute-start.1 = (bf16[2,2,112,192]{2,3,1,0:T(8,128)(2,1)S(1)}, bf16[2,2,112,192]{2,3,1,0:T(8,128)(2,1)S(1)}, u32[]{:S(2)}, u32[]{:S(2)}) collective-permute-start(bf16[2,2,112,192]{2,3,1,0:T(8,128)(2,1)S(1)} %maximum_bitcast_fusion), channel_id=1, source_target_pairs={{0,2},{2,4},{4,6},{6,8},{8,10},{10,12},{12,14},{3,1},{5,3},{7,5},{... | collective-permute-start | bytes 516104 | tf_op jit(solution)/shard_map/ppermute | solution.py:164
  12.6 1.8 %collective-permute-start.2 = (bf16[2,2,112,192]{2,3,1,0:T(8,128)(2,1)S(1)}, bf16[2,2,112,192]{2,3,1,0:T(8,128)(2,1)S(1)}, u32[]{:S(2)}, u32[]{:S(2)}) collective-permute-start(bf16[2,2,112,192]{2,3,1,0:T(8,128)(2,1)S(1)} %collective-permute-done.1), channel_id=1, source_target_pairs={{0,1},{1,0},{2,3},{3,2},{4,5},{5,4},{6,7},{7,6},{8,9},{9,8},{10,11... | collective-permute-start | bytes 516104 | tf_op jit(solution)/shard_map/ppermute | solution.py:165
  15.2 8.4 %copy-start.2 = (bf16[192,192]{1,0:T(8,128)(2,1)S(1)}, bf16[192,192]{1,0:T(8,128)(2,1)}, u32[]{:S(2)}) copy-start(bf16[192,192]{1,0:T(8,128)(2,1)} %param.23) | copy-start | bytes 221188
  15.2 8.4 %copy-start.3 = (f32[192]{0:T(256)S(1)}, f32[192]{0:T(256)}, u32[]{:S(2)}) copy-start(f32[192]{0:T(256)} %param.24) | copy-start | bytes 2308
  24.9 18.5 %collective-permute-start.3 = (bf16[1,224,192]{1,2,0:T(8,128)(2,1)S(1)}, bf16[1,224,192]{1,2,0:T(8,128)(2,1)S(1)}, u32[]{:S(2)}, u32[]{:S(2)}) collective-permute-start(bf16[1,224,192]{1,2,0:T(8,128)(2,1)S(1)} %bitcast.72), channel_id=1, source_target_pairs={{0,2},{2,0},{1,3},{3,1},{4,6},{6,4},{5,7},{7,5},{8,10},{10,8},{9,1... | collective-permute-start | bytes 258056 | tf_op jit(solution)/shard_map/ppermute | solution.py:192
  44.1 6.8 %copy-start.5 = (bf16[192,192]{1,0:T(8,128)(2,1)S(1)}, bf16[192,192]{1,0:T(8,128)(2,1)}, u32[]{:S(2)}) copy-start(bf16[192,192]{1,0:T(8,128)(2,1)} %param.28) | copy-start | bytes 221188
  44.1 6.8 %copy-start.6 = (bf16[192,192]{1,0:T(8,128)(2,1)S(1)}, bf16[192,192]{1,0:T(8,128)(2,1)}, u32[]{:S(2)}) copy-start(bf16[192,192]{1,0:T(8,128)(2,1)} %param.26) | copy-start | bytes 221188
  44.1 6.8 %copy-start.7 = (f32[192]{0:T(256)S(1)}, f32[192]{0:T(256)}, u32[]{:S(2)}) copy-start(f32[192]{0:T(256)} %param.27) | copy-start | bytes 2308
  44.5 6.8 %copy-start.1 = (f32[1,224,192]{2,1,0:T(8,128)S(1)}, f32[1,224,192]{2,1,0:T(8,128)}, u32[]{:S(2)}) copy-start(f32[1,224,192]{2,1,0:T(8,128)} %get-tuple-element.7) | copy-start | bytes 516100
  44.5 6.8 %copy-start.4 = (f32[192]{0:T(256)S(1)}, f32[192]{0:T(256)}, u32[]{:S(2)}) copy-start(f32[192]{0:T(256)} %param.29) | copy-start | bytes 2308
  44.6 5.8 %collective-permute-start.4 = (f32[1,224,194]{1,2,0:T(8,128)S(1)}, f32[1,224,194]{1,2,0:T(8,128)S(1)}, u32[]{:S(2)}, u32[]{:S(2)}) collective-permute-start(f32[1,224,194]{1,2,0:T(8,128)S(1)} %pad_maximum_fusion.1), channel_id=1, source_target_pairs={{0,2},{2,0},{1,3},{3,1},{4,6},{6,4},{5,7},{7,5},{8,10},{10,8},{9,1... | collective-permute-start | bytes 521480 | tf_op jit(solution)/shard_map/ppermute | solution.py:205

commit v8 on v7

--- a/solution.py
+++ b/solution.py
@@ -5,6 +5,7 @@
 import jax.numpy as jnp
 from jax import lax
 from jax.experimental import pallas as pl
+from jax.experimental.layout import Layout, with_layout_constraint
 from jax.experimental.pallas import tpu as pltpu
 from jax.sharding import PartitionSpec as P
 
@@ -145,7 +146,7 @@
     w_out,
     b_out,
 ):
-    own = frames[:, 0]
+    own = with_layout_constraint(frames[:, 0], Layout(major_to_minor=(0, 1, 2, 3)))
     frame_count, row_count, col_count, channels = own.shape
     inner = lax.axis_size("inner")
     bands = lax.axis_size("outer") * inner

time: 52.4 us -> 52.5 us (level)
  waiting for transfers between devices: 11.5 us -> 12.7 us
  other arithmetic: 2.32 us -> 1.49 us
    unnamed x16 -> x21, local copies, waits for them, and re-layouts: 0.04 us -> 1.75 us
    ppermute x2 -> x0, local copies, waits for them, and re-layouts: 1.65 us -> none  [the longest x1 0.83 us: local(): swapped = lax.ppermute(arrived, 'tm', [(0, 1), (1, 0)])]
    select_n x1, other arithmetic: 0.91 us -> 0.02 us  [local(): even = jnp.where(is_first, own, partner)]
    ppermute x1, waiting for transfers between devices: 5.27 us -> 5.97 us  [local(): arrived = lax.ppermute(edge, ('outer', 'inner', 'tm'), up + down)]
    ppermute x1, waiting for transfers between devices: 0.01 us -> 0.7 us  [local(): swapped = lax.ppermute(arrived, 'tm', [(0, 1), (1, 0)])]
  transfers between devices with their start and end apart: 5 -> 5, of which waited for: 3 -> 4; matrix products, arithmetic and copies ran while one was open for 6% -> 4% of each run, Pallas kernels for 0% -> 0%
where the time goes in v8:
time: 52.5 us; the launch traced here: 52.3 us
  blocking collectives  15.1 us (29%)
  waiting for transfers between devices  12.7 us (24%)
  starting transfers between devices  7.9 us (15%)
  Pallas kernels  7.34 us (14%)
  local copies, waits for them, and re-layouts  4.14 us (8%)
  matrix products  3.39 us (6%)
  other arithmetic  1.49 us (3%)
    all_gather x1, blocking collectives, local(): keys = lax.all_gather(normed, 'outer', axis=1, tiled=True)  15.1 us
    pallas_call x1, Pallas kernels, resnet_block(): pl.pallas_call(functools.partial(block_kernel, cols, frame_count), out_sh...  7.34 us
    ppermute x1, waiting for transfers between devices, local(): arrived = lax.ppermute(edge, ('outer', 'inner', 'tm'), up + down)  5.97 us
    ppermute x1, waiting for transfers between devices, local(): returned = lax.ppermute(partial(partner_queries), 'inner', swap)  5.06 us
    ppermute x1, starting transfers between devices, local(): arrived = lax.ppermute(edge, ('outer', 'inner', 'tm'), up + down)  4.76 us
    ppermute x1, starting transfers between devices, local(): partner_queries = lax.ppermute(folded, 'inner', swap)  2.55 us
    unnamed x21, local copies, waits for them, and re-layouts  1.75 us
    dot_general x1, matrix products, local(): jnp.dot(query, w_key.T, preferred_element_type=jnp.float32)  1.3 us
  transfers between devices with their start and end apart: 5, of which 4 were waited for; matrix products, arithmetic and copies ran while one was open for 4% of the time, Pallas kernels for 0%

profile of v8, /device:TPU:0, one launch (start us, length us, event | category | flops | bytes accessed | tf_op | source)
XLA Modules:
  0.0 52.3 jit_solution(2022162073383347478)
XLA Ops:
  0.0 0.0 copy-start
  0.0 1.0 %copy.23 = bf16[1,1,2,112,192]{4,3,2,1,0:T(8,128)(2,1)S(1)} copy(bf16[1,1,2,112,192]{3,4,2,1,0:T(8,128)(2,1)} %param.15) | data formatting | bytes 172032 | tf_op args[0]
  1.0 0.5 collective-permute-start
  1.6 1.0 %collective-permute-done = bf16[1,2,112,192]{3,2,1,0:T(8,128)(2,1)S(1)} collective-permute-done((bf16[1,2,112,192]{3,2,1,0:T(8,128)(2,1)S(1)}, bf16[1,2,112,192]{3,2,1,0:T(8,128)(2,1)S(1)}, u32[]{:S(2)}, u32[]{:S(2)}) %collective-permute-start) | collective-permute-done | bytes 86048 | tf_op jit(solution)/shard_map/ppermute | solution.py:157
  2.6 4.8 %collective-permute-start.1 = (bf16[2,2,112,192]{3,2,1,0:T(8,128)(2,1)S(1)}, bf16[2,2,112,192]{3,2,1,0:T(8,128)(2,1)S(1)}, u32[]{:S(2)}, u32[]{:S(2)}) collective-permute-start(bf16[2,2,112,192]{3,2,1,0:T(8,128)(2,1)S(1)} %maximum_bitcast_fusion), channel_id=1, source_target_pairs={{0,2},{2,4},{4,6},{6,8},{8,10},{10,12},{12,14},{3,1},{5,3},{7,5},{... | collective-permute-start | bytes 516104 | tf_op jit(solution)/shard_map/ppermute | solution.py:165
  7.4 6.0 %collective-permute-done.1 = bf16[2,2,112,192]{3,2,1,0:T(8,128)(2,1)S(1)} collective-permute-done((bf16[2,2,112,192]{3,2,1,0:T(8,128)(2,1)S(1)}, bf16[2,2,112,192]{3,2,1,0:T(8,128)(2,1)S(1)}, u32[]{:S(2)}, u32[]{:S(2)}) %collective-permute-start.1) | collective-permute-done | bytes 172064 | tf_op jit(solution)/shard_map/ppermute | solution.py:165
  13.3 0.0 collective-permute-start.2
  13.3 0.8 %pad_maximum_fusion.seq_ref = bf16[2,224,192]{2,1,0:T(8,128)(2,1)} fusion(bf16[1,224,192]{2,1,0:T(8,128)(2,1)S(1)} %bitcast.67, bf16[1,224,192]{2,1,0:T(8,128)(2,1)S(1)} %bitcast.65), kind=kLoop, calls=%fused_computation.18 | loop fusion | flops 86016 | bytes 344064 | tf_op jit(solution)/shard_map/stack | solution.py:160
  14.1 0.7 %collective-permute-done.2 = bf16[2,2,112,192]{3,2,1,0:T(8,128)(2,1)S(1)} collective-permute-done((bf16[2,2,112,192]{3,2,1,0:T(8,128)(2,1)S(1)}, bf16[2,2,112,192]{3,2,1,0:T(8,128)(2,1)S(1)}, u32[]{:S(2)}, u32[]{:S(2)}) %collective-permute-start.2) | collective-permute-done | bytes 172064 | tf_op jit(solution)/shard_map/ppermute | solution.py:166
  14.8 0.7 %copy-done.3 = bf16[2,2,112,192]{3,2,1,0:T(8,128)(2,1)} copy-done((bf16[2,2,112,192]{3,2,1,0:T(8,128)(2,1)}, bf16[2,2,112,192]{3,2,1,0:T(8,128)(2,1)S(1)}, u32[]{:S(2)}) %copy-start.3) | copy-done | bytes 172056
  15.5 7.3 %shard_map.145 = (f32[1,224,192]{2,1,0:T(8,128)}, bf16[1,224,192]{2,1,0:T(8,128)(2,1)}) custom-call(bf16[2,224,192]{2,1,0:T(8,128)(2,1)} %pad_maximum_fusion.seq_ref, bf16[2,224,192]{2,1,0:T(8,128)(2,1)} %bitcast.72, bf16[2,224,192]{2,1,0:T(8,128)(2,1)} %bitcast.73, f32[1,192]{1,0:T(1,128)} %bitcast.81, bf16[27,192,192]{2,1,0:T(8,128)(2,1)} %bitcast.62, ...), custom_call_target="tpu_custom_call" | custom-call | tf_op jit(solution)/shard_map/pallas_call | solution.py:122
  22.9 1.0 %copy.24 = bf16[1,2,112,192]{2,3,0,1:T(8,128)(2,1)S(1)} copy(bf16[1,2,112,192]{3,2,1,0:T(8,128)(2,1)} %bitcast.70) | data formatting | bytes 172032 | tf_op jit(solution)/shard_map/reshape | solution.py:182
  23.9 1.3 %fusion.3 = bf16[224,192]{0,1:T(8,128)(2,1)S(1)} fusion(bf16[192,192]{1,0:T(8,128)(2,1)S(1)} %copy-done, bf16[192,192]{1,0:T(8,128)(2,1)S(1)} %copy-done.4, bf16[1,224,192]{2,1,0:T(8,128)(2,1)} %get-tuple-element.8, f32[192]{0:T(256)S(1)} %copy-done.5), kind=kOutput, calls=%fused_computation.8 | convolution fusion | flops 33202176 | bytes 320256 | tf_op jit(solution)/shard_map/dot_general | solution.py:188
  25.2 2.5 %collective-permute-start.3 = (bf16[1,224,192]{1,2,0:T(8,128)(2,1)S(1)}, bf16[1,224,192]{1,2,0:T(8,128)(2,1)S(1)}, u32[]{:S(2)}, u32[]{:S(2)}) collective-permute-start(bf16[1,224,192]{1,2,0:T(8,128)(2,1)S(1)} %bitcast.71), channel_id=1, source_target_pairs={{0,2},{2,0},{1,3},{3,1},{4,6},{6,4},{5,7},{7,5},{8,10},{10,8},{9,1... | collective-permute-start | bytes 258056 | tf_op jit(solution)/shard_map/ppermute | solution.py:193
  27.7 15.1 %all_gather.3 = bf16[1,8,112,192]{2,3,0,1:T(8,128)(2,1)S(1)} all-gather(bf16[1,2,112,192]{2,3,0,1:T(8,128)(2,1)S(1)} %copy.24), channel_id=1, replica_groups=mesh['clips'=2,'outer'=4,'inner'=2,'tm'=2] {'outer'}, dimensions={1}, use_global_device_ids=true | all-gather | bytes 430080 | tf_op jit(solution)/shard_map/all_gather | solution.py:194
  42.8 0.3 copy.25
  43.1 0.3 reshape.115
  43.4 0.0 collective-permute-done.3
  43.4 0.4 fusion.35
  43.8 0.3 fusion.7
  44.1 0.0 copy-start.7
  44.1 0.0 copy-start.8
  44.1 0.0 copy-start.9
  44.1 0.4 convolution_bitcast_fusion
  44.6 0.0 copy-start.6
  44.6 0.1 collective-permute-start.4
  44.7 0.4 fusion.34
  45.1 0.3 fusion.5
  45.4 5.1 %collective-permute-done.4 = f32[1,224,194]{1,2,0:T(8,128)S(1)} collective-permute-done((f32[1,224,194]{1,2,0:T(8,128)S(1)}, f32[1,224,194]{1,2,0:T(8,128)S(1)}, u32[]{:S(2)}, u32[]{:S(2)}) %collective-permute-start.4) | collective-permute-done | bytes 173856 | tf_op jit(solution)/shard_map/ppermute | solution.py:206
  50.5 0.4 fusion
  50.9 0.5 fusion.4
  51.4 0.8 %copy.27 = f32[1,1,2,112,192]{3,4,2,1,0:T(8,128)} copy(f32[1,1,2,112,192]{4,3,2,1,0:T(8,128)S(1)} %bitcast.68) | data formatting | bytes 344064 | tf_op jit(solution)/shard_map/reshape | solution.py:224
  (19 shorter events, 0.2 us)
Async XLA Ops:
  0.0 23.9 %copy-start = (bf16[192,192]{1,0:T(8,128)(2,1)S(1)}, bf16[192,192]{1,0:T(8,128)(2,1)}, u32[]{:S(2)}) copy-start(bf16[192,192]{1,0:T(8,128)(2,1)} %param.25) | copy-start | bytes 221188
  1.0 1.5 %collective-permute-start = (bf16[1,2,112,192]{3,2,1,0:T(8,128)(2,1)S(1)}, bf16[1,2,112,192]{3,2,1,0:T(8,128)(2,1)S(1)}, u32[]{:S(2)}, u32[]{:S(2)}) collective-permute-start(bf16[1,2,112,192]{3,2,1,0:T(8,128)(2,1)S(1)} %bitcast.69), channel_id=1, source_target_pairs={{0,1},{1,0},{2,3},{3,2},{4,5},{5,4},{6,7},{7,6},{8,9},{9,8},{10,11... | collective-permute-start | bytes 258056 | tf_op jit(solution)/shard_map/ppermute | solution.py:157
  2.6 10.7 %collective-permute-start.1 = (bf16[2,2,112,192]{3,2,1,0:T(8,128)(2,1)S(1)}, bf16[2,2,112,192]{3,2,1,0:T(8,128)(2,1)S(1)}, u32[]{:S(2)}, u32[]{:S(2)}) collective-permute-start(bf16[2,2,112,192]{3,2,1,0:T(8,128)(2,1)S(1)} %maximum_bitcast_fusion), channel_id=1, source_target_pairs={{0,2},{2,4},{4,6},{6,8},{8,10},{10,12},{12,14},{3,1},{5,3},{7,5},{... | collective-permute-start | bytes 516104 | tf_op jit(solution)/shard_map/ppermute | solution.py:165
  13.3 1.5 %copy-start.2 = (bf16[2,2,112,192]{3,2,1,0:T(8,128)(2,1)}, bf16[2,2,112,192]{3,2,1,0:T(8,128)(2,1)S(1)}, u32[]{:S(2)}) copy-start(bf16[2,2,112,192]{3,2,1,0:T(8,128)(2,1)S(1)} %collective-permute-done.1) | copy-start | bytes 516100
  13.3 1.5 %collective-permute-start.2 = (bf16[2,2,112,192]{3,2,1,0:T(8,128)(2,1)S(1)}, bf16[2,2,112,192]{3,2,1,0:T(8,128)(2,1)S(1)}, u32[]{:S(2)}, u32[]{:S(2)}) collective-permute-start(bf16[2,2,112,192]{3,2,1,0:T(8,128)(2,1)S(1)} %collective-permute-done.1), channel_id=1, source_target_pairs={{0,1},{1,0},{2,3},{3,2},{4,5},{5,4},{6,7},{7,6},{8,9},{9,8},{10,11... | collective-permute-start | bytes 516104 | tf_op jit(solution)/shard_map/ppermute | solution.py:166
  14.8 0.7 %copy-start.3 = (bf16[2,2,112,192]{3,2,1,0:T(8,128)(2,1)}, bf16[2,2,112,192]{3,2,1,0:T(8,128)(2,1)S(1)}, u32[]{:S(2)}) copy-start(bf16[2,2,112,192]{3,2,1,0:T(8,128)(2,1)S(1)} %collective-permute-done.2) | copy-start | bytes 516100
  15.5 8.4 %copy-start.4 = (bf16[192,192]{1,0:T(8,128)(2,1)S(1)}, bf16[192,192]{1,0:T(8,128)(2,1)}, u32[]{:S(2)}) copy-start(bf16[192,192]{1,0:T(8,128)(2,1)} %param.23) | copy-start | bytes 221188
  15.5 8.4 %copy-start.5 = (f32[192]{0:T(256)S(1)}, f32[192]{0:T(256)}, u32[]{:S(2)}) copy-start(f32[192]{0:T(256)} %param.24) | copy-start | bytes 2308
  25.2 18.2 %collective-permute-start.3 = (bf16[1,224,192]{1,2,0:T(8,128)(2,1)S(1)}, bf16[1,224,192]{1,2,0:T(8,128)(2,1)S(1)}, u32[]{:S(2)}, u32[]{:S(2)}) collective-permute-start(bf16[1,224,192]{1,2,0:T(8,128)(2,1)S(1)} %bitcast.71), channel_id=1, source_target_pairs={{0,2},{2,0},{1,3},{3,1},{4,6},{6,4},{5,7},{7,5},{8,10},{10,8},{9,1... | collective-permute-start | bytes 258056 | tf_op jit(solution)/shard_map/ppermute | solution.py:193
  44.1 6.8 %copy-start.7 = (bf16[192,192]{1,0:T(8,128)(2,1)S(1)}, bf16[192,192]{1,0:T(8,128)(2,1)}, u32[]{:S(2)}) copy-start(bf16[192,192]{1,0:T(8,128)(2,1)} %param.28) | copy-start | bytes 221188
  44.1 6.8 %copy-start.8 = (bf16[192,192]{1,0:T(8,128)(2,1)S(1)}, bf16[192,192]{1,0:T(8,128)(2,1)}, u32[]{:S(2)}) copy-start(bf16[192,192]{1,0:T(8,128)(2,1)} %param.26) | copy-start | bytes 221188
  44.1 6.8 %copy-start.9 = (f32[192]{0:T(256)S(1)}, f32[192]{0:T(256)}, u32[]{:S(2)}) copy-start(f32[192]{0:T(256)} %param.27) | copy-start | bytes 2308
  44.6 6.8 %copy-start.1 = (f32[1,224,192]{2,1,0:T(8,128)S(1)}, f32[1,224,192]{2,1,0:T(8,128)}, u32[]{:S(2)}) copy-start(f32[1,224,192]{2,1,0:T(8,128)} %get-tuple-element.7) | copy-start | bytes 516100
  44.6 6.8 %copy-start.6 = (f32[192]{0:T(256)S(1)}, f32[192]{0:T(256)}, u32[]{:S(2)}) copy-start(f32[192]{0:T(256)} %param.29) | copy-start | bytes 2308
  44.6 5.8 %collective-permute-start.4 = (f32[1,224,194]{1,2,0:T(8,128)S(1)}, f32[1,224,194]{1,2,0:T(8,128)S(1)}, u32[]{:S(2)}, u32[]{:S(2)}) collective-permute-start(f32[1,224,194]{1,2,0:T(8,128)S(1)} %pad_maximum_fusion.1), channel_id=1, source_target_pairs={{0,2},{2,0},{1,3},{3,1},{4,6},{6,4},{5,7},{7,5},{8,10},{10,8},{9,1... | collective-permute-start | bytes 521480 | tf_op jit(solution)/shard_map/ppermute | solution.py:206

commit v9 on v8

--- a/solution.py
+++ b/solution.py
@@ -49,7 +49,7 @@
     return v * (1.0 / (1.0 + jnp.exp(-v)))
 
 def block_kernel(cols, frame_count, seq_ref, arrived_ref, swapped_ref, g1_ref, w1_ref, b1_ref, g2_ref,
-                 w2_ref, b2_ref, ga_ref, res_ref, normed_ref):
+                 w2_ref, b2_ref, ga_ref, wq_ref, bq_ref, wkt_ref, res_ref, normed_ref, folded_ref):
     total = 2 * frame_count
     p_out = seq_ref.shape[1]
     p_mid = p_out + 2 * cols
@@ -113,20 +113,25 @@
         own = jnp.where(first, seq_ref[2 * k], seq_ref[2 * k + 1])
         res = own.astype(jnp.float32) + out2
         res_ref[k] = res
-        normed_ref[k] = _rms(res, ga).astype(jnp.bfloat16)
-
-def resnet_block(seq, arrived, swapped, g1, w1, b1, g2, w2, b2, ga, cols):
+        normed = _rms(res, ga).astype(jnp.bfloat16)
+        normed_ref[k] = normed
+        query = jnp.dot(normed, wq_ref[...], preferred_element_type=jnp.float32) + bq_ref[...]
+        folded = jnp.dot(query.astype(jnp.bfloat16), wkt_ref[...], preferred_element_type=jnp.float32)
+        folded_ref[k] = (folded * (1.0 / math.sqrt(res.shape[-1]))).astype(jnp.bfloat16)
+
+def resnet_block(seq, arrived, swapped, g1, w1, b1, g2, w2, b2, ga, wq, bq, wk, cols):
     total, p_out, c = seq.shape
     frame_count = total // 2
     vm = pl.BlockSpec(memory_space=pltpu.VMEM)
     return pl.pallas_call(
         functools.partial(block_kernel, cols, frame_count),
         out_shape=(jax.ShapeDtypeStruct((frame_count, p_out, c), jnp.float32),
+                   jax.ShapeDtypeStruct((frame_count, p_out, c), jnp.bfloat16),
                    jax.ShapeDtypeStruct((frame_count, p_out, c), jnp.bfloat16)),
-        in_specs=[vm] * 10,
-        out_specs=(vm, vm),
+        in_specs=[vm] * 13,
+        out_specs=(vm, vm, vm),
     )(seq, arrived, swapped, g1.reshape(1, c), w1.reshape(27, c, c), b1.reshape(1, c), g2.reshape(1, c),
-      w2.reshape(27, c, c), b2.reshape(1, c), ga.reshape(1, c))
+      w2.reshape(27, c, c), b2.reshape(1, c), ga.reshape(1, c), wq, bq.reshape(1, c), wk.T)
 
 
 def local(
@@ -166,7 +171,7 @@
     swapped = lax.ppermute(arrived, "tm", [(0, 1), (1, 0)])
 
     token_count = row_count * col_count
-    residual, normed = resnet_block(
+    residual, normed, folded = resnet_block(
         seq.reshape(2 * frame_count, -1, channels),
         arrived.reshape(2 * frame_count, -1, channels),
         swapped.reshape(2 * frame_count, -1, channels),
@@ -177,16 +182,12 @@
         conv2_weight,
         conv2_bias,
         attn_gain,
+        w_query,
+        b_query,
+        w_key,
         col_count,
     )
     normed = normed.reshape(frame_count, row_count, col_count, channels)
-    flat = normed.reshape(frame_count * token_count, channels)
-    query = (jnp.dot(flat, w_query, preferred_element_type=jnp.float32) + b_query).astype(
-        jnp.bfloat16
-    )
-    folded = (
-        jnp.dot(query, w_key.T, preferred_element_type=jnp.float32) * (1.0 / math.sqrt(channels))
-    ).astype(jnp.bfloat16)
     folded = folded.reshape(frame_count, token_count, channels)
 
     swap = [(0, 1), (1, 0)]

time: 52.5 us -> 52.5 us (level)
  local copies, waits for them, and re-layouts: 4.14 us -> 5.84 us
  matrix products: 3.39 us -> 2.03 us
  waiting for transfers between devices: 12.7 us -> 12 us
    unnamed x21 -> x18, local copies, waits for them, and re-layouts: 1.75 us -> 3.45 us
    dot_general x1 -> x0, matrix products: 1.3 us -> none  [local(): jnp.dot(query, w_key.T, preferred_element_type=jnp.float32)]
    ppermute x1, waiting for transfers between devices: 0.7 us -> 0.01 us  [local(): swapped = lax.ppermute(arrived, 'tm', [(0, 1), (1, 0)])]
  transfers between devices with their start and end apart: 5 -> 5, of which waited for: 4 -> 3; matrix products, arithmetic and copies ran while one was open for 4% -> 7% of each run, Pallas kernels for 0% -> 0%
where the time goes in v9:
time: 52.5 us; the launch traced here: 52.3 us
  blocking collectives  15.3 us (29%)
  waiting for transfers between devices  12 us (23%)
  starting transfers between devices  7.9 us (15%)
  Pallas kernels  7.59 us (14%)
  local copies, waits for them, and re-layouts  5.84 us (11%)
  matrix products  2.03 us (4%)
  other arithmetic  1.43 us (3%)
    all_gather x1, blocking collectives, local(): keys = lax.all_gather(normed, 'outer', axis=1, tiled=True)  15.3 us
    pallas_call x1, Pallas kernels, resnet_block(): pl.pallas_call(functools.partial(block_kernel, cols, frame_count), out_sh...  7.59 us
    ppermute x1, waiting for transfers between devices, local(): arrived = lax.ppermute(edge, ('outer', 'inner', 'tm'), up + down)  5.97 us
    ppermute x1, waiting for transfers between devices, local(): returned = lax.ppermute(partial(partner_queries), 'inner', swap)  5.08 us
    ppermute x1, starting transfers between devices, local(): arrived = lax.ppermute(edge, ('outer', 'inner', 'tm'), up + down)  4.76 us
    unnamed x18, local copies, waits for them, and re-layouts  3.45 us
    ppermute x1, starting transfers between devices, local(): partner_queries = lax.ppermute(folded, 'inner', swap)  2.55 us
  transfers between devices with their start and end apart: 5, of which 3 were waited for; matrix products, arithmetic and copies ran while one was open for 7% of the time, Pallas kernels for 0%

profile of v9, /device:TPU:0, one launch (start us, length us, event | category | flops | bytes accessed | tf_op | source)
XLA Modules:
  0.0 52.3 jit_solution(6949312878803911096)
XLA Ops:
  0.0 0.0 copy-start
  0.0 1.0 %copy.25 = bf16[1,1,2,112,192]{4,3,2,1,0:T(8,128)(2,1)S(1)} copy(bf16[1,1,2,112,192]{3,4,2,1,0:T(8,128)(2,1)} %param.15) | data formatting | bytes 172032 | tf_op args[0]
  1.0 0.5 collective-permute-start
  1.6 1.0 %collective-permute-done = bf16[1,2,112,192]{3,2,1,0:T(8,128)(2,1)S(1)} collective-permute-done((bf16[1,2,112,192]{3,2,1,0:T(8,128)(2,1)S(1)}, bf16[1,2,112,192]{3,2,1,0:T(8,128)(2,1)S(1)}, u32[]{:S(2)}, u32[]{:S(2)}) %collective-permute-start) | collective-permute-done | bytes 86048 | tf_op jit(solution)/shard_map/ppermute | solution.py:162
  2.6 4.8 %collective-permute-start.1 = (bf16[2,2,112,192]{3,2,1,0:T(8,128)(2,1)S(1)}, bf16[2,2,112,192]{3,2,1,0:T(8,128)(2,1)S(1)}, u32[]{:S(2)}, u32[]{:S(2)}) collective-permute-start(bf16[2,2,112,192]{3,2,1,0:T(8,128)(2,1)S(1)} %maximum_bitcast_fusion), channel_id=1, source_target_pairs={{0,2},{2,4},{4,6},{6,8},{8,10},{10,12},{12,14},{3,1},{5,3},{7,5},{... | collective-permute-start | bytes 516104 | tf_op jit(solution)/shard_map/ppermute | solution.py:170
  7.4 6.0 %collective-permute-done.1 = bf16[2,2,112,192]{3,2,1,0:T(8,128)(2,1)S(1)} collective-permute-done((bf16[2,2,112,192]{3,2,1,0:T(8,128)(2,1)S(1)}, bf16[2,2,112,192]{3,2,1,0:T(8,128)(2,1)S(1)}, u32[]{:S(2)}, u32[]{:S(2)}) %collective-permute-start.1) | collective-permute-done | bytes 172064 | tf_op jit(solution)/shard_map/ppermute | solution.py:170
  13.3 0.0 collective-permute-start.2
  13.3 1.7 %copy.26 = bf16[192,192]{0,1:T(8,128)(2,1)} copy(bf16[192,192]{1,0:T(8,128)(2,1)} %param.25) | data formatting | bytes 147456 | tf_op args[10]
  15.1 0.7 %pad_maximum_fusion.seq_ref = bf16[2,224,192]{2,1,0:T(8,128)(2,1)} fusion(bf16[1,224,192]{2,1,0:T(8,128)(2,1)S(1)} %bitcast.66, bf16[1,224,192]{2,1,0:T(8,128)(2,1)S(1)} %bitcast.64), kind=kLoop, calls=%fused_computation.14 | loop fusion | flops 86016 | bytes 344064 | tf_op jit(solution)/shard_map/stack | solution.py:165
  15.8 0.0 collective-permute-done.2
  15.8 0.7 %copy-done.3 = bf16[2,2,112,192]{3,2,1,0:T(8,128)(2,1)} copy-done((bf16[2,2,112,192]{3,2,1,0:T(8,128)(2,1)}, bf16[2,2,112,192]{3,2,1,0:T(8,128)(2,1)S(1)}, u32[]{:S(2)}) %copy-start.3) | copy-done | bytes 172056
  16.5 7.6 %shard_map.145 = (f32[1,224,192]{2,1,0:T(8,128)}, bf16[1,224,192]{2,1,0:T(8,128)(2,1)}, bf16[1,224,192]{2,1,0:T(8,128)(2,1)}) custom-call(bf16[2,224,192]{2,1,0:T(8,128)(2,1)} %pad_maximum_fusion.seq_ref, bf16[2,224,192]{2,1,0:T(8,128)(2,1)} %bitcast.70, bf16[2,224,192]{2,1,0:T(8,128)(2,1)} %bitcast.71, f32[1,192]{1,0:T(1,128)} %bitcast.78, ...), custom_call_target="tpu_custom_call" | custom-call | tf_op jit(solution)/shard_map/pallas_call | solution.py:126
  24.0 1.0 %copy.27 = bf16[1,2,112,192]{2,3,0,1:T(8,128)(2,1)S(1)} copy(bf16[1,2,112,192]{3,2,1,0:T(8,128)(2,1)} %bitcast.72) | data formatting | bytes 172032 | tf_op jit(solution)/shard_map/reshape | solution.py:190
  25.1 2.5 %collective-permute-start.3 = (bf16[1,224,192]{2,1,0:T(8,128)(2,1)}, bf16[1,224,192]{2,1,0:T(8,128)(2,1)S(1)}, u32[]{:S(2)}, u32[]{:S(2)}) collective-permute-start(bf16[1,224,192]{2,1,0:T(8,128)(2,1)} %get-tuple-element.9), channel_id=1, source_target_pairs={{0,2},{2,0},{1,3},{3,1},{4,6},{6,4},{5,7},{7,5},{8,10},{10,8},{9,1... | collective-permute-start | bytes 258056 | tf_op jit(solution)/shard_map/ppermute | solution.py:194
  27.6 15.3 %all_gather.3 = bf16[1,8,112,192]{2,3,0,1:T(8,128)(2,1)S(1)} all-gather(bf16[1,2,112,192]{2,3,0,1:T(8,128)(2,1)S(1)} %copy.27), channel_id=1, replica_groups=mesh['clips'=2,'outer'=4,'inner'=2,'tm'=2] {'outer'}, dimensions={1}, use_global_device_ids=true | all-gather | bytes 430080 | tf_op jit(solution)/shard_map/all_gather | solution.py:195
  42.9 0.3 copy.28
  43.2 0.3 reshape.117
  43.5 0.0 collective-permute-done.3
  43.5 0.4 fusion.32
  43.8 0.3 fusion.5
  44.1 0.0 copy-start.6
  44.1 0.0 copy-start.7
  44.2 0.4 convolution_bitcast_fusion
  44.6 0.0 copy-start.1
  44.6 0.0 copy-start.5
  44.6 0.1 collective-permute-start.4
  44.7 0.4 fusion.31
  45.1 0.3 fusion.3
  45.4 5.1 %collective-permute-done.4 = f32[1,224,194]{1,2,0:T(8,128)S(1)} collective-permute-done((f32[1,224,194]{1,2,0:T(8,128)S(1)}, f32[1,224,194]{1,2,0:T(8,128)S(1)}, u32[]{:S(2)}, u32[]{:S(2)}) %collective-permute-start.4) | collective-permute-done | bytes 173856 | tf_op jit(solution)/shard_map/ppermute | solution.py:207
  50.5 0.4 fusion
  50.9 0.5 fusion.2
  51.5 0.8 %copy.30 = f32[1,1,2,112,192]{3,4,2,1,0:T(8,128)} copy(f32[1,1,2,112,192]{4,3,2,1,0:T(8,128)S(1)} %bitcast.67) | data formatting | bytes 344064 | tf_op jit(solution)/shard_map/reshape | solution.py:225
  (15 shorter events, 0.1 us)
Async XLA Ops:
  0.0 50.9 %copy-start = (bf16[192,192]{1,0:T(8,128)(2,1)S(1)}, bf16[192,192]{1,0:T(8,128)(2,1)}, u32[]{:S(2)}) copy-start(bf16[192,192]{1,0:T(8,128)(2,1)} %param.28) | copy-start | bytes 221188
  1.0 1.5 %collective-permute-start = (bf16[1,2,112,192]{3,2,1,0:T(8,128)(2,1)S(1)}, bf16[1,2,112,192]{3,2,1,0:T(8,128)(2,1)S(1)}, u32[]{:S(2)}, u32[]{:S(2)}) collective-permute-start(bf16[1,2,112,192]{3,2,1,0:T(8,128)(2,1)S(1)} %bitcast.68), channel_id=1, source_target_pairs={{0,1},{1,0},{2,3},{3,2},{4,5},{5,4},{6,7},{7,6},{8,9},{9,8},{10,11... | collective-permute-start | bytes 258056 | tf_op jit(solution)/shard_map/ppermute | solution.py:162
  2.6 10.7 %collective-permute-start.1 = (bf16[2,2,112,192]{3,2,1,0:T(8,128)(2,1)S(1)}, bf16[2,2,112,192]{3,2,1,0:T(8,128)(2,1)S(1)}, u32[]{:S(2)}, u32[]{:S(2)}) collective-permute-start(bf16[2,2,112,192]{3,2,1,0:T(8,128)(2,1)S(1)} %maximum_bitcast_fusion), channel_id=1, source_target_pairs={{0,2},{2,4},{4,6},{6,8},{8,10},{10,12},{12,14},{3,1},{5,3},{7,5},{... | collective-permute-start | bytes 516104 | tf_op jit(solution)/shard_map/ppermute | solution.py:170
  13.3 2.5 %copy-start.2 = (bf16[2,2,112,192]{3,2,1,0:T(8,128)(2,1)}, bf16[2,2,112,192]{3,2,1,0:T(8,128)(2,1)S(1)}, u32[]{:S(2)}) copy-start(bf16[2,2,112,192]{3,2,1,0:T(8,128)(2,1)S(1)} %collective-permute-done.1) | copy-start | bytes 516100
  13.3 2.4 %collective-permute-start.2 = (bf16[2,2,112,192]{3,2,1,0:T(8,128)(2,1)S(1)}, bf16[2,2,112,192]{3,2,1,0:T(8,128)(2,1)S(1)}, u32[]{:S(2)}, u32[]{:S(2)}) collective-permute-start(bf16[2,2,112,192]{3,2,1,0:T(8,128)(2,1)S(1)} %collective-permute-done.1), channel_id=1, source_target_pairs={{0,1},{1,0},{2,3},{3,2},{4,5},{5,4},{6,7},{7,6},{8,9},{9,8},{10,11... | collective-permute-start | bytes 516104 | tf_op jit(solution)/shard_map/ppermute | solution.py:171
  15.8 0.7 %copy-start.3 = (bf16[2,2,112,192]{3,2,1,0:T(8,128)(2,1)}, bf16[2,2,112,192]{3,2,1,0:T(8,128)(2,1)S(1)}, u32[]{:S(2)}) copy-start(bf16[2,2,112,192]{3,2,1,0:T(8,128)(2,1)S(1)} %collective-permute-done.2) | copy-start | bytes 516100
  25.1 18.4 %collective-permute-start.3 = (bf16[1,224,192]{2,1,0:T(8,128)(2,1)}, bf16[1,224,192]{2,1,0:T(8,128)(2,1)S(1)}, u32[]{:S(2)}, u32[]{:S(2)}) collective-permute-start(bf16[1,224,192]{2,1,0:T(8,128)(2,1)} %get-tuple-element.9), channel_id=1, source_target_pairs={{0,2},{2,0},{1,3},{3,1},{4,6},{6,4},{5,7},{7,5},{8,10},{10,8},{9,1... | collective-permute-start | bytes 258056 | tf_op jit(solution)/shard_map/ppermute | solution.py:194
  42.9 1.8 %copy-start.4 = (bf16[1,224,192]{2,1,0:T(8,128)(2,1)S(1)}, bf16[1,224,192]{2,1,0:T(8,128)(2,1)}, u32[]{:S(2)}) copy-start(bf16[1,224,192]{2,1,0:T(8,128)(2,1)} %get-tuple-element.9) | copy-start | bytes 258052
  44.1 6.8 %copy-start.6 = (bf16[192,192]{1,0:T(8,128)(2,1)S(1)}, bf16[192,192]{1,0:T(8,128)(2,1)}, u32[]{:S(2)}) copy-start(bf16[192,192]{1,0:T(8,128)(2,1)} %param.26) | copy-start | bytes 221188
  44.1 6.8 %copy-start.7 = (f32[192]{0:T(256)S(1)}, f32[192]{0:T(256)}, u32[]{:S(2)}) copy-start(f32[192]{0:T(256)} %param.27) | copy-start | bytes 2308
  44.6 6.8 %copy-start.1 = (f32[1,224,192]{2,1,0:T(8,128)S(1)}, f32[1,224,192]{2,1,0:T(8,128)}, u32[]{:S(2)}) copy-start(f32[1,224,192]{2,1,0:T(8,128)} %get-tuple-element.8) | copy-start | bytes 516100
  44.6 6.8 %copy-start.5 = (f32[192]{0:T(256)S(1)}, f32[192]{0:T(256)}, u32[]{:S(2)}) copy-start(f32[192]{0:T(256)} %param.29) | copy-start | bytes 2308
  44.6 5.8 %collective-permute-start.4 = (f32[1,224,194]{1,2,0:T(8,128)S(1)}, f32[1,224,194]{1,2,0:T(8,128)S(1)}, u32[]{:S(2)}, u32[]{:S(2)}) collective-permute-start(f32[1,224,194]{1,2,0:T(8,128)S(1)} %pad_maximum_fusion.1), channel_id=1, source_target_pairs={{0,2},{2,0},{1,3},{3,1},{4,6},{6,4},{5,7},{7,5},{8,10},{10,8},{9,1... | collective-permute-start | bytes 521480 | tf_op jit(solution)/shard_map/ppermute | solution.py:207

commit v10 on v9

--- a/solution.py
+++ b/solution.py
@@ -49,7 +49,7 @@
     return v * (1.0 / (1.0 + jnp.exp(-v)))
 
 def block_kernel(cols, frame_count, seq_ref, arrived_ref, swapped_ref, g1_ref, w1_ref, b1_ref, g2_ref,
-                 w2_ref, b2_ref, ga_ref, wq_ref, bq_ref, wkt_ref, res_ref, normed_ref, folded_ref):
+                 w2_ref, b2_ref, ga_ref, wq_ref, bq_ref, wk_ref, res_ref, normed_ref, folded_ref):
     total = 2 * frame_count
     p_out = seq_ref.shape[1]
     p_mid = p_out + 2 * cols
@@ -116,7 +116,10 @@
         normed = _rms(res, ga).astype(jnp.bfloat16)
         normed_ref[k] = normed
         query = jnp.dot(normed, wq_ref[...], preferred_element_type=jnp.float32) + bq_ref[...]
-        folded = jnp.dot(query.astype(jnp.bfloat16), wkt_ref[...], preferred_element_type=jnp.float32)
+        folded = lax.dot_general(
+            query.astype(jnp.bfloat16), wk_ref[...], (((1,), (1,)), ((), ())),
+            preferred_element_type=jnp.float32,
+        )
         folded_ref[k] = (folded * (1.0 / math.sqrt(res.shape[-1]))).astype(jnp.bfloat16)
 
 def resnet_block(seq, arrived, swapped, g1, w1, b1, g2, w2, b2, ga, wq, bq, wk, cols):
@@ -131,7 +134,7 @@
         in_specs=[vm] * 13,
         out_specs=(vm, vm, vm),
     )(seq, arrived, swapped, g1.reshape(1, c), w1.reshape(27, c, c), b1.reshape(1, c), g2.reshape(1, c),
-      w2.reshape(27, c, c), b2.reshape(1, c), ga.reshape(1, c), wq, bq.reshape(1, c), wk.T)
+      w2.reshape(27, c, c), b2.reshape(1, c), ga.reshape(1, c), wq, bq.reshape(1, c), wk)
 
 
 def local(

time: 52.5 us -> 51.3 us (0.977)
  local copies, waits for them, and re-layouts: 5.84 us -> 4.13 us
  waiting for transfers between devices: 12 us -> 12.7 us
    unnamed x18 -> x17, local copies, waits for them, and re-layouts: 3.45 us -> 1.74 us
    ppermute x1, waiting for transfers between devices: 0.01 us -> 0.71 us  [local(): swapped = lax.ppermute(arrived, 'tm', [(0, 1), (1, 0)])]
  transfers between devices with their start and end apart: 5 -> 5, of which waited for: 3 -> 4; matrix products, arithmetic and copies ran while one was open for 7% -> 4% of each run, Pallas kernels for 0% -> 0%
where the time goes in v10:
time: 51.3 us; the launch traced here: 51.1 us
  blocking collectives  15.1 us (29%)
  waiting for transfers between devices  12.7 us (25%)
  starting transfers between devices  7.9 us (15%)
  Pallas kernels  7.59 us (15%)
  local copies, waits for them, and re-layouts  4.13 us (8%)
  matrix products  2.03 us (4%)
  other arithmetic  1.48 us (3%)
    all_gather x1, blocking collectives, local(): keys = lax.all_gather(normed, 'outer', axis=1, tiled=True)  15.1 us
    pallas_call x1, Pallas kernels, resnet_block(): pl.pallas_call(functools.partial(block_kernel, cols, frame_count), out_sh...  7.59 us
    ppermute x1, waiting for transfers between devices, local(): arrived = lax.ppermute(edge, ('outer', 'inner', 'tm'), up + down)  5.97 us
    ppermute x1, waiting for transfers between devices, local(): returned = lax.ppermute(partial(partner_queries), 'inner', swap)  5.08 us
    ppermute x1, starting transfers between devices, local(): arrived = lax.ppermute(edge, ('outer', 'inner', 'tm'), up + down)  4.76 us
    ppermute x1, starting transfers between devices, local(): partner_queries = lax.ppermute(folded, 'inner', swap)  2.54 us
    unnamed x17, local copies, waits for them, and re-layouts  1.74 us
  transfers between devices with their start and end apart: 5, of which 4 were waited for; matrix products, arithmetic and copies ran while one was open for 4% of the time, Pallas kernels for 0%

profile of v10, /device:TPU:0, one launch (start us, length us, event | category | flops | bytes accessed | tf_op | source)
XLA Modules:
  0.0 51.1 jit_solution(297188736266385246)
XLA Ops:
  0.0 1.0 %copy.23 = bf16[1,1,2,112,192]{4,3,2,1,0:T(8,128)(2,1)S(1)} copy(bf16[1,1,2,112,192]{3,4,2,1,0:T(8,128)(2,1)} %param.15) | data formatting | bytes 172032 | tf_op args[0]
  1.0 0.5 %collective-permute-start = (bf16[1,2,112,192]{3,2,1,0:T(8,128)(2,1)S(1)}, bf16[1,2,112,192]{3,2,1,0:T(8,128)(2,1)S(1)}, u32[]{:S(2)}, u32[]{:S(2)}) collective-permute-start(bf16[1,2,112,192]{3,2,1,0:T(8,128)(2,1)S(1)} %bitcast.67), channel_id=1, source_target_pairs={{0,1},{1,0},{2,3},{3,2},{4,5},{5,4},{6,7},{7,6},{8,9},{9,8},{10,11... | collective-permute-start | bytes 258056 | tf_op jit(solution)/shard_map/ppermute | solution.py:165
  1.6 1.0 %collective-permute-done = bf16[1,2,112,192]{3,2,1,0:T(8,128)(2,1)S(1)} collective-permute-done((bf16[1,2,112,192]{3,2,1,0:T(8,128)(2,1)S(1)}, bf16[1,2,112,192]{3,2,1,0:T(8,128)(2,1)S(1)}, u32[]{:S(2)}, u32[]{:S(2)}) %collective-permute-start) | collective-permute-done | bytes 86048 | tf_op jit(solution)/shard_map/ppermute | solution.py:165
  2.6 4.8 %collective-permute-start.1 = (bf16[2,2,112,192]{3,2,1,0:T(8,128)(2,1)S(1)}, bf16[2,2,112,192]{3,2,1,0:T(8,128)(2,1)S(1)}, u32[]{:S(2)}, u32[]{:S(2)}) collective-permute-start(bf16[2,2,112,192]{3,2,1,0:T(8,128)(2,1)S(1)} %maximum_bitcast_fusion), channel_id=1, source_target_pairs={{0,2},{2,4},{4,6},{6,8},{8,10},{10,12},{12,14},{3,1},{5,3},{7,5},{... | collective-permute-start | bytes 516104 | tf_op jit(solution)/shard_map/ppermute | solution.py:173
  7.4 6.0 %collective-permute-done.1 = bf16[2,2,112,192]{3,2,1,0:T(8,128)(2,1)S(1)} collective-permute-done((bf16[2,2,112,192]{3,2,1,0:T(8,128)(2,1)S(1)}, bf16[2,2,112,192]{3,2,1,0:T(8,128)(2,1)S(1)}, u32[]{:S(2)}, u32[]{:S(2)}) %collective-permute-start.1) | collective-permute-done | bytes 172064 | tf_op jit(solution)/shard_map/ppermute | solution.py:173
  13.3 0.0 collective-permute-start.2
  13.3 0.8 %pad_maximum_fusion.seq_ref = bf16[2,224,192]{2,1,0:T(8,128)(2,1)} fusion(bf16[1,224,192]{2,1,0:T(8,128)(2,1)S(1)} %bitcast.65, bf16[1,224,192]{2,1,0:T(8,128)(2,1)S(1)} %bitcast.63), kind=kLoop, calls=%fused_computation.14 | loop fusion | flops 86016 | bytes 344064 | tf_op jit(solution)/shard_map/stack | solution.py:168
  14.1 0.7 %collective-permute-done.2 = bf16[2,2,112,192]{3,2,1,0:T(8,128)(2,1)S(1)} collective-permute-done((bf16[2,2,112,192]{3,2,1,0:T(8,128)(2,1)S(1)}, bf16[2,2,112,192]{3,2,1,0:T(8,128)(2,1)S(1)}, u32[]{:S(2)}, u32[]{:S(2)}) %collective-permute-start.2) | collective-permute-done | bytes 172064 | tf_op jit(solution)/shard_map/ppermute | solution.py:174
  14.8 0.0 copy-done.2
  14.8 0.7 %copy-done.3 = bf16[2,2,112,192]{3,2,1,0:T(8,128)(2,1)} copy-done((bf16[2,2,112,192]{3,2,1,0:T(8,128)(2,1)}, bf16[2,2,112,192]{3,2,1,0:T(8,128)(2,1)S(1)}, u32[]{:S(2)}) %copy-start.3) | copy-done | bytes 172056
  15.5 7.6 %shard_map.145 = (f32[1,224,192]{2,1,0:T(8,128)}, bf16[1,224,192]{2,1,0:T(8,128)(2,1)}, bf16[1,224,192]{2,1,0:T(8,128)(2,1)}) custom-call(bf16[2,224,192]{2,1,0:T(8,128)(2,1)} %pad_maximum_fusion.seq_ref, bf16[2,224,192]{2,1,0:T(8,128)(2,1)} %bitcast.68, bf16[2,224,192]{2,1,0:T(8,128)(2,1)} %bitcast.69, f32[1,192]{1,0:T(1,128)} %bitcast.76, ...), custom_call_target="tpu_custom_call" | custom-call | tf_op jit(solution)/shard_map/pallas_call | solution.py:129
  23.1 1.0 %copy.24 = bf16[1,2,112,192]{2,3,0,1:T(8,128)(2,1)S(1)} copy(bf16[1,2,112,192]{3,2,1,0:T(8,128)(2,1)} %bitcast.70) | data formatting | bytes 172032 | tf_op jit(solution)/shard_map/reshape | solution.py:193
  24.1 2.5 %collective-permute-start.3 = (bf16[1,224,192]{2,1,0:T(8,128)(2,1)}, bf16[1,224,192]{2,1,0:T(8,128)(2,1)S(1)}, u32[]{:S(2)}, u32[]{:S(2)}) collective-permute-start(bf16[1,224,192]{2,1,0:T(8,128)(2,1)} %get-tuple-element.9), channel_id=1, source_target_pairs={{0,2},{2,0},{1,3},{3,1},{4,6},{6,4},{5,7},{7,5},{8,10},{10,8},{9,1... | collective-permute-start | bytes 258056 | tf_op jit(solution)/shard_map/ppermute | solution.py:197
  26.6 15.1 %all_gather.3 = bf16[1,8,112,192]{2,3,0,1:T(8,128)(2,1)S(1)} all-gather(bf16[1,2,112,192]{2,3,0,1:T(8,128)(2,1)S(1)} %copy.24), channel_id=1, replica_groups=mesh['clips'=2,'outer'=4,'inner'=2,'tm'=2] {'outer'}, dimensions={1}, use_global_device_ids=true | all-gather | bytes 430080 | tf_op jit(solution)/shard_map/all_gather | solution.py:198
  41.7 0.3 copy.25
  42.0 0.3 reshape.117
  42.3 0.0 collective-permute-done.3
  42.3 0.4 fusion.32
  42.7 0.3 fusion.5
  43.0 0.0 copy-start.6
  43.0 0.0 copy-start.7
  43.0 0.4 convolution_bitcast_fusion
  43.4 0.0 copy-start.1
  43.4 0.0 copy-start.5
  43.5 0.1 collective-permute-start.4
  43.6 0.0 copy-done.4
  43.6 0.4 fusion.31
  43.9 0.3 fusion.3
  44.2 5.1 %collective-permute-done.4 = f32[1,224,194]{1,2,0:T(8,128)S(1)} collective-permute-done((f32[1,224,194]{1,2,0:T(8,128)S(1)}, f32[1,224,194]{1,2,0:T(8,128)S(1)}, u32[]{:S(2)}, u32[]{:S(2)}) %collective-permute-start.4) | collective-permute-done | bytes 173856 | tf_op jit(solution)/shard_map/ppermute | solution.py:210
  49.3 0.4 fusion
  49.8 0.5 fusion.2
  50.3 0.8 %copy.27 = f32[1,1,2,112,192]{3,4,2,1,0:T(8,128)} copy(f32[1,1,2,112,192]{4,3,2,1,0:T(8,128)S(1)} %bitcast.66) | data formatting | bytes 344064 | tf_op jit(solution)/shard_map/reshape | solution.py:228
  (14 shorter events, 0.1 us)
Async XLA Ops:
  0.0 49.8 %copy-start = (bf16[192,192]{1,0:T(8,128)(2,1)S(1)}, bf16[192,192]{1,0:T(8,128)(2,1)}, u32[]{:S(2)}) copy-start(bf16[192,192]{1,0:T(8,128)(2,1)} %param.28) | copy-start | bytes 221188
  1.0 1.5 %collective-permute-start = (bf16[1,2,112,192]{3,2,1,0:T(8,128)(2,1)S(1)}, bf16[1,2,112,192]{3,2,1,0:T(8,128)(2,1)S(1)}, u32[]{:S(2)}, u32[]{:S(2)}) collective-permute-start(bf16[1,2,112,192]{3,2,1,0:T(8,128)(2,1)S(1)} %bitcast.67), channel_id=1, source_target_pairs={{0,1},{1,0},{2,3},{3,2},{4,5},{5,4},{6,7},{7,6},{8,9},{9,8},{10,11... | collective-permute-start | bytes 258056 | tf_op jit(solution)/shard_map/ppermute | solution.py:165
  2.6 10.7 %collective-permute-start.1 = (bf16[2,2,112,192]{3,2,1,0:T(8,128)(2,1)S(1)}, bf16[2,2,112,192]{3,2,1,0:T(8,128)(2,1)S(1)}, u32[]{:S(2)}, u32[]{:S(2)}) collective-permute-start(bf16[2,2,112,192]{3,2,1,0:T(8,128)(2,1)S(1)} %maximum_bitcast_fusion), channel_id=1, source_target_pairs={{0,2},{2,4},{4,6},{6,8},{8,10},{10,12},{12,14},{3,1},{5,3},{7,5},{... | collective-permute-start | bytes 516104 | tf_op jit(solution)/shard_map/ppermute | solution.py:173
  13.3 1.5 %copy-start.2 = (bf16[2,2,112,192]{3,2,1,0:T(8,128)(2,1)}, bf16[2,2,112,192]{3,2,1,0:T(8,128)(2,1)S(1)}, u32[]{:S(2)}) copy-start(bf16[2,2,112,192]{3,2,1,0:T(8,128)(2,1)S(1)} %collective-permute-done.1) | copy-start | bytes 516100
  13.3 1.5 %collective-permute-start.2 = (bf16[2,2,112,192]{3,2,1,0:T(8,128)(2,1)S(1)}, bf16[2,2,112,192]{3,2,1,0:T(8,128)(2,1)S(1)}, u32[]{:S(2)}, u32[]{:S(2)}) collective-permute-start(bf16[2,2,112,192]{3,2,1,0:T(8,128)(2,1)S(1)} %collective-permute-done.1), channel_id=1, source_target_pairs={{0,1},{1,0},{2,3},{3,2},{4,5},{5,4},{6,7},{7,6},{8,9},{9,8},{10,11... | collective-permute-start | bytes 516104 | tf_op jit(solution)/shard_map/ppermute | solution.py:174
  14.8 0.7 %copy-start.3 = (bf16[2,2,112,192]{3,2,1,0:T(8,128)(2,1)}, bf16[2,2,112,192]{3,2,1,0:T(8,128)(2,1)S(1)}, u32[]{:S(2)}) copy-start(bf16[2,2,112,192]{3,2,1,0:T(8,128)(2,1)S(1)} %collective-permute-done.2) | copy-start | bytes 516100
  24.1 18.2 %collective-permute-start.3 = (bf16[1,224,192]{2,1,0:T(8,128)(2,1)}, bf16[1,224,192]{2,1,0:T(8,128)(2,1)S(1)}, u32[]{:S(2)}, u32[]{:S(2)}) collective-permute-start(bf16[1,224,192]{2,1,0:T(8,128)(2,1)} %get-tuple-element.9), channel_id=1, source_target_pairs={{0,2},{2,0},{1,3},{3,1},{4,6},{6,4},{5,7},{7,5},{8,10},{10,8},{9,1... | collective-permute-start | bytes 258056 | tf_op jit(solution)/shard_map/ppermute | solution.py:197
  41.7 1.8 %copy-start.4 = (bf16[1,224,192]{2,1,0:T(8,128)(2,1)S(1)}, bf16[1,224,192]{2,1,0:T(8,128)(2,1)}, u32[]{:S(2)}) copy-start(bf16[1,224,192]{2,1,0:T(8,128)(2,1)} %get-tuple-element.9) | copy-start | bytes 258052
  43.0 6.8 %copy-start.6 = (bf16[192,192]{1,0:T(8,128)(2,1)S(1)}, bf16[192,192]{1,0:T(8,128)(2,1)}, u32[]{:S(2)}) copy-start(bf16[192,192]{1,0:T(8,128)(2,1)} %param.26) | copy-start | bytes 221188
  43.0 6.8 %copy-start.7 = (f32[192]{0:T(256)S(1)}, f32[192]{0:T(256)}, u32[]{:S(2)}) copy-start(f32[192]{0:T(256)} %param.27) | copy-start | bytes 2308
  43.4 6.8 %copy-start.1 = (f32[1,224,192]{2,1,0:T(8,128)S(1)}, f32[1,224,192]{2,1,0:T(8,128)}, u32[]{:S(2)}) copy-start(f32[1,224,192]{2,1,0:T(8,128)} %get-tuple-element.8) | copy-start | bytes 516100
  43.4 6.8 %copy-start.5 = (f32[192]{0:T(256)S(1)}, f32[192]{0:T(256)}, u32[]{:S(2)}) copy-start(f32[192]{0:T(256)} %param.29) | copy-start | bytes 2308
  43.5 5.8 %collective-permute-start.4 = (f32[1,224,194]{1,2,0:T(8,128)S(1)}, f32[1,224,194]{1,2,0:T(8,128)S(1)}, u32[]{:S(2)}, u32[]{:S(2)}) collective-permute-start(f32[1,224,194]{1,2,0:T(8,128)S(1)} %pad_maximum_fusion.1), channel_id=1, source_target_pairs={{0,2},{2,0},{1,3},{3,1},{4,6},{6,4},{5,7},{7,5},{8,10},{10,8},{9,1... | collective-permute-start | bytes 521480 | tf_op jit(solution)/shard_map/ppermute | solution.py:210

commit v11 on v10

--- a/solution.py
+++ b/solution.py
@@ -91,10 +91,22 @@
     inside = (row >= lo) & (row < hi)
     g2 = g2_ref[...]
     b1 = b1_ref[...]
+    acc = [None] * total
+    for p in range(3):
+        outs = [j for j in range(total) if j + p - 2 >= 0]
+        if not outs:
+            continue
+        for q in range(3):
+            for s in range(3):
+                pieces = [act1[j + p - 2][s][q * cols: q * cols + p_mid] for j in outs]
+                window = pieces[0] if len(pieces) == 1 else jnp.concatenate(pieces, axis=0)
+                part = jnp.dot(window, w1_ref[(p * 3 + q) * 3 + s], preferred_element_type=jnp.float32)
+                for i, j in enumerate(outs):
+                    piece = part[i * p_mid: (i + 1) * p_mid]
+                    acc[j] = piece if acc[j] is None else acc[j] + piece
     act2 = []
     for j in range(total):
-        srcs = [act1[j + p - 2] if j + p - 2 >= 0 else None for p in range(3)]
-        out1 = conv_frame(srcs, w1_ref, p_mid) + b1
+        out1 = acc[j] + b1
         act2.append(jnp.where(inside, _silu(_rms(out1, g2)), 0.0).astype(jnp.bfloat16).astype(jnp.float32))
     b2 = b2_ref[...]
     ga = ga_ref[...]

time: 51.3 us -> 52 us (1.014)
  Pallas kernels: 7.59 us -> 8.23 us
    pallas_call x1, Pallas kernels: 7.59 us -> 8.23 us  [resnet_block(): pl.pallas_call(functools.partial(block_kernel, cols, frame_count), out_sh...]
where the time goes in v11:
time: 52 us; the launch traced here: 51.8 us
  blocking collectives  15.1 us (29%)
  waiting for transfers between devices  12.7 us (24%)
  Pallas kernels  8.23 us (16%)
  starting transfers between devices  7.9 us (15%)
  local copies, waits for them, and re-layouts  4.13 us (8%)
  matrix products  2.03 us (4%)
  other arithmetic  1.48 us (3%)
    all_gather x1, blocking collectives, local(): keys = lax.all_gather(normed, 'outer', axis=1, tiled=True)  15.1 us
    pallas_call x1, Pallas kernels, resnet_block(): pl.pallas_call(functools.partial(block_kernel, cols, frame_count), out_sh...  8.23 us
    ppermute x1, waiting for transfers between devices, local(): arrived = lax.ppermute(edge, ('outer', 'inner', 'tm'), up + down)  5.97 us
    ppermute x1, waiting for transfers between devices, local(): returned = lax.ppermute(partial(partner_queries), 'inner', swap)  5.08 us
    ppermute x1, starting transfers between devices, local(): arrived = lax.ppermute(edge, ('outer', 'inner', 'tm'), up + down)  4.76 us
    ppermute x1, starting transfers between devices, local(): partner_queries = lax.ppermute(folded, 'inner', swap)  2.55 us
    unnamed x17, local copies, waits for them, and re-layouts  1.74 us
  transfers between devices with their start and end apart: 5, of which 4 were waited for; matrix products, arithmetic and copies ran while one was open for 4% of the time, Pallas kernels for 0%

profile of v11, /device:TPU:0, one launch (start us, length us, event | category | flops | bytes accessed | tf_op | source)
XLA Modules:
  0.0 51.8 jit_solution(6074215506661262791)
XLA Ops:
  0.0 1.0 %copy.23 = bf16[1,1,2,112,192]{4,3,2,1,0:T(8,128)(2,1)S(1)} copy(bf16[1,1,2,112,192]{3,4,2,1,0:T(8,128)(2,1)} %param.15) | data formatting | bytes 172032 | tf_op args[0]
  1.0 0.5 %collective-permute-start = (bf16[1,2,112,192]{3,2,1,0:T(8,128)(2,1)S(1)}, bf16[1,2,112,192]{3,2,1,0:T(8,128)(2,1)S(1)}, u32[]{:S(2)}, u32[]{:S(2)}) collective-permute-start(bf16[1,2,112,192]{3,2,1,0:T(8,128)(2,1)S(1)} %bitcast.67), channel_id=1, source_target_pairs={{0,1},{1,0},{2,3},{3,2},{4,5},{5,4},{6,7},{7,6},{8,9},{9,8},{10,11... | collective-permute-start | bytes 258056 | tf_op jit(solution)/shard_map/ppermute | solution.py:177
  1.6 1.0 %collective-permute-done = bf16[1,2,112,192]{3,2,1,0:T(8,128)(2,1)S(1)} collective-permute-done((bf16[1,2,112,192]{3,2,1,0:T(8,128)(2,1)S(1)}, bf16[1,2,112,192]{3,2,1,0:T(8,128)(2,1)S(1)}, u32[]{:S(2)}, u32[]{:S(2)}) %collective-permute-start) | collective-permute-done | bytes 86048 | tf_op jit(solution)/shard_map/ppermute | solution.py:177
  2.6 4.8 %collective-permute-start.1 = (bf16[2,2,112,192]{3,2,1,0:T(8,128)(2,1)S(1)}, bf16[2,2,112,192]{3,2,1,0:T(8,128)(2,1)S(1)}, u32[]{:S(2)}, u32[]{:S(2)}) collective-permute-start(bf16[2,2,112,192]{3,2,1,0:T(8,128)(2,1)S(1)} %maximum_bitcast_fusion), channel_id=1, source_target_pairs={{0,2},{2,4},{4,6},{6,8},{8,10},{10,12},{12,14},{3,1},{5,3},{7,5},{... | collective-permute-start | bytes 516104 | tf_op jit(solution)/shard_map/ppermute | solution.py:185
  7.4 6.0 %collective-permute-done.1 = bf16[2,2,112,192]{3,2,1,0:T(8,128)(2,1)S(1)} collective-permute-done((bf16[2,2,112,192]{3,2,1,0:T(8,128)(2,1)S(1)}, bf16[2,2,112,192]{3,2,1,0:T(8,128)(2,1)S(1)}, u32[]{:S(2)}, u32[]{:S(2)}) %collective-permute-start.1) | collective-permute-done | bytes 172064 | tf_op jit(solution)/shard_map/ppermute | solution.py:185
  13.3 0.0 collective-permute-start.2
  13.3 0.8 %pad_maximum_fusion.seq_ref = bf16[2,224,192]{2,1,0:T(8,128)(2,1)} fusion(bf16[1,224,192]{2,1,0:T(8,128)(2,1)S(1)} %bitcast.65, bf16[1,224,192]{2,1,0:T(8,128)(2,1)S(1)} %bitcast.63), kind=kLoop, calls=%fused_computation.14 | loop fusion | flops 86016 | bytes 344064 | tf_op jit(solution)/shard_map/stack | solution.py:180
  14.1 0.7 %collective-permute-done.2 = bf16[2,2,112,192]{3,2,1,0:T(8,128)(2,1)S(1)} collective-permute-done((bf16[2,2,112,192]{3,2,1,0:T(8,128)(2,1)S(1)}, bf16[2,2,112,192]{3,2,1,0:T(8,128)(2,1)S(1)}, u32[]{:S(2)}, u32[]{:S(2)}) %collective-permute-start.2) | collective-permute-done | bytes 172064 | tf_op jit(solution)/shard_map/ppermute | solution.py:186
  14.8 0.0 copy-done.2
  14.8 0.7 %copy-done.3 = bf16[2,2,112,192]{3,2,1,0:T(8,128)(2,1)} copy-done((bf16[2,2,112,192]{3,2,1,0:T(8,128)(2,1)}, bf16[2,2,112,192]{3,2,1,0:T(8,128)(2,1)S(1)}, u32[]{:S(2)}) %copy-start.3) | copy-done | bytes 172056
  15.5 8.2 %shard_map.145 = (f32[1,224,192]{2,1,0:T(8,128)}, bf16[1,224,192]{2,1,0:T(8,128)(2,1)}, bf16[1,224,192]{2,1,0:T(8,128)(2,1)}) custom-call(bf16[2,224,192]{2,1,0:T(8,128)(2,1)} %pad_maximum_fusion.seq_ref, bf16[2,224,192]{2,1,0:T(8,128)(2,1)} %bitcast.68, bf16[2,224,192]{2,1,0:T(8,128)(2,1)} %bitcast.69, f32[1,192]{1,0:T(1,128)} %bitcast.76, ...), custom_call_target="tpu_custom_call" | custom-call | tf_op jit(solution)/shard_map/pallas_call | solution.py:141
  23.7 1.0 %copy.24 = bf16[1,2,112,192]{2,3,0,1:T(8,128)(2,1)S(1)} copy(bf16[1,2,112,192]{3,2,1,0:T(8,128)(2,1)} %bitcast.70) | data formatting | bytes 172032 | tf_op jit(solution)/shard_map/reshape | solution.py:205
  24.7 2.5 %collective-permute-start.3 = (bf16[1,224,192]{2,1,0:T(8,128)(2,1)}, bf16[1,224,192]{2,1,0:T(8,128)(2,1)S(1)}, u32[]{:S(2)}, u32[]{:S(2)}) collective-permute-start(bf16[1,224,192]{2,1,0:T(8,128)(2,1)} %get-tuple-element.9), channel_id=1, source_target_pairs={{0,2},{2,0},{1,3},{3,1},{4,6},{6,4},{5,7},{7,5},{8,10},{10,8},{9,1... | collective-permute-start | bytes 258056 | tf_op jit(solution)/shard_map/ppermute | solution.py:209
  27.3 15.1 %all_gather.3 = bf16[1,8,112,192]{2,3,0,1:T(8,128)(2,1)S(1)} all-gather(bf16[1,2,112,192]{2,3,0,1:T(8,128)(2,1)S(1)} %copy.24), channel_id=1, replica_groups=mesh['clips'=2,'outer'=4,'inner'=2,'tm'=2] {'outer'}, dimensions={1}, use_global_device_ids=true | all-gather | bytes 430080 | tf_op jit(solution)/shard_map/all_gather | solution.py:210
  42.4 0.3 copy.25
  42.6 0.3 reshape.117
  43.0 0.0 collective-permute-done.3
  43.0 0.4 fusion.32
  43.3 0.3 fusion.5
  43.6 0.0 copy-start.6
  43.6 0.0 copy-start.7
  43.6 0.4 convolution_bitcast_fusion
  44.1 0.0 copy-start.1
  44.1 0.0 copy-start.5
  44.1 0.1 collective-permute-start.4
  44.2 0.0 copy-done.4
  44.2 0.4 fusion.31
  44.6 0.3 fusion.3
  44.9 5.1 %collective-permute-done.4 = f32[1,224,194]{1,2,0:T(8,128)S(1)} collective-permute-done((f32[1,224,194]{1,2,0:T(8,128)S(1)}, f32[1,224,194]{1,2,0:T(8,128)S(1)}, u32[]{:S(2)}, u32[]{:S(2)}) %collective-permute-start.4) | collective-permute-done | bytes 173856 | tf_op jit(solution)/shard_map/ppermute | solution.py:222
  50.0 0.4 fusion
  50.4 0.5 fusion.2
  51.0 0.8 %copy.27 = f32[1,1,2,112,192]{3,4,2,1,0:T(8,128)} copy(f32[1,1,2,112,192]{4,3,2,1,0:T(8,128)S(1)} %bitcast.66) | data formatting | bytes 344064 | tf_op jit(solution)/shard_map/reshape | solution.py:240
  (14 shorter events, 0.1 us)
Async XLA Ops:
  0.0 50.4 %copy-start = (bf16[192,192]{1,0:T(8,128)(2,1)S(1)}, bf16[192,192]{1,0:T(8,128)(2,1)}, u32[]{:S(2)}) copy-start(bf16[192,192]{1,0:T(8,128)(2,1)} %param.28) | copy-start | bytes 221188
  1.0 1.5 %collective-permute-start = (bf16[1,2,112,192]{3,2,1,0:T(8,128)(2,1)S(1)}, bf16[1,2,112,192]{3,2,1,0:T(8,128)(2,1)S(1)}, u32[]{:S(2)}, u32[]{:S(2)}) collective-permute-start(bf16[1,2,112,192]{3,2,1,0:T(8,128)(2,1)S(1)} %bitcast.67), channel_id=1, source_target_pairs={{0,1},{1,0},{2,3},{3,2},{4,5},{5,4},{6,7},{7,6},{8,9},{9,8},{10,11... | collective-permute-start | bytes 258056 | tf_op jit(solution)/shard_map/ppermute | solution.py:177
  2.6 10.7 %collective-permute-start.1 = (bf16[2,2,112,192]{3,2,1,0:T(8,128)(2,1)S(1)}, bf16[2,2,112,192]{3,2,1,0:T(8,128)(2,1)S(1)}, u32[]{:S(2)}, u32[]{:S(2)}) collective-permute-start(bf16[2,2,112,192]{3,2,1,0:T(8,128)(2,1)S(1)} %maximum_bitcast_fusion), channel_id=1, source_target_pairs={{0,2},{2,4},{4,6},{6,8},{8,10},{10,12},{12,14},{3,1},{5,3},{7,5},{... | collective-permute-start | bytes 516104 | tf_op jit(solution)/shard_map/ppermute | solution.py:185
  13.3 1.5 %copy-start.2 = (bf16[2,2,112,192]{3,2,1,0:T(8,128)(2,1)}, bf16[2,2,112,192]{3,2,1,0:T(8,128)(2,1)S(1)}, u32[]{:S(2)}) copy-start(bf16[2,2,112,192]{3,2,1,0:T(8,128)(2,1)S(1)} %collective-permute-done.1) | copy-start | bytes 516100
  13.3 1.5 %collective-permute-start.2 = (bf16[2,2,112,192]{3,2,1,0:T(8,128)(2,1)S(1)}, bf16[2,2,112,192]{3,2,1,0:T(8,128)(2,1)S(1)}, u32[]{:S(2)}, u32[]{:S(2)}) collective-permute-start(bf16[2,2,112,192]{3,2,1,0:T(8,128)(2,1)S(1)} %collective-permute-done.1), channel_id=1, source_target_pairs={{0,1},{1,0},{2,3},{3,2},{4,5},{5,4},{6,7},{7,6},{8,9},{9,8},{10,11... | collective-permute-start | bytes 516104 | tf_op jit(solution)/shard_map/ppermute | solution.py:186
  14.8 0.7 %copy-start.3 = (bf16[2,2,112,192]{3,2,1,0:T(8,128)(2,1)}, bf16[2,2,112,192]{3,2,1,0:T(8,128)(2,1)S(1)}, u32[]{:S(2)}) copy-start(bf16[2,2,112,192]{3,2,1,0:T(8,128)(2,1)S(1)} %collective-permute-done.2) | copy-start | bytes 516100
  24.7 18.2 %collective-permute-start.3 = (bf16[1,224,192]{2,1,0:T(8,128)(2,1)}, bf16[1,224,192]{2,1,0:T(8,128)(2,1)S(1)}, u32[]{:S(2)}, u32[]{:S(2)}) collective-permute-start(bf16[1,224,192]{2,1,0:T(8,128)(2,1)} %get-tuple-element.9), channel_id=1, source_target_pairs={{0,2},{2,0},{1,3},{3,1},{4,6},{6,4},{5,7},{7,5},{8,10},{10,8},{9,1... | collective-permute-start | bytes 258056 | tf_op jit(solution)/shard_map/ppermute | solution.py:209
  42.4 1.8 %copy-start.4 = (bf16[1,224,192]{2,1,0:T(8,128)(2,1)S(1)}, bf16[1,224,192]{2,1,0:T(8,128)(2,1)}, u32[]{:S(2)}) copy-start(bf16[1,224,192]{2,1,0:T(8,128)(2,1)} %get-tuple-element.9) | copy-start | bytes 258052
  43.6 6.8 %copy-start.6 = (bf16[192,192]{1,0:T(8,128)(2,1)S(1)}, bf16[192,192]{1,0:T(8,128)(2,1)}, u32[]{:S(2)}) copy-start(bf16[192,192]{1,0:T(8,128)(2,1)} %param.26) | copy-start | bytes 221188
  43.6 6.8 %copy-start.7 = (f32[192]{0:T(256)S(1)}, f32[192]{0:T(256)}, u32[]{:S(2)}) copy-start(f32[192]{0:T(256)} %param.27) | copy-start | bytes 2308
  44.1 6.8 %copy-start.1 = (f32[1,224,192]{2,1,0:T(8,128)S(1)}, f32[1,224,192]{2,1,0:T(8,128)}, u32[]{:S(2)}) copy-start(f32[1,224,192]{2,1,0:T(8,128)} %get-tuple-element.8) | copy-start | bytes 516100
  44.1 6.8 %copy-start.5 = (f32[192]{0:T(256)S(1)}, f32[192]{0:T(256)}, u32[]{:S(2)}) copy-start(f32[192]{0:T(256)} %param.29) | copy-start | bytes 2308
  44.1 5.8 %collective-permute-start.4 = (f32[1,224,194]{1,2,0:T(8,128)S(1)}, f32[1,224,194]{1,2,0:T(8,128)S(1)}, u32[]{:S(2)}, u32[]{:S(2)}) collective-permute-start(f32[1,224,194]{1,2,0:T(8,128)S(1)} %pad_maximum_fusion.1), channel_id=1, source_target_pairs={{0,2},{2,0},{1,3},{3,1},{4,6},{6,4},{5,7},{7,5},{8,10},{10,8},{9,1... | collective-permute-start | bytes 521480 | tf_op jit(solution)/shard_map/ppermute | solution.py:222

commit v12 on v10

--- a/solution.py
+++ b/solution.py
@@ -205,17 +205,20 @@
         accum = jnp.einsum(
             "fqk,fkc->fqc", weights.astype(jnp.bfloat16), keys, preferred_element_type=jnp.float32
         )
-        return jnp.concatenate([accum, top, total], axis=-1)
-
-    returned = lax.ppermute(partial(partner_queries), "inner", swap)
-    mine = partial(folded)
-    top_mine = mine[..., channels : channels + 1]
-    top_back = returned[..., channels : channels + 1]
+        return accum, jnp.concatenate([top, total], axis=-1)
+
+    back_accum, back_stats = partial(partner_queries)
+    returned_accum, returned_stats = lax.ppermute(
+        (back_accum.astype(jnp.bfloat16), back_stats), "inner", swap
+    )
+    mine_accum, mine_stats = partial(folded)
+    top_mine = mine_stats[..., :1]
+    top_back = returned_stats[..., :1]
     highest = jnp.maximum(top_mine, top_back)
     scale_mine = jnp.exp(top_mine - highest)
     scale_back = jnp.exp(top_back - highest)
-    total = mine[..., channels + 1 :] * scale_mine + returned[..., channels + 1 :] * scale_back
-    accum = mine[..., :channels] * scale_mine + returned[..., :channels] * scale_back
+    total = mine_stats[..., 1:] * scale_mine + returned_stats[..., 1:] * scale_back
+    accum = mine_accum * scale_mine + returned_accum.astype(jnp.float32) * scale_back
     mixed = (accum / total).astype(jnp.bfloat16).reshape(-1, channels)
     value = (jnp.dot(mixed, w_value, preferred_element_type=jnp.float32) + b_value).astype(
         jnp.bfloat16

time: 51.3 us -> 51.3 us (level)
  waiting for transfers between devices: 12.7 us -> 9.8 us
  starting transfers between devices: 7.9 us -> 9.97 us
  matrix products: 2.03 us -> 2.93 us
    ppermute x1 -> x2, waiting for transfers between devices: 5.08 us -> 2.16 us  [local(): lax.ppermute((back_accum.astype(jnp.bfloat16), back_stats), 'inner', swap)]
    ppermute x1 -> x2, starting transfers between devices: 0.07 us -> 2.15 us  [local(): lax.ppermute((back_accum.astype(jnp.bfloat16), back_stats), 'inner', swap)]
    dot_general x2, matrix products: 0.72 us -> 1.62 us  [partial(): jnp.einsum('fqc,fkc->fqk', queries, keys, preferred_element_type=jnp.floa...]
    unnamed x17 -> x15, local copies, waits for them, and re-layouts: 1.74 us -> 1.73 us
  transfers between devices with their start and end apart: 5 -> 6, of which waited for: 4 -> 5; matrix products, arithmetic and copies ran while one was open for 4% -> 7% of each run, Pallas kernels for 0% -> 0%
where the time goes in v12:
time: 51.3 us; the launch traced here: 51.1 us
  blocking collectives  15.1 us (29%)
  starting transfers between devices  9.97 us (19%)
  waiting for transfers between devices  9.8 us (19%)
  Pallas kernels  7.59 us (15%)
  local copies, waits for them, and re-layouts  4.12 us (8%)
  matrix products  2.93 us (6%)
  other arithmetic  1.46 us (3%)
    all_gather x1, blocking collectives, local(): keys = lax.all_gather(normed, 'outer', axis=1, tiled=True)  15.1 us
    pallas_call x1, Pallas kernels, resnet_block(): pl.pallas_call(functools.partial(block_kernel, cols, frame_count), out_sh...  7.59 us
    ppermute x1, waiting for transfers between devices, local(): arrived = lax.ppermute(edge, ('outer', 'inner', 'tm'), up + down)  5.97 us
    ppermute x1, starting transfers between devices, local(): arrived = lax.ppermute(edge, ('outer', 'inner', 'tm'), up + down)  4.76 us
    ppermute x1, starting transfers between devices, local(): partner_queries = lax.ppermute(folded, 'inner', swap)  2.54 us
    ppermute x2, waiting for transfers between devices, local(): lax.ppermute((back_accum.astype(jnp.bfloat16), back_stats), 'inner', swap)  2.16 us
    ppermute x2, starting transfers between devices, local(): lax.ppermute((back_accum.astype(jnp.bfloat16), back_stats), 'inner', swap)  2.15 us
    unnamed x15, local copies, waits for them, and re-layouts  1.73 us
  transfers between devices with their start and end apart: 6, of which 5 were waited for; matrix products, arithmetic and copies ran while one was open for 7% of the time, Pallas kernels for 0%

profile of v12, /device:TPU:0, one launch (start us, length us, event | category | flops | bytes accessed | tf_op | source)
XLA Modules:
  0.0 51.1 jit_solution(7334960484970070566)
XLA Ops:
  0.0 1.0 %copy.26 = bf16[1,1,2,112,192]{4,3,2,1,0:T(8,128)(2,1)S(1)} copy(bf16[1,1,2,112,192]{3,4,2,1,0:T(8,128)(2,1)} %param.15) | data formatting | bytes 172032 | tf_op args[0]
  1.0 0.5 %collective-permute-start = (bf16[1,2,112,192]{3,2,1,0:T(8,128)(2,1)S(1)}, bf16[1,2,112,192]{3,2,1,0:T(8,128)(2,1)S(1)}, u32[]{:S(2)}, u32[]{:S(2)}) collective-permute-start(bf16[1,2,112,192]{3,2,1,0:T(8,128)(2,1)S(1)} %bitcast.67), channel_id=1, source_target_pairs={{0,1},{1,0},{2,3},{3,2},{4,5},{5,4},{6,7},{7,6},{8,9},{9,8},{10,11... | collective-permute-start | bytes 258056 | tf_op jit(solution)/shard_map/ppermute | solution.py:165
  1.6 1.0 %collective-permute-done = bf16[1,2,112,192]{3,2,1,0:T(8,128)(2,1)S(1)} collective-permute-done((bf16[1,2,112,192]{3,2,1,0:T(8,128)(2,1)S(1)}, bf16[1,2,112,192]{3,2,1,0:T(8,128)(2,1)S(1)}, u32[]{:S(2)}, u32[]{:S(2)}) %collective-permute-start) | collective-permute-done | bytes 86048 | tf_op jit(solution)/shard_map/ppermute | solution.py:165
  2.6 4.8 %collective-permute-start.1 = (bf16[2,2,112,192]{3,2,1,0:T(8,128)(2,1)S(1)}, bf16[2,2,112,192]{3,2,1,0:T(8,128)(2,1)S(1)}, u32[]{:S(2)}, u32[]{:S(2)}) collective-permute-start(bf16[2,2,112,192]{3,2,1,0:T(8,128)(2,1)S(1)} %maximum_bitcast_fusion), channel_id=1, source_target_pairs={{0,2},{2,4},{4,6},{6,8},{8,10},{10,12},{12,14},{3,1},{5,3},{7,5},{... | collective-permute-start | bytes 516104 | tf_op jit(solution)/shard_map/ppermute | solution.py:173
  7.4 6.0 %collective-permute-done.1 = bf16[2,2,112,192]{3,2,1,0:T(8,128)(2,1)S(1)} collective-permute-done((bf16[2,2,112,192]{3,2,1,0:T(8,128)(2,1)S(1)}, bf16[2,2,112,192]{3,2,1,0:T(8,128)(2,1)S(1)}, u32[]{:S(2)}, u32[]{:S(2)}) %collective-permute-start.1) | collective-permute-done | bytes 172064 | tf_op jit(solution)/shard_map/ppermute | solution.py:173
  13.3 0.0 collective-permute-start.2
  13.3 0.8 %pad_maximum_fusion.seq_ref = bf16[2,224,192]{2,1,0:T(8,128)(2,1)} fusion(bf16[1,224,192]{2,1,0:T(8,128)(2,1)S(1)} %bitcast.65, bf16[1,224,192]{2,1,0:T(8,128)(2,1)S(1)} %bitcast.63), kind=kLoop, calls=%fused_computation.15 | loop fusion | flops 86016 | bytes 344064 | tf_op jit(solution)/shard_map/stack | solution.py:168
  14.1 0.7 %collective-permute-done.2 = bf16[2,2,112,192]{3,2,1,0:T(8,128)(2,1)S(1)} collective-permute-done((bf16[2,2,112,192]{3,2,1,0:T(8,128)(2,1)S(1)}, bf16[2,2,112,192]{3,2,1,0:T(8,128)(2,1)S(1)}, u32[]{:S(2)}, u32[]{:S(2)}) %collective-permute-start.2) | collective-permute-done | bytes 172064 | tf_op jit(solution)/shard_map/ppermute | solution.py:174
  14.8 0.7 %copy-done.3 = bf16[2,2,112,192]{3,2,1,0:T(8,128)(2,1)} copy-done((bf16[2,2,112,192]{3,2,1,0:T(8,128)(2,1)}, bf16[2,2,112,192]{3,2,1,0:T(8,128)(2,1)S(1)}, u32[]{:S(2)}) %copy-start.3) | copy-done | bytes 172056
  15.5 7.6 %shard_map.145 = (f32[1,224,192]{2,1,0:T(8,128)}, bf16[1,224,192]{2,1,0:T(8,128)(2,1)}, bf16[1,224,192]{2,1,0:T(8,128)(2,1)}) custom-call(bf16[2,224,192]{2,1,0:T(8,128)(2,1)} %pad_maximum_fusion.seq_ref, bf16[2,224,192]{2,1,0:T(8,128)(2,1)} %bitcast.68, bf16[2,224,192]{2,1,0:T(8,128)(2,1)} %bitcast.69, f32[1,192]{1,0:T(1,128)} %bitcast.76, ...), custom_call_target="tpu_custom_call" | custom-call | tf_op jit(solution)/shard_map/pallas_call | solution.py:129
  23.1 1.0 %copy.27 = bf16[1,2,112,192]{2,3,0,1:T(8,128)(2,1)S(1)} copy(bf16[1,2,112,192]{3,2,1,0:T(8,128)(2,1)} %bitcast.70) | data formatting | bytes 172032 | tf_op jit(solution)/shard_map/reshape | solution.py:193
  24.1 2.5 %collective-permute-start.3 = (bf16[1,224,192]{2,1,0:T(8,128)(2,1)}, bf16[1,224,192]{2,1,0:T(8,128)(2,1)S(1)}, u32[]{:S(2)}, u32[]{:S(2)}) collective-permute-start(bf16[1,224,192]{2,1,0:T(8,128)(2,1)} %get-tuple-element.9), channel_id=1, source_target_pairs={{0,2},{2,0},{1,3},{3,1},{4,6},{6,4},{5,7},{7,5},{8,10},{10,8},{9,1... | collective-permute-start | bytes 258056 | tf_op jit(solution)/shard_map/ppermute | solution.py:197
  26.6 15.1 %all_gather.3 = bf16[1,8,112,192]{2,3,0,1:T(8,128)(2,1)S(1)} all-gather(bf16[1,2,112,192]{2,3,0,1:T(8,128)(2,1)S(1)} %copy.27), channel_id=1, replica_groups=mesh['clips'=2,'outer'=4,'inner'=2,'tm'=2] {'outer'}, dimensions={1}, use_global_device_ids=true | all-gather | bytes 430080 | tf_op jit(solution)/shard_map/all_gather | solution.py:198
  41.7 0.3 copy.28
  42.0 0.3 reshape.118
  42.3 1.3 %fusion.27 = (f32[224]{0:T(256)S(1)}, f32[224,896]{1,0:T(8,128)S(1)}) fusion(bf16[896,192]{0,1:T(8,128)(2,1)S(1)} %reshape.118, bf16[1,224,192]{2,1,0:T(8,128)(2,1)} %get-tuple-element.9), kind=kOutput, calls=%fused_computation.36 | convolution fusion | flops 77270816 | bytes 1233792 | tf_op jit(solution)/shard_map/fqc,fkc->fqk/dot_general | solution.py:201
  43.6 0.0 copy-start.5
  43.6 0.0 copy-start.6
  43.6 0.3 fusion.4
  43.9 0.0 copy-start.4
  43.9 0.0 collective-permute-done.3
  43.9 0.4 fusion.28
  44.3 0.3 fusion.7
  44.6 0.1 collective-permute-start.4
  44.7 0.4 fusion.2
  45.1 2.1 %collective-permute-start.5 = (bf16[1,224,192]{1,2,0:T(8,128)(2,1)S(1)}, bf16[1,224,192]{1,2,0:T(8,128)(2,1)S(1)}, u32[]{:S(2)}, u32[]{:S(2)}) collective-permute-start(bf16[1,224,192]{1,2,0:T(8,128)(2,1)S(1)} %fusion.2), channel_id=1, source_target_pairs={{0,2},{2,0},{1,3},{3,1},{4,6},{6,4},{5,7},{7,5},{8,10},{10,8},{9,1... | collective-permute-start | bytes 258056 | tf_op jit(solution)/shard_map/ppermute | solution.py:211
  47.2 1.1 %collective-permute-done.4 = f32[1,224,2]{1,2,0:T(2,128)S(1)} collective-permute-done((f32[1,224,2]{1,2,0:T(2,128)S(1)}, f32[1,224,2]{1,2,0:T(2,128)S(1)}, u32[]{:S(2)}, u32[]{:S(2)}) %collective-permute-start.4) | collective-permute-done | bytes 1824 | tf_op jit(solution)/shard_map/ppermute | solution.py:211
  48.2 0.4 fusion
  48.7 1.1 %collective-permute-done.5 = bf16[1,224,192]{1,2,0:T(8,128)(2,1)S(1)} collective-permute-done((bf16[1,224,192]{1,2,0:T(8,128)(2,1)S(1)}, bf16[1,224,192]{1,2,0:T(8,128)(2,1)S(1)}, u32[]{:S(2)}, u32[]{:S(2)}) %collective-permute-start.5) | collective-permute-done | bytes 86048 | tf_op jit(solution)/shard_map/ppermute | solution.py:211
  49.8 0.0 copy-done
  49.8 0.5 fusion.3
  50.3 0.8 %copy.30 = f32[1,1,2,112,192]{3,4,2,1,0:T(8,128)} copy(f32[1,1,2,112,192]{4,3,2,1,0:T(8,128)S(1)} %bitcast.66) | data formatting | bytes 344064 | tf_op jit(solution)/shard_map/reshape | solution.py:231
  (14 shorter events, 0.1 us)
Async XLA Ops:
  0.0 49.8 %copy-start = (bf16[192,192]{1,0:T(8,128)(2,1)S(1)}, bf16[192,192]{1,0:T(8,128)(2,1)}, u32[]{:S(2)}) copy-start(bf16[192,192]{1,0:T(8,128)(2,1)} %param.28) | copy-start | bytes 221188
  1.0 1.5 %collective-permute-start = (bf16[1,2,112,192]{3,2,1,0:T(8,128)(2,1)S(1)}, bf16[1,2,112,192]{3,2,1,0:T(8,128)(2,1)S(1)}, u32[]{:S(2)}, u32[]{:S(2)}) collective-permute-start(bf16[1,2,112,192]{3,2,1,0:T(8,128)(2,1)S(1)} %bitcast.67), channel_id=1, source_target_pairs={{0,1},{1,0},{2,3},{3,2},{4,5},{5,4},{6,7},{7,6},{8,9},{9,8},{10,11... | collective-permute-start | bytes 258056 | tf_op jit(solution)/shard_map/ppermute | solution.py:165
  2.6 10.7 %collective-permute-start.1 = (bf16[2,2,112,192]{3,2,1,0:T(8,128)(2,1)S(1)}, bf16[2,2,112,192]{3,2,1,0:T(8,128)(2,1)S(1)}, u32[]{:S(2)}, u32[]{:S(2)}) collective-permute-start(bf16[2,2,112,192]{3,2,1,0:T(8,128)(2,1)S(1)} %maximum_bitcast_fusion), channel_id=1, source_target_pairs={{0,2},{2,4},{4,6},{6,8},{8,10},{10,12},{12,14},{3,1},{5,3},{7,5},{... | collective-permute-start | bytes 516104 | tf_op jit(solution)/shard_map/ppermute | solution.py:173
  13.3 1.5 %copy-start.2 = (bf16[2,2,112,192]{3,2,1,0:T(8,128)(2,1)}, bf16[2,2,112,192]{3,2,1,0:T(8,128)(2,1)S(1)}, u32[]{:S(2)}) copy-start(bf16[2,2,112,192]{3,2,1,0:T(8,128)(2,1)S(1)} %collective-permute-done.1) | copy-start | bytes 516100
  13.3 1.5 %collective-permute-start.2 = (bf16[2,2,112,192]{3,2,1,0:T(8,128)(2,1)S(1)}, bf16[2,2,112,192]{3,2,1,0:T(8,128)(2,1)S(1)}, u32[]{:S(2)}, u32[]{:S(2)}) collective-permute-start(bf16[2,2,112,192]{3,2,1,0:T(8,128)(2,1)S(1)} %collective-permute-done.1), channel_id=1, source_target_pairs={{0,1},{1,0},{2,3},{3,2},{4,5},{5,4},{6,7},{7,6},{8,9},{9,8},{10,11... | collective-permute-start | bytes 516104 | tf_op jit(solution)/shard_map/ppermute | solution.py:174
  14.8 0.7 %copy-start.3 = (bf16[2,2,112,192]{3,2,1,0:T(8,128)(2,1)}, bf16[2,2,112,192]{3,2,1,0:T(8,128)(2,1)S(1)}, u32[]{:S(2)}) copy-start(bf16[2,2,112,192]{3,2,1,0:T(8,128)(2,1)S(1)} %collective-permute-done.2) | copy-start | bytes 516100
  24.1 19.8 %collective-permute-start.3 = (bf16[1,224,192]{2,1,0:T(8,128)(2,1)}, bf16[1,224,192]{2,1,0:T(8,128)(2,1)S(1)}, u32[]{:S(2)}, u32[]{:S(2)}) collective-permute-start(bf16[1,224,192]{2,1,0:T(8,128)(2,1)} %get-tuple-element.9), channel_id=1, source_target_pairs={{0,2},{2,0},{1,3},{3,1},{4,6},{6,4},{5,7},{7,5},{8,10},{10,8},{9,1... | collective-permute-start | bytes 258056 | tf_op jit(solution)/shard_map/ppermute | solution.py:197
  43.6 6.2 %copy-start.5 = (bf16[192,192]{1,0:T(8,128)(2,1)S(1)}, bf16[192,192]{1,0:T(8,128)(2,1)}, u32[]{:S(2)}) copy-start(bf16[192,192]{1,0:T(8,128)(2,1)} %param.26) | copy-start | bytes 221188
  43.6 6.2 %copy-start.6 = (f32[192]{0:T(256)S(1)}, f32[192]{0:T(256)}, u32[]{:S(2)}) copy-start(f32[192]{0:T(256)} %param.27) | copy-start | bytes 2308
  43.9 6.4 %copy-start.1 = (f32[1,224,192]{2,1,0:T(8,128)S(1)}, f32[1,224,192]{2,1,0:T(8,128)}, u32[]{:S(2)}) copy-start(f32[1,224,192]{2,1,0:T(8,128)} %get-tuple-element.8) | copy-start | bytes 516100
  43.9 6.4 %copy-start.4 = (f32[192]{0:T(256)S(1)}, f32[192]{0:T(256)}, u32[]{:S(2)}) copy-start(f32[192]{0:T(256)} %param.29) | copy-start | bytes 2308
  44.6 3.7 %collective-permute-start.4 = (f32[1,224,2]{1,2,0:T(2,128)S(1)}, f32[1,224,2]{1,2,0:T(2,128)S(1)}, u32[]{:S(2)}, u32[]{:S(2)}) collective-permute-start(f32[1,224,2]{1,2,0:T(2,128)S(1)} %pad_maximum_fusion.1), channel_id=1, source_target_pairs={{0,2},{2,0},{1,3},{3,1},{4,6},{6,4},{5,7},{7,5},{8,10},{10,8},{9,1... | collective-permute-start | bytes 5384 | tf_op jit(solution)/shard_map/ppermute | solution.py:211
  45.1 4.7 %collective-permute-start.5 = (bf16[1,224,192]{1,2,0:T(8,128)(2,1)S(1)}, bf16[1,224,192]{1,2,0:T(8,128)(2,1)S(1)}, u32[]{:S(2)}, u32[]{:S(2)}) collective-permute-start(bf16[1,224,192]{1,2,0:T(8,128)(2,1)S(1)} %fusion.2), channel_id=1, source_target_pairs={{0,2},{2,0},{1,3},{3,1},{4,6},{6,4},{5,7},{7,5},{8,10},{10,8},{9,1... | collective-permute-start | bytes 258056 | tf_op jit(solution)/shard_map/ppermute | solution.py:211

commit v13 on v12

--- a/solution.py
+++ b/solution.py
@@ -208,9 +208,17 @@
         return accum, jnp.concatenate([top, total], axis=-1)
 
     back_accum, back_stats = partial(partner_queries)
-    returned_accum, returned_stats = lax.ppermute(
-        (back_accum.astype(jnp.bfloat16), back_stats), "inner", swap
-    )
+    parts = []
+    rest = back_stats
+    for _ in range(3):
+        head = lax.reduce_precision(rest, exponent_bits=8, mantissa_bits=7)
+        parts.append(head)
+        rest = rest - head
+    packed = jnp.concatenate([back_accum] + parts, axis=-1).astype(jnp.bfloat16)
+    returned = lax.ppermute(packed, "inner", swap).astype(jnp.float32)
+    returned_accum = returned[..., :channels]
+    pieces = [returned[..., channels + 2 * i : channels + 2 * i + 2] for i in range(3)]
+    returned_stats = pieces[0] + (pieces[1] + pieces[2])
     mine_accum, mine_stats = partial(folded)
     top_mine = mine_stats[..., :1]
     top_back = returned_stats[..., :1]
@@ -218,7 +226,7 @@
     scale_mine = jnp.exp(top_mine - highest)
     scale_back = jnp.exp(top_back - highest)
     total = mine_stats[..., 1:] * scale_mine + returned_stats[..., 1:] * scale_back
-    accum = mine_accum * scale_mine + returned_accum.astype(jnp.float32) * scale_back
+    accum = mine_accum * scale_mine + returned_accum * scale_back
     mixed = (accum / total).astype(jnp.bfloat16).reshape(-1, channels)
     value = (jnp.dot(mixed, w_value, preferred_element_type=jnp.float32) + b_value).astype(
         jnp.bfloat16

time: 51.3 us -> 51.5 us (level)
  waiting for transfers between devices: 9.8 us -> 12 us
  starting transfers between devices: 9.97 us -> 7.9 us
    ppermute x2 -> x1, waiting for transfers between devices: 2.16 us -> 4.36 us  [local(): returned = lax.ppermute(packed, 'inner', swap).astype(jnp.float32)]
    ppermute x2 -> x1, starting transfers between devices: 2.15 us -> 0.07 us  [local(): returned = lax.ppermute(packed, 'inner', swap).astype(jnp.float32)]
  transfers between devices with their start and end apart: 6 -> 5, of which waited for: 5 -> 4; matrix products, arithmetic and copies ran while one was open for 7% -> 6% of each run, Pallas kernels for 0% -> 0%
where the time goes in v13:
time: 51.5 us; the launch traced here: 51.3 us
  blocking collectives  15.1 us (29%)
  waiting for transfers between devices  12 us (23%)
  starting transfers between devices  7.9 us (15%)
  Pallas kernels  7.59 us (15%)
  local copies, waits for them, and re-layouts  4.12 us (8%)
  matrix products  2.93 us (6%)
  other arithmetic  1.51 us (3%)
    all_gather x1, blocking collectives, local(): keys = lax.all_gather(normed, 'outer', axis=1, tiled=True)  15.1 us
    pallas_call x1, Pallas kernels, resnet_block(): pl.pallas_call(functools.partial(block_kernel, cols, frame_count), out_sh...  7.59 us
    ppermute x1, waiting for transfers between devices, local(): arrived = lax.ppermute(edge, ('outer', 'inner', 'tm'), up + down)  5.97 us
    ppermute x1, starting transfers between devices, local(): arrived = lax.ppermute(edge, ('outer', 'inner', 'tm'), up + down)  4.76 us
    ppermute x1, waiting for transfers between devices, local(): returned = lax.ppermute(packed, 'inner', swap).astype(jnp.float32)  4.36 us
    ppermute x1, starting transfers between devices, local(): partner_queries = lax.ppermute(folded, 'inner', swap)  2.54 us
    unnamed x15, local copies, waits for them, and re-layouts  1.73 us
    dot_general x2, matrix products, partial(): jnp.einsum('fqc,fkc->fqk', queries, keys, preferred_element_type=jnp.floa...  1.62 us
  transfers between devices with their start and end apart: 5, of which 4 were waited for; matrix products, arithmetic and copies ran while one was open for 6% of the time, Pallas kernels for 0%

profile of v13, /device:TPU:0, one launch (start us, length us, event | category | flops | bytes accessed | tf_op | source)
XLA Modules:
  0.0 51.3 jit_solution(874440886012901942)
XLA Ops:
  0.0 1.0 %copy.23 = bf16[1,1,2,112,192]{4,3,2,1,0:T(8,128)(2,1)S(1)} copy(bf16[1,1,2,112,192]{3,4,2,1,0:T(8,128)(2,1)} %param.15) | data formatting | bytes 172032 | tf_op args[0]
  1.0 0.5 %collective-permute-start = (bf16[1,2,112,192]{3,2,1,0:T(8,128)(2,1)S(1)}, bf16[1,2,112,192]{3,2,1,0:T(8,128)(2,1)S(1)}, u32[]{:S(2)}, u32[]{:S(2)}) collective-permute-start(bf16[1,2,112,192]{3,2,1,0:T(8,128)(2,1)S(1)} %bitcast.73), channel_id=1, source_target_pairs={{0,1},{1,0},{2,3},{3,2},{4,5},{5,4},{6,7},{7,6},{8,9},{9,8},{10,11... | collective-permute-start | bytes 258056 | tf_op jit(solution)/shard_map/ppermute | solution.py:165
  1.6 1.0 %collective-permute-done = bf16[1,2,112,192]{3,2,1,0:T(8,128)(2,1)S(1)} collective-permute-done((bf16[1,2,112,192]{3,2,1,0:T(8,128)(2,1)S(1)}, bf16[1,2,112,192]{3,2,1,0:T(8,128)(2,1)S(1)}, u32[]{:S(2)}, u32[]{:S(2)}) %collective-permute-start) | collective-permute-done | bytes 86048 | tf_op jit(solution)/shard_map/ppermute | solution.py:165
  2.6 4.8 %collective-permute-start.1 = (bf16[2,2,112,192]{3,2,1,0:T(8,128)(2,1)S(1)}, bf16[2,2,112,192]{3,2,1,0:T(8,128)(2,1)S(1)}, u32[]{:S(2)}, u32[]{:S(2)}) collective-permute-start(bf16[2,2,112,192]{3,2,1,0:T(8,128)(2,1)S(1)} %maximum_bitcast_fusion), channel_id=1, source_target_pairs={{0,2},{2,4},{4,6},{6,8},{8,10},{10,12},{12,14},{3,1},{5,3},{7,5},{... | collective-permute-start | bytes 516104 | tf_op jit(solution)/shard_map/ppermute | solution.py:173
  7.4 6.0 %collective-permute-done.1 = bf16[2,2,112,192]{3,2,1,0:T(8,128)(2,1)S(1)} collective-permute-done((bf16[2,2,112,192]{3,2,1,0:T(8,128)(2,1)S(1)}, bf16[2,2,112,192]{3,2,1,0:T(8,128)(2,1)S(1)}, u32[]{:S(2)}, u32[]{:S(2)}) %collective-permute-start.1) | collective-permute-done | bytes 172064 | tf_op jit(solution)/shard_map/ppermute | solution.py:173
  13.3 0.0 collective-permute-start.2
  13.3 0.8 %pad_maximum_fusion.seq_ref = bf16[2,224,192]{2,1,0:T(8,128)(2,1)} fusion(bf16[1,224,192]{2,1,0:T(8,128)(2,1)S(1)} %bitcast.71, bf16[1,224,192]{2,1,0:T(8,128)(2,1)S(1)} %bitcast.69), kind=kLoop, calls=%fused_computation.15 | loop fusion | flops 86016 | bytes 344064 | tf_op jit(solution)/shard_map/stack | solution.py:168
  14.1 0.7 %collective-permute-done.2 = bf16[2,2,112,192]{3,2,1,0:T(8,128)(2,1)S(1)} collective-permute-done((bf16[2,2,112,192]{3,2,1,0:T(8,128)(2,1)S(1)}, bf16[2,2,112,192]{3,2,1,0:T(8,128)(2,1)S(1)}, u32[]{:S(2)}, u32[]{:S(2)}) %collective-permute-start.2) | collective-permute-done | bytes 172064 | tf_op jit(solution)/shard_map/ppermute | solution.py:174
  14.8 0.0 copy-done.2
  14.8 0.7 %copy-done.3 = bf16[2,2,112,192]{3,2,1,0:T(8,128)(2,1)} copy-done((bf16[2,2,112,192]{3,2,1,0:T(8,128)(2,1)}, bf16[2,2,112,192]{3,2,1,0:T(8,128)(2,1)S(1)}, u32[]{:S(2)}) %copy-start.3) | copy-done | bytes 172056
  15.5 7.6 %shard_map.145 = (f32[1,224,192]{2,1,0:T(8,128)}, bf16[1,224,192]{2,1,0:T(8,128)(2,1)}, bf16[1,224,192]{2,1,0:T(8,128)(2,1)}) custom-call(bf16[2,224,192]{2,1,0:T(8,128)(2,1)} %pad_maximum_fusion.seq_ref, bf16[2,224,192]{2,1,0:T(8,128)(2,1)} %bitcast.74, bf16[2,224,192]{2,1,0:T(8,128)(2,1)} %bitcast.75, f32[1,192]{1,0:T(1,128)} %bitcast.82, ...), custom_call_target="tpu_custom_call" | custom-call | tf_op jit(solution)/shard_map/pallas_call | solution.py:129
  23.1 1.0 %copy.24 = bf16[1,2,112,192]{2,3,0,1:T(8,128)(2,1)S(1)} copy(bf16[1,2,112,192]{3,2,1,0:T(8,128)(2,1)} %bitcast.76) | data formatting | bytes 172032 | tf_op jit(solution)/shard_map/reshape | solution.py:193
  24.1 2.5 %collective-permute-start.3 = (bf16[1,224,192]{2,1,0:T(8,128)(2,1)}, bf16[1,224,192]{2,1,0:T(8,128)(2,1)S(1)}, u32[]{:S(2)}, u32[]{:S(2)}) collective-permute-start(bf16[1,224,192]{2,1,0:T(8,128)(2,1)} %get-tuple-element.9), channel_id=1, source_target_pairs={{0,2},{2,0},{1,3},{3,1},{4,6},{6,4},{5,7},{7,5},{8,10},{10,8},{9,1... | collective-permute-start | bytes 258056 | tf_op jit(solution)/shard_map/ppermute | solution.py:197
  26.6 15.1 %all_gather.3 = bf16[1,8,112,192]{2,3,0,1:T(8,128)(2,1)S(1)} all-gather(bf16[1,2,112,192]{2,3,0,1:T(8,128)(2,1)S(1)} %copy.24), channel_id=1, replica_groups=mesh['clips'=2,'outer'=4,'inner'=2,'tm'=2] {'outer'}, dimensions={1}, use_global_device_ids=true | all-gather | bytes 430080 | tf_op jit(solution)/shard_map/all_gather | solution.py:198
  41.7 0.3 copy.25
  42.0 0.3 reshape.290
  42.3 1.3 %fusion.38 = (f32[224]{0:T(256)S(1)}, f32[224,896]{1,0:T(8,128)S(1)}) fusion(bf16[896,192]{0,1:T(8,128)(2,1)S(1)} %reshape.290, bf16[1,224,192]{2,1,0:T(8,128)(2,1)} %get-tuple-element.9), kind=kOutput, calls=%fused_computation.51 | convolution fusion | flops 77270816 | bytes 1233792 | tf_op jit(solution)/shard_map/fqc,fkc->fqk/dot_general | solution.py:201
  43.6 0.0 collective-permute-done.3
  43.6 0.4 fusion.39
  43.9 0.0 copy-start.5
  44.0 0.0 copy-start.6
  44.0 0.3 fusion.6
  44.2 0.0 copy-start.1
  44.3 0.0 copy-start.4
  44.3 0.4 fusion.2
  44.8 0.1 collective-permute-start.4
  44.8 0.3 fusion.4
  45.1 4.4 %collective-permute-done.4 = bf16[1,224,198]{1,2,0:T(8,128)(2,1)S(1)} collective-permute-done((bf16[1,224,198]{1,2,0:T(8,128)(2,1)S(1)}, bf16[1,224,198]{1,2,0:T(8,128)(2,1)S(1)}, u32[]{:S(2)}, u32[]{:S(2)}) %collective-permute-start.4) | collective-permute-done | bytes 88736 | tf_op jit(solution)/shard_map/ppermute | solution.py:218
  49.5 0.4 fusion
  50.0 0.5 fusion.3
  50.5 0.0 copy-done.1
  50.5 0.8 %copy.27 = f32[1,1,2,112,192]{3,4,2,1,0:T(8,128)} copy(f32[1,1,2,112,192]{4,3,2,1,0:T(8,128)S(1)} %bitcast.72) | data formatting | bytes 344064 | tf_op jit(solution)/shard_map/reshape | solution.py:239
  (15 shorter events, 0.2 us)
Async XLA Ops:
  0.0 50.0 %copy-start = (bf16[192,192]{1,0:T(8,128)(2,1)S(1)}, bf16[192,192]{1,0:T(8,128)(2,1)}, u32[]{:S(2)}) copy-start(bf16[192,192]{1,0:T(8,128)(2,1)} %param.28) | copy-start | bytes 221188
  1.0 1.5 %collective-permute-start = (bf16[1,2,112,192]{3,2,1,0:T(8,128)(2,1)S(1)}, bf16[1,2,112,192]{3,2,1,0:T(8,128)(2,1)S(1)}, u32[]{:S(2)}, u32[]{:S(2)}) collective-permute-start(bf16[1,2,112,192]{3,2,1,0:T(8,128)(2,1)S(1)} %bitcast.73), channel_id=1, source_target_pairs={{0,1},{1,0},{2,3},{3,2},{4,5},{5,4},{6,7},{7,6},{8,9},{9,8},{10,11... | collective-permute-start | bytes 258056 | tf_op jit(solution)/shard_map/ppermute | solution.py:165
  2.6 10.7 %collective-permute-start.1 = (bf16[2,2,112,192]{3,2,1,0:T(8,128)(2,1)S(1)}, bf16[2,2,112,192]{3,2,1,0:T(8,128)(2,1)S(1)}, u32[]{:S(2)}, u32[]{:S(2)}) collective-permute-start(bf16[2,2,112,192]{3,2,1,0:T(8,128)(2,1)S(1)} %maximum_bitcast_fusion), channel_id=1, source_target_pairs={{0,2},{2,4},{4,6},{6,8},{8,10},{10,12},{12,14},{3,1},{5,3},{7,5},{... | collective-permute-start | bytes 516104 | tf_op jit(solution)/shard_map/ppermute | solution.py:173
  13.3 1.5 %copy-start.2 = (bf16[2,2,112,192]{3,2,1,0:T(8,128)(2,1)}, bf16[2,2,112,192]{3,2,1,0:T(8,128)(2,1)S(1)}, u32[]{:S(2)}) copy-start(bf16[2,2,112,192]{3,2,1,0:T(8,128)(2,1)S(1)} %collective-permute-done.1) | copy-start | bytes 516100
  13.3 1.5 %collective-permute-start.2 = (bf16[2,2,112,192]{3,2,1,0:T(8,128)(2,1)S(1)}, bf16[2,2,112,192]{3,2,1,0:T(8,128)(2,1)S(1)}, u32[]{:S(2)}, u32[]{:S(2)}) collective-permute-start(bf16[2,2,112,192]{3,2,1,0:T(8,128)(2,1)S(1)} %collective-permute-done.1), channel_id=1, source_target_pairs={{0,1},{1,0},{2,3},{3,2},{4,5},{5,4},{6,7},{7,6},{8,9},{9,8},{10,11... | collective-permute-start | bytes 516104 | tf_op jit(solution)/shard_map/ppermute | solution.py:174
  14.8 0.7 %copy-start.3 = (bf16[2,2,112,192]{3,2,1,0:T(8,128)(2,1)}, bf16[2,2,112,192]{3,2,1,0:T(8,128)(2,1)S(1)}, u32[]{:S(2)}) copy-start(bf16[2,2,112,192]{3,2,1,0:T(8,128)(2,1)S(1)} %collective-permute-done.2) | copy-start | bytes 516100
  24.1 19.5 %collective-permute-start.3 = (bf16[1,224,192]{2,1,0:T(8,128)(2,1)}, bf16[1,224,192]{2,1,0:T(8,128)(2,1)S(1)}, u32[]{:S(2)}, u32[]{:S(2)}) collective-permute-start(bf16[1,224,192]{2,1,0:T(8,128)(2,1)} %get-tuple-element.9), channel_id=1, source_target_pairs={{0,2},{2,0},{1,3},{3,1},{4,6},{6,4},{5,7},{7,5},{8,10},{10,8},{9,1... | collective-permute-start | bytes 258056 | tf_op jit(solution)/shard_map/ppermute | solution.py:197
  43.9 6.0 %copy-start.5 = (bf16[192,192]{1,0:T(8,128)(2,1)S(1)}, bf16[192,192]{1,0:T(8,128)(2,1)}, u32[]{:S(2)}) copy-start(bf16[192,192]{1,0:T(8,128)(2,1)} %param.26) | copy-start | bytes 221188
  44.0 6.0 %copy-start.6 = (f32[192]{0:T(256)S(1)}, f32[192]{0:T(256)}, u32[]{:S(2)}) copy-start(f32[192]{0:T(256)} %param.27) | copy-start | bytes 2308
  44.2 6.2 %copy-start.1 = (f32[1,224,192]{2,1,0:T(8,128)S(1)}, f32[1,224,192]{2,1,0:T(8,128)}, u32[]{:S(2)}) copy-start(f32[1,224,192]{2,1,0:T(8,128)} %get-tuple-element.8) | copy-start | bytes 516100
  44.3 6.2 %copy-start.4 = (f32[192]{0:T(256)S(1)}, f32[192]{0:T(256)}, u32[]{:S(2)}) copy-start(f32[192]{0:T(256)} %param.29) | copy-start | bytes 2308
  44.8 4.7 %collective-permute-start.4 = (bf16[1,224,198]{1,2,0:T(8,128)(2,1)S(1)}, bf16[1,224,198]{1,2,0:T(8,128)(2,1)S(1)}, u32[]{:S(2)}, u32[]{:S(2)}) collective-permute-start(bf16[1,224,198]{1,2,0:T(8,128)(2,1)S(1)} %pad_maximum_fusion.1), channel_id=1, source_target_pairs={{0,2},{2,0},{1,3},{3,1},{4,6},{6,4},{5,7},{7,5},{8,10},{10,8},{9,1... | collective-permute-start | bytes 266120 | tf_op jit(solution)/shard_map/ppermute | solution.py:218

commit v14 on v12

--- a/solution.py
+++ b/solution.py
@@ -195,7 +195,15 @@
 
     swap = [(0, 1), (1, 0)]
     partner_queries = lax.ppermute(folded, "inner", swap)
-    keys = lax.all_gather(normed, "outer", axis=1, tiled=True)
+    spans = lax.axis_size("outer")
+    if spans <= 4:
+        shares = [normed] + [
+            lax.ppermute(normed, "outer", [(i, (i + k) % spans) for i in range(spans)])
+            for k in range(1, spans)
+        ]
+        keys = jnp.concatenate(shares, axis=1)
+    else:
+        keys = lax.all_gather(normed, "outer", axis=1, tiled=True)
     keys = keys.reshape(frame_count, -1, channels)
     def partial(queries):
         scores = jnp.einsum("fqc,fkc->fqk", queries, keys, preferred_element_type=jnp.float32)

time: 51.3 us -> 48.5 us (0.945)
  blocking collectives: 15.1 us -> 0 us
  waiting for transfers between devices: 9.8 us -> 19 us
  starting transfers between devices: 9.97 us -> 14.6 us
  local copies, waits for them, and re-layouts: 4.12 us -> 2.55 us
  other arithmetic: 1.46 us -> 2.43 us
  matrix products: 2.93 us -> 2.02 us
    all_gather x1 -> x0, blocking collectives: 15.1 us -> none  [local(): keys = lax.all_gather(normed, 'outer', axis=1, tiled=True)]
    ppermute x0 -> x3, waiting for transfers between devices: none -> 7.1 us  [local(): lax.ppermute(normed, 'outer', [(i, (i + k) % spans) for i in range(spans)])]
    ppermute x0 -> x3, starting transfers between devices: none -> 4.61 us  [local(): lax.ppermute(normed, 'outer', [(i, (i + k) % spans) for i in range(spans)])]
    ppermute x2, waiting for transfers between devices: 2.16 us -> 4.25 us  [local(): lax.ppermute((back_accum.astype(jnp.bfloat16), back_stats), 'inner', swap)]
    reshape x1 -> x0, local copies, waits for them, and re-layouts: 1.01 us -> none  [local(): normed = normed.reshape(frame_count, row_count, col_count, channels)]
    concatenate x0 -> x1, other arithmetic: none -> 1 us  [local(): keys = jnp.concatenate(shares, axis=1)]
    dot_general x2, matrix products: 1.62 us -> 0.85 us  [partial(): jnp.einsum('fqc,fkc->fqk', queries, keys, preferred_element_type=jnp.floa...]
    unnamed x15 -> x17, local copies, waits for them, and re-layouts: 1.73 us -> 1.74 us
  transfers between devices with their start and end apart: 6 -> 9, of which waited for: 5 -> 6; matrix products, arithmetic and copies ran while one was open for 7% -> 4% of each run, Pallas kernels for 0% -> 0%
where the time goes in v14:
time: 48.5 us; the launch traced here: 48.3 us
  waiting for transfers between devices  19 us (39%)
  starting transfers between devices  14.6 us (30%)
  Pallas kernels  7.58 us (16%)
  local copies, waits for them, and re-layouts  2.55 us (5%)
  other arithmetic  2.43 us (5%)
  matrix products  2.02 us (4%)
    pallas_call x1, Pallas kernels, resnet_block(): pl.pallas_call(functools.partial(block_kernel, cols, frame_count), out_sh...  7.58 us
    ppermute x3, waiting for transfers between devices, local(): lax.ppermute(normed, 'outer', [(i, (i + k) % spans) for i in range(spans)])  7.1 us
    ppermute x1, waiting for transfers between devices, local(): arrived = lax.ppermute(edge, ('outer', 'inner', 'tm'), up + down)  5.97 us
    ppermute x1, starting transfers between devices, local(): arrived = lax.ppermute(edge, ('outer', 'inner', 'tm'), up + down)  4.76 us
    ppermute x3, starting transfers between devices, local(): lax.ppermute(normed, 'outer', [(i, (i + k) % spans) for i in range(spans)])  4.61 us
    ppermute x2, waiting for transfers between devices, local(): lax.ppermute((back_accum.astype(jnp.bfloat16), back_stats), 'inner', swap)  4.25 us
    ppermute x1, starting transfers between devices, local(): partner_queries = lax.ppermute(folded, 'inner', swap)  2.48 us
    ppermute x2, starting transfers between devices, local(): lax.ppermute((back_accum.astype(jnp.bfloat16), back_stats), 'inner', swap)  2.22 us
  transfers between devices with their start and end apart: 9, of which 6 were waited for; matrix products, arithmetic and copies ran while one was open for 4% of the time, Pallas kernels for 0%

profile of v14, /device:TPU:0, one launch (start us, length us, event | category | flops | bytes accessed | tf_op | source)
XLA Modules:
  0.0 48.3 jit_solution(11498387571297531958)
XLA Ops:
  0.0 1.0 %copy.19 = bf16[1,1,2,112,192]{4,3,2,1,0:T(8,128)(2,1)S(1)} copy(bf16[1,1,2,112,192]{3,4,2,1,0:T(8,128)(2,1)} %param.15) | data formatting | bytes 172032 | tf_op args[0]
  1.0 0.5 %collective-permute-start = (bf16[1,2,112,192]{3,2,1,0:T(8,128)(2,1)S(1)}, bf16[1,2,112,192]{3,2,1,0:T(8,128)(2,1)S(1)}, u32[]{:S(2)}, u32[]{:S(2)}) collective-permute-start(bf16[1,2,112,192]{3,2,1,0:T(8,128)(2,1)S(1)} %bitcast.75), channel_id=1, source_target_pairs={{0,1},{1,0},{2,3},{3,2},{4,5},{5,4},{6,7},{7,6},{8,9},{9,8},{10,11... | collective-permute-start | bytes 258056 | tf_op jit(solution)/shard_map/ppermute | solution.py:165
  1.6 1.0 %collective-permute-done = bf16[1,2,112,192]{3,2,1,0:T(8,128)(2,1)S(1)} collective-permute-done((bf16[1,2,112,192]{3,2,1,0:T(8,128)(2,1)S(1)}, bf16[1,2,112,192]{3,2,1,0:T(8,128)(2,1)S(1)}, u32[]{:S(2)}, u32[]{:S(2)}) %collective-permute-start) | collective-permute-done | bytes 86048 | tf_op jit(solution)/shard_map/ppermute | solution.py:165
  2.6 4.8 %collective-permute-start.1 = (bf16[2,2,112,192]{3,2,1,0:T(8,128)(2,1)S(1)}, bf16[2,2,112,192]{3,2,1,0:T(8,128)(2,1)S(1)}, u32[]{:S(2)}, u32[]{:S(2)}) collective-permute-start(bf16[2,2,112,192]{3,2,1,0:T(8,128)(2,1)S(1)} %maximum_bitcast_fusion), channel_id=1, source_target_pairs={{0,2},{2,4},{4,6},{6,8},{8,10},{10,12},{12,14},{3,1},{5,3},{7,5},{... | collective-permute-start | bytes 516104 | tf_op jit(solution)/shard_map/ppermute | solution.py:173
  7.4 6.0 %collective-permute-done.1 = bf16[2,2,112,192]{3,2,1,0:T(8,128)(2,1)S(1)} collective-permute-done((bf16[2,2,112,192]{3,2,1,0:T(8,128)(2,1)S(1)}, bf16[2,2,112,192]{3,2,1,0:T(8,128)(2,1)S(1)}, u32[]{:S(2)}, u32[]{:S(2)}) %collective-permute-start.1) | collective-permute-done | bytes 172064 | tf_op jit(solution)/shard_map/ppermute | solution.py:173
  13.3 0.0 collective-permute-start.2
  13.3 0.8 %pad_maximum_fusion.1.seq_ref = bf16[2,224,192]{2,1,0:T(8,128)(2,1)} fusion(bf16[1,224,192]{2,1,0:T(8,128)(2,1)S(1)} %bitcast.73, bf16[1,224,192]{2,1,0:T(8,128)(2,1)S(1)} %bitcast.71), kind=kLoop, calls=%fused_computation.20 | loop fusion | flops 86016 | bytes 344064 | tf_op jit(solution)/shard_map/stack | solution.py:168
  14.1 0.7 %collective-permute-done.2 = bf16[2,2,112,192]{3,2,1,0:T(8,128)(2,1)S(1)} collective-permute-done((bf16[2,2,112,192]{3,2,1,0:T(8,128)(2,1)S(1)}, bf16[2,2,112,192]{3,2,1,0:T(8,128)(2,1)S(1)}, u32[]{:S(2)}, u32[]{:S(2)}) %collective-permute-start.2) | collective-permute-done | bytes 172064 | tf_op jit(solution)/shard_map/ppermute | solution.py:174
  14.8 0.7 %copy-done.3 = bf16[2,2,112,192]{3,2,1,0:T(8,128)(2,1)} copy-done((bf16[2,2,112,192]{3,2,1,0:T(8,128)(2,1)}, bf16[2,2,112,192]{3,2,1,0:T(8,128)(2,1)S(1)}, u32[]{:S(2)}) %copy-start.3) | copy-done | bytes 172056
  15.5 7.6 %shard_map.145 = (f32[1,224,192]{2,1,0:T(8,128)}, bf16[1,224,192]{2,1,0:T(8,128)(2,1)}, bf16[1,224,192]{2,1,0:T(8,128)(2,1)}) custom-call(bf16[2,224,192]{2,1,0:T(8,128)(2,1)} %pad_maximum_fusion.1.seq_ref, bf16[2,224,192]{2,1,0:T(8,128)(2,1)} %bitcast.76, bf16[2,224,192]{2,1,0:T(8,128)(2,1)} %bitcast.77, f32[1,192]{1,0:T(1,128)} %bitcast.86, ...), custom_call_target="tpu_custom_call" | custom-call | tf_op jit(solution)/shard_map/pallas_call | solution.py:129
  23.1 3.2 %collective-permute-start.5 = (bf16[1,2,112,192]{3,2,1,0:T(8,128)(2,1)}, bf16[1,2,112,192]{3,2,1,0:T(8,128)(2,1)S(1)}, u32[]{:S(2)}, u32[]{:S(2)}) collective-permute-start(bf16[1,2,112,192]{3,2,1,0:T(8,128)(2,1)} %bitcast.78), channel_id=1, source_target_pairs={{0,12},{4,0},{8,4},{12,8},{1,13},{5,1},{9,5},{13,9},{2,14},{6,2},{... | collective-permute-start | bytes 258056 | tf_op jit(solution)/shard_map/ppermute | solution.py:201
  26.3 1.4 %collective-permute-start.3 = (bf16[1,2,112,192]{3,2,1,0:T(8,128)(2,1)}, bf16[1,2,112,192]{3,2,1,0:T(8,128)(2,1)S(1)}, u32[]{:S(2)}, u32[]{:S(2)}) collective-permute-start(bf16[1,2,112,192]{3,2,1,0:T(8,128)(2,1)} %bitcast.80), channel_id=1, source_target_pairs={{0,4},{4,8},{8,12},{12,0},{1,5},{5,9},{9,13},{13,1},{2,6},{6,10},{... | collective-permute-start | bytes 258056 | tf_op jit(solution)/shard_map/ppermute | solution.py:201
  27.7 2.5 %collective-permute-start.6 = (bf16[1,224,192]{2,1,0:T(8,128)(2,1)}, bf16[1,224,192]{2,1,0:T(8,128)(2,1)S(1)}, u32[]{:S(2)}, u32[]{:S(2)}) collective-permute-start(bf16[1,224,192]{2,1,0:T(8,128)(2,1)} %get-tuple-element.9), channel_id=1, source_target_pairs={{0,2},{2,0},{1,3},{3,1},{4,6},{6,4},{5,7},{7,5},{8,10},{10,8},{9,1... | collective-permute-start | bytes 258056 | tf_op jit(solution)/shard_map/ppermute | solution.py:197
  30.2 0.0 collective-permute-done.5
  30.2 7.1 %collective-permute-done.4 = bf16[1,2,112,192]{3,2,1,0:T(8,128)(2,1)S(1)} collective-permute-done((bf16[1,2,112,192]{3,2,1,0:T(8,128)(2,1)}, bf16[1,2,112,192]{3,2,1,0:T(8,128)(2,1)S(1)}, u32[]{:S(2)}, u32[]{:S(2)}) %collective-permute-start.4) | collective-permute-done | bytes 86048 | tf_op jit(solution)/shard_map/ppermute | solution.py:201
  37.3 1.0 %pad_maximum_fusion = bf16[1,8,112,192]{3,2,1,0:T(8,128)(2,1)S(1)} fusion(bf16[1,2,112,192]{3,2,1,0:T(8,128)(2,1)S(1)} %collective-permute-done.5, bf16[1,2,112,192]{3,2,1,0:T(8,128)(2,1)S(1)} %collective-permute-done.4, bf16[1,2,112,192]{3,2,1,0:T(8,128)(2,1)S(1)} %collective-permute-done.3, bf16[1,2,112,192]{3,2,1,0:T(8,128)(2,1)} %bitcast.81), kind=kLoop, calls=%fused_computation.17 | loop fusion | flops 516096 | bytes 688128 | tf_op jit(solution)/shard_map/concatenate | solution.py:204
  38.3 0.0 collective-permute-done.6
  38.3 0.4 fusion.28
  38.7 0.3 fusion.11
  39.0 0.0 copy-start.5
  39.0 0.0 copy-start.6
  39.0 0.0 copy-start.7
  39.0 0.4 fusion.7
  39.5 0.4 fusion.27
  39.9 2.1 %collective-permute-start.7 = (f32[1,224,2]{1,2,0:T(2,128)S(1)}, f32[1,224,2]{1,2,0:T(2,128)S(1)}, u32[]{:S(2)}, u32[]{:S(2)}) collective-permute-start(f32[1,224,2]{1,2,0:T(2,128)S(1)} %pad_maximum_fusion.2), channel_id=1, source_target_pairs={{0,2},{2,0},{1,3},{3,1},{4,6},{6,4},{5,7},{7,5},{8,10},{10,8},{9,1... | collective-permute-start | bytes 5384 | tf_op jit(solution)/shard_map/ppermute | solution.py:219
  42.1 0.1 collective-permute-start.8
  42.1 0.3 fusion.8
  42.4 1.2 %collective-permute-done.7 = f32[1,224,2]{1,2,0:T(2,128)S(1)} collective-permute-done((f32[1,224,2]{1,2,0:T(2,128)S(1)}, f32[1,224,2]{1,2,0:T(2,128)S(1)}, u32[]{:S(2)}, u32[]{:S(2)}) %collective-permute-start.7) | collective-permute-done | bytes 1824 | tf_op jit(solution)/shard_map/ppermute | solution.py:219
  43.6 3.0 %collective-permute-done.8 = bf16[1,224,192]{1,2,0:T(8,128)(2,1)S(1)} collective-permute-done((bf16[1,224,192]{1,2,0:T(8,128)(2,1)S(1)}, bf16[1,224,192]{1,2,0:T(8,128)(2,1)S(1)}, u32[]{:S(2)}, u32[]{:S(2)}) %collective-permute-start.8) | collective-permute-done | bytes 86048 | tf_op jit(solution)/shard_map/ppermute | solution.py:219
  46.7 0.4 fusion.6
  47.1 0.3 fusion.5
  47.5 0.8 %copy.21 = f32[1,1,2,112,192]{3,4,2,1,0:T(8,128)} copy(f32[1,1,2,112,192]{4,3,2,1,0:T(8,128)S(1)} %bitcast.74) | data formatting | bytes 344064 | tf_op jit(solution)/shard_map/reshape | solution.py:239
  (19 shorter events, 0.1 us)
Async XLA Ops:
  0.0 47.1 %copy-start = (bf16[192,192]{1,0:T(8,128)(2,1)S(1)}, bf16[192,192]{1,0:T(8,128)(2,1)}, u32[]{:S(2)}) copy-start(bf16[192,192]{1,0:T(8,128)(2,1)} %param.28) | copy-start | bytes 221188
  1.0 1.5 %collective-permute-start = (bf16[1,2,112,192]{3,2,1,0:T(8,128)(2,1)S(1)}, bf16[1,2,112,192]{3,2,1,0:T(8,128)(2,1)S(1)}, u32[]{:S(2)}, u32[]{:S(2)}) collective-permute-start(bf16[1,2,112,192]{3,2,1,0:T(8,128)(2,1)S(1)} %bitcast.75), channel_id=1, source_target_pairs={{0,1},{1,0},{2,3},{3,2},{4,5},{5,4},{6,7},{7,6},{8,9},{9,8},{10,11... | collective-permute-start | bytes 258056 | tf_op jit(solution)/shard_map/ppermute | solution.py:165
  2.6 10.7 %collective-permute-start.1 = (bf16[2,2,112,192]{3,2,1,0:T(8,128)(2,1)S(1)}, bf16[2,2,112,192]{3,2,1,0:T(8,128)(2,1)S(1)}, u32[]{:S(2)}, u32[]{:S(2)}) collective-permute-start(bf16[2,2,112,192]{3,2,1,0:T(8,128)(2,1)S(1)} %maximum_bitcast_fusion), channel_id=1, source_target_pairs={{0,2},{2,4},{4,6},{6,8},{8,10},{10,12},{12,14},{3,1},{5,3},{7,5},{... | collective-permute-start | bytes 516104 | tf_op jit(solution)/shard_map/ppermute | solution.py:173
  13.3 1.5 %copy-start.2 = (bf16[2,2,112,192]{3,2,1,0:T(8,128)(2,1)}, bf16[2,2,112,192]{3,2,1,0:T(8,128)(2,1)S(1)}, u32[]{:S(2)}) copy-start(bf16[2,2,112,192]{3,2,1,0:T(8,128)(2,1)S(1)} %collective-permute-done.1) | copy-start | bytes 516100
  13.3 1.5 %collective-permute-start.2 = (bf16[2,2,112,192]{3,2,1,0:T(8,128)(2,1)S(1)}, bf16[2,2,112,192]{3,2,1,0:T(8,128)(2,1)S(1)}, u32[]{:S(2)}, u32[]{:S(2)}) collective-permute-start(bf16[2,2,112,192]{3,2,1,0:T(8,128)(2,1)S(1)} %collective-permute-done.1), channel_id=1, source_target_pairs={{0,1},{1,0},{2,3},{3,2},{4,5},{5,4},{6,7},{7,6},{8,9},{9,8},{10,11... | collective-permute-start | bytes 516104 | tf_op jit(solution)/shard_map/ppermute | solution.py:174
  14.8 0.7 %copy-start.3 = (bf16[2,2,112,192]{3,2,1,0:T(8,128)(2,1)}, bf16[2,2,112,192]{3,2,1,0:T(8,128)(2,1)S(1)}, u32[]{:S(2)}) copy-start(bf16[2,2,112,192]{3,2,1,0:T(8,128)(2,1)S(1)} %collective-permute-done.2) | copy-start | bytes 516100
  23.1 16.4 %copy-start.4 = (bf16[1,224,192]{2,1,0:T(8,128)(2,1)S(1)}, bf16[1,224,192]{2,1,0:T(8,128)(2,1)}, u32[]{:S(2)}) copy-start(bf16[1,224,192]{2,1,0:T(8,128)(2,1)} %get-tuple-element.9) | copy-start | bytes 258052
  23.1 7.1 %collective-permute-start.5 = (bf16[1,2,112,192]{3,2,1,0:T(8,128)(2,1)}, bf16[1,2,112,192]{3,2,1,0:T(8,128)(2,1)S(1)}, u32[]{:S(2)}, u32[]{:S(2)}) collective-permute-start(bf16[1,2,112,192]{3,2,1,0:T(8,128)(2,1)} %bitcast.78), channel_id=1, source_target_pairs={{0,12},{4,0},{8,4},{12,8},{1,13},{5,1},{9,5},{13,9},{2,14},{6,2},{... | collective-permute-start | bytes 258056 | tf_op jit(solution)/shard_map/ppermute | solution.py:201
  26.3 11.0 %collective-permute-start.4 = (bf16[1,2,112,192]{3,2,1,0:T(8,128)(2,1)}, bf16[1,2,112,192]{3,2,1,0:T(8,128)(2,1)S(1)}, u32[]{:S(2)}, u32[]{:S(2)}) collective-permute-start(bf16[1,2,112,192]{3,2,1,0:T(8,128)(2,1)} %bitcast.79), channel_id=1, source_target_pairs={{0,8},{4,12},{8,0},{12,4},{1,9},{5,13},{9,1},{13,5},{2,10},{6,14},... | collective-permute-start | bytes 258056 | tf_op jit(solution)/shard_map/ppermute | solution.py:201
  26.3 11.0 %collective-permute-start.3 = (bf16[1,2,112,192]{3,2,1,0:T(8,128)(2,1)}, bf16[1,2,112,192]{3,2,1,0:T(8,128)(2,1)S(1)}, u32[]{:S(2)}, u32[]{:S(2)}) collective-permute-start(bf16[1,2,112,192]{3,2,1,0:T(8,128)(2,1)} %bitcast.80), channel_id=1, source_target_pairs={{0,4},{4,8},{8,12},{12,0},{1,5},{5,9},{9,13},{13,1},{2,6},{6,10},{... | collective-permute-start | bytes 258056 | tf_op jit(solution)/shard_map/ppermute | solution.py:201
  27.7 10.6 %collective-permute-start.6 = (bf16[1,224,192]{2,1,0:T(8,128)(2,1)}, bf16[1,224,192]{2,1,0:T(8,128)(2,1)S(1)}, u32[]{:S(2)}, u32[]{:S(2)}) collective-permute-start(bf16[1,224,192]{2,1,0:T(8,128)(2,1)} %get-tuple-element.9), channel_id=1, source_target_pairs={{0,2},{2,0},{1,3},{3,1},{4,6},{6,4},{5,7},{7,5},{8,10},{10,8},{9,1... | collective-permute-start | bytes 258056 | tf_op jit(solution)/shard_map/ppermute | solution.py:197
  39.0 8.1 %copy-start.5 = (bf16[192,192]{1,0:T(8,128)(2,1)S(1)}, bf16[192,192]{1,0:T(8,128)(2,1)}, u32[]{:S(2)}) copy-start(bf16[192,192]{1,0:T(8,128)(2,1)} %param.26) | copy-start | bytes 221188
  39.0 8.1 %copy-start.6 = (f32[192]{0:T(256)S(1)}, f32[192]{0:T(256)}, u32[]{:S(2)}) copy-start(f32[192]{0:T(256)} %param.27) | copy-start | bytes 2308
  39.0 8.5 %copy-start.1 = (f32[1,224,192]{2,1,0:T(8,128)S(1)}, f32[1,224,192]{2,1,0:T(8,128)}, u32[]{:S(2)}) copy-start(f32[1,224,192]{2,1,0:T(8,128)} %get-tuple-element.8) | copy-start | bytes 516100
  39.0 8.5 %copy-start.7 = (f32[192]{0:T(256)S(1)}, f32[192]{0:T(256)}, u32[]{:S(2)}) copy-start(f32[192]{0:T(256)} %param.29) | copy-start | bytes 2308
  39.9 3.7 %collective-permute-start.7 = (f32[1,224,2]{1,2,0:T(2,128)S(1)}, f32[1,224,2]{1,2,0:T(2,128)S(1)}, u32[]{:S(2)}, u32[]{:S(2)}) collective-permute-start(f32[1,224,2]{1,2,0:T(2,128)S(1)} %pad_maximum_fusion.2), channel_id=1, source_target_pairs={{0,2},{2,0},{1,3},{3,1},{4,6},{6,4},{5,7},{7,5},{8,10},{10,8},{9,1... | collective-permute-start | bytes 5384 | tf_op jit(solution)/shard_map/ppermute | solution.py:219
  42.1 4.6 %collective-permute-start.8 = (bf16[1,224,192]{1,2,0:T(8,128)(2,1)S(1)}, bf16[1,224,192]{1,2,0:T(8,128)(2,1)S(1)}, u32[]{:S(2)}, u32[]{:S(2)}) collective-permute-start(bf16[1,224,192]{1,2,0:T(8,128)(2,1)S(1)} %fusion.7), channel_id=1, source_target_pairs={{0,2},{2,0},{1,3},{3,1},{4,6},{6,4},{5,7},{7,5},{8,10},{10,8},{9,1... | collective-permute-start | bytes 258056 | tf_op jit(solution)/shard_map/ppermute | solution.py:219

commit v15 on v13

--- a/solution.py
+++ b/solution.py
@@ -195,7 +195,15 @@
 
     swap = [(0, 1), (1, 0)]
     partner_queries = lax.ppermute(folded, "inner", swap)
-    keys = lax.all_gather(normed, "outer", axis=1, tiled=True)
+    spans = lax.axis_size("outer")
+    if spans <= 4:
+        shares = [normed] + [
+            lax.ppermute(normed, "outer", [(i, (i + k) % spans) for i in range(spans)])
+            for k in range(1, spans)
+        ]
+        keys = jnp.concatenate(shares, axis=1)
+    else:
+        keys = lax.all_gather(normed, "outer", axis=1, tiled=True)
     keys = keys.reshape(frame_count, -1, channels)
     def partial(queries):
         scores = jnp.einsum("fqc,fkc->fqk", queries, keys, preferred_element_type=jnp.float32)

time: 51.5 us -> 46.6 us (0.905)
  blocking collectives: 15.1 us -> 0 us
  starting transfers between devices: 7.9 us -> 14.5 us
  waiting for transfers between devices: 12 us -> 17.1 us
  local copies, waits for them, and re-layouts: 4.12 us -> 2.55 us
  other arithmetic: 1.51 us -> 2.49 us
  matrix products: 2.93 us -> 2.02 us
    all_gather x1 -> x0, blocking collectives: 15.1 us -> none  [local(): keys = lax.all_gather(normed, 'outer', axis=1, tiled=True)]
    ppermute x0 -> x3, waiting for transfers between devices: none -> 7.1 us  [local(): lax.ppermute(normed, 'outer', [(i, (i + k) % spans) for i in range(spans)])]
    ppermute x0 -> x3, starting transfers between devices: none -> 4.61 us  [local(): lax.ppermute(normed, 'outer', [(i, (i + k) % spans) for i in range(spans)])]
    ppermute x1, starting transfers between devices: 0.07 us -> 2.14 us  [local(): returned = lax.ppermute(packed, 'inner', swap).astype(jnp.float32)]
    ppermute x1, waiting for transfers between devices: 4.36 us -> 2.36 us  [local(): returned = lax.ppermute(packed, 'inner', swap).astype(jnp.float32)]
    reshape x1 -> x0, local copies, waits for them, and re-layouts: 1.01 us -> none  [local(): normed = normed.reshape(frame_count, row_count, col_count, channels)]
    concatenate x0 -> x1, other arithmetic: none -> 1 us  [local(): keys = jnp.concatenate(shares, axis=1)]
    dot_general x2, matrix products: 1.62 us -> 0.85 us  [partial(): jnp.einsum('fqc,fkc->fqk', queries, keys, preferred_element_type=jnp.floa...]
  transfers between devices with their start and end apart: 5 -> 8, of which waited for: 4 -> 5; matrix products, arithmetic and copies ran while one was open for 6% -> 4% of each run, Pallas kernels for 0% -> 0%
where the time goes in v15:
time: 46.6 us; the launch traced here: 46.5 us
  waiting for transfers between devices  17.1 us (37%)
  starting transfers between devices  14.5 us (31%)
  Pallas kernels  7.58 us (16%)
  local copies, waits for them, and re-layouts  2.55 us (5%)
  other arithmetic  2.49 us (5%)
  matrix products  2.02 us (4%)
    pallas_call x1, Pallas kernels, resnet_block(): pl.pallas_call(functools.partial(block_kernel, cols, frame_count), out_sh...  7.58 us
    ppermute x3, waiting for transfers between devices, local(): lax.ppermute(normed, 'outer', [(i, (i + k) % spans) for i in range(spans)])  7.1 us
    ppermute x1, waiting for transfers between devices, local(): arrived = lax.ppermute(edge, ('outer', 'inner', 'tm'), up + down)  5.97 us
    ppermute x1, starting transfers between devices, local(): arrived = lax.ppermute(edge, ('outer', 'inner', 'tm'), up + down)  4.76 us
    ppermute x3, starting transfers between devices, local(): lax.ppermute(normed, 'outer', [(i, (i + k) % spans) for i in range(spans)])  4.61 us
    ppermute x1, starting transfers between devices, local(): partner_queries = lax.ppermute(folded, 'inner', swap)  2.48 us
    ppermute x1, waiting for transfers between devices, local(): returned = lax.ppermute(packed, 'inner', swap).astype(jnp.float32)  2.36 us
    ppermute x1, starting transfers between devices, local(): returned = lax.ppermute(packed, 'inner', swap).astype(jnp.float32)  2.14 us
  transfers between devices with their start and end apart: 8, of which 5 were waited for; matrix products, arithmetic and copies ran while one was open for 4% of the time, Pallas kernels for 0%

profile of v15, /device:TPU:0, one launch (start us, length us, event | category | flops | bytes accessed | tf_op | source)
XLA Modules:
  0.0 46.5 jit_solution(5458368690310862666)
XLA Ops:
  0.0 1.0 %copy.16 = bf16[1,1,2,112,192]{4,3,2,1,0:T(8,128)(2,1)S(1)} copy(bf16[1,1,2,112,192]{3,4,2,1,0:T(8,128)(2,1)} %param.15) | data formatting | bytes 172032 | tf_op args[0]
  1.0 0.5 %collective-permute-start = (bf16[1,2,112,192]{3,2,1,0:T(8,128)(2,1)S(1)}, bf16[1,2,112,192]{3,2,1,0:T(8,128)(2,1)S(1)}, u32[]{:S(2)}, u32[]{:S(2)}) collective-permute-start(bf16[1,2,112,192]{3,2,1,0:T(8,128)(2,1)S(1)} %bitcast.81), channel_id=1, source_target_pairs={{0,1},{1,0},{2,3},{3,2},{4,5},{5,4},{6,7},{7,6},{8,9},{9,8},{10,11... | collective-permute-start | bytes 258056 | tf_op jit(solution)/shard_map/ppermute | solution.py:165
  1.6 1.0 %collective-permute-done = bf16[1,2,112,192]{3,2,1,0:T(8,128)(2,1)S(1)} collective-permute-done((bf16[1,2,112,192]{3,2,1,0:T(8,128)(2,1)S(1)}, bf16[1,2,112,192]{3,2,1,0:T(8,128)(2,1)S(1)}, u32[]{:S(2)}, u32[]{:S(2)}) %collective-permute-start) | collective-permute-done | bytes 86048 | tf_op jit(solution)/shard_map/ppermute | solution.py:165
  2.6 4.8 %collective-permute-start.1 = (bf16[2,2,112,192]{3,2,1,0:T(8,128)(2,1)S(1)}, bf16[2,2,112,192]{3,2,1,0:T(8,128)(2,1)S(1)}, u32[]{:S(2)}, u32[]{:S(2)}) collective-permute-start(bf16[2,2,112,192]{3,2,1,0:T(8,128)(2,1)S(1)} %maximum_bitcast_fusion), channel_id=1, source_target_pairs={{0,2},{2,4},{4,6},{6,8},{8,10},{10,12},{12,14},{3,1},{5,3},{7,5},{... | collective-permute-start | bytes 516104 | tf_op jit(solution)/shard_map/ppermute | solution.py:173
  7.4 6.0 %collective-permute-done.1 = bf16[2,2,112,192]{3,2,1,0:T(8,128)(2,1)S(1)} collective-permute-done((bf16[2,2,112,192]{3,2,1,0:T(8,128)(2,1)S(1)}, bf16[2,2,112,192]{3,2,1,0:T(8,128)(2,1)S(1)}, u32[]{:S(2)}, u32[]{:S(2)}) %collective-permute-start.1) | collective-permute-done | bytes 172064 | tf_op jit(solution)/shard_map/ppermute | solution.py:173
  13.3 0.0 collective-permute-start.2
  13.3 0.8 %pad_maximum_fusion.1.seq_ref = bf16[2,224,192]{2,1,0:T(8,128)(2,1)} fusion(bf16[1,224,192]{2,1,0:T(8,128)(2,1)S(1)} %bitcast.79, bf16[1,224,192]{2,1,0:T(8,128)(2,1)S(1)} %bitcast.77), kind=kLoop, calls=%fused_computation.20 | loop fusion | flops 86016 | bytes 344064 | tf_op jit(solution)/shard_map/stack | solution.py:168
  14.1 0.7 %collective-permute-done.2 = bf16[2,2,112,192]{3,2,1,0:T(8,128)(2,1)S(1)} collective-permute-done((bf16[2,2,112,192]{3,2,1,0:T(8,128)(2,1)S(1)}, bf16[2,2,112,192]{3,2,1,0:T(8,128)(2,1)S(1)}, u32[]{:S(2)}, u32[]{:S(2)}) %collective-permute-start.2) | collective-permute-done | bytes 172064 | tf_op jit(solution)/shard_map/ppermute | solution.py:174
  14.8 0.7 %copy-done.3 = bf16[2,2,112,192]{3,2,1,0:T(8,128)(2,1)} copy-done((bf16[2,2,112,192]{3,2,1,0:T(8,128)(2,1)}, bf16[2,2,112,192]{3,2,1,0:T(8,128)(2,1)S(1)}, u32[]{:S(2)}) %copy-start.3) | copy-done | bytes 172056
  15.5 7.6 %shard_map.145 = (f32[1,224,192]{2,1,0:T(8,128)}, bf16[1,224,192]{2,1,0:T(8,128)(2,1)}, bf16[1,224,192]{2,1,0:T(8,128)(2,1)}) custom-call(bf16[2,224,192]{2,1,0:T(8,128)(2,1)} %pad_maximum_fusion.1.seq_ref, bf16[2,224,192]{2,1,0:T(8,128)(2,1)} %bitcast.82, bf16[2,224,192]{2,1,0:T(8,128)(2,1)} %bitcast.83, f32[1,192]{1,0:T(1,128)} %bitcast.92, ...), custom_call_target="tpu_custom_call" | custom-call | tf_op jit(solution)/shard_map/pallas_call | solution.py:129
  23.1 3.2 %collective-permute-start.5 = (bf16[1,2,112,192]{3,2,1,0:T(8,128)(2,1)}, bf16[1,2,112,192]{3,2,1,0:T(8,128)(2,1)S(1)}, u32[]{:S(2)}, u32[]{:S(2)}) collective-permute-start(bf16[1,2,112,192]{3,2,1,0:T(8,128)(2,1)} %bitcast.84), channel_id=1, source_target_pairs={{0,12},{4,0},{8,4},{12,8},{1,13},{5,1},{9,5},{13,9},{2,14},{6,2},{... | collective-permute-start | bytes 258056 | tf_op jit(solution)/shard_map/ppermute | solution.py:201
  26.3 0.0 collective-permute-start.4
  26.3 1.4 %collective-permute-start.3 = (bf16[1,2,112,192]{3,2,1,0:T(8,128)(2,1)}, bf16[1,2,112,192]{3,2,1,0:T(8,128)(2,1)S(1)}, u32[]{:S(2)}, u32[]{:S(2)}) collective-permute-start(bf16[1,2,112,192]{3,2,1,0:T(8,128)(2,1)} %bitcast.86), channel_id=1, source_target_pairs={{0,4},{4,8},{8,12},{12,0},{1,5},{5,9},{9,13},{13,1},{2,6},{6,10},{... | collective-permute-start | bytes 258056 | tf_op jit(solution)/shard_map/ppermute | solution.py:201
  27.7 2.5 %collective-permute-start.6 = (bf16[1,224,192]{2,1,0:T(8,128)(2,1)}, bf16[1,224,192]{2,1,0:T(8,128)(2,1)S(1)}, u32[]{:S(2)}, u32[]{:S(2)}) collective-permute-start(bf16[1,224,192]{2,1,0:T(8,128)(2,1)} %get-tuple-element.9), channel_id=1, source_target_pairs={{0,2},{2,0},{1,3},{3,1},{4,6},{6,4},{5,7},{7,5},{8,10},{10,8},{9,1... | collective-permute-start | bytes 258056 | tf_op jit(solution)/shard_map/ppermute | solution.py:197
  30.2 0.0 collective-permute-done.5
  30.2 7.1 %collective-permute-done.4 = bf16[1,2,112,192]{3,2,1,0:T(8,128)(2,1)S(1)} collective-permute-done((bf16[1,2,112,192]{3,2,1,0:T(8,128)(2,1)}, bf16[1,2,112,192]{3,2,1,0:T(8,128)(2,1)S(1)}, u32[]{:S(2)}, u32[]{:S(2)}) %collective-permute-start.4) | collective-permute-done | bytes 86048 | tf_op jit(solution)/shard_map/ppermute | solution.py:201
  37.3 0.0 collective-permute-done.3
  37.3 1.0 %pad_maximum_fusion = bf16[1,8,112,192]{3,2,1,0:T(8,128)(2,1)S(1)} fusion(bf16[1,2,112,192]{3,2,1,0:T(8,128)(2,1)S(1)} %collective-permute-done.5, bf16[1,2,112,192]{3,2,1,0:T(8,128)(2,1)S(1)} %collective-permute-done.4, bf16[1,2,112,192]{3,2,1,0:T(8,128)(2,1)S(1)} %collective-permute-done.3, bf16[1,2,112,192]{3,2,1,0:T(8,128)(2,1)} %bitcast.87), kind=kLoop, calls=%fused_computation.17 | loop fusion | flops 516096 | bytes 688128 | tf_op jit(solution)/shard_map/concatenate | solution.py:204
  38.3 0.0 collective-permute-done.6
  38.3 0.4 fusion.34
  38.7 0.3 fusion.10
  39.0 0.0 copy-start.5
  39.0 0.0 copy-start.6
  39.0 0.4 fusion.7
  39.5 0.0 copy-start.7
  39.5 0.4 fusion.33
  40.0 2.1 %collective-permute-start.7 = (bf16[1,224,198]{1,2,0:T(8,128)(2,1)S(1)}, bf16[1,224,198]{1,2,0:T(8,128)(2,1)S(1)}, u32[]{:S(2)}, u32[]{:S(2)}) collective-permute-start(bf16[1,224,198]{1,2,0:T(8,128)(2,1)S(1)} %pad_maximum_fusion.2), channel_id=1, source_target_pairs={{0,2},{2,0},{1,3},{3,1},{4,6},{6,4},{5,7},{7,5},{8,10},{10,8},{9,1... | collective-permute-start | bytes 266120 | tf_op jit(solution)/shard_map/ppermute | solution.py:226
  42.1 0.3 fusion.8
  42.4 2.4 %collective-permute-done.7 = bf16[1,224,198]{1,2,0:T(8,128)(2,1)S(1)} collective-permute-done((bf16[1,224,198]{1,2,0:T(8,128)(2,1)S(1)}, bf16[1,224,198]{1,2,0:T(8,128)(2,1)S(1)}, u32[]{:S(2)}, u32[]{:S(2)}) %collective-permute-start.7) | collective-permute-done | bytes 88736 | tf_op jit(solution)/shard_map/ppermute | solution.py:226
  44.8 0.4 fusion.6
  45.2 0.3 fusion.5
  45.7 0.8 %copy.18 = f32[1,1,2,112,192]{3,4,2,1,0:T(8,128)} copy(f32[1,1,2,112,192]{4,3,2,1,0:T(8,128)S(1)} %bitcast.80) | data formatting | bytes 344064 | tf_op jit(solution)/shard_map/reshape | solution.py:247
  (20 shorter events, 0.2 us)
Async XLA Ops:
  0.0 45.2 %copy-start = (bf16[192,192]{1,0:T(8,128)(2,1)S(1)}, bf16[192,192]{1,0:T(8,128)(2,1)}, u32[]{:S(2)}) copy-start(bf16[192,192]{1,0:T(8,128)(2,1)} %param.28) | copy-start | bytes 221188
  1.0 1.5 %collective-permute-start = (bf16[1,2,112,192]{3,2,1,0:T(8,128)(2,1)S(1)}, bf16[1,2,112,192]{3,2,1,0:T(8,128)(2,1)S(1)}, u32[]{:S(2)}, u32[]{:S(2)}) collective-permute-start(bf16[1,2,112,192]{3,2,1,0:T(8,128)(2,1)S(1)} %bitcast.81), channel_id=1, source_target_pairs={{0,1},{1,0},{2,3},{3,2},{4,5},{5,4},{6,7},{7,6},{8,9},{9,8},{10,11... | collective-permute-start | bytes 258056 | tf_op jit(solution)/shard_map/ppermute | solution.py:165
  2.6 10.7 %collective-permute-start.1 = (bf16[2,2,112,192]{3,2,1,0:T(8,128)(2,1)S(1)}, bf16[2,2,112,192]{3,2,1,0:T(8,128)(2,1)S(1)}, u32[]{:S(2)}, u32[]{:S(2)}) collective-permute-start(bf16[2,2,112,192]{3,2,1,0:T(8,128)(2,1)S(1)} %maximum_bitcast_fusion), channel_id=1, source_target_pairs={{0,2},{2,4},{4,6},{6,8},{8,10},{10,12},{12,14},{3,1},{5,3},{7,5},{... | collective-permute-start | bytes 516104 | tf_op jit(solution)/shard_map/ppermute | solution.py:173
  13.3 1.5 %copy-start.2 = (bf16[2,2,112,192]{3,2,1,0:T(8,128)(2,1)}, bf16[2,2,112,192]{3,2,1,0:T(8,128)(2,1)S(1)}, u32[]{:S(2)}) copy-start(bf16[2,2,112,192]{3,2,1,0:T(8,128)(2,1)S(1)} %collective-permute-done.1) | copy-start | bytes 516100
  13.3 1.5 %collective-permute-start.2 = (bf16[2,2,112,192]{3,2,1,0:T(8,128)(2,1)S(1)}, bf16[2,2,112,192]{3,2,1,0:T(8,128)(2,1)S(1)}, u32[]{:S(2)}, u32[]{:S(2)}) collective-permute-start(bf16[2,2,112,192]{3,2,1,0:T(8,128)(2,1)S(1)} %collective-permute-done.1), channel_id=1, source_target_pairs={{0,1},{1,0},{2,3},{3,2},{4,5},{5,4},{6,7},{7,6},{8,9},{9,8},{10,11... | collective-permute-start | bytes 516104 | tf_op jit(solution)/shard_map/ppermute | solution.py:174
  14.8 0.7 %copy-start.3 = (bf16[2,2,112,192]{3,2,1,0:T(8,128)(2,1)}, bf16[2,2,112,192]{3,2,1,0:T(8,128)(2,1)S(1)}, u32[]{:S(2)}) copy-start(bf16[2,2,112,192]{3,2,1,0:T(8,128)(2,1)S(1)} %collective-permute-done.2) | copy-start | bytes 516100
  23.1 16.4 %copy-start.4 = (bf16[1,224,192]{2,1,0:T(8,128)(2,1)S(1)}, bf16[1,224,192]{2,1,0:T(8,128)(2,1)}, u32[]{:S(2)}) copy-start(bf16[1,224,192]{2,1,0:T(8,128)(2,1)} %get-tuple-element.9) | copy-start | bytes 258052
  23.1 7.1 %collective-permute-start.5 = (bf16[1,2,112,192]{3,2,1,0:T(8,128)(2,1)}, bf16[1,2,112,192]{3,2,1,0:T(8,128)(2,1)S(1)}, u32[]{:S(2)}, u32[]{:S(2)}) collective-permute-start(bf16[1,2,112,192]{3,2,1,0:T(8,128)(2,1)} %bitcast.84), channel_id=1, source_target_pairs={{0,12},{4,0},{8,4},{12,8},{1,13},{5,1},{9,5},{13,9},{2,14},{6,2},{... | collective-permute-start | bytes 258056 | tf_op jit(solution)/shard_map/ppermute | solution.py:201
  26.3 11.0 %collective-permute-start.4 = (bf16[1,2,112,192]{3,2,1,0:T(8,128)(2,1)}, bf16[1,2,112,192]{3,2,1,0:T(8,128)(2,1)S(1)}, u32[]{:S(2)}, u32[]{:S(2)}) collective-permute-start(bf16[1,2,112,192]{3,2,1,0:T(8,128)(2,1)} %bitcast.85), channel_id=1, source_target_pairs={{0,8},{4,12},{8,0},{12,4},{1,9},{5,13},{9,1},{13,5},{2,10},{6,14},... | collective-permute-start | bytes 258056 | tf_op jit(solution)/shard_map/ppermute | solution.py:201
  26.3 11.0 %collective-permute-start.3 = (bf16[1,2,112,192]{3,2,1,0:T(8,128)(2,1)}, bf16[1,2,112,192]{3,2,1,0:T(8,128)(2,1)S(1)}, u32[]{:S(2)}, u32[]{:S(2)}) collective-permute-start(bf16[1,2,112,192]{3,2,1,0:T(8,128)(2,1)} %bitcast.86), channel_id=1, source_target_pairs={{0,4},{4,8},{8,12},{12,0},{1,5},{5,9},{9,13},{13,1},{2,6},{6,10},{... | collective-permute-start | bytes 258056 | tf_op jit(solution)/shard_map/ppermute | solution.py:201
  27.7 10.6 %collective-permute-start.6 = (bf16[1,224,192]{2,1,0:T(8,128)(2,1)}, bf16[1,224,192]{2,1,0:T(8,128)(2,1)S(1)}, u32[]{:S(2)}, u32[]{:S(2)}) collective-permute-start(bf16[1,224,192]{2,1,0:T(8,128)(2,1)} %get-tuple-element.9), channel_id=1, source_target_pairs={{0,2},{2,0},{1,3},{3,1},{4,6},{6,4},{5,7},{7,5},{8,10},{10,8},{9,1... | collective-permute-start | bytes 258056 | tf_op jit(solution)/shard_map/ppermute | solution.py:197
  39.0 6.2 %copy-start.5 = (bf16[192,192]{1,0:T(8,128)(2,1)S(1)}, bf16[192,192]{1,0:T(8,128)(2,1)}, u32[]{:S(2)}) copy-start(bf16[192,192]{1,0:T(8,128)(2,1)} %param.26) | copy-start | bytes 221188
  39.0 6.2 %copy-start.6 = (f32[192]{0:T(256)S(1)}, f32[192]{0:T(256)}, u32[]{:S(2)}) copy-start(f32[192]{0:T(256)} %param.27) | copy-start | bytes 2308
  39.5 6.1 %copy-start.1 = (f32[1,224,192]{2,1,0:T(8,128)S(1)}, f32[1,224,192]{2,1,0:T(8,128)}, u32[]{:S(2)}) copy-start(f32[1,224,192]{2,1,0:T(8,128)} %get-tuple-element.8) | copy-start | bytes 516100
  39.5 6.1 %copy-start.7 = (f32[192]{0:T(256)S(1)}, f32[192]{0:T(256)}, u32[]{:S(2)}) copy-start(f32[192]{0:T(256)} %param.29) | copy-start | bytes 2308
  40.0 4.8 %collective-permute-start.7 = (bf16[1,224,198]{1,2,0:T(8,128)(2,1)S(1)}, bf16[1,224,198]{1,2,0:T(8,128)(2,1)S(1)}, u32[]{:S(2)}, u32[]{:S(2)}) collective-permute-start(bf16[1,224,198]{1,2,0:T(8,128)(2,1)S(1)} %pad_maximum_fusion.2), channel_id=1, source_target_pairs={{0,2},{2,0},{1,3},{3,1},{4,6},{6,4},{5,7},{7,5},{8,10},{10,8},{9,1... | collective-permute-start | bytes 266120 | tf_op jit(solution)/shard_map/ppermute | solution.py:226

commit v16 on v15

--- a/solution.py
+++ b/solution.py
@@ -197,10 +197,11 @@
     partner_queries = lax.ppermute(folded, "inner", swap)
     spans = lax.axis_size("outer")
     if spans <= 4:
-        shares = [normed] + [
-            lax.ppermute(normed, "outer", [(i, (i + k) % spans) for i in range(spans)])
-            for k in range(1, spans)
-        ]
+        if spans & (spans - 1) == 0:
+            routes = [[(i, i ^ k) for i in range(spans)] for k in range(1, spans)]
+        else:
+            routes = [[(i, (i + k) % spans) for i in range(spans)] for k in range(1, spans)]
+        shares = [normed] + [lax.ppermute(normed, "outer", route) for route in routes]
         keys = jnp.concatenate(shares, axis=1)
     else:
         keys = lax.all_gather(normed, "outer", axis=1, tiled=True)

time: 46.6 us -> 46.6 us (level)
  transfers between devices with their start and end apart: 8 -> 8, of which waited for: 5 -> 6; matrix products, arithmetic and copies ran while one was open for 4% -> 4% of each run, Pallas kernels for 0% -> 0%
where the time goes in v16:
time: 46.6 us; the launch traced here: 46.5 us
  waiting for transfers between devices  16.9 us (36%)
  starting transfers between devices  14.7 us (32%)
  Pallas kernels  7.58 us (16%)
  local copies, waits for them, and re-layouts  2.55 us (5%)
  other arithmetic  2.49 us (5%)
  matrix products  2.02 us (4%)
    pallas_call x1, Pallas kernels, resnet_block(): pl.pallas_call(functools.partial(block_kernel, cols, frame_count), out_sh...  7.58 us
    ppermute x3, waiting for transfers between devices, local(): lax.ppermute(normed, 'outer', route)  6.92 us
    ppermute x1, waiting for transfers between devices, local(): arrived = lax.ppermute(edge, ('outer', 'inner', 'tm'), up + down)  5.97 us
    ppermute x1, starting transfers between devices, local(): arrived = lax.ppermute(edge, ('outer', 'inner', 'tm'), up + down)  4.76 us
    ppermute x3, starting transfers between devices, local(): lax.ppermute(normed, 'outer', route)  4.39 us
    ppermute x1, starting transfers between devices, local(): returned = lax.ppermute(packed, 'inner', swap).astype(jnp.float32)  2.55 us
    ppermute x1, starting transfers between devices, local(): partner_queries = lax.ppermute(folded, 'inner', swap)  2.48 us
    ppermute x1, waiting for transfers between devices, local(): returned = lax.ppermute(packed, 'inner', swap).astype(jnp.float32)  2.36 us
  transfers between devices with their start and end apart: 8, of which 6 were waited for; matrix products, arithmetic and copies ran while one was open for 4% of the time, Pallas kernels for 0%

profile of v16, /device:TPU:0, one launch (start us, length us, event | category | flops | bytes accessed | tf_op | source)
XLA Modules:
  0.0 46.5 jit_solution(13240746751805440033)
XLA Ops:
  0.0 1.0 %copy.16 = bf16[1,1,2,112,192]{4,3,2,1,0:T(8,128)(2,1)S(1)} copy(bf16[1,1,2,112,192]{3,4,2,1,0:T(8,128)(2,1)} %param.15) | data formatting | bytes 172032 | tf_op args[0]
  1.0 0.5 %collective-permute-start = (bf16[1,2,112,192]{3,2,1,0:T(8,128)(2,1)S(1)}, bf16[1,2,112,192]{3,2,1,0:T(8,128)(2,1)S(1)}, u32[]{:S(2)}, u32[]{:S(2)}) collective-permute-start(bf16[1,2,112,192]{3,2,1,0:T(8,128)(2,1)S(1)} %bitcast.81), channel_id=1, source_target_pairs={{0,1},{1,0},{2,3},{3,2},{4,5},{5,4},{6,7},{7,6},{8,9},{9,8},{10,11... | collective-permute-start | bytes 258056 | tf_op jit(solution)/shard_map/ppermute | solution.py:165
  1.6 1.0 %collective-permute-done = bf16[1,2,112,192]{3,2,1,0:T(8,128)(2,1)S(1)} collective-permute-done((bf16[1,2,112,192]{3,2,1,0:T(8,128)(2,1)S(1)}, bf16[1,2,112,192]{3,2,1,0:T(8,128)(2,1)S(1)}, u32[]{:S(2)}, u32[]{:S(2)}) %collective-permute-start) | collective-permute-done | bytes 86048 | tf_op jit(solution)/shard_map/ppermute | solution.py:165
  2.6 4.8 %collective-permute-start.1 = (bf16[2,2,112,192]{3,2,1,0:T(8,128)(2,1)S(1)}, bf16[2,2,112,192]{3,2,1,0:T(8,128)(2,1)S(1)}, u32[]{:S(2)}, u32[]{:S(2)}) collective-permute-start(bf16[2,2,112,192]{3,2,1,0:T(8,128)(2,1)S(1)} %maximum_bitcast_fusion), channel_id=1, source_target_pairs={{0,2},{2,4},{4,6},{6,8},{8,10},{10,12},{12,14},{3,1},{5,3},{7,5},{... | collective-permute-start | bytes 516104 | tf_op jit(solution)/shard_map/ppermute | solution.py:173
  7.4 6.0 %collective-permute-done.1 = bf16[2,2,112,192]{3,2,1,0:T(8,128)(2,1)S(1)} collective-permute-done((bf16[2,2,112,192]{3,2,1,0:T(8,128)(2,1)S(1)}, bf16[2,2,112,192]{3,2,1,0:T(8,128)(2,1)S(1)}, u32[]{:S(2)}, u32[]{:S(2)}) %collective-permute-start.1) | collective-permute-done | bytes 172064 | tf_op jit(solution)/shard_map/ppermute | solution.py:173
  13.3 0.0 collective-permute-start.2
  13.3 0.8 %pad_maximum_fusion.1.seq_ref = bf16[2,224,192]{2,1,0:T(8,128)(2,1)} fusion(bf16[1,224,192]{2,1,0:T(8,128)(2,1)S(1)} %bitcast.79, bf16[1,224,192]{2,1,0:T(8,128)(2,1)S(1)} %bitcast.77), kind=kLoop, calls=%fused_computation.20 | loop fusion | flops 86016 | bytes 344064 | tf_op jit(solution)/shard_map/stack | solution.py:168
  14.1 0.7 %collective-permute-done.2 = bf16[2,2,112,192]{3,2,1,0:T(8,128)(2,1)S(1)} collective-permute-done((bf16[2,2,112,192]{3,2,1,0:T(8,128)(2,1)S(1)}, bf16[2,2,112,192]{3,2,1,0:T(8,128)(2,1)S(1)}, u32[]{:S(2)}, u32[]{:S(2)}) %collective-permute-start.2) | collective-permute-done | bytes 172064 | tf_op jit(solution)/shard_map/ppermute | solution.py:174
  14.8 0.7 %copy-done.3 = bf16[2,2,112,192]{3,2,1,0:T(8,128)(2,1)} copy-done((bf16[2,2,112,192]{3,2,1,0:T(8,128)(2,1)}, bf16[2,2,112,192]{3,2,1,0:T(8,128)(2,1)S(1)}, u32[]{:S(2)}) %copy-start.3) | copy-done | bytes 172056
  15.5 7.6 %shard_map.145 = (f32[1,224,192]{2,1,0:T(8,128)}, bf16[1,224,192]{2,1,0:T(8,128)(2,1)}, bf16[1,224,192]{2,1,0:T(8,128)(2,1)}) custom-call(bf16[2,224,192]{2,1,0:T(8,128)(2,1)} %pad_maximum_fusion.1.seq_ref, bf16[2,224,192]{2,1,0:T(8,128)(2,1)} %bitcast.82, bf16[2,224,192]{2,1,0:T(8,128)(2,1)} %bitcast.83, f32[1,192]{1,0:T(1,128)} %bitcast.92, ...), custom_call_target="tpu_custom_call" | custom-call | tf_op jit(solution)/shard_map/pallas_call | solution.py:129
  23.1 3.2 %collective-permute-start.5 = (bf16[1,2,112,192]{3,2,1,0:T(8,128)(2,1)}, bf16[1,2,112,192]{3,2,1,0:T(8,128)(2,1)S(1)}, u32[]{:S(2)}, u32[]{:S(2)}) collective-permute-start(bf16[1,2,112,192]{3,2,1,0:T(8,128)(2,1)} %bitcast.84), channel_id=1, source_target_pairs={{0,12},{4,8},{8,4},{12,0},{1,13},{5,9},{9,5},{13,1},{2,14},{6,10},... | collective-permute-start | bytes 258056 | tf_op jit(solution)/shard_map/ppermute | solution.py:204
  26.3 0.0 collective-permute-start.4
  26.3 1.2 %collective-permute-start.3 = (bf16[1,2,112,192]{3,2,1,0:T(8,128)(2,1)}, bf16[1,2,112,192]{3,2,1,0:T(8,128)(2,1)S(1)}, u32[]{:S(2)}, u32[]{:S(2)}) collective-permute-start(bf16[1,2,112,192]{3,2,1,0:T(8,128)(2,1)} %bitcast.86), channel_id=1, source_target_pairs={{0,4},{4,0},{8,12},{12,8},{1,5},{5,1},{9,13},{13,9},{2,6},{6,2},{1... | collective-permute-start | bytes 258056 | tf_op jit(solution)/shard_map/ppermute | solution.py:204
  27.5 2.5 %collective-permute-start.6 = (bf16[1,224,192]{2,1,0:T(8,128)(2,1)}, bf16[1,224,192]{2,1,0:T(8,128)(2,1)S(1)}, u32[]{:S(2)}, u32[]{:S(2)}) collective-permute-start(bf16[1,224,192]{2,1,0:T(8,128)(2,1)} %get-tuple-element.9), channel_id=1, source_target_pairs={{0,2},{2,0},{1,3},{3,1},{4,6},{6,4},{5,7},{7,5},{8,10},{10,8},{9,1... | collective-permute-start | bytes 258056 | tf_op jit(solution)/shard_map/ppermute | solution.py:197
  30.0 1.2 %collective-permute-done.5 = bf16[1,2,112,192]{3,2,1,0:T(8,128)(2,1)S(1)} collective-permute-done((bf16[1,2,112,192]{3,2,1,0:T(8,128)(2,1)}, bf16[1,2,112,192]{3,2,1,0:T(8,128)(2,1)S(1)}, u32[]{:S(2)}, u32[]{:S(2)}) %collective-permute-start.5) | collective-permute-done | bytes 86048 | tf_op jit(solution)/shard_map/ppermute | solution.py:204
  31.2 5.7 %collective-permute-done.4 = bf16[1,2,112,192]{3,2,1,0:T(8,128)(2,1)S(1)} collective-permute-done((bf16[1,2,112,192]{3,2,1,0:T(8,128)(2,1)}, bf16[1,2,112,192]{3,2,1,0:T(8,128)(2,1)S(1)}, u32[]{:S(2)}, u32[]{:S(2)}) %collective-permute-start.4) | collective-permute-done | bytes 86048 | tf_op jit(solution)/shard_map/ppermute | solution.py:204
  36.9 0.0 collective-permute-done.3
  36.9 1.0 %pad_maximum_fusion = bf16[1,8,112,192]{3,2,1,0:T(8,128)(2,1)S(1)} fusion(bf16[1,2,112,192]{3,2,1,0:T(8,128)(2,1)S(1)} %collective-permute-done.5, bf16[1,2,112,192]{3,2,1,0:T(8,128)(2,1)S(1)} %collective-permute-done.4, bf16[1,2,112,192]{3,2,1,0:T(8,128)(2,1)S(1)} %collective-permute-done.3, bf16[1,2,112,192]{3,2,1,0:T(8,128)(2,1)} %bitcast.87), kind=kLoop, calls=%fused_computation.17 | loop fusion | flops 516096 | bytes 688128 | tf_op jit(solution)/shard_map/concatenate | solution.py:205
  37.9 0.0 collective-permute-done.6
  37.9 0.4 fusion.34
  38.3 0.3 fusion.10
  38.6 0.0 copy-start.5
  38.6 0.0 copy-start.6
  38.6 0.4 fusion.7
  39.1 0.0 copy-start.7
  39.1 0.4 fusion.33
  39.6 2.5 %collective-permute-start.7 = (bf16[1,224,198]{1,2,0:T(8,128)(2,1)S(1)}, bf16[1,224,198]{1,2,0:T(8,128)(2,1)S(1)}, u32[]{:S(2)}, u32[]{:S(2)}) collective-permute-start(bf16[1,224,198]{1,2,0:T(8,128)(2,1)S(1)} %pad_maximum_fusion.2), channel_id=1, source_target_pairs={{0,2},{2,0},{1,3},{3,1},{4,6},{6,4},{5,7},{7,5},{8,10},{10,8},{9,1... | collective-permute-start | bytes 266120 | tf_op jit(solution)/shard_map/ppermute | solution.py:227
  42.1 0.3 fusion.8
  42.4 2.4 %collective-permute-done.7 = bf16[1,224,198]{1,2,0:T(8,128)(2,1)S(1)} collective-permute-done((bf16[1,224,198]{1,2,0:T(8,128)(2,1)S(1)}, bf16[1,224,198]{1,2,0:T(8,128)(2,1)S(1)}, u32[]{:S(2)}, u32[]{:S(2)}) %collective-permute-start.7) | collective-permute-done | bytes 88736 | tf_op jit(solution)/shard_map/ppermute | solution.py:227
  44.8 0.4 fusion.6
  45.2 0.3 fusion.5
  45.7 0.8 %copy.18 = f32[1,1,2,112,192]{3,4,2,1,0:T(8,128)} copy(f32[1,1,2,112,192]{4,3,2,1,0:T(8,128)S(1)} %bitcast.80) | data formatting | bytes 344064 | tf_op jit(solution)/shard_map/reshape | solution.py:248
  (20 shorter events, 0.2 us)
Async XLA Ops:
  0.0 45.2 %copy-start = (bf16[192,192]{1,0:T(8,128)(2,1)S(1)}, bf16[192,192]{1,0:T(8,128)(2,1)}, u32[]{:S(2)}) copy-start(bf16[192,192]{1,0:T(8,128)(2,1)} %param.28) | copy-start | bytes 221188
  1.0 1.5 %collective-permute-start = (bf16[1,2,112,192]{3,2,1,0:T(8,128)(2,1)S(1)}, bf16[1,2,112,192]{3,2,1,0:T(8,128)(2,1)S(1)}, u32[]{:S(2)}, u32[]{:S(2)}) collective-permute-start(bf16[1,2,112,192]{3,2,1,0:T(8,128)(2,1)S(1)} %bitcast.81), channel_id=1, source_target_pairs={{0,1},{1,0},{2,3},{3,2},{4,5},{5,4},{6,7},{7,6},{8,9},{9,8},{10,11... | collective-permute-start | bytes 258056 | tf_op jit(solution)/shard_map/ppermute | solution.py:165
  2.6 10.7 %collective-permute-start.1 = (bf16[2,2,112,192]{3,2,1,0:T(8,128)(2,1)S(1)}, bf16[2,2,112,192]{3,2,1,0:T(8,128)(2,1)S(1)}, u32[]{:S(2)}, u32[]{:S(2)}) collective-permute-start(bf16[2,2,112,192]{3,2,1,0:T(8,128)(2,1)S(1)} %maximum_bitcast_fusion), channel_id=1, source_target_pairs={{0,2},{2,4},{4,6},{6,8},{8,10},{10,12},{12,14},{3,1},{5,3},{7,5},{... | collective-permute-start | bytes 516104 | tf_op jit(solution)/shard_map/ppermute | solution.py:173
  13.3 1.5 %copy-start.2 = (bf16[2,2,112,192]{3,2,1,0:T(8,128)(2,1)}, bf16[2,2,112,192]{3,2,1,0:T(8,128)(2,1)S(1)}, u32[]{:S(2)}) copy-start(bf16[2,2,112,192]{3,2,1,0:T(8,128)(2,1)S(1)} %collective-permute-done.1) | copy-start | bytes 516100
  13.3 1.5 %collective-permute-start.2 = (bf16[2,2,112,192]{3,2,1,0:T(8,128)(2,1)S(1)}, bf16[2,2,112,192]{3,2,1,0:T(8,128)(2,1)S(1)}, u32[]{:S(2)}, u32[]{:S(2)}) collective-permute-start(bf16[2,2,112,192]{3,2,1,0:T(8,128)(2,1)S(1)} %collective-permute-done.1), channel_id=1, source_target_pairs={{0,1},{1,0},{2,3},{3,2},{4,5},{5,4},{6,7},{7,6},{8,9},{9,8},{10,11... | collective-permute-start | bytes 516104 | tf_op jit(solution)/shard_map/ppermute | solution.py:174
  14.8 0.7 %copy-start.3 = (bf16[2,2,112,192]{3,2,1,0:T(8,128)(2,1)}, bf16[2,2,112,192]{3,2,1,0:T(8,128)(2,1)S(1)}, u32[]{:S(2)}) copy-start(bf16[2,2,112,192]{3,2,1,0:T(8,128)(2,1)S(1)} %collective-permute-done.2) | copy-start | bytes 516100
  23.1 16.0 %copy-start.4 = (bf16[1,224,192]{2,1,0:T(8,128)(2,1)S(1)}, bf16[1,224,192]{2,1,0:T(8,128)(2,1)}, u32[]{:S(2)}) copy-start(bf16[1,224,192]{2,1,0:T(8,128)(2,1)} %get-tuple-element.9) | copy-start | bytes 258052
  23.1 8.1 %collective-permute-start.5 = (bf16[1,2,112,192]{3,2,1,0:T(8,128)(2,1)}, bf16[1,2,112,192]{3,2,1,0:T(8,128)(2,1)S(1)}, u32[]{:S(2)}, u32[]{:S(2)}) collective-permute-start(bf16[1,2,112,192]{3,2,1,0:T(8,128)(2,1)} %bitcast.84), channel_id=1, source_target_pairs={{0,12},{4,8},{8,4},{12,0},{1,13},{5,9},{9,5},{13,1},{2,14},{6,10},... | collective-permute-start | bytes 258056 | tf_op jit(solution)/shard_map/ppermute | solution.py:204
  26.3 10.6 %collective-permute-start.4 = (bf16[1,2,112,192]{3,2,1,0:T(8,128)(2,1)}, bf16[1,2,112,192]{3,2,1,0:T(8,128)(2,1)S(1)}, u32[]{:S(2)}, u32[]{:S(2)}) collective-permute-start(bf16[1,2,112,192]{3,2,1,0:T(8,128)(2,1)} %bitcast.85), channel_id=1, source_target_pairs={{0,8},{4,12},{8,0},{12,4},{1,9},{5,13},{9,1},{13,5},{2,10},{6,14},... | collective-permute-start | bytes 258056 | tf_op jit(solution)/shard_map/ppermute | solution.py:204
  26.3 10.6 %collective-permute-start.3 = (bf16[1,2,112,192]{3,2,1,0:T(8,128)(2,1)}, bf16[1,2,112,192]{3,2,1,0:T(8,128)(2,1)S(1)}, u32[]{:S(2)}, u32[]{:S(2)}) collective-permute-start(bf16[1,2,112,192]{3,2,1,0:T(8,128)(2,1)} %bitcast.86), channel_id=1, source_target_pairs={{0,4},{4,0},{8,12},{12,8},{1,5},{5,1},{9,13},{13,9},{2,6},{6,2},{1... | collective-permute-start | bytes 258056 | tf_op jit(solution)/shard_map/ppermute | solution.py:204
  27.5 10.4 %collective-permute-start.6 = (bf16[1,224,192]{2,1,0:T(8,128)(2,1)}, bf16[1,224,192]{2,1,0:T(8,128)(2,1)S(1)}, u32[]{:S(2)}, u32[]{:S(2)}) collective-permute-start(bf16[1,224,192]{2,1,0:T(8,128)(2,1)} %get-tuple-element.9), channel_id=1, source_target_pairs={{0,2},{2,0},{1,3},{3,1},{4,6},{6,4},{5,7},{7,5},{8,10},{10,8},{9,1... | collective-permute-start | bytes 258056 | tf_op jit(solution)/shard_map/ppermute | solution.py:197
  38.6 6.6 %copy-start.5 = (bf16[192,192]{1,0:T(8,128)(2,1)S(1)}, bf16[192,192]{1,0:T(8,128)(2,1)}, u32[]{:S(2)}) copy-start(bf16[192,192]{1,0:T(8,128)(2,1)} %param.26) | copy-start | bytes 221188
  38.6 6.6 %copy-start.6 = (f32[192]{0:T(256)S(1)}, f32[192]{0:T(256)}, u32[]{:S(2)}) copy-start(f32[192]{0:T(256)} %param.27) | copy-start | bytes 2308
  39.0 6.6 %copy-start.1 = (f32[1,224,192]{2,1,0:T(8,128)S(1)}, f32[1,224,192]{2,1,0:T(8,128)}, u32[]{:S(2)}) copy-start(f32[1,224,192]{2,1,0:T(8,128)} %get-tuple-element.8) | copy-start | bytes 516100
  39.1 6.6 %copy-start.7 = (f32[192]{0:T(256)S(1)}, f32[192]{0:T(256)}, u32[]{:S(2)}) copy-start(f32[192]{0:T(256)} %param.29) | copy-start | bytes 2308
  39.6 5.2 %collective-permute-start.7 = (bf16[1,224,198]{1,2,0:T(8,128)(2,1)S(1)}, bf16[1,224,198]{1,2,0:T(8,128)(2,1)S(1)}, u32[]{:S(2)}, u32[]{:S(2)}) collective-permute-start(bf16[1,224,198]{1,2,0:T(8,128)(2,1)S(1)} %pad_maximum_fusion.2), channel_id=1, source_target_pairs={{0,2},{2,0},{1,3},{3,1},{4,6},{6,4},{5,7},{7,5},{8,10},{10,8},{9,1... | collective-permute-start | bytes 266120 | tf_op jit(solution)/shard_map/ppermute | solution.py:227

commit v17 on v15

--- a/solution.py
+++ b/solution.py
@@ -201,17 +201,22 @@
             lax.ppermute(normed, "outer", [(i, (i + k) % spans) for i in range(spans)])
             for k in range(1, spans)
         ]
-        keys = jnp.concatenate(shares, axis=1)
     else:
-        keys = lax.all_gather(normed, "outer", axis=1, tiled=True)
-    keys = keys.reshape(frame_count, -1, channels)
+        shares = [lax.all_gather(normed, "outer", axis=1, tiled=True)]
+    shares = [share.reshape(frame_count, -1, channels) for share in shares]
     def partial(queries):
-        scores = jnp.einsum("fqc,fkc->fqk", queries, keys, preferred_element_type=jnp.float32)
-        top = jnp.max(scores, axis=-1, keepdims=True)
-        weights = jnp.exp(scores - top)
-        total = jnp.sum(weights, axis=-1, keepdims=True)
-        accum = jnp.einsum(
-            "fqk,fkc->fqc", weights.astype(jnp.bfloat16), keys, preferred_element_type=jnp.float32
+        scores = [
+            jnp.einsum("fqc,fkc->fqk", queries, share, preferred_element_type=jnp.float32)
+            for share in shares
+        ]
+        top = functools.reduce(jnp.maximum, [jnp.max(x, axis=-1, keepdims=True) for x in scores])
+        weights = [jnp.exp(x - top) for x in scores]
+        total = sum(jnp.sum(w, axis=-1, keepdims=True) for w in weights)
+        accum = sum(
+            jnp.einsum(
+                "fqk,fkc->fqc", w.astype(jnp.bfloat16), share, preferred_element_type=jnp.float32
+            )
+            for w, share in zip(weights, shares)
         )
         return accum, jnp.concatenate([top, total], axis=-1)
 

time: 46.6 us -> 48.4 us (1.039)
  matrix products: 2.02 us -> 7.75 us
  waiting for transfers between devices: 17.1 us -> 14.2 us
  other arithmetic: 2.49 us -> 1.27 us
    dot_general x4 -> x16, matrix products: 1.67 us -> 7.4 us  [the longest x8 5.53 us: partial(): jnp.einsum('fqc,fkc->fqk', queries, share, preferred_element_type=jnp.flo...]
    ppermute x3, waiting for transfers between devices: 7.1 us -> 4.78 us  [local(): lax.ppermute(normed, 'outer', [(i, (i + k) % spans) for i in range(spans)])]
    concatenate x1 -> x0, other arithmetic: 1 us -> none  [local(): keys = jnp.concatenate(shares, axis=1)]
    ppermute x1, waiting for transfers between devices: 2.36 us -> 1.74 us  [local(): returned = lax.ppermute(packed, 'inner', swap).astype(jnp.float32)]
  transfers between devices with their start and end apart: 8 -> 8, of which waited for: 5 -> 6; matrix products, arithmetic and copies ran while one was open for 4% -> 13% of each run, Pallas kernels for 0% -> 0%
where the time goes in v17:
time: 48.4 us; the launch traced here: 48.1 us
  starting transfers between devices  14.5 us (30%)
  waiting for transfers between devices  14.2 us (29%)
  matrix products  7.75 us (16%)
  Pallas kernels  7.59 us (16%)
  local copies, waits for them, and re-layouts  2.56 us (5%)
  other arithmetic  1.27 us (3%)
    pallas_call x1, Pallas kernels, resnet_block(): pl.pallas_call(functools.partial(block_kernel, cols, frame_count), out_sh...  7.59 us
    ppermute x1, waiting for transfers between devices, local(): arrived = lax.ppermute(edge, ('outer', 'inner', 'tm'), up + down)  5.97 us
    dot_general x8, matrix products, partial(): jnp.einsum('fqc,fkc->fqk', queries, share, preferred_element_type=jnp.flo...  5.53 us
    ppermute x3, waiting for transfers between devices, local(): lax.ppermute(normed, 'outer', [(i, (i + k) % spans) for i in range(spans)])  4.78 us
    ppermute x1, starting transfers between devices, local(): arrived = lax.ppermute(edge, ('outer', 'inner', 'tm'), up + down)  4.76 us
    ppermute x3, starting transfers between devices, local(): lax.ppermute(normed, 'outer', [(i, (i + k) % spans) for i in range(spans)])  4.61 us
    ppermute x1, starting transfers between devices, local(): partner_queries = lax.ppermute(folded, 'inner', swap)  2.48 us
    ppermute x1, starting transfers between devices, local(): returned = lax.ppermute(packed, 'inner', swap).astype(jnp.float32)  2.14 us
  transfers between devices with their start and end apart: 8, of which 6 were waited for; matrix products, arithmetic and copies ran while one was open for 13% of the time, Pallas kernels for 0%

profile of v17, /device:TPU:0, one launch (start us, length us, event | category | flops | bytes accessed | tf_op | source)
XLA Modules:
  0.0 48.1 jit_solution(4683726090636037325)
XLA Ops:
  0.0 1.0 %copy.16 = bf16[1,1,2,112,192]{4,3,2,1,0:T(8,128)(2,1)S(1)} copy(bf16[1,1,2,112,192]{3,4,2,1,0:T(8,128)(2,1)} %param.15) | data formatting | bytes 172032 | tf_op args[0]
  1.0 0.5 %collective-permute-start = (bf16[1,2,112,192]{3,2,1,0:T(8,128)(2,1)S(1)}, bf16[1,2,112,192]{3,2,1,0:T(8,128)(2,1)S(1)}, u32[]{:S(2)}, u32[]{:S(2)}) collective-permute-start(bf16[1,2,112,192]{3,2,1,0:T(8,128)(2,1)S(1)} %bitcast.139), channel_id=1, source_target_pairs={{0,1},{1,0},{2,3},{3,2},{4,5},{5,4},{6,7},{7,6},{8,9},{9,8},{10,11... | collective-permute-start | bytes 258056 | tf_op jit(solution)/shard_map/ppermute | solution.py:165
  1.6 1.0 %collective-permute-done = bf16[1,2,112,192]{3,2,1,0:T(8,128)(2,1)S(1)} collective-permute-done((bf16[1,2,112,192]{3,2,1,0:T(8,128)(2,1)S(1)}, bf16[1,2,112,192]{3,2,1,0:T(8,128)(2,1)S(1)}, u32[]{:S(2)}, u32[]{:S(2)}) %collective-permute-start) | collective-permute-done | bytes 86048 | tf_op jit(solution)/shard_map/ppermute | solution.py:165
  2.6 4.8 %collective-permute-start.1 = (bf16[2,2,112,192]{3,2,1,0:T(8,128)(2,1)S(1)}, bf16[2,2,112,192]{3,2,1,0:T(8,128)(2,1)S(1)}, u32[]{:S(2)}, u32[]{:S(2)}) collective-permute-start(bf16[2,2,112,192]{3,2,1,0:T(8,128)(2,1)S(1)} %maximum_bitcast_fusion), channel_id=1, source_target_pairs={{0,2},{2,4},{4,6},{6,8},{8,10},{10,12},{12,14},{3,1},{5,3},{7,5},{... | collective-permute-start | bytes 516104 | tf_op jit(solution)/shard_map/ppermute | solution.py:173
  7.4 6.0 %collective-permute-done.1 = bf16[2,2,112,192]{3,2,1,0:T(8,128)(2,1)S(1)} collective-permute-done((bf16[2,2,112,192]{3,2,1,0:T(8,128)(2,1)S(1)}, bf16[2,2,112,192]{3,2,1,0:T(8,128)(2,1)S(1)}, u32[]{:S(2)}, u32[]{:S(2)}) %collective-permute-start.1) | collective-permute-done | bytes 172064 | tf_op jit(solution)/shard_map/ppermute | solution.py:173
  13.3 0.8 %pad_maximum_fusion.seq_ref = bf16[2,224,192]{2,1,0:T(8,128)(2,1)} fusion(bf16[1,224,192]{2,1,0:T(8,128)(2,1)S(1)} %bitcast.137, bf16[1,224,192]{2,1,0:T(8,128)(2,1)S(1)} %bitcast.135), kind=kLoop, calls=%fused_computation.17 | loop fusion | flops 86016 | bytes 344064 | tf_op jit(solution)/shard_map/stack | solution.py:168
  14.1 0.7 %collective-permute-done.2 = bf16[2,2,112,192]{3,2,1,0:T(8,128)(2,1)S(1)} collective-permute-done((bf16[2,2,112,192]{3,2,1,0:T(8,128)(2,1)S(1)}, bf16[2,2,112,192]{3,2,1,0:T(8,128)(2,1)S(1)}, u32[]{:S(2)}, u32[]{:S(2)}) %collective-permute-start.2) | collective-permute-done | bytes 172064 | tf_op jit(solution)/shard_map/ppermute | solution.py:174
  14.8 0.7 %copy-done.4 = bf16[2,2,112,192]{3,2,1,0:T(8,128)(2,1)} copy-done((bf16[2,2,112,192]{3,2,1,0:T(8,128)(2,1)}, bf16[2,2,112,192]{3,2,1,0:T(8,128)(2,1)S(1)}, u32[]{:S(2)}) %copy-start.4) | copy-done | bytes 172056
  15.5 7.6 %shard_map.145 = (f32[1,224,192]{2,1,0:T(8,128)}, bf16[1,224,192]{2,1,0:T(8,128)(2,1)}, bf16[1,224,192]{2,1,0:T(8,128)(2,1)}) custom-call(bf16[2,224,192]{2,1,0:T(8,128)(2,1)} %pad_maximum_fusion.seq_ref, bf16[2,224,192]{2,1,0:T(8,128)(2,1)} %bitcast.140, bf16[2,224,192]{2,1,0:T(8,128)(2,1)} %bitcast.141, f32[1,192]{1,0:T(1,128)} %bitcast.146, ...), custom_call_target="tpu_custom_call" | custom-call | tf_op jit(solution)/shard_map/pallas_call | solution.py:129
  23.1 3.2 %collective-permute-start.5 = (bf16[1,2,112,192]{3,2,1,0:T(8,128)(2,1)}, bf16[1,2,112,192]{3,2,1,0:T(8,128)(2,1)S(1)}, u32[]{:S(2)}, u32[]{:S(2)}) collective-permute-start(bf16[1,2,112,192]{3,2,1,0:T(8,128)(2,1)} %bitcast.127), channel_id=1, source_target_pairs={{0,12},{4,0},{8,4},{12,8},{1,13},{5,1},{9,5},{13,9},{2,14},{6,2},{... | collective-permute-start | bytes 258056 | tf_op jit(solution)/shard_map/ppermute | solution.py:201
  26.3 1.4 %collective-permute-start.3 = (bf16[1,2,112,192]{3,2,1,0:T(8,128)(2,1)}, bf16[1,2,112,192]{3,2,1,0:T(8,128)(2,1)S(1)}, u32[]{:S(2)}, u32[]{:S(2)}) collective-permute-start(bf16[1,2,112,192]{3,2,1,0:T(8,128)(2,1)} %bitcast.129), channel_id=1, source_target_pairs={{0,4},{4,8},{8,12},{12,0},{1,5},{5,9},{9,13},{13,1},{2,6},{6,10},{... | collective-permute-start | bytes 258056 | tf_op jit(solution)/shard_map/ppermute | solution.py:201
  27.7 2.5 %collective-permute-start.6 = (bf16[1,224,192]{2,1,0:T(8,128)(2,1)}, bf16[1,224,192]{2,1,0:T(8,128)(2,1)S(1)}, u32[]{:S(2)}, u32[]{:S(2)}) collective-permute-start(bf16[1,224,192]{2,1,0:T(8,128)(2,1)} %get-tuple-element.9), channel_id=1, source_target_pairs={{0,2},{2,0},{1,3},{3,1},{4,6},{6,4},{5,7},{7,5},{8,10},{10,8},{9,1... | collective-permute-start | bytes 258056 | tf_op jit(solution)/shard_map/ppermute | solution.py:197
  30.2 1.2 %fusion.83 = (f32[224]{0:T(256)S(1)}, f32[224,224]{0,1:T(8,128)S(1)}) fusion(bf16[1,224,192]{2,1,0:T(8,128)(2,1)} %get-tuple-element.10, bf16[1,224,192]{2,1,0:T(8,128)(2,1)} %get-tuple-element.9), kind=kOutput, calls=%fused_computation.106 | convolution fusion | flops 19317536 | bytes 373632 | tf_op jit(solution)/shard_map/fqc,fkc->fqk/dot_general | solution.py:209
  31.4 4.2 %collective-permute-done.3 = bf16[1,2,112,192]{3,2,1,0:T(8,128)(2,1)S(1)} collective-permute-done((bf16[1,2,112,192]{3,2,1,0:T(8,128)(2,1)}, bf16[1,2,112,192]{3,2,1,0:T(8,128)(2,1)S(1)}, u32[]{:S(2)}, u32[]{:S(2)}) %collective-permute-start.3) | collective-permute-done | bytes 86048 | tf_op jit(solution)/shard_map/ppermute | solution.py:201
  35.5 1.1 %fusion.84 = (f32[224]{0:T(256)S(1)}, f32[224,224]{0,1:T(8,128)S(1)}) fusion(bf16[224,192]{1,0:T(8,128)(2,1)S(1)} %bitcast.123, bf16[1,224,192]{2,1,0:T(8,128)(2,1)} %get-tuple-element.9), kind=kOutput, calls=%fused_computation.107 | convolution fusion | flops 19317536 | bytes 373632 | tf_op jit(solution)/shard_map/fqc,fkc->fqk/dot_general | solution.py:209
  36.7 0.6 %collective-permute-done.4 = bf16[1,2,112,192]{3,2,1,0:T(8,128)(2,1)S(1)} collective-permute-done((bf16[1,2,112,192]{3,2,1,0:T(8,128)(2,1)}, bf16[1,2,112,192]{3,2,1,0:T(8,128)(2,1)S(1)}, u32[]{:S(2)}, u32[]{:S(2)}) %collective-permute-start.4) | collective-permute-done | bytes 86048 | tf_op jit(solution)/shard_map/ppermute | solution.py:201
  37.3 1.1 %fusion.82 = (f32[224]{0:T(256)S(1)}, f32[224,224]{0,1:T(8,128)S(1)}) fusion(bf16[224,192]{1,0:T(8,128)(2,1)S(1)} %bitcast.130, bf16[1,224,192]{2,1,0:T(8,128)(2,1)} %get-tuple-element.9), kind=kOutput, calls=%fused_computation.105 | convolution fusion | flops 19317536 | bytes 373632 | tf_op jit(solution)/shard_map/fqc,fkc->fqk/dot_general | solution.py:209
  38.4 1.1 %fusion.81 = (f32[224]{0:T(256)S(1)}, f32[224,224]{0,1:T(8,128)S(1)}) fusion(bf16[224,192]{1,0:T(8,128)(2,1)S(1)} %bitcast.119, bf16[1,224,192]{2,1,0:T(8,128)(2,1)} %get-tuple-element.9), kind=kOutput, calls=%fused_computation.104 | convolution fusion | flops 19317536 | bytes 373632 | tf_op jit(solution)/shard_map/fqc,fkc->fqk/dot_general | solution.py:209
  39.6 0.2 fusion.88
  39.8 0.2 fusion.86
  40.1 0.2 fusion.85
  40.3 0.2 fusion.87
  40.6 0.2 fusion.29
  40.8 0.2 fusion.32
  41.2 0.2 convolution_add_fusion.2
  41.5 0.2 fusion.11
  41.8 2.1 %collective-permute-start.7 = (bf16[1,224,198]{1,2,0:T(8,128)(2,1)S(1)}, bf16[1,224,198]{1,2,0:T(8,128)(2,1)S(1)}, u32[]{:S(2)}, u32[]{:S(2)}) collective-permute-start(bf16[1,224,198]{1,2,0:T(8,128)(2,1)S(1)} %pad_maximum_fusion.1), channel_id=1, source_target_pairs={{0,2},{2,0},{1,3},{3,1},{4,6},{6,4},{5,7},{7,5},{8,10},{10,8},{9,1... | collective-permute-start | bytes 266120 | tf_op jit(solution)/shard_map/ppermute | solution.py:231
  44.6 0.2 convolution_add_fusion.4
  44.8 1.7 %collective-permute-done.7 = bf16[1,224,198]{1,2,0:T(8,128)(2,1)S(1)} collective-permute-done((bf16[1,224,198]{1,2,0:T(8,128)(2,1)S(1)}, bf16[1,224,198]{1,2,0:T(8,128)(2,1)S(1)}, u32[]{:S(2)}, u32[]{:S(2)}) %collective-permute-start.7) | collective-permute-done | bytes 88736 | tf_op jit(solution)/shard_map/ppermute | solution.py:231
  46.6 0.2 fusion.10
  46.9 0.3 fusion.9
  47.3 0.8 %copy.18 = f32[1,1,2,112,192]{3,4,2,1,0:T(8,128)} copy(f32[1,1,2,112,192]{4,3,2,1,0:T(8,128)S(1)} %bitcast.138) | data formatting | bytes 344064 | tf_op jit(solution)/shard_map/reshape | solution.py:252
  (35 shorter events, 1.0 us)
Async XLA Ops:
  0.0 46.9 %copy-start = (bf16[192,192]{1,0:T(8,128)(2,1)S(1)}, bf16[192,192]{1,0:T(8,128)(2,1)}, u32[]{:S(2)}) copy-start(bf16[192,192]{1,0:T(8,128)(2,1)} %param.28) | copy-start | bytes 221188
  1.0 1.5 %collective-permute-start = (bf16[1,2,112,192]{3,2,1,0:T(8,128)(2,1)S(1)}, bf16[1,2,112,192]{3,2,1,0:T(8,128)(2,1)S(1)}, u32[]{:S(2)}, u32[]{:S(2)}) collective-permute-start(bf16[1,2,112,192]{3,2,1,0:T(8,128)(2,1)S(1)} %bitcast.139), channel_id=1, source_target_pairs={{0,1},{1,0},{2,3},{3,2},{4,5},{5,4},{6,7},{7,6},{8,9},{9,8},{10,11... | collective-permute-start | bytes 258056 | tf_op jit(solution)/shard_map/ppermute | solution.py:165
  2.6 10.7 %collective-permute-start.1 = (bf16[2,2,112,192]{3,2,1,0:T(8,128)(2,1)S(1)}, bf16[2,2,112,192]{3,2,1,0:T(8,128)(2,1)S(1)}, u32[]{:S(2)}, u32[]{:S(2)}) collective-permute-start(bf16[2,2,112,192]{3,2,1,0:T(8,128)(2,1)S(1)} %maximum_bitcast_fusion), channel_id=1, source_target_pairs={{0,2},{2,4},{4,6},{6,8},{8,10},{10,12},{12,14},{3,1},{5,3},{7,5},{... | collective-permute-start | bytes 516104 | tf_op jit(solution)/shard_map/ppermute | solution.py:173
  13.3 1.5 %copy-start.3 = (bf16[2,2,112,192]{3,2,1,0:T(8,128)(2,1)}, bf16[2,2,112,192]{3,2,1,0:T(8,128)(2,1)S(1)}, u32[]{:S(2)}) copy-start(bf16[2,2,112,192]{3,2,1,0:T(8,128)(2,1)S(1)} %collective-permute-done.1) | copy-start | bytes 516100
  13.3 1.5 %collective-permute-start.2 = (bf16[2,2,112,192]{3,2,1,0:T(8,128)(2,1)S(1)}, bf16[2,2,112,192]{3,2,1,0:T(8,128)(2,1)S(1)}, u32[]{:S(2)}, u32[]{:S(2)}) collective-permute-start(bf16[2,2,112,192]{3,2,1,0:T(8,128)(2,1)S(1)} %collective-permute-done.1), channel_id=1, source_target_pairs={{0,1},{1,0},{2,3},{3,2},{4,5},{5,4},{6,7},{7,6},{8,9},{9,8},{10,11... | collective-permute-start | bytes 516104 | tf_op jit(solution)/shard_map/ppermute | solution.py:174
  14.8 0.7 %copy-start.4 = (bf16[2,2,112,192]{3,2,1,0:T(8,128)(2,1)}, bf16[2,2,112,192]{3,2,1,0:T(8,128)(2,1)S(1)}, u32[]{:S(2)}) copy-start(bf16[2,2,112,192]{3,2,1,0:T(8,128)(2,1)S(1)} %collective-permute-done.2) | copy-start | bytes 516100
  23.1 17.2 %copy-start.1 = (bf16[1,224,192]{2,1,0:T(8,128)(2,1)S(1)}, bf16[1,224,192]{2,1,0:T(8,128)(2,1)}, u32[]{:S(2)}) copy-start(bf16[1,224,192]{2,1,0:T(8,128)(2,1)} %get-tuple-element.10) | copy-start | bytes 258052
  23.1 15.3 %collective-permute-start.5 = (bf16[1,2,112,192]{3,2,1,0:T(8,128)(2,1)}, bf16[1,2,112,192]{3,2,1,0:T(8,128)(2,1)S(1)}, u32[]{:S(2)}, u32[]{:S(2)}) collective-permute-start(bf16[1,2,112,192]{3,2,1,0:T(8,128)(2,1)} %bitcast.127), channel_id=1, source_target_pairs={{0,12},{4,0},{8,4},{12,8},{1,13},{5,1},{9,5},{13,9},{2,14},{6,2},{... | collective-permute-start | bytes 258056 | tf_op jit(solution)/shard_map/ppermute | solution.py:201
  26.3 11.0 %collective-permute-start.4 = (bf16[1,2,112,192]{3,2,1,0:T(8,128)(2,1)}, bf16[1,2,112,192]{3,2,1,0:T(8,128)(2,1)S(1)}, u32[]{:S(2)}, u32[]{:S(2)}) collective-permute-start(bf16[1,2,112,192]{3,2,1,0:T(8,128)(2,1)} %bitcast.128), channel_id=1, source_target_pairs={{0,8},{4,12},{8,0},{12,4},{1,9},{5,13},{9,1},{13,5},{2,10},{6,14},... | collective-permute-start | bytes 258056 | tf_op jit(solution)/shard_map/ppermute | solution.py:201
  26.3 9.2 %collective-permute-start.3 = (bf16[1,2,112,192]{3,2,1,0:T(8,128)(2,1)}, bf16[1,2,112,192]{3,2,1,0:T(8,128)(2,1)S(1)}, u32[]{:S(2)}, u32[]{:S(2)}) collective-permute-start(bf16[1,2,112,192]{3,2,1,0:T(8,128)(2,1)} %bitcast.129), channel_id=1, source_target_pairs={{0,4},{4,8},{8,12},{12,0},{1,5},{5,9},{9,13},{13,1},{2,6},{6,10},{... | collective-permute-start | bytes 258056 | tf_op jit(solution)/shard_map/ppermute | solution.py:201
  27.7 11.9 %collective-permute-start.6 = (bf16[1,224,192]{2,1,0:T(8,128)(2,1)}, bf16[1,224,192]{2,1,0:T(8,128)(2,1)S(1)}, u32[]{:S(2)}, u32[]{:S(2)}) collective-permute-start(bf16[1,224,192]{2,1,0:T(8,128)(2,1)} %get-tuple-element.9), channel_id=1, source_target_pairs={{0,2},{2,0},{1,3},{3,1},{4,6},{6,4},{5,7},{7,5},{8,10},{10,8},{9,1... | collective-permute-start | bytes 258056 | tf_op jit(solution)/shard_map/ppermute | solution.py:197
  41.4 5.5 %copy-start.5 = (bf16[192,192]{1,0:T(8,128)(2,1)S(1)}, bf16[192,192]{1,0:T(8,128)(2,1)}, u32[]{:S(2)}) copy-start(bf16[192,192]{1,0:T(8,128)(2,1)} %param.26) | copy-start | bytes 221188
  41.5 5.5 %copy-start.6 = (f32[192]{0:T(256)S(1)}, f32[192]{0:T(256)}, u32[]{:S(2)}) copy-start(f32[192]{0:T(256)} %param.27) | copy-start | bytes 2308
  41.7 5.6 %copy-start.2 = (f32[1,224,192]{2,1,0:T(8,128)S(1)}, f32[1,224,192]{2,1,0:T(8,128)}, u32[]{:S(2)}) copy-start(f32[1,224,192]{2,1,0:T(8,128)} %get-tuple-element.8) | copy-start | bytes 516100
  41.7 5.6 %copy-start.7 = (f32[192]{0:T(256)S(1)}, f32[192]{0:T(256)}, u32[]{:S(2)}) copy-start(f32[192]{0:T(256)} %param.29) | copy-start | bytes 2308
  41.8 4.8 %collective-permute-start.7 = (bf16[1,224,198]{1,2,0:T(8,128)(2,1)S(1)}, bf16[1,224,198]{1,2,0:T(8,128)(2,1)S(1)}, u32[]{:S(2)}, u32[]{:S(2)}) collective-permute-start(bf16[1,224,198]{1,2,0:T(8,128)(2,1)S(1)} %pad_maximum_fusion.1), channel_id=1, source_target_pairs={{0,2},{2,0},{1,3},{3,1},{4,6},{6,4},{5,7},{7,5},{8,10},{10,8},{9,1... | collective-permute-start | bytes 266120 | tf_op jit(solution)/shard_map/ppermute | solution.py:231

commit v18 on v15

--- a/solution.py
+++ b/solution.py
@@ -48,17 +48,21 @@
 def _silu(v):
     return v * (1.0 / (1.0 + jnp.exp(-v)))
 
-def block_kernel(cols, frame_count, seq_ref, arrived_ref, swapped_ref, g1_ref, w1_ref, b1_ref, g2_ref,
+def block_kernel(cols, frame_count, own_ref, partner_ref, arrived_ref, swapped_ref, g1_ref, w1_ref, b1_ref, g2_ref,
                  w2_ref, b2_ref, ga_ref, wq_ref, bq_ref, wk_ref, res_ref, normed_ref, folded_ref):
     total = 2 * frame_count
-    p_out = seq_ref.shape[1]
+    p_out = own_ref.shape[1]
     p_mid = p_out + 2 * cols
     first = lax.axis_index("tm") == 0
+
+    def band_of(t):
+        mine, other = own_ref[t // 2], partner_ref[t // 2]
+        return jnp.where(first, mine, other) if t % 2 == 0 else jnp.where(first, other, mine)
 
     def extended(t):
         above = jnp.where(first, arrived_ref[t], swapped_ref[t])
         below = jnp.where(first, swapped_ref[t], arrived_ref[t])
-        return jnp.concatenate([above, seq_ref[t], below], axis=0)
+        return jnp.concatenate([above, band_of(t), below], axis=0)
 
     def shifted(a):
         n = a.shape[0]
@@ -110,8 +114,7 @@
             return shifted(jnp.where(first, a, b))
         srcs = [pick(2 * k - 2), pick(2 * k - 1), pick(2 * k)]
         out2 = conv_frame(srcs, w2_ref, p_out) + b2
-        own = jnp.where(first, seq_ref[2 * k], seq_ref[2 * k + 1])
-        res = own.astype(jnp.float32) + out2
+        res = own_ref[k].astype(jnp.float32) + out2
         res_ref[k] = res
         normed = _rms(res, ga).astype(jnp.bfloat16)
         normed_ref[k] = normed
@@ -122,18 +125,17 @@
         )
         folded_ref[k] = (folded * (1.0 / math.sqrt(res.shape[-1]))).astype(jnp.bfloat16)
 
-def resnet_block(seq, arrived, swapped, g1, w1, b1, g2, w2, b2, ga, wq, bq, wk, cols):
-    total, p_out, c = seq.shape
-    frame_count = total // 2
+def resnet_block(own, partner, arrived, swapped, g1, w1, b1, g2, w2, b2, ga, wq, bq, wk, cols):
+    frame_count, p_out, c = own.shape
     vm = pl.BlockSpec(memory_space=pltpu.VMEM)
     return pl.pallas_call(
         functools.partial(block_kernel, cols, frame_count),
         out_shape=(jax.ShapeDtypeStruct((frame_count, p_out, c), jnp.float32),
                    jax.ShapeDtypeStruct((frame_count, p_out, c), jnp.bfloat16),
                    jax.ShapeDtypeStruct((frame_count, p_out, c), jnp.bfloat16)),
-        in_specs=[vm] * 13,
+        in_specs=[vm] * 14,
         out_specs=(vm, vm, vm),
-    )(seq, arrived, swapped, g1.reshape(1, c), w1.reshape(27, c, c), b1.reshape(1, c), g2.reshape(1, c),
+    )(own, partner, arrived, swapped, g1.reshape(1, c), w1.reshape(27, c, c), b1.reshape(1, c), g2.reshape(1, c),
       w2.reshape(27, c, c), b2.reshape(1, c), ga.reshape(1, c), wq, bq.reshape(1, c), wk)
 
 
@@ -175,7 +177,8 @@
 
     token_count = row_count * col_count
     residual, normed, folded = resnet_block(
-        seq.reshape(2 * frame_count, -1, channels),
+        own.reshape(frame_count, -1, channels),
+        partner.reshape(frame_count, -1, channels),
         arrived.reshape(2 * frame_count, -1, channels),
         swapped.reshape(2 * frame_count, -1, channels),
         norm1_gain,

time: 46.6 us -> 46.7 us (level)
  waiting for transfers between devices: 17.1 us -> 17.9 us
  other arithmetic: 2.49 us -> 1.73 us
    ppermute x1, waiting for transfers between devices: 0.72 us -> 1.49 us  [local(): swapped = lax.ppermute(arrived, 'tm', [(0, 1), (1, 0)])]
    another operation x1, other arithmetic: 0.76 us -> 0.02 us  [local(): jnp.stack([even, odd], axis=1)]
    unnamed x17 -> x21, local copies, waits for them, and re-layouts: 1.74 us -> 1.75 us
  transfers between devices with their start and end apart: 8 -> 8, of which waited for: 5 -> 5; matrix products, arithmetic and copies ran while one was open for 4% -> 3% of each run, Pallas kernels for 0% -> 0%
where the time goes in v18:
time: 46.7 us; the launch traced here: 46.5 us
  waiting for transfers between devices  17.9 us (38%)
  starting transfers between devices  14.5 us (31%)
  Pallas kernels  7.62 us (16%)
  local copies, waits for them, and re-layouts  2.56 us (5%)
  matrix products  2.02 us (4%)
  other arithmetic  1.73 us (4%)
    pallas_call x1, Pallas kernels, resnet_block(): pl.pallas_call(functools.partial(block_kernel, cols, frame_count), out_sh...  7.62 us
    ppermute x3, waiting for transfers between devices, local(): lax.ppermute(normed, 'outer', [(i, (i + k) % spans) for i in range(spans)])  7.1 us
    ppermute x1, waiting for transfers between devices, local(): arrived = lax.ppermute(edge, ('outer', 'inner', 'tm'), up + down)  5.97 us
    ppermute x1, starting transfers between devices, local(): arrived = lax.ppermute(edge, ('outer', 'inner', 'tm'), up + down)  4.76 us
    ppermute x3, starting transfers between devices, local(): lax.ppermute(normed, 'outer', [(i, (i + k) % spans) for i in range(spans)])  4.62 us
    ppermute x1, starting transfers between devices, local(): partner_queries = lax.ppermute(folded, 'inner', swap)  2.48 us
    ppermute x1, waiting for transfers between devices, local(): returned = lax.ppermute(packed, 'inner', swap).astype(jnp.float32)  2.36 us
    ppermute x1, starting transfers between devices, local(): returned = lax.ppermute(packed, 'inner', swap).astype(jnp.float32)  2.13 us
  transfers between devices with their start and end apart: 8, of which 5 were waited for; matrix products, arithmetic and copies ran while one was open for 3% of the time, Pallas kernels for 0%

profile of v18, /device:TPU:0, one launch (start us, length us, event | category | flops | bytes accessed | tf_op | source)
XLA Modules:
  0.0 46.5 jit_solution(18312257142289539362)
XLA Ops:
  0.0 1.0 %copy.16 = bf16[1,1,2,112,192]{4,3,2,1,0:T(8,128)(2,1)S(1)} copy(bf16[1,1,2,112,192]{3,4,2,1,0:T(8,128)(2,1)} %param.15) | data formatting | bytes 172032 | tf_op args[0]
  1.0 0.0 copy-start.1
  1.0 0.5 %collective-permute-start = (bf16[1,2,112,192]{3,2,1,0:T(8,128)(2,1)S(1)}, bf16[1,2,112,192]{3,2,1,0:T(8,128)(2,1)S(1)}, u32[]{:S(2)}, u32[]{:S(2)}) collective-permute-start(bf16[1,2,112,192]{3,2,1,0:T(8,128)(2,1)S(1)} %bitcast.79), channel_id=1, source_target_pairs={{0,1},{1,0},{2,3},{3,2},{4,5},{5,4},{6,7},{7,6},{8,9},{9,8},{10,11... | collective-permute-start | bytes 258056 | tf_op jit(solution)/shard_map/ppermute | solution.py:167
  1.6 1.0 %collective-permute-done = bf16[1,2,112,192]{3,2,1,0:T(8,128)(2,1)S(1)} collective-permute-done((bf16[1,2,112,192]{3,2,1,0:T(8,128)(2,1)S(1)}, bf16[1,2,112,192]{3,2,1,0:T(8,128)(2,1)S(1)}, u32[]{:S(2)}, u32[]{:S(2)}) %collective-permute-start) | collective-permute-done | bytes 86048 | tf_op jit(solution)/shard_map/ppermute | solution.py:167
  2.6 4.8 %collective-permute-start.1 = (bf16[2,2,112,192]{3,2,1,0:T(8,128)(2,1)S(1)}, bf16[2,2,112,192]{3,2,1,0:T(8,128)(2,1)S(1)}, u32[]{:S(2)}, u32[]{:S(2)}) collective-permute-start(bf16[2,2,112,192]{3,2,1,0:T(8,128)(2,1)S(1)} %maximum_bitcast_fusion), channel_id=1, source_target_pairs={{0,2},{2,4},{4,6},{6,8},{8,10},{10,12},{12,14},{3,1},{5,3},{7,5},{... | collective-permute-start | bytes 516104 | tf_op jit(solution)/shard_map/ppermute | solution.py:175
  7.4 6.0 %collective-permute-done.1 = bf16[2,2,112,192]{3,2,1,0:T(8,128)(2,1)S(1)} collective-permute-done((bf16[2,2,112,192]{3,2,1,0:T(8,128)(2,1)S(1)}, bf16[2,2,112,192]{3,2,1,0:T(8,128)(2,1)S(1)}, u32[]{:S(2)}, u32[]{:S(2)}) %collective-permute-start.1) | collective-permute-done | bytes 172064 | tf_op jit(solution)/shard_map/ppermute | solution.py:175
  13.3 0.0 collective-permute-start.2
  13.3 1.5 %collective-permute-done.2 = bf16[2,2,112,192]{3,2,1,0:T(8,128)(2,1)S(1)} collective-permute-done((bf16[2,2,112,192]{3,2,1,0:T(8,128)(2,1)S(1)}, bf16[2,2,112,192]{3,2,1,0:T(8,128)(2,1)S(1)}, u32[]{:S(2)}, u32[]{:S(2)}) %collective-permute-start.2) | collective-permute-done | bytes 172064 | tf_op jit(solution)/shard_map/ppermute | solution.py:176
  14.8 0.7 %copy-done.5 = bf16[2,2,112,192]{3,2,1,0:T(8,128)(2,1)} copy-done((bf16[2,2,112,192]{3,2,1,0:T(8,128)(2,1)}, bf16[2,2,112,192]{3,2,1,0:T(8,128)(2,1)S(1)}, u32[]{:S(2)}) %copy-start.5) | copy-done | bytes 172056
  15.5 7.6 %shard_map.145 = (f32[1,224,192]{2,1,0:T(8,128)}, bf16[1,224,192]{2,1,0:T(8,128)(2,1)}, bf16[1,224,192]{2,1,0:T(8,128)(2,1)}) custom-call(bf16[1,224,192]{2,1,0:T(8,128)(2,1)} %bitcast.80, bf16[1,224,192]{2,1,0:T(8,128)(2,1)} %bitcast.82, bf16[2,224,192]{2,1,0:T(8,128)(2,1)} %bitcast.83, bf16[2,224,192]{2,1,0:T(8,128)(2,1)} %bitcast.84, f32[1,192]{1,0:T(1,128)} %bitcast.93, ...), custom_call_target="tpu_custom_call" | custom-call | tf_op jit(solution)/shard_map/pallas_call | solution.py:131
  23.1 3.2 %collective-permute-start.5 = (bf16[1,2,112,192]{3,2,1,0:T(8,128)(2,1)}, bf16[1,2,112,192]{3,2,1,0:T(8,128)(2,1)S(1)}, u32[]{:S(2)}, u32[]{:S(2)}) collective-permute-start(bf16[1,2,112,192]{3,2,1,0:T(8,128)(2,1)} %bitcast.85), channel_id=1, source_target_pairs={{0,12},{4,0},{8,4},{12,8},{1,13},{5,1},{9,5},{13,9},{2,14},{6,2},{... | collective-permute-start | bytes 258056 | tf_op jit(solution)/shard_map/ppermute | solution.py:204
  26.4 0.0 collective-permute-start.4
  26.4 1.4 %collective-permute-start.3 = (bf16[1,2,112,192]{3,2,1,0:T(8,128)(2,1)}, bf16[1,2,112,192]{3,2,1,0:T(8,128)(2,1)S(1)}, u32[]{:S(2)}, u32[]{:S(2)}) collective-permute-start(bf16[1,2,112,192]{3,2,1,0:T(8,128)(2,1)} %bitcast.87), channel_id=1, source_target_pairs={{0,4},{4,8},{8,12},{12,0},{1,5},{5,9},{9,13},{13,1},{2,6},{6,10},{... | collective-permute-start | bytes 258056 | tf_op jit(solution)/shard_map/ppermute | solution.py:204
  27.8 2.5 %collective-permute-start.6 = (bf16[1,224,192]{2,1,0:T(8,128)(2,1)}, bf16[1,224,192]{2,1,0:T(8,128)(2,1)S(1)}, u32[]{:S(2)}, u32[]{:S(2)}) collective-permute-start(bf16[1,224,192]{2,1,0:T(8,128)(2,1)} %get-tuple-element.9), channel_id=1, source_target_pairs={{0,2},{2,0},{1,3},{3,1},{4,6},{6,4},{5,7},{7,5},{8,10},{10,8},{9,1... | collective-permute-start | bytes 258056 | tf_op jit(solution)/shard_map/ppermute | solution.py:200
  30.2 0.0 collective-permute-done.5
  30.2 7.1 %collective-permute-done.4 = bf16[1,2,112,192]{3,2,1,0:T(8,128)(2,1)S(1)} collective-permute-done((bf16[1,2,112,192]{3,2,1,0:T(8,128)(2,1)}, bf16[1,2,112,192]{3,2,1,0:T(8,128)(2,1)S(1)}, u32[]{:S(2)}, u32[]{:S(2)}) %collective-permute-start.4) | collective-permute-done | bytes 86048 | tf_op jit(solution)/shard_map/ppermute | solution.py:204
  37.3 0.0 collective-permute-done.3
  37.3 1.0 %pad_maximum_fusion = bf16[1,8,112,192]{3,2,1,0:T(8,128)(2,1)S(1)} fusion(bf16[1,2,112,192]{3,2,1,0:T(8,128)(2,1)S(1)} %collective-permute-done.5, bf16[1,2,112,192]{3,2,1,0:T(8,128)(2,1)S(1)} %collective-permute-done.4, bf16[1,2,112,192]{3,2,1,0:T(8,128)(2,1)S(1)} %collective-permute-done.3, bf16[1,2,112,192]{3,2,1,0:T(8,128)(2,1)} %bitcast.88), kind=kLoop, calls=%fused_computation.17 | loop fusion | flops 516096 | bytes 688128 | tf_op jit(solution)/shard_map/concatenate | solution.py:207
  38.3 0.0 collective-permute-done.6
  38.4 0.4 fusion.34
  38.8 0.3 fusion.10
  39.1 0.0 copy-start.7
  39.1 0.0 copy-start.8
  39.1 0.4 fusion.7
  39.5 0.0 copy-start.9
  39.5 0.4 fusion.33
  40.0 2.1 %collective-permute-start.7 = (bf16[1,224,198]{1,2,0:T(8,128)(2,1)S(1)}, bf16[1,224,198]{1,2,0:T(8,128)(2,1)S(1)}, u32[]{:S(2)}, u32[]{:S(2)}) collective-permute-start(bf16[1,224,198]{1,2,0:T(8,128)(2,1)S(1)} %pad_maximum_fusion.1), channel_id=1, source_target_pairs={{0,2},{2,0},{1,3},{3,1},{4,6},{6,4},{5,7},{7,5},{8,10},{10,8},{9,1... | collective-permute-start | bytes 266120 | tf_op jit(solution)/shard_map/ppermute | solution.py:229
  42.2 0.3 fusion.8
  42.4 2.4 %collective-permute-done.7 = bf16[1,224,198]{1,2,0:T(8,128)(2,1)S(1)} collective-permute-done((bf16[1,224,198]{1,2,0:T(8,128)(2,1)S(1)}, bf16[1,224,198]{1,2,0:T(8,128)(2,1)S(1)}, u32[]{:S(2)}, u32[]{:S(2)}) %collective-permute-start.7) | collective-permute-done | bytes 88736 | tf_op jit(solution)/shard_map/ppermute | solution.py:229
  44.9 0.4 fusion.6
  45.3 0.3 fusion.5
  45.7 0.8 %copy.18 = f32[1,1,2,112,192]{3,4,2,1,0:T(8,128)} copy(f32[1,1,2,112,192]{4,3,2,1,0:T(8,128)S(1)} %bitcast.81) | data formatting | bytes 344064 | tf_op jit(solution)/shard_map/reshape | solution.py:250
  (23 shorter events, 0.2 us)
Async XLA Ops:
  0.0 45.3 %copy-start = (bf16[192,192]{1,0:T(8,128)(2,1)S(1)}, bf16[192,192]{1,0:T(8,128)(2,1)}, u32[]{:S(2)}) copy-start(bf16[192,192]{1,0:T(8,128)(2,1)} %param.28) | copy-start | bytes 221188
  1.0 13.8 %copy-start.1 = (bf16[1,1,2,112,192]{4,3,2,1,0:T(8,128)(2,1)}, bf16[1,1,2,112,192]{4,3,2,1,0:T(8,128)(2,1)S(1)}, u32[]{:S(2)}) copy-start(bf16[1,1,2,112,192]{4,3,2,1,0:T(8,128)(2,1)S(1)} %copy.16) | copy-start | bytes 258052
  1.0 1.5 %collective-permute-start = (bf16[1,2,112,192]{3,2,1,0:T(8,128)(2,1)S(1)}, bf16[1,2,112,192]{3,2,1,0:T(8,128)(2,1)S(1)}, u32[]{:S(2)}, u32[]{:S(2)}) collective-permute-start(bf16[1,2,112,192]{3,2,1,0:T(8,128)(2,1)S(1)} %bitcast.79), channel_id=1, source_target_pairs={{0,1},{1,0},{2,3},{3,2},{4,5},{5,4},{6,7},{7,6},{8,9},{9,8},{10,11... | collective-permute-start | bytes 258056 | tf_op jit(solution)/shard_map/ppermute | solution.py:167
  2.5 12.3 %copy-start.2 = (bf16[1,2,112,192]{3,2,1,0:T(8,128)(2,1)}, bf16[1,2,112,192]{3,2,1,0:T(8,128)(2,1)S(1)}, u32[]{:S(2)}) copy-start(bf16[1,2,112,192]{3,2,1,0:T(8,128)(2,1)S(1)} %collective-permute-done) | copy-start | bytes 258052
  2.6 10.7 %collective-permute-start.1 = (bf16[2,2,112,192]{3,2,1,0:T(8,128)(2,1)S(1)}, bf16[2,2,112,192]{3,2,1,0:T(8,128)(2,1)S(1)}, u32[]{:S(2)}, u32[]{:S(2)}) collective-permute-start(bf16[2,2,112,192]{3,2,1,0:T(8,128)(2,1)S(1)} %maximum_bitcast_fusion), channel_id=1, source_target_pairs={{0,2},{2,4},{4,6},{6,8},{8,10},{10,12},{12,14},{3,1},{5,3},{7,5},{... | collective-permute-start | bytes 516104 | tf_op jit(solution)/shard_map/ppermute | solution.py:175
  13.3 1.5 %copy-start.4 = (bf16[2,2,112,192]{3,2,1,0:T(8,128)(2,1)}, bf16[2,2,112,192]{3,2,1,0:T(8,128)(2,1)S(1)}, u32[]{:S(2)}) copy-start(bf16[2,2,112,192]{3,2,1,0:T(8,128)(2,1)S(1)} %collective-permute-done.1) | copy-start | bytes 516100
  13.3 1.5 %collective-permute-start.2 = (bf16[2,2,112,192]{3,2,1,0:T(8,128)(2,1)S(1)}, bf16[2,2,112,192]{3,2,1,0:T(8,128)(2,1)S(1)}, u32[]{:S(2)}, u32[]{:S(2)}) collective-permute-start(bf16[2,2,112,192]{3,2,1,0:T(8,128)(2,1)S(1)} %collective-permute-done.1), channel_id=1, source_target_pairs={{0,1},{1,0},{2,3},{3,2},{4,5},{5,4},{6,7},{7,6},{8,9},{9,8},{10,11... | collective-permute-start | bytes 516104 | tf_op jit(solution)/shard_map/ppermute | solution.py:176
  14.8 0.7 %copy-start.5 = (bf16[2,2,112,192]{3,2,1,0:T(8,128)(2,1)}, bf16[2,2,112,192]{3,2,1,0:T(8,128)(2,1)S(1)}, u32[]{:S(2)}) copy-start(bf16[2,2,112,192]{3,2,1,0:T(8,128)(2,1)S(1)} %collective-permute-done.2) | copy-start | bytes 516100
  23.1 16.4 %copy-start.6 = (bf16[1,224,192]{2,1,0:T(8,128)(2,1)S(1)}, bf16[1,224,192]{2,1,0:T(8,128)(2,1)}, u32[]{:S(2)}) copy-start(bf16[1,224,192]{2,1,0:T(8,128)(2,1)} %get-tuple-element.9) | copy-start | bytes 258052
  23.1 7.1 %collective-permute-start.5 = (bf16[1,2,112,192]{3,2,1,0:T(8,128)(2,1)}, bf16[1,2,112,192]{3,2,1,0:T(8,128)(2,1)S(1)}, u32[]{:S(2)}, u32[]{:S(2)}) collective-permute-start(bf16[1,2,112,192]{3,2,1,0:T(8,128)(2,1)} %bitcast.85), channel_id=1, source_target_pairs={{0,12},{4,0},{8,4},{12,8},{1,13},{5,1},{9,5},{13,9},{2,14},{6,2},{... | collective-permute-start | bytes 258056 | tf_op jit(solution)/shard_map/ppermute | solution.py:204
  26.4 11.0 %collective-permute-start.4 = (bf16[1,2,112,192]{3,2,1,0:T(8,128)(2,1)}, bf16[1,2,112,192]{3,2,1,0:T(8,128)(2,1)S(1)}, u32[]{:S(2)}, u32[]{:S(2)}) collective-permute-start(bf16[1,2,112,192]{3,2,1,0:T(8,128)(2,1)} %bitcast.86), channel_id=1, source_target_pairs={{0,8},{4,12},{8,0},{12,4},{1,9},{5,13},{9,1},{13,5},{2,10},{6,14},... | collective-permute-start | bytes 258056 | tf_op jit(solution)/shard_map/ppermute | solution.py:204
  26.4 11.0 %collective-permute-start.3 = (bf16[1,2,112,192]{3,2,1,0:T(8,128)(2,1)}, bf16[1,2,112,192]{3,2,1,0:T(8,128)(2,1)S(1)}, u32[]{:S(2)}, u32[]{:S(2)}) collective-permute-start(bf16[1,2,112,192]{3,2,1,0:T(8,128)(2,1)} %bitcast.87), channel_id=1, source_target_pairs={{0,4},{4,8},{8,12},{12,0},{1,5},{5,9},{9,13},{13,1},{2,6},{6,10},{... | collective-permute-start | bytes 258056 | tf_op jit(solution)/shard_map/ppermute | solution.py:204
  27.8 10.6 %collective-permute-start.6 = (bf16[1,224,192]{2,1,0:T(8,128)(2,1)}, bf16[1,224,192]{2,1,0:T(8,128)(2,1)S(1)}, u32[]{:S(2)}, u32[]{:S(2)}) collective-permute-start(bf16[1,224,192]{2,1,0:T(8,128)(2,1)} %get-tuple-element.9), channel_id=1, source_target_pairs={{0,2},{2,0},{1,3},{3,1},{4,6},{6,4},{5,7},{7,5},{8,10},{10,8},{9,1... | collective-permute-start | bytes 258056 | tf_op jit(solution)/shard_map/ppermute | solution.py:200
  39.1 6.2 %copy-start.7 = (bf16[192,192]{1,0:T(8,128)(2,1)S(1)}, bf16[192,192]{1,0:T(8,128)(2,1)}, u32[]{:S(2)}) copy-start(bf16[192,192]{1,0:T(8,128)(2,1)} %param.26) | copy-start | bytes 221188
  39.1 6.2 %copy-start.8 = (f32[192]{0:T(256)S(1)}, f32[192]{0:T(256)}, u32[]{:S(2)}) copy-start(f32[192]{0:T(256)} %param.27) | copy-start | bytes 2308
  39.5 6.1 %copy-start.3 = (f32[1,224,192]{2,1,0:T(8,128)S(1)}, f32[1,224,192]{2,1,0:T(8,128)}, u32[]{:S(2)}) copy-start(f32[1,224,192]{2,1,0:T(8,128)} %get-tuple-element.8) | copy-start | bytes 516100
  39.5 6.1 %copy-start.9 = (f32[192]{0:T(256)S(1)}, f32[192]{0:T(256)}, u32[]{:S(2)}) copy-start(f32[192]{0:T(256)} %param.29) | copy-start | bytes 2308
  40.0 4.8 %collective-permute-start.7 = (bf16[1,224,198]{1,2,0:T(8,128)(2,1)S(1)}, bf16[1,224,198]{1,2,0:T(8,128)(2,1)S(1)}, u32[]{:S(2)}, u32[]{:S(2)}) collective-permute-start(bf16[1,224,198]{1,2,0:T(8,128)(2,1)S(1)} %pad_maximum_fusion.1), channel_id=1, source_target_pairs={{0,2},{2,0},{1,3},{3,1},{4,6},{6,4},{5,7},{7,5},{8,10},{10,8},{9,1... | collective-permute-start | bytes 266120 | tf_op jit(solution)/shard_map/ppermute | solution.py:229

commit v19 on v15

--- a/solution.py
+++ b/solution.py
@@ -239,11 +239,14 @@
     value = (jnp.dot(mixed, w_value, preferred_element_type=jnp.float32) + b_value).astype(
         jnp.bfloat16
     )
+    shape = (frame_count * row_count, col_count, channels)
+    projected = jnp.einsum(
+        "rwc,cd->rdw", value.reshape(shape), w_out, preferred_element_type=jnp.float32
+    )
     decoded = (
-        residual.reshape(-1, channels)
-        + jnp.dot(value, w_out, preferred_element_type=jnp.float32)
-        + b_out
-    )
+        jnp.swapaxes(residual.reshape(shape), 1, 2) + projected + b_out[None, :, None]
+    )
+    decoded = jnp.swapaxes(decoded, 1, 2)
     return decoded.reshape(frame_count, 1, row_count, col_count, channels)
 
 

time: 46.6 us -> 46.8 us (level)
  waiting for transfers between devices: 17.1 us -> 16 us
  other arithmetic: 2.49 us -> 3.23 us
    ppermute x3, waiting for transfers between devices: 7.1 us -> 5.96 us  [local(): lax.ppermute(normed, 'outer', [(i, (i + k) % spans) for i in range(spans)])]
    reshape x0 -> x1, other arithmetic: none -> 0.78 us  [local(): return decoded.reshape(frame_count, 1, row_count, col_count, channels)]
    dot_general x1 -> x2, matrix products: 0.35 us -> 0.84 us  [the longest x1 0.61 us: local(): jnp.dot(mixed, w_value, preferred_element_type=jnp.float32) + b_value]
    reshape x1 -> x2, local copies, waits for them, and re-layouts: 0.81 us -> 1.17 us  [the longest x1 1.07 us: local(): residual.reshape(shape)]
    unnamed x17 -> x15, local copies, waits for them, and re-layouts: 1.74 us -> 1.73 us
  transfers between devices with their start and end apart: 8 -> 8, of which waited for: 5 -> 5; matrix products, arithmetic and copies ran while one was open for 4% -> 7% of each run, Pallas kernels for 0% -> 0%
where the time goes in v19:
time: 46.8 us; the launch traced here: 46.6 us
  waiting for transfers between devices  16 us (34%)
  starting transfers between devices  14.6 us (31%)
  Pallas kernels  7.59 us (16%)
  other arithmetic  3.23 us (7%)
  local copies, waits for them, and re-layouts  2.9 us (6%)
  matrix products  2.1 us (4%)
    pallas_call x1, Pallas kernels, resnet_block(): pl.pallas_call(functools.partial(block_kernel, cols, frame_count), out_sh...  7.59 us
    ppermute x1, waiting for transfers between devices, local(): arrived = lax.ppermute(edge, ('outer', 'inner', 'tm'), up + down)  5.97 us
    ppermute x3, waiting for transfers between devices, local(): lax.ppermute(normed, 'outer', [(i, (i + k) % spans) for i in range(spans)])  5.96 us
    ppermute x1, starting transfers between devices, local(): arrived = lax.ppermute(edge, ('outer', 'inner', 'tm'), up + down)  4.76 us
    ppermute x3, starting transfers between devices, local(): lax.ppermute(normed, 'outer', [(i, (i + k) % spans) for i in range(spans)])  4.61 us
    ppermute x1, starting transfers between devices, local(): partner_queries = lax.ppermute(folded, 'inner', swap)  2.55 us
    ppermute x1, waiting for transfers between devices, local(): returned = lax.ppermute(packed, 'inner', swap).astype(jnp.float32)  2.36 us
    ppermute x1, starting transfers between devices, local(): returned = lax.ppermute(packed, 'inner', swap).astype(jnp.float32)  2.14 us
  transfers between devices with their start and end apart: 8, of which 5 were waited for; matrix products, arithmetic and copies ran while one was open for 7% of the time, Pallas kernels for 0%

profile of v19, /device:TPU:0, one launch (start us, length us, event | category | flops | bytes accessed | tf_op | source)
XLA Modules:
  0.0 46.6 jit_solution(3980850176144797065)
XLA Ops:
  0.0 1.0 %copy.16 = bf16[1,1,2,112,192]{4,3,2,1,0:T(8,128)(2,1)S(1)} copy(bf16[1,1,2,112,192]{3,4,2,1,0:T(8,128)(2,1)} %param.15) | data formatting | bytes 172032 | tf_op args[0]
  1.0 0.5 %collective-permute-start = (bf16[1,2,112,192]{3,2,1,0:T(8,128)(2,1)S(1)}, bf16[1,2,112,192]{3,2,1,0:T(8,128)(2,1)S(1)}, u32[]{:S(2)}, u32[]{:S(2)}) collective-permute-start(bf16[1,2,112,192]{3,2,1,0:T(8,128)(2,1)S(1)} %bitcast.85), channel_id=1, source_target_pairs={{0,1},{1,0},{2,3},{3,2},{4,5},{5,4},{6,7},{7,6},{8,9},{9,8},{10,11... | collective-permute-start | bytes 258056 | tf_op jit(solution)/shard_map/ppermute | solution.py:165
  1.6 1.0 %collective-permute-done = bf16[1,2,112,192]{3,2,1,0:T(8,128)(2,1)S(1)} collective-permute-done((bf16[1,2,112,192]{3,2,1,0:T(8,128)(2,1)S(1)}, bf16[1,2,112,192]{3,2,1,0:T(8,128)(2,1)S(1)}, u32[]{:S(2)}, u32[]{:S(2)}) %collective-permute-start) | collective-permute-done | bytes 86048 | tf_op jit(solution)/shard_map/ppermute | solution.py:165
  2.6 4.8 %collective-permute-start.1 = (bf16[2,2,112,192]{3,2,1,0:T(8,128)(2,1)S(1)}, bf16[2,2,112,192]{3,2,1,0:T(8,128)(2,1)S(1)}, u32[]{:S(2)}, u32[]{:S(2)}) collective-permute-start(bf16[2,2,112,192]{3,2,1,0:T(8,128)(2,1)S(1)} %maximum_bitcast_fusion), channel_id=1, source_target_pairs={{0,2},{2,4},{4,6},{6,8},{8,10},{10,12},{12,14},{3,1},{5,3},{7,5},{... | collective-permute-start | bytes 516104 | tf_op jit(solution)/shard_map/ppermute | solution.py:173
  7.4 6.0 %collective-permute-done.1 = bf16[2,2,112,192]{3,2,1,0:T(8,128)(2,1)S(1)} collective-permute-done((bf16[2,2,112,192]{3,2,1,0:T(8,128)(2,1)S(1)}, bf16[2,2,112,192]{3,2,1,0:T(8,128)(2,1)S(1)}, u32[]{:S(2)}, u32[]{:S(2)}) %collective-permute-start.1) | collective-permute-done | bytes 172064 | tf_op jit(solution)/shard_map/ppermute | solution.py:173
  13.3 0.8 %pad_maximum_fusion.1.seq_ref = bf16[2,224,192]{2,1,0:T(8,128)(2,1)} fusion(bf16[1,224,192]{2,1,0:T(8,128)(2,1)S(1)} %bitcast.84, bf16[1,224,192]{2,1,0:T(8,128)(2,1)S(1)} %bitcast.82), kind=kLoop, calls=%fused_computation.19 | loop fusion | flops 86016 | bytes 344064 | tf_op jit(solution)/shard_map/stack | solution.py:168
  14.1 0.7 %collective-permute-done.2 = bf16[2,2,112,192]{3,2,1,0:T(8,128)(2,1)S(1)} collective-permute-done((bf16[2,2,112,192]{3,2,1,0:T(8,128)(2,1)S(1)}, bf16[2,2,112,192]{3,2,1,0:T(8,128)(2,1)S(1)}, u32[]{:S(2)}, u32[]{:S(2)}) %collective-permute-start.2) | collective-permute-done | bytes 172064 | tf_op jit(solution)/shard_map/ppermute | solution.py:174
  14.8 0.7 %copy-done.2 = bf16[2,2,112,192]{3,2,1,0:T(8,128)(2,1)} copy-done((bf16[2,2,112,192]{3,2,1,0:T(8,128)(2,1)}, bf16[2,2,112,192]{3,2,1,0:T(8,128)(2,1)S(1)}, u32[]{:S(2)}) %copy-start.2) | copy-done | bytes 172056
  15.5 7.6 %shard_map.145 = (f32[1,224,192]{2,1,0:T(8,128)}, bf16[1,224,192]{2,1,0:T(8,128)(2,1)}, bf16[1,224,192]{2,1,0:T(8,128)(2,1)}) custom-call(bf16[2,224,192]{2,1,0:T(8,128)(2,1)} %pad_maximum_fusion.1.seq_ref, bf16[2,224,192]{2,1,0:T(8,128)(2,1)} %bitcast.87, bf16[2,224,192]{2,1,0:T(8,128)(2,1)} %bitcast.88, f32[1,192]{1,0:T(1,128)} %bitcast.97, ...), custom_call_target="tpu_custom_call" | custom-call | tf_op jit(solution)/shard_map/pallas_call | solution.py:129
  23.1 3.2 %collective-permute-start.5 = (bf16[1,2,112,192]{3,2,1,0:T(8,128)(2,1)}, bf16[1,2,112,192]{3,2,1,0:T(8,128)(2,1)S(1)}, u32[]{:S(2)}, u32[]{:S(2)}) collective-permute-start(bf16[1,2,112,192]{3,2,1,0:T(8,128)(2,1)} %bitcast.89), channel_id=1, source_target_pairs={{0,12},{4,0},{8,4},{12,8},{1,13},{5,1},{9,5},{13,9},{2,14},{6,2},{... | collective-permute-start | bytes 258056 | tf_op jit(solution)/shard_map/ppermute | solution.py:201
  26.3 0.0 collective-permute-start.4
  26.3 1.4 %collective-permute-start.3 = (bf16[1,2,112,192]{3,2,1,0:T(8,128)(2,1)}, bf16[1,2,112,192]{3,2,1,0:T(8,128)(2,1)S(1)}, u32[]{:S(2)}, u32[]{:S(2)}) collective-permute-start(bf16[1,2,112,192]{3,2,1,0:T(8,128)(2,1)} %bitcast.91), channel_id=1, source_target_pairs={{0,4},{4,8},{8,12},{12,0},{1,5},{5,9},{9,13},{13,1},{2,6},{6,10},{... | collective-permute-start | bytes 258056 | tf_op jit(solution)/shard_map/ppermute | solution.py:201
  27.7 1.1 %copy.19 = f32[2,112,192]{1,2,0:T(8,128)S(1)} copy(f32[2,112,192]{2,1,0:T(8,128)} %bitcast.86) | data formatting | bytes 344064 | tf_op jit(solution)/shard_map/reshape | solution.py:247
  28.8 2.5 %collective-permute-start.6 = (bf16[1,224,192]{2,1,0:T(8,128)(2,1)}, bf16[1,224,192]{2,1,0:T(8,128)(2,1)S(1)}, u32[]{:S(2)}, u32[]{:S(2)}) collective-permute-start(bf16[1,224,192]{2,1,0:T(8,128)(2,1)} %get-tuple-element.9), channel_id=1, source_target_pairs={{0,2},{2,0},{1,3},{3,1},{4,6},{6,4},{5,7},{7,5},{8,10},{10,8},{9,1... | collective-permute-start | bytes 258056 | tf_op jit(solution)/shard_map/ppermute | solution.py:197
  31.3 6.0 %collective-permute-done.4 = bf16[1,2,112,192]{3,2,1,0:T(8,128)(2,1)S(1)} collective-permute-done((bf16[1,2,112,192]{3,2,1,0:T(8,128)(2,1)}, bf16[1,2,112,192]{3,2,1,0:T(8,128)(2,1)S(1)}, u32[]{:S(2)}, u32[]{:S(2)}) %collective-permute-start.4) | collective-permute-done | bytes 86048 | tf_op jit(solution)/shard_map/ppermute | solution.py:201
  37.3 0.0 collective-permute-done.3
  37.3 1.0 %pad_maximum_fusion = bf16[1,8,112,192]{3,2,1,0:T(8,128)(2,1)S(1)} fusion(bf16[1,2,112,192]{3,2,1,0:T(8,128)(2,1)S(1)} %collective-permute-done.5, bf16[1,2,112,192]{3,2,1,0:T(8,128)(2,1)S(1)} %collective-permute-done.4, bf16[1,2,112,192]{3,2,1,0:T(8,128)(2,1)S(1)} %collective-permute-done.3, bf16[1,2,112,192]{3,2,1,0:T(8,128)(2,1)} %bitcast.92), kind=kLoop, calls=%fused_computation.16 | loop fusion | flops 516096 | bytes 688128 | tf_op jit(solution)/shard_map/concatenate | solution.py:204
  38.3 0.0 collective-permute-done.6
  38.3 0.4 fusion.39
  38.7 0.0 copy-start.6
  38.7 0.3 fusion.9
  39.0 0.4 fusion.6
  39.4 0.0 copy-start.4
  39.4 0.0 copy-start.5
  39.5 0.4 fusion.38
  39.9 2.1 %collective-permute-start.7 = (bf16[1,224,198]{1,2,0:T(8,128)(2,1)S(1)}, bf16[1,224,198]{1,2,0:T(8,128)(2,1)S(1)}, u32[]{:S(2)}, u32[]{:S(2)}) collective-permute-start(bf16[1,224,198]{1,2,0:T(8,128)(2,1)S(1)} %pad_maximum_fusion.2), channel_id=1, source_target_pairs={{0,2},{2,0},{1,3},{3,1},{4,6},{6,4},{5,7},{7,5},{8,10},{10,8},{9,1... | collective-permute-start | bytes 266120 | tf_op jit(solution)/shard_map/ppermute | solution.py:226
  42.1 0.3 fusion.7
  42.4 2.4 %collective-permute-done.7 = bf16[1,224,198]{1,2,0:T(8,128)(2,1)S(1)} collective-permute-done((bf16[1,224,198]{1,2,0:T(8,128)(2,1)S(1)}, bf16[1,224,198]{1,2,0:T(8,128)(2,1)S(1)}, u32[]{:S(2)}, u32[]{:S(2)}) %collective-permute-start.7) | collective-permute-done | bytes 88736 | tf_op jit(solution)/shard_map/ppermute | solution.py:226
  44.8 0.6 %fusion.4 = bf16[224,192]{0,1:T(8,128)(2,1)S(1)} fusion(bf16[192,192]{1,0:T(8,128)(2,1)S(1)} %copy-done, bf16[896,192]{1,0:T(8,128)(2,1)S(1)} %bitcast.78, f32[224,896]{1,0:T(8,128)S(1)} %get-tuple-element.20, f32[224]{0:T(256)S(1)} %get-tuple-element.19, f32[1,224,198]{1,2,0:T(8,128)S(1)} %convert_element_type.28, f32[192]{0:T(256)S(1)} %copy-done.6, ...), kind=kOutput, calls=%fused_computation.6 | convolution fusion | flops 94287872 | bytes 1647616 | tf_op jit(solution)/shard_map/dot_general | solution.py:239
  45.4 0.1 reshape.296
  45.5 0.2 fusion.21
  45.8 0.8 %add_bitcast_fusion = f32[1,1,2,112,192]{3,4,2,1,0:T(8,128)} fusion(f32[2,112,192]{1,2,0:T(8,128)S(1)} %copy.19, f32[2,112,192]{1,2,0:T(8,128)S(1)} %fusion.21, f32[192]{0:T(256)S(1)} %copy-done.5), kind=kLoop, calls=%fused_computation.22 | loop fusion | flops 86016 | bytes 516864 | tf_op jit(solution)/shard_map/reshape | solution.py:250
  (19 shorter events, 0.2 us)
Async XLA Ops:
  0.0 44.8 %copy-start = (bf16[192,192]{1,0:T(8,128)(2,1)S(1)}, bf16[192,192]{1,0:T(8,128)(2,1)}, u32[]{:S(2)}) copy-start(bf16[192,192]{1,0:T(8,128)(2,1)} %param.26) | copy-start | bytes 221188
  1.0 1.5 %collective-permute-start = (bf16[1,2,112,192]{3,2,1,0:T(8,128)(2,1)S(1)}, bf16[1,2,112,192]{3,2,1,0:T(8,128)(2,1)S(1)}, u32[]{:S(2)}, u32[]{:S(2)}) collective-permute-start(bf16[1,2,112,192]{3,2,1,0:T(8,128)(2,1)S(1)} %bitcast.85), channel_id=1, source_target_pairs={{0,1},{1,0},{2,3},{3,2},{4,5},{5,4},{6,7},{7,6},{8,9},{9,8},{10,11... | collective-permute-start | bytes 258056 | tf_op jit(solution)/shard_map/ppermute | solution.py:165
  2.6 10.7 %collective-permute-start.1 = (bf16[2,2,112,192]{3,2,1,0:T(8,128)(2,1)S(1)}, bf16[2,2,112,192]{3,2,1,0:T(8,128)(2,1)S(1)}, u32[]{:S(2)}, u32[]{:S(2)}) collective-permute-start(bf16[2,2,112,192]{3,2,1,0:T(8,128)(2,1)S(1)} %maximum_bitcast_fusion), channel_id=1, source_target_pairs={{0,2},{2,4},{4,6},{6,8},{8,10},{10,12},{12,14},{3,1},{5,3},{7,5},{... | collective-permute-start | bytes 516104 | tf_op jit(solution)/shard_map/ppermute | solution.py:173
  13.3 1.5 %copy-start.1 = (bf16[2,2,112,192]{3,2,1,0:T(8,128)(2,1)}, bf16[2,2,112,192]{3,2,1,0:T(8,128)(2,1)S(1)}, u32[]{:S(2)}) copy-start(bf16[2,2,112,192]{3,2,1,0:T(8,128)(2,1)S(1)} %collective-permute-done.1) | copy-start | bytes 516100
  13.3 1.5 %collective-permute-start.2 = (bf16[2,2,112,192]{3,2,1,0:T(8,128)(2,1)S(1)}, bf16[2,2,112,192]{3,2,1,0:T(8,128)(2,1)S(1)}, u32[]{:S(2)}, u32[]{:S(2)}) collective-permute-start(bf16[2,2,112,192]{3,2,1,0:T(8,128)(2,1)S(1)} %collective-permute-done.1), channel_id=1, source_target_pairs={{0,1},{1,0},{2,3},{3,2},{4,5},{5,4},{6,7},{7,6},{8,9},{9,8},{10,11... | collective-permute-start | bytes 516104 | tf_op jit(solution)/shard_map/ppermute | solution.py:174
  14.8 0.7 %copy-start.2 = (bf16[2,2,112,192]{3,2,1,0:T(8,128)(2,1)}, bf16[2,2,112,192]{3,2,1,0:T(8,128)(2,1)S(1)}, u32[]{:S(2)}) copy-start(bf16[2,2,112,192]{3,2,1,0:T(8,128)(2,1)S(1)} %collective-permute-done.2) | copy-start | bytes 516100
  23.1 16.3 %copy-start.3 = (bf16[1,224,192]{2,1,0:T(8,128)(2,1)S(1)}, bf16[1,224,192]{2,1,0:T(8,128)(2,1)}, u32[]{:S(2)}) copy-start(bf16[1,224,192]{2,1,0:T(8,128)(2,1)} %get-tuple-element.9) | copy-start | bytes 258052
  23.1 8.2 %collective-permute-start.5 = (bf16[1,2,112,192]{3,2,1,0:T(8,128)(2,1)}, bf16[1,2,112,192]{3,2,1,0:T(8,128)(2,1)S(1)}, u32[]{:S(2)}, u32[]{:S(2)}) collective-permute-start(bf16[1,2,112,192]{3,2,1,0:T(8,128)(2,1)} %bitcast.89), channel_id=1, source_target_pairs={{0,12},{4,0},{8,4},{12,8},{1,13},{5,1},{9,5},{13,9},{2,14},{6,2},{... | collective-permute-start | bytes 258056 | tf_op jit(solution)/shard_map/ppermute | solution.py:201
  26.3 11.0 %collective-permute-start.4 = (bf16[1,2,112,192]{3,2,1,0:T(8,128)(2,1)}, bf16[1,2,112,192]{3,2,1,0:T(8,128)(2,1)S(1)}, u32[]{:S(2)}, u32[]{:S(2)}) collective-permute-start(bf16[1,2,112,192]{3,2,1,0:T(8,128)(2,1)} %bitcast.90), channel_id=1, source_target_pairs={{0,8},{4,12},{8,0},{12,4},{1,9},{5,13},{9,1},{13,5},{2,10},{6,14},... | collective-permute-start | bytes 258056 | tf_op jit(solution)/shard_map/ppermute | solution.py:201
  26.3 11.0 %collective-permute-start.3 = (bf16[1,2,112,192]{3,2,1,0:T(8,128)(2,1)}, bf16[1,2,112,192]{3,2,1,0:T(8,128)(2,1)S(1)}, u32[]{:S(2)}, u32[]{:S(2)}) collective-permute-start(bf16[1,2,112,192]{3,2,1,0:T(8,128)(2,1)} %bitcast.91), channel_id=1, source_target_pairs={{0,4},{4,8},{8,12},{12,0},{1,5},{5,9},{9,13},{13,1},{2,6},{6,10},{... | collective-permute-start | bytes 258056 | tf_op jit(solution)/shard_map/ppermute | solution.py:201
  28.8 9.5 %collective-permute-start.6 = (bf16[1,224,192]{2,1,0:T(8,128)(2,1)}, bf16[1,224,192]{2,1,0:T(8,128)(2,1)S(1)}, u32[]{:S(2)}, u32[]{:S(2)}) collective-permute-start(bf16[1,224,192]{2,1,0:T(8,128)(2,1)} %get-tuple-element.9), channel_id=1, source_target_pairs={{0,2},{2,0},{1,3},{3,1},{4,6},{6,4},{5,7},{7,5},{8,10},{10,8},{9,1... | collective-permute-start | bytes 258056 | tf_op jit(solution)/shard_map/ppermute | solution.py:197
  38.7 6.1 %copy-start.6 = (f32[192]{0:T(256)S(1)}, f32[192]{0:T(256)}, u32[]{:S(2)}) copy-start(f32[192]{0:T(256)} %param.27) | copy-start | bytes 2308
  39.4 6.1 %copy-start.4 = (bf16[192,192]{1,0:T(8,128)(2,1)S(1)}, bf16[192,192]{1,0:T(8,128)(2,1)}, u32[]{:S(2)}) copy-start(bf16[192,192]{1,0:T(8,128)(2,1)} %param.28) | copy-start | bytes 221188
  39.4 6.3 %copy-start.5 = (f32[192]{0:T(256)S(1)}, f32[192]{0:T(256)}, u32[]{:S(2)}) copy-start(f32[192]{0:T(256)} %param.29) | copy-start | bytes 2308
  39.9 4.8 %collective-permute-start.7 = (bf16[1,224,198]{1,2,0:T(8,128)(2,1)S(1)}, bf16[1,224,198]{1,2,0:T(8,128)(2,1)S(1)}, u32[]{:S(2)}, u32[]{:S(2)}) collective-permute-start(bf16[1,224,198]{1,2,0:T(8,128)(2,1)S(1)} %pad_maximum_fusion.2), channel_id=1, source_target_pairs={{0,2},{2,0},{1,3},{3,1},{4,6},{6,4},{5,7},{7,5},{8,10},{10,8},{9,1... | collective-permute-start | bytes 266120 | tf_op jit(solution)/shard_map/ppermute | solution.py:226
